TPU v7x, 32 devices: a whole 2x2x4 slice. The times are simulated.
32 devices in a mesh: gx: 4 (over y, x), gy: 8 (over z, core).
Axes of the slice: x: 2, y: 2, z: 4, core: 2. Of those that a mesh axis runs over, the one named last changes fastest.
Arguments:
- basis: float32 [4, 8, 3, 32, 192], P('gx', 'gy'), may hold values from -6 to 6
- coupling: bfloat16 [4, 8, 81, 192, 192], P('gx', 'gy'), as said below
- cpl_dst: int32 [4, 8, 81], P('gx', 'gy'), may hold values from 0 to 3, as said below
- cpl_src: int32 [4, 8, 81], P('gx', 'gy'), may hold values from 0 to 26, as said below
Outputs:
- subspace: float32 [4, 8, 3, 32, 192], P('gx', 'gy')
Inputs may be any that keep to these rules, and one draw needn't show every extreme that they name: `cpl_dst`: on each column the live slots come first; a live slot holds its target block's height 0 to 2, every later slot holds 3. The columns at gx index 0 have all 81 slots live. `cpl_src`: A live slot holds (3 dx + dy) * 3 + z for a source block in the column at offsets dx - 1, dy - 1 (periodic) and height z, within one height of the target block, periodically; each source block and column offset appears at most once per target; empty slots hold 0. `coupling`: the assembled matrix is symmetric: for every live slot that couples block i to block j there is a live slot on j's column that couples j to i and holds the transposed block.
All inputs are finite; a program needn't handle non-finite values.
Results may differ from a plain program's by a relative error of at most 0.0085.
Values may be sent and summed in bfloat16 or wider, within the bound.
No kernel may reach another device: no remote copies, remote signals or barrier semaphores. Data moves between devices by JAX's collectives and lax.ppermute only.
A program may use at most 64 MiB of HBM per device.

v0:
```python
import math

import jax
import jax.numpy as jnp
from jax import lax
from jax.sharding import PartitionSpec as P

DEGREE = 8
STEPS = 2


CENTER = 5.0
HALF = 3.0
LOWEST = 0.5


def with_halo(cells, sides, width):
    for axis, dim in sides:
        count = lax.axis_size(axis)
        head = lax.slice_in_dim(cells, 0, width, axis=dim)
        tail = lax.slice_in_dim(cells, cells.shape[dim] - width, cells.shape[dim], axis=dim)
        cells = jnp.concatenate(
            [
                lax.ppermute(tail, axis, [(i, (i + 1) % count) for i in range(count)]),
                cells,
                lax.ppermute(head, axis, [((i + 1) % count, i) for i in range(count)]),
            ],
            axis=dim,
        )
    return cells


def dense_coupling(matrices, targets, sources, depth, order):
    slots = matrices.shape[0]
    cells = len(order)
    match = (targets[:, None, None] == jnp.arange(depth, dtype=jnp.int32)[None, :, None]) & (
        sources[:, None, None] == jnp.array(order, dtype=jnp.int32)[None, None, :]
    )
    select = match.reshape(slots, depth * cells).astype(matrices.dtype)
    blocks = jnp.einsum("sc,sij->cij", select, matrices, preferred_element_type=jnp.float32)
    return blocks.astype(matrices.dtype).reshape(depth, cells, matrices.shape[1], matrices.shape[2])


def all_sum(value, axes):
    for axis in axes:
        count = lax.axis_size(axis)
        if count & (count - 1):
            value = lax.psum(value, axis)
            continue
        stride = 1
        while stride < count:
            value = value + lax.ppermute(value, axis, [(i, i ^ stride) for i in range(count)])
            stride *= 2
    return value


def orthonormal(filtered, rows_total):
    partial_gram = jnp.einsum(
        "zvd,zwd->vw", filtered, filtered, precision=lax.Precision.HIGHEST
    )
    gram_matrix = all_sum(partial_gram, ("gx", "gy"))
    factor = jnp.linalg.cholesky(gram_matrix)
    identity = jnp.eye(filtered.shape[1], dtype=jnp.float32)
    inverse = jax.scipy.linalg.solve_triangular(factor, identity, lower=True)
    result = jnp.einsum("vw,zwd->zvd", inverse, filtered, precision=lax.Precision.HIGHEST)
    return result * math.sqrt(rows_total)


def local(basis, coupling, cpl_dst, cpl_src):
    column_depth = basis.shape[2]
    vector_count = basis.shape[3]
    block_rows = basis.shape[4]
    rows_total = lax.axis_size("gx") * lax.axis_size("gy") * column_depth * block_rows
    columns = [(1, 1), (0, 1), (2, 1)] + [(dx, 0) for dx in range(3)] + [(dx, 2) for dx in range(3)]
    order = [(3 * dx + dy) * column_depth + z for dx, dy in columns for z in range(column_depth)]
    dense = dense_coupling(coupling[0, 0], cpl_dst[0, 0], cpl_src[0, 0], column_depth, order)
    dense_own = dense[:, :column_depth]
    dense_side = dense[:, column_depth:3 * column_depth]
    dense_low = dense[:, 3 * column_depth:6 * column_depth]
    dense_high = dense[:, 6 * column_depth:]

    def shift(value, axis, step):
        count = lax.axis_size(axis)
        return lax.ppermute(value, axis, [(i, (i + step) % count) for i in range(count)])

    def part(cells, blocks):
        return jnp.einsum("kvj,tkij->tvi", cells, blocks, preferred_element_type=jnp.float32)

    def apply_operator(current):
        rounded = current.astype(jnp.bfloat16)
        left = shift(rounded, "gx", 1)
        right = shift(rounded, "gx", -1)
        image = part(rounded, dense_own)
        strip = jnp.stack([left, rounded, right])
        low = shift(strip, "gy", 1)
        high = shift(strip, "gy", -1)
        image = image + part(jnp.concatenate([left, right]), dense_side)
        image = image + part(low.reshape(3 * column_depth, vector_count, block_rows), dense_low)
        return image + part(high.reshape(3 * column_depth, vector_count, block_rows), dense_high)

    sigma_one = HALF / (LOWEST - CENTER)
    current_basis = basis[0, 0]
    for outer in range(STEPS):
        previous = current_basis
        current = sigma_one / HALF * (apply_operator(previous) - CENTER * previous)
        sigma_now = sigma_one
        for inner in range(1, DEGREE):
            sigma_next = 1.0 / (2.0 / sigma_one - sigma_now)
            image = apply_operator(current)
            following = (
                2.0 * sigma_next / HALF * (image - CENTER * current)
                - sigma_now * sigma_next * previous
            )
            previous, current, sigma_now = (current, following, sigma_next)
        current_basis = orthonormal(current, rows_total)
    return current_basis[None, None]


def solution(mesh):
    placed = (
        P("gx", "gy", None, None, None),
        P("gx", "gy", None, None, None),
        P("gx", "gy", None),
        P("gx", "gy", None),
    )
    return jax.shard_map(
        local,
        mesh=mesh,
        in_specs=placed,
        out_specs=P("gx", "gy", None, None, None),
        check_vma=False,
    )
```

profile of v0, /device:TPU:0, one launch (start us, length us, event | category | flops | bytes accessed | tf_op | source)
XLA Modules:
  0.0 293.2 jit_solution(14770806020265728597)
XLA Ops:
  0.9 3.0 %collective-permute-start = (bf16[3,32,192]{2,1,0:T(8,128)(2,1)S(1)}, bf16[3,32,192]{2,1,0:T(8,128)(2,1)S(1)}, u32[]{:S(2)}, u32[]{:S(2)}) collective-permute-start(bf16[3,32,192]{2,1,0:T(8,128)(2,1)S(1)} %get-tuple-element.16), channel_id=1, source_target_pairs={{0,8},{8,16},{16,24},{24,0},{1,9},{9,17},{17,25},{25,1},{2,10},{10... | collective-permute-start | bytes 110600 | tf_op jit(solution)/shard_map/ppermute | solution.py:84
  6.4 12.9 %fusion.2 = bf16[81,192,192]{2,0,1:T(8,128)(2,1)} fusion(pred[81,81,1]{0,1,2:T(8,128)(4,1)S(1)} %reshape.228, bf16[81,192,192]{2,1,0:T(8,128)(2,1)} %bitcast.975), kind=kOutput, calls=%fused_computation.2 | convolution fusion | flops 486715392 | bytes 11950497 | tf_op jit(solution)/shard_map/sc,sij->cij/dot_general | solution.py:40
  19.3 5.4 %copy.18 = bf16[81,192,192]{2,1,0:T(8,128)(2,1)S(1)} copy(bf16[81,192,192]{2,0,1:T(8,128)(2,1)} %fusion.2) | data formatting | bytes 11943936 | tf_op jit(solution)/shard_map/convert_element_type | solution.py:41
  25.1 2.9 %collective-permute-start.3 = (bf16[3,3,32,192]{3,2,1,0:T(8,128)(2,1)S(1)}, bf16[3,3,32,192]{3,2,1,0:T(8,128)(2,1)S(1)}, u32[]{:S(2)}, u32[]{:S(2)}) collective-permute-start(bf16[3,3,32,192]{3,2,1,0:T(8,128)(2,1)S(1)} %pad_maximum_fusion), channel_id=1, source_target_pairs={{0,7},{1,0},{2,1},{3,2},{4,3},{5,4},{6,5},{7,6},{8,15},{9,8},{10,9... | collective-permute-start | bytes 331784 | tf_op jit(solution)/shard_map/ppermute | solution.py:84
  28.7 2.3 collective-permute-done.3
  31.8 2.6 collective-permute-done.2
  36.0 2.3 collective-permute-start.5
  38.7 1.7 collective-permute-done.4
  42.9 2.3 collective-permute-done.7
  46.0 2.6 collective-permute-done.6
  52.9 1.7 collective-permute-done.8
  56.5 2.6 collective-permute-done.11
  60.0 2.3 collective-permute-done.10
  70.0 2.8 collective-permute-done.15
  73.7 2.1 collective-permute-done.14
  83.7 2.8 collective-permute-done.19
  87.4 2.1 collective-permute-done.18
  90.4 1.9 collective-permute-start.20
  93.7 1.7 collective-permute-done.20
  97.9 2.6 collective-permute-done.23
  101.4 2.3 collective-permute-done.22
  111.7 2.4 collective-permute-done.27
  115.0 2.5 collective-permute-done.26
  119.4 2.0 collective-permute-start.29
  125.1 2.6 collective-permute-done.31
  128.5 2.3 collective-permute-done.30
  133.5 2.3 collective-permute-done.32
  137.0 2.6 collective-permute-done.33
  140.8 3.7 %collective-permute-done.35 = f32[32,32]{0,1:T(8,128)S(1)} collective-permute-done((f32[32,32]{0,1:T(8,128)S(1)}, f32[32,32]{0,1:T(8,128)S(1)}, u32[]{:S(2)}, u32[]{:S(2)}) %collective-permute-start.35) | collective-permute-done | bytes 4128 | tf_op jit(solution)/shard_map/ppermute | solution.py:52
  144.5 4.6 %collective-permute-done.36 = f32[32,32]{0,1:T(8,128)S(1)} collective-permute-done((f32[32,32]{0,1:T(8,128)S(1)}, f32[32,32]{0,1:T(8,128)S(1)}, u32[]{:S(2)}, u32[]{:S(2)}) %collective-permute-start.36) | collective-permute-done | bytes 4128 | tf_op jit(solution)/shard_map/ppermute | solution.py:52
  149.2 2.9 cholesky.44
  153.5 2.4 custom-call.6
  162.6 2.1 fusion.103
  166.1 2.6 convolution_bitcast_fusion.14
  169.8 2.2 collective-permute-start.41
  173.1 1.7 collective-permute-done.41
  176.1 2.6 collective-permute-start.44
  179.3 2.1 collective-permute-done.44
  182.2 2.8 collective-permute-done.43
  187.2 1.8 collective-permute-start.46
  189.4 1.7 collective-permute-done.45
  192.5 2.9 %collective-permute-done.48 = bf16[3,3,32,192]{3,2,1,0:T(8,128)(2,1)S(1)} collective-permute-done((bf16[3,3,32,192]{3,2,1,0:T(8,128)(2,1)S(1)}, bf16[3,3,32,192]{3,2,1,0:T(8,128)(2,1)S(1)}, u32[]{:S(2)}, u32[]{:S(2)}) %collective-permute-start.48) | collective-permute-done | bytes 110624 | tf_op jit(solution)/shard_map/ppermute | solution.py:84
  198.8 2.1 collective-permute-start.49
  206.5 2.6 collective-permute-done.52
  210.0 2.3 collective-permute-done.51
  216.6 1.7 collective-permute-done.53
  220.0 2.9 %collective-permute-done.56 = bf16[3,3,32,192]{3,2,1,0:T(8,128)(2,1)S(1)} collective-permute-done((bf16[3,3,32,192]{3,2,1,0:T(8,128)(2,1)S(1)}, bf16[3,3,32,192]{3,2,1,0:T(8,128)(2,1)S(1)}, u32[]{:S(2)}, u32[]{:S(2)}) %collective-permute-start.56) | collective-permute-done | bytes 110624 | tf_op jit(solution)/shard_map/ppermute | solution.py:84
  223.8 1.7 collective-permute-done.55
  226.5 1.9 collective-permute-start.57
  229.9 1.7 collective-permute-done.57
  234.0 2.6 collective-permute-done.60
  237.5 2.3 collective-permute-done.59
  244.1 1.7 collective-permute-done.61
  247.5 2.9 %collective-permute-done.64 = bf16[3,3,32,192]{3,2,1,0:T(8,128)(2,1)S(1)} collective-permute-done((bf16[3,3,32,192]{3,2,1,0:T(8,128)(2,1)S(1)}, bf16[3,3,32,192]{3,2,1,0:T(8,128)(2,1)S(1)}, u32[]{:S(2)}, u32[]{:S(2)}) %collective-permute-start.64) | collective-permute-done | bytes 110624 | tf_op jit(solution)/shard_map/ppermute | solution.py:84
  251.3 1.8 collective-permute-done.63
  257.4 1.7 collective-permute-done.65
  261.2 2.6 collective-permute-done.68
  264.7 2.3 collective-permute-done.67
  269.7 2.3 collective-permute-done.69
  273.1 2.6 collective-permute-done.70
  276.9 3.7 %collective-permute-done.72 = f32[32,32]{0,1:T(8,128)S(1)} collective-permute-done((f32[32,32]{0,1:T(8,128)S(1)}, f32[32,32]{0,1:T(8,128)S(1)}, u32[]{:S(2)}, u32[]{:S(2)}) %collective-permute-start.72) | collective-permute-done | bytes 4128 | tf_op jit(solution)/shard_map/ppermute | solution.py:52
  280.6 4.6 %collective-permute-done.73 = f32[32,32]{0,1:T(8,128)S(1)} collective-permute-done((f32[32,32]{0,1:T(8,128)S(1)}, f32[32,32]{0,1:T(8,128)S(1)}, u32[]{:S(2)}, u32[]{:S(2)}) %collective-permute-start.73) | collective-permute-done | bytes 4128 | tf_op jit(solution)/shard_map/ppermute | solution.py:52
  285.3 2.9 cholesky.55
  289.6 2.4 custom-call.7
  (211 shorter events, 124.0 us)
Async XLA Ops:
  0.9 24.1 %collective-permute-start = (bf16[3,32,192]{2,1,0:T(8,128)(2,1)S(1)}, bf16[3,32,192]{2,1,0:T(8,128)(2,1)S(1)}, u32[]{:S(2)}, u32[]{:S(2)}) collective-permute-start(bf16[3,32,192]{2,1,0:T(8,128)(2,1)S(1)} %get-tuple-element.16), channel_id=1, source_target_pairs={{0,8},{8,16},{16,24},{24,0},{1,9},{9,17},{17,25},{25,1},{2,10},{10... | collective-permute-start | bytes 110600 | tf_op jit(solution)/shard_map/ppermute | solution.py:84
  3.9 21.2 %collective-permute-start.1 = (bf16[3,32,192]{2,1,0:T(8,128)(2,1)S(1)}, bf16[3,32,192]{2,1,0:T(8,128)(2,1)S(1)}, u32[]{:S(2)}, u32[]{:S(2)}) collective-permute-start(bf16[3,32,192]{2,1,0:T(8,128)(2,1)S(1)} %get-tuple-element.16), channel_id=1, source_target_pairs={{0,24},{8,0},{16,8},{24,16},{1,25},{9,1},{17,9},{25,17},{2,26},{10... | collective-permute-start | bytes 110600 | tf_op jit(solution)/shard_map/ppermute | solution.py:84
  25.1 5.8 %collective-permute-start.3 = (bf16[3,3,32,192]{3,2,1,0:T(8,128)(2,1)S(1)}, bf16[3,3,32,192]{3,2,1,0:T(8,128)(2,1)S(1)}, u32[]{:S(2)}, u32[]{:S(2)}) collective-permute-start(bf16[3,3,32,192]{3,2,1,0:T(8,128)(2,1)S(1)} %pad_maximum_fusion), channel_id=1, source_target_pairs={{0,7},{1,0},{2,1},{3,2},{4,3},{5,4},{6,5},{7,6},{8,15},{9,8},{10,9... | collective-permute-start | bytes 331784 | tf_op jit(solution)/shard_map/ppermute | solution.py:84
  28.1 6.4 %collective-permute-start.2 = (bf16[3,3,32,192]{3,2,1,0:T(8,128)(2,1)S(1)}, bf16[3,3,32,192]{3,2,1,0:T(8,128)(2,1)S(1)}, u32[]{:S(2)}, u32[]{:S(2)}) collective-permute-start(bf16[3,3,32,192]{3,2,1,0:T(8,128)(2,1)S(1)} %pad_maximum_fusion), channel_id=1, source_target_pairs={{0,1},{1,2},{2,3},{3,4},{4,5},{5,6},{6,7},{7,0},{8,9},{9,10},{10,1... | collective-permute-start | bytes 331784 | tf_op jit(solution)/shard_map/ppermute | solution.py:84
  35.4 5.0 %collective-permute-start.4 = (bf16[3,32,192]{2,1,0:T(8,128)(2,1)S(1)}, bf16[3,32,192]{2,1,0:T(8,128)(2,1)S(1)}, u32[]{:S(2)}, u32[]{:S(2)}) collective-permute-start(bf16[3,32,192]{2,1,0:T(8,128)(2,1)S(1)} %get-tuple-element.17), channel_id=1, source_target_pairs={{0,8},{8,16},{16,24},{24,0},{1,9},{9,17},{17,25},{25,1},{2,10},{10... | collective-permute-start | bytes 110600 | tf_op jit(solution)/shard_map/ppermute | solution.py:84
  36.0 5.0 %collective-permute-start.5 = (bf16[3,32,192]{2,1,0:T(8,128)(2,1)S(1)}, bf16[3,32,192]{2,1,0:T(8,128)(2,1)S(1)}, u32[]{:S(2)}, u32[]{:S(2)}) collective-permute-start(bf16[3,32,192]{2,1,0:T(8,128)(2,1)S(1)} %get-tuple-element.17), channel_id=1, source_target_pairs={{0,24},{8,0},{16,8},{24,16},{1,25},{9,1},{17,9},{25,17},{2,26},{10... | collective-permute-start | bytes 110600 | tf_op jit(solution)/shard_map/ppermute | solution.py:84
  41.0 4.1 %collective-permute-start.7 = (bf16[3,3,32,192]{3,2,1,0:T(8,128)(2,1)S(1)}, bf16[3,3,32,192]{3,2,1,0:T(8,128)(2,1)S(1)}, u32[]{:S(2)}, u32[]{:S(2)}) collective-permute-start(bf16[3,3,32,192]{3,2,1,0:T(8,128)(2,1)S(1)} %pad_maximum_fusion.1), channel_id=1, source_target_pairs={{0,7},{1,0},{2,1},{3,2},{4,3},{5,4},{6,5},{7,6},{8,15},{9,8},{10,9... | collective-permute-start | bytes 331784 | tf_op jit(solution)/shard_map/ppermute | solution.py:84
  42.2 6.4 %collective-permute-start.6 = (bf16[3,3,32,192]{3,2,1,0:T(8,128)(2,1)S(1)}, bf16[3,3,32,192]{3,2,1,0:T(8,128)(2,1)S(1)}, u32[]{:S(2)}, u32[]{:S(2)}) collective-permute-start(bf16[3,3,32,192]{3,2,1,0:T(8,128)(2,1)S(1)} %pad_maximum_fusion.1), channel_id=1, source_target_pairs={{0,1},{1,2},{2,3},{3,4},{4,5},{5,6},{6,7},{7,0},{8,9},{9,10},{10,1... | collective-permute-start | bytes 331784 | tf_op jit(solution)/shard_map/ppermute | solution.py:84
  49.6 5.0 %collective-permute-start.8 = (bf16[3,32,192]{2,1,0:T(8,128)(2,1)S(1)}, bf16[3,32,192]{2,1,0:T(8,128)(2,1)S(1)}, u32[]{:S(2)}, u32[]{:S(2)}) collective-permute-start(bf16[3,32,192]{2,1,0:T(8,128)(2,1)S(1)} %get-tuple-element.19), channel_id=1, source_target_pairs={{0,8},{8,16},{16,24},{24,0},{1,9},{9,17},{17,25},{25,1},{2,10},{10... | collective-permute-start | bytes 110600 | tf_op jit(solution)/shard_map/ppermute | solution.py:84
  50.9 4.1 %collective-permute-start.9 = (bf16[3,32,192]{2,1,0:T(8,128)(2,1)S(1)}, bf16[3,32,192]{2,1,0:T(8,128)(2,1)S(1)}, u32[]{:S(2)}, u32[]{:S(2)}) collective-permute-start(bf16[3,32,192]{2,1,0:T(8,128)(2,1)S(1)} %get-tuple-element.19), channel_id=1, source_target_pairs={{0,24},{8,0},{16,8},{24,16},{1,25},{9,1},{17,9},{25,17},{2,26},{10... | collective-permute-start | bytes 110600 | tf_op jit(solution)/shard_map/ppermute | solution.py:84
  55.0 4.1 %collective-permute-start.11 = (bf16[3,3,32,192]{3,2,1,0:T(8,128)(2,1)S(1)}, bf16[3,3,32,192]{3,2,1,0:T(8,128)(2,1)S(1)}, u32[]{:S(2)}, u32[]{:S(2)}) collective-permute-start(bf16[3,3,32,192]{3,2,1,0:T(8,128)(2,1)S(1)} %pad_maximum_fusion.2), channel_id=1, source_target_pairs={{0,7},{1,0},{2,1},{3,2},{4,3},{5,4},{6,5},{7,6},{8,15},{9,8},{10,9... | collective-permute-start | bytes 331784 | tf_op jit(solution)/shard_map/ppermute | solution.py:84
  55.9 6.4 %collective-permute-start.10 = (bf16[3,3,32,192]{3,2,1,0:T(8,128)(2,1)S(1)}, bf16[3,3,32,192]{3,2,1,0:T(8,128)(2,1)S(1)}, u32[]{:S(2)}, u32[]{:S(2)}) collective-permute-start(bf16[3,3,32,192]{3,2,1,0:T(8,128)(2,1)S(1)} %pad_maximum_fusion.2), channel_id=1, source_target_pairs={{0,1},{1,2},{2,3},{3,4},{4,5},{5,6},{6,7},{7,0},{8,9},{9,10},{10,1... | collective-permute-start | bytes 331784 | tf_op jit(solution)/shard_map/ppermute | solution.py:84
  63.2 5.0 %collective-permute-start.12 = (bf16[3,32,192]{2,1,0:T(8,128)(2,1)S(1)}, bf16[3,32,192]{2,1,0:T(8,128)(2,1)S(1)}, u32[]{:S(2)}, u32[]{:S(2)}) collective-permute-start(bf16[3,32,192]{2,1,0:T(8,128)(2,1)S(1)} %get-tuple-element.21), channel_id=1, source_target_pairs={{0,8},{8,16},{16,24},{24,0},{1,9},{9,17},{17,25},{25,1},{2,10},{10... | collective-permute-start | bytes 110600 | tf_op jit(solution)/shard_map/ppermute | solution.py:84
  64.5 4.1 %collective-permute-start.13 = (bf16[3,32,192]{2,1,0:T(8,128)(2,1)S(1)}, bf16[3,32,192]{2,1,0:T(8,128)(2,1)S(1)}, u32[]{:S(2)}, u32[]{:S(2)}) collective-permute-start(bf16[3,32,192]{2,1,0:T(8,128)(2,1)S(1)} %get-tuple-element.21), channel_id=1, source_target_pairs={{0,24},{8,0},{16,8},{24,16},{1,25},{9,1},{17,9},{25,17},{2,26},{10... | collective-permute-start | bytes 110600 | tf_op jit(solution)/shard_map/ppermute | solution.py:84
  68.6 4.1 %collective-permute-start.15 = (bf16[3,3,32,192]{3,2,1,0:T(8,128)(2,1)S(1)}, bf16[3,3,32,192]{3,2,1,0:T(8,128)(2,1)S(1)}, u32[]{:S(2)}, u32[]{:S(2)}) collective-permute-start(bf16[3,3,32,192]{3,2,1,0:T(8,128)(2,1)S(1)} %pad_maximum_fusion.3), channel_id=1, source_target_pairs={{0,7},{1,0},{2,1},{3,2},{4,3},{5,4},{6,5},{7,6},{8,15},{9,8},{10,9... | collective-permute-start | bytes 331784 | tf_op jit(solution)/shard_map/ppermute | solution.py:84
  69.4 6.4 %collective-permute-start.14 = (bf16[3,3,32,192]{3,2,1,0:T(8,128)(2,1)S(1)}, bf16[3,3,32,192]{3,2,1,0:T(8,128)(2,1)S(1)}, u32[]{:S(2)}, u32[]{:S(2)}) collective-permute-start(bf16[3,3,32,192]{3,2,1,0:T(8,128)(2,1)S(1)} %pad_maximum_fusion.3), channel_id=1, source_target_pairs={{0,1},{1,2},{2,3},{3,4},{4,5},{5,6},{6,7},{7,0},{8,9},{9,10},{10,1... | collective-permute-start | bytes 331784 | tf_op jit(solution)/shard_map/ppermute | solution.py:84
  76.7 5.0 %collective-permute-start.16 = (bf16[3,32,192]{2,1,0:T(8,128)(2,1)S(1)}, bf16[3,32,192]{2,1,0:T(8,128)(2,1)S(1)}, u32[]{:S(2)}, u32[]{:S(2)}) collective-permute-start(bf16[3,32,192]{2,1,0:T(8,128)(2,1)S(1)} %get-tuple-element.23), channel_id=1, source_target_pairs={{0,8},{8,16},{16,24},{24,0},{1,9},{9,17},{17,25},{25,1},{2,10},{10... | collective-permute-start | bytes 110600 | tf_op jit(solution)/shard_map/ppermute | solution.py:84
  78.2 4.1 %collective-permute-start.17 = (bf16[3,32,192]{2,1,0:T(8,128)(2,1)S(1)}, bf16[3,32,192]{2,1,0:T(8,128)(2,1)S(1)}, u32[]{:S(2)}, u32[]{:S(2)}) collective-permute-start(bf16[3,32,192]{2,1,0:T(8,128)(2,1)S(1)} %get-tuple-element.23), channel_id=1, source_target_pairs={{0,24},{8,0},{16,8},{24,16},{1,25},{9,1},{17,9},{25,17},{2,26},{10... | collective-permute-start | bytes 110600 | tf_op jit(solution)/shard_map/ppermute | solution.py:84
  82.4 4.1 %collective-permute-start.19 = (bf16[3,3,32,192]{3,2,1,0:T(8,128)(2,1)S(1)}, bf16[3,3,32,192]{3,2,1,0:T(8,128)(2,1)S(1)}, u32[]{:S(2)}, u32[]{:S(2)}) collective-permute-start(bf16[3,3,32,192]{3,2,1,0:T(8,128)(2,1)S(1)} %pad_maximum_fusion.4), channel_id=1, source_target_pairs={{0,7},{1,0},{2,1},{3,2},{4,3},{5,4},{6,5},{7,6},{8,15},{9,8},{10,9... | collective-permute-start | bytes 331784 | tf_op jit(solution)/shard_map/ppermute | solution.py:84
  83.1 6.4 %collective-permute-start.18 = (bf16[3,3,32,192]{3,2,1,0:T(8,128)(2,1)S(1)}, bf16[3,3,32,192]{3,2,1,0:T(8,128)(2,1)S(1)}, u32[]{:S(2)}, u32[]{:S(2)}) collective-permute-start(bf16[3,3,32,192]{3,2,1,0:T(8,128)(2,1)S(1)} %pad_maximum_fusion.4), channel_id=1, source_target_pairs={{0,1},{1,2},{2,3},{3,4},{4,5},{5,6},{6,7},{7,0},{8,9},{9,10},{10,1... | collective-permute-start | bytes 331784 | tf_op jit(solution)/shard_map/ppermute | solution.py:84
  90.4 5.0 %collective-permute-start.20 = (bf16[3,32,192]{2,1,0:T(8,128)(2,1)S(1)}, bf16[3,32,192]{2,1,0:T(8,128)(2,1)S(1)}, u32[]{:S(2)}, u32[]{:S(2)}) collective-permute-start(bf16[3,32,192]{2,1,0:T(8,128)(2,1)S(1)} %get-tuple-element.25), channel_id=1, source_target_pairs={{0,8},{8,16},{16,24},{24,0},{1,9},{9,17},{17,25},{25,1},{2,10},{10... | collective-permute-start | bytes 110600 | tf_op jit(solution)/shard_map/ppermute | solution.py:84
  92.2 4.1 %collective-permute-start.21 = (bf16[3,32,192]{2,1,0:T(8,128)(2,1)S(1)}, bf16[3,32,192]{2,1,0:T(8,128)(2,1)S(1)}, u32[]{:S(2)}, u32[]{:S(2)}) collective-permute-start(bf16[3,32,192]{2,1,0:T(8,128)(2,1)S(1)} %get-tuple-element.25), channel_id=1, source_target_pairs={{0,24},{8,0},{16,8},{24,16},{1,25},{9,1},{17,9},{25,17},{2,26},{10... | collective-permute-start | bytes 110600 | tf_op jit(solution)/shard_map/ppermute | solution.py:84
  96.4 4.1 %collective-permute-start.23 = (bf16[3,3,32,192]{3,2,1,0:T(8,128)(2,1)S(1)}, bf16[3,3,32,192]{3,2,1,0:T(8,128)(2,1)S(1)}, u32[]{:S(2)}, u32[]{:S(2)}) collective-permute-start(bf16[3,3,32,192]{3,2,1,0:T(8,128)(2,1)S(1)} %pad_maximum_fusion.5), channel_id=1, source_target_pairs={{0,7},{1,0},{2,1},{3,2},{4,3},{5,4},{6,5},{7,6},{8,15},{9,8},{10,9... | collective-permute-start | bytes 331784 | tf_op jit(solution)/shard_map/ppermute | solution.py:84
  97.3 6.4 %collective-permute-start.22 = (bf16[3,3,32,192]{3,2,1,0:T(8,128)(2,1)S(1)}, bf16[3,3,32,192]{3,2,1,0:T(8,128)(2,1)S(1)}, u32[]{:S(2)}, u32[]{:S(2)}) collective-permute-start(bf16[3,3,32,192]{3,2,1,0:T(8,128)(2,1)S(1)} %pad_maximum_fusion.5), channel_id=1, source_target_pairs={{0,1},{1,2},{2,3},{3,4},{4,5},{5,6},{6,7},{7,0},{8,9},{9,10},{10,1... | collective-permute-start | bytes 331784 | tf_op jit(solution)/shard_map/ppermute | solution.py:84
  104.6 5.0 %collective-permute-start.24 = (bf16[3,32,192]{2,1,0:T(8,128)(2,1)S(1)}, bf16[3,32,192]{2,1,0:T(8,128)(2,1)S(1)}, u32[]{:S(2)}, u32[]{:S(2)}) collective-permute-start(bf16[3,32,192]{2,1,0:T(8,128)(2,1)S(1)} %get-tuple-element.27), channel_id=1, source_target_pairs={{0,8},{8,16},{16,24},{24,0},{1,9},{9,17},{17,25},{25,1},{2,10},{10... | collective-permute-start | bytes 110600 | tf_op jit(solution)/shard_map/ppermute | solution.py:84
  105.9 4.1 %collective-permute-start.25 = (bf16[3,32,192]{2,1,0:T(8,128)(2,1)S(1)}, bf16[3,32,192]{2,1,0:T(8,128)(2,1)S(1)}, u32[]{:S(2)}, u32[]{:S(2)}) collective-permute-start(bf16[3,32,192]{2,1,0:T(8,128)(2,1)S(1)} %get-tuple-element.27), channel_id=1, source_target_pairs={{0,24},{8,0},{16,8},{24,16},{1,25},{9,1},{17,9},{25,17},{2,26},{10... | collective-permute-start | bytes 110600 | tf_op jit(solution)/shard_map/ppermute | solution.py:84
  110.0 4.1 %collective-permute-start.27 = (bf16[3,3,32,192]{3,2,1,0:T(8,128)(2,1)S(1)}, bf16[3,3,32,192]{3,2,1,0:T(8,128)(2,1)S(1)}, u32[]{:S(2)}, u32[]{:S(2)}) collective-permute-start(bf16[3,3,32,192]{3,2,1,0:T(8,128)(2,1)S(1)} %pad_maximum_fusion.6), channel_id=1, source_target_pairs={{0,7},{1,0},{2,1},{3,2},{4,3},{5,4},{6,5},{7,6},{8,15},{9,8},{10,9... | collective-permute-start | bytes 331784 | tf_op jit(solution)/shard_map/ppermute | solution.py:84
  111.1 6.4 %collective-permute-start.26 = (bf16[3,3,32,192]{3,2,1,0:T(8,128)(2,1)S(1)}, bf16[3,3,32,192]{3,2,1,0:T(8,128)(2,1)S(1)}, u32[]{:S(2)}, u32[]{:S(2)}) collective-permute-start(bf16[3,3,32,192]{3,2,1,0:T(8,128)(2,1)S(1)} %pad_maximum_fusion.6), channel_id=1, source_target_pairs={{0,1},{1,2},{2,3},{3,4},{4,5},{5,6},{6,7},{7,0},{8,9},{9,10},{10,1... | collective-permute-start | bytes 331784 | tf_op jit(solution)/shard_map/ppermute | solution.py:84
  118.4 5.0 %collective-permute-start.28 = (bf16[3,32,192]{2,1,0:T(8,128)(2,1)S(1)}, bf16[3,32,192]{2,1,0:T(8,128)(2,1)S(1)}, u32[]{:S(2)}, u32[]{:S(2)}) collective-permute-start(bf16[3,32,192]{2,1,0:T(8,128)(2,1)S(1)} %get-tuple-element.29), channel_id=1, source_target_pairs={{0,8},{8,16},{16,24},{24,0},{1,9},{9,17},{17,25},{25,1},{2,10},{10... | collective-permute-start | bytes 110600 | tf_op jit(solution)/shard_map/ppermute | solution.py:84
  119.4 4.1 %collective-permute-start.29 = (bf16[3,32,192]{2,1,0:T(8,128)(2,1)S(1)}, bf16[3,32,192]{2,1,0:T(8,128)(2,1)S(1)}, u32[]{:S(2)}, u32[]{:S(2)}) collective-permute-start(bf16[3,32,192]{2,1,0:T(8,128)(2,1)S(1)} %get-tuple-element.29), channel_id=1, source_target_pairs={{0,24},{8,0},{16,8},{24,16},{1,25},{9,1},{17,9},{25,17},{2,26},{10... | collective-permute-start | bytes 110600 | tf_op jit(solution)/shard_map/ppermute | solution.py:84
  123.5 4.1 %collective-permute-start.31 = (bf16[3,3,32,192]{3,2,1,0:T(8,128)(2,1)S(1)}, bf16[3,3,32,192]{3,2,1,0:T(8,128)(2,1)S(1)}, u32[]{:S(2)}, u32[]{:S(2)}) collective-permute-start(bf16[3,3,32,192]{3,2,1,0:T(8,128)(2,1)S(1)} %pad_maximum_fusion.7), channel_id=1, source_target_pairs={{0,7},{1,0},{2,1},{3,2},{4,3},{5,4},{6,5},{7,6},{8,15},{9,8},{10,9... | collective-permute-start | bytes 331784 | tf_op jit(solution)/shard_map/ppermute | solution.py:84
  124.5 6.4 %collective-permute-start.30 = (bf16[3,3,32,192]{3,2,1,0:T(8,128)(2,1)S(1)}, bf16[3,3,32,192]{3,2,1,0:T(8,128)(2,1)S(1)}, u32[]{:S(2)}, u32[]{:S(2)}) collective-permute-start(bf16[3,3,32,192]{3,2,1,0:T(8,128)(2,1)S(1)} %pad_maximum_fusion.7), channel_id=1, source_target_pairs={{0,1},{1,2},{2,3},{3,4},{4,5},{5,6},{6,7},{7,0},{8,9},{9,10},{10,1... | collective-permute-start | bytes 331784 | tf_op jit(solution)/shard_map/ppermute | solution.py:84
  144.5 4.6 %collective-permute-start.36 = (f32[32,32]{0,1:T(8,128)S(1)}, f32[32,32]{0,1:T(8,128)S(1)}, u32[]{:S(2)}, u32[]{:S(2)}) collective-permute-start(f32[32,32]{0,1:T(8,128)S(1)} %add.296), channel_id=1, source_target_pairs={{0,4},{1,5},{2,6},{3,7},{4,0},{5,1},{6,2},{7,3},{8,12},{9,13},{10,... | collective-permute-start | bytes 12296 | tf_op jit(solution)/shard_map/ppermute | solution.py:52
  156.4 5.0 %collective-permute-start.37 = (bf16[3,32,192]{2,1,0:T(8,128)(2,1)S(1)}, bf16[3,32,192]{2,1,0:T(8,128)(2,1)S(1)}, u32[]{:S(2)}, u32[]{:S(2)}) collective-permute-start(bf16[3,32,192]{2,1,0:T(8,128)(2,1)S(1)} %get-tuple-element.14), channel_id=1, source_target_pairs={{0,8},{8,16},{16,24},{24,0},{1,9},{9,17},{17,25},{25,1},{2,10},{10... | collective-permute-start | bytes 110600 | tf_op jit(solution)/shard_map/ppermute | solution.py:84
  157.9 4.1 %collective-permute-start.38 = (bf16[3,32,192]{2,1,0:T(8,128)(2,1)S(1)}, bf16[3,32,192]{2,1,0:T(8,128)(2,1)S(1)}, u32[]{:S(2)}, u32[]{:S(2)}) collective-permute-start(bf16[3,32,192]{2,1,0:T(8,128)(2,1)S(1)} %get-tuple-element.14), channel_id=1, source_target_pairs={{0,24},{8,0},{16,8},{24,16},{1,25},{9,1},{17,9},{25,17},{2,26},{10... | collective-permute-start | bytes 110600 | tf_op jit(solution)/shard_map/ppermute | solution.py:84
  162.0 4.1 %collective-permute-start.40 = (bf16[3,3,32,192]{3,2,1,0:T(8,128)(2,1)S(1)}, bf16[3,3,32,192]{3,2,1,0:T(8,128)(2,1)S(1)}, u32[]{:S(2)}, u32[]{:S(2)}) collective-permute-start(bf16[3,3,32,192]{3,2,1,0:T(8,128)(2,1)S(1)} %pad_maximum_fusion.8), channel_id=1, source_target_pairs={{0,7},{1,0},{2,1},{3,2},{4,3},{5,4},{6,5},{7,6},{8,15},{9,8},{10,9... | collective-permute-start | bytes 331784 | tf_op jit(solution)/shard_map/ppermute | solution.py:84
  162.1 6.7 %collective-permute-start.39 = (bf16[3,3,32,192]{3,2,1,0:T(8,128)(2,1)S(1)}, bf16[3,3,32,192]{3,2,1,0:T(8,128)(2,1)S(1)}, u32[]{:S(2)}, u32[]{:S(2)}) collective-permute-start(bf16[3,3,32,192]{3,2,1,0:T(8,128)(2,1)S(1)} %pad_maximum_fusion.8), channel_id=1, source_target_pairs={{0,1},{1,2},{2,3},{3,4},{4,5},{5,6},{6,7},{7,0},{8,9},{9,10},{10,1... | collective-permute-start | bytes 331784 | tf_op jit(solution)/shard_map/ppermute | solution.py:84
  169.8 5.0 %collective-permute-start.41 = (bf16[3,32,192]{2,1,0:T(8,128)(2,1)S(1)}, bf16[3,32,192]{2,1,0:T(8,128)(2,1)S(1)}, u32[]{:S(2)}, u32[]{:S(2)}) collective-permute-start(bf16[3,32,192]{2,1,0:T(8,128)(2,1)S(1)} %get-tuple-element.12), channel_id=1, source_target_pairs={{0,8},{8,16},{16,24},{24,0},{1,9},{9,17},{17,25},{25,1},{2,10},{10... | collective-permute-start | bytes 110600 | tf_op jit(solution)/shard_map/ppermute | solution.py:84
  171.9 4.1 %collective-permute-start.42 = (bf16[3,32,192]{2,1,0:T(8,128)(2,1)S(1)}, bf16[3,32,192]{2,1,0:T(8,128)(2,1)S(1)}, u32[]{:S(2)}, u32[]{:S(2)}) collective-permute-start(bf16[3,32,192]{2,1,0:T(8,128)(2,1)S(1)} %get-tuple-element.12), channel_id=1, source_target_pairs={{0,24},{8,0},{16,8},{24,16},{1,25},{9,1},{17,9},{25,17},{2,26},{10... | collective-permute-start | bytes 110600 | tf_op jit(solution)/shard_map/ppermute | solution.py:84
  176.1 5.3 %collective-permute-start.44 = (bf16[3,3,32,192]{3,2,1,0:T(8,128)(2,1)S(1)}, bf16[3,3,32,192]{3,2,1,0:T(8,128)(2,1)S(1)}, u32[]{:S(2)}, u32[]{:S(2)}) collective-permute-start(bf16[3,3,32,192]{3,2,1,0:T(8,128)(2,1)S(1)} %pad_maximum_fusion.9), channel_id=1, source_target_pairs={{0,7},{1,0},{2,1},{3,2},{4,3},{5,4},{6,5},{7,6},{8,15},{9,8},{10,9... | collective-permute-start | bytes 331784 | tf_op jit(solution)/shard_map/ppermute | solution.py:84
  178.7 6.4 %collective-permute-start.43 = (bf16[3,3,32,192]{3,2,1,0:T(8,128)(2,1)S(1)}, bf16[3,3,32,192]{3,2,1,0:T(8,128)(2,1)S(1)}, u32[]{:S(2)}, u32[]{:S(2)}) collective-permute-start(bf16[3,3,32,192]{3,2,1,0:T(8,128)(2,1)S(1)} %pad_maximum_fusion.9), channel_id=1, source_target_pairs={{0,1},{1,2},{2,3},{3,4},{4,5},{5,6},{6,7},{7,0},{8,9},{9,10},{10,1... | collective-permute-start | bytes 331784 | tf_op jit(solution)/shard_map/ppermute | solution.py:84
  186.0 5.0 %collective-permute-start.45 = (bf16[3,32,192]{2,1,0:T(8,128)(2,1)S(1)}, bf16[3,32,192]{2,1,0:T(8,128)(2,1)S(1)}, u32[]{:S(2)}, u32[]{:S(2)}) collective-permute-start(bf16[3,32,192]{2,1,0:T(8,128)(2,1)S(1)} %get-tuple-element.10), channel_id=1, source_target_pairs={{0,8},{8,16},{16,24},{24,0},{1,9},{9,17},{17,25},{25,1},{2,10},{10... | collective-permute-start | bytes 110600 | tf_op jit(solution)/shard_map/ppermute | solution.py:84
  187.2 4.1 %collective-permute-start.46 = (bf16[3,32,192]{2,1,0:T(8,128)(2,1)S(1)}, bf16[3,32,192]{2,1,0:T(8,128)(2,1)S(1)}, u32[]{:S(2)}, u32[]{:S(2)}) collective-permute-start(bf16[3,32,192]{2,1,0:T(8,128)(2,1)S(1)} %get-tuple-element.10), channel_id=1, source_target_pairs={{0,24},{8,0},{16,8},{24,16},{1,25},{9,1},{17,9},{25,17},{2,26},{10... | collective-permute-start | bytes 110600 | tf_op jit(solution)/shard_map/ppermute | solution.py:84
  191.3 4.1 %collective-permute-start.48 = (bf16[3,3,32,192]{3,2,1,0:T(8,128)(2,1)S(1)}, bf16[3,3,32,192]{3,2,1,0:T(8,128)(2,1)S(1)}, u32[]{:S(2)}, u32[]{:S(2)}) collective-permute-start(bf16[3,3,32,192]{3,2,1,0:T(8,128)(2,1)S(1)} %pad_maximum_fusion.10), channel_id=1, source_target_pairs={{0,7},{1,0},{2,1},{3,2},{4,3},{5,4},{6,5},{7,6},{8,15},{9,8},{10,9... | collective-permute-start | bytes 331784 | tf_op jit(solution)/shard_map/ppermute | solution.py:84
  191.4 6.4 %collective-permute-start.47 = (bf16[3,3,32,192]{3,2,1,0:T(8,128)(2,1)S(1)}, bf16[3,3,32,192]{3,2,1,0:T(8,128)(2,1)S(1)}, u32[]{:S(2)}, u32[]{:S(2)}) collective-permute-start(bf16[3,3,32,192]{3,2,1,0:T(8,128)(2,1)S(1)} %pad_maximum_fusion.10), channel_id=1, source_target_pairs={{0,1},{1,2},{2,3},{3,4},{4,5},{5,6},{6,7},{7,0},{8,9},{9,10},{10,1... | collective-permute-start | bytes 331784 | tf_op jit(solution)/shard_map/ppermute | solution.py:84
  198.8 5.0 %collective-permute-start.49 = (bf16[3,32,192]{2,1,0:T(8,128)(2,1)S(1)}, bf16[3,32,192]{2,1,0:T(8,128)(2,1)S(1)}, u32[]{:S(2)}, u32[]{:S(2)}) collective-permute-start(bf16[3,32,192]{2,1,0:T(8,128)(2,1)S(1)} %get-tuple-element.8), channel_id=1, source_target_pairs={{0,8},{8,16},{16,24},{24,0},{1,9},{9,17},{17,25},{25,1},{2,10},{10... | collective-permute-start | bytes 110600 | tf_op jit(solution)/shard_map/ppermute | solution.py:84
  200.9 4.1 %collective-permute-start.50 = (bf16[3,32,192]{2,1,0:T(8,128)(2,1)S(1)}, bf16[3,32,192]{2,1,0:T(8,128)(2,1)S(1)}, u32[]{:S(2)}, u32[]{:S(2)}) collective-permute-start(bf16[3,32,192]{2,1,0:T(8,128)(2,1)S(1)} %get-tuple-element.8), channel_id=1, source_target_pairs={{0,24},{8,0},{16,8},{24,16},{1,25},{9,1},{17,9},{25,17},{2,26},{10... | collective-permute-start | bytes 110600 | tf_op jit(solution)/shard_map/ppermute | solution.py:84
  205.0 4.1 %collective-permute-start.52 = (bf16[3,3,32,192]{3,2,1,0:T(8,128)(2,1)S(1)}, bf16[3,3,32,192]{3,2,1,0:T(8,128)(2,1)S(1)}, u32[]{:S(2)}, u32[]{:S(2)}) collective-permute-start(bf16[3,3,32,192]{3,2,1,0:T(8,128)(2,1)S(1)} %pad_maximum_fusion.11), channel_id=1, source_target_pairs={{0,7},{1,0},{2,1},{3,2},{4,3},{5,4},{6,5},{7,6},{8,15},{9,8},{10,9... | collective-permute-start | bytes 331784 | tf_op jit(solution)/shard_map/ppermute | solution.py:84
  205.9 6.4 %collective-permute-start.51 = (bf16[3,3,32,192]{3,2,1,0:T(8,128)(2,1)S(1)}, bf16[3,3,32,192]{3,2,1,0:T(8,128)(2,1)S(1)}, u32[]{:S(2)}, u32[]{:S(2)}) collective-permute-start(bf16[3,3,32,192]{3,2,1,0:T(8,128)(2,1)S(1)} %pad_maximum_fusion.11), channel_id=1, source_target_pairs={{0,1},{1,2},{2,3},{3,4},{4,5},{5,6},{6,7},{7,0},{8,9},{9,10},{10,1... | collective-permute-start | bytes 331784 | tf_op jit(solution)/shard_map/ppermute | solution.py:84
  213.2 5.0 %collective-permute-start.53 = (bf16[3,32,192]{2,1,0:T(8,128)(2,1)S(1)}, bf16[3,32,192]{2,1,0:T(8,128)(2,1)S(1)}, u32[]{:S(2)}, u32[]{:S(2)}) collective-permute-start(bf16[3,32,192]{2,1,0:T(8,128)(2,1)S(1)} %get-tuple-element.31), channel_id=1, source_target_pairs={{0,8},{8,16},{16,24},{24,0},{1,9},{9,17},{17,25},{25,1},{2,10},{10... | collective-permute-start | bytes 110600 | tf_op jit(solution)/shard_map/ppermute | solution.py:84
  214.7 4.1 %collective-permute-start.54 = (bf16[3,32,192]{2,1,0:T(8,128)(2,1)S(1)}, bf16[3,32,192]{2,1,0:T(8,128)(2,1)S(1)}, u32[]{:S(2)}, u32[]{:S(2)}) collective-permute-start(bf16[3,32,192]{2,1,0:T(8,128)(2,1)S(1)} %get-tuple-element.31), channel_id=1, source_target_pairs={{0,24},{8,0},{16,8},{24,16},{1,25},{9,1},{17,9},{25,17},{2,26},{10... | collective-permute-start | bytes 110600 | tf_op jit(solution)/shard_map/ppermute | solution.py:84
  218.8 4.1 %collective-permute-start.56 = (bf16[3,3,32,192]{3,2,1,0:T(8,128)(2,1)S(1)}, bf16[3,3,32,192]{3,2,1,0:T(8,128)(2,1)S(1)}, u32[]{:S(2)}, u32[]{:S(2)}) collective-permute-start(bf16[3,3,32,192]{3,2,1,0:T(8,128)(2,1)S(1)} %pad_maximum_fusion.12), channel_id=1, source_target_pairs={{0,7},{1,0},{2,1},{3,2},{4,3},{5,4},{6,5},{7,6},{8,15},{9,8},{10,9... | collective-permute-start | bytes 331784 | tf_op jit(solution)/shard_map/ppermute | solution.py:84
  219.2 6.4 %collective-permute-start.55 = (bf16[3,3,32,192]{3,2,1,0:T(8,128)(2,1)S(1)}, bf16[3,3,32,192]{3,2,1,0:T(8,128)(2,1)S(1)}, u32[]{:S(2)}, u32[]{:S(2)}) collective-permute-start(bf16[3,3,32,192]{3,2,1,0:T(8,128)(2,1)S(1)} %pad_maximum_fusion.12), channel_id=1, source_target_pairs={{0,1},{1,2},{2,3},{3,4},{4,5},{5,6},{6,7},{7,0},{8,9},{9,10},{10,1... | collective-permute-start | bytes 331784 | tf_op jit(solution)/shard_map/ppermute | solution.py:84
  226.5 5.0 %collective-permute-start.57 = (bf16[3,32,192]{2,1,0:T(8,128)(2,1)S(1)}, bf16[3,32,192]{2,1,0:T(8,128)(2,1)S(1)}, u32[]{:S(2)}, u32[]{:S(2)}) collective-permute-start(bf16[3,32,192]{2,1,0:T(8,128)(2,1)S(1)} %get-tuple-element.33), channel_id=1, source_target_pairs={{0,8},{8,16},{16,24},{24,0},{1,9},{9,17},{17,25},{25,1},{2,10},{10... | collective-permute-start | bytes 110600 | tf_op jit(solution)/shard_map/ppermute | solution.py:84
  228.4 4.1 %collective-permute-start.58 = (bf16[3,32,192]{2,1,0:T(8,128)(2,1)S(1)}, bf16[3,32,192]{2,1,0:T(8,128)(2,1)S(1)}, u32[]{:S(2)}, u32[]{:S(2)}) collective-permute-start(bf16[3,32,192]{2,1,0:T(8,128)(2,1)S(1)} %get-tuple-element.33), channel_id=1, source_target_pairs={{0,24},{8,0},{16,8},{24,16},{1,25},{9,1},{17,9},{25,17},{2,26},{10... | collective-permute-start | bytes 110600 | tf_op jit(solution)/shard_map/ppermute | solution.py:84
  232.5 4.1 %collective-permute-start.60 = (bf16[3,3,32,192]{3,2,1,0:T(8,128)(2,1)S(1)}, bf16[3,3,32,192]{3,2,1,0:T(8,128)(2,1)S(1)}, u32[]{:S(2)}, u32[]{:S(2)}) collective-permute-start(bf16[3,3,32,192]{3,2,1,0:T(8,128)(2,1)S(1)} %pad_maximum_fusion.13), channel_id=1, source_target_pairs={{0,7},{1,0},{2,1},{3,2},{4,3},{5,4},{6,5},{7,6},{8,15},{9,8},{10,9... | collective-permute-start | bytes 331784 | tf_op jit(solution)/shard_map/ppermute | solution.py:84
  233.4 6.4 %collective-permute-start.59 = (bf16[3,3,32,192]{3,2,1,0:T(8,128)(2,1)S(1)}, bf16[3,3,32,192]{3,2,1,0:T(8,128)(2,1)S(1)}, u32[]{:S(2)}, u32[]{:S(2)}) collective-permute-start(bf16[3,3,32,192]{3,2,1,0:T(8,128)(2,1)S(1)} %pad_maximum_fusion.13), channel_id=1, source_target_pairs={{0,1},{1,2},{2,3},{3,4},{4,5},{5,6},{6,7},{7,0},{8,9},{9,10},{10,1... | collective-permute-start | bytes 331784 | tf_op jit(solution)/shard_map/ppermute | solution.py:84
  240.7 5.0 %collective-permute-start.61 = (bf16[3,32,192]{2,1,0:T(8,128)(2,1)S(1)}, bf16[3,32,192]{2,1,0:T(8,128)(2,1)S(1)}, u32[]{:S(2)}, u32[]{:S(2)}) collective-permute-start(bf16[3,32,192]{2,1,0:T(8,128)(2,1)S(1)} %get-tuple-element.35), channel_id=1, source_target_pairs={{0,8},{8,16},{16,24},{24,0},{1,9},{9,17},{17,25},{25,1},{2,10},{10... | collective-permute-start | bytes 110600 | tf_op jit(solution)/shard_map/ppermute | solution.py:84
  246.3 4.1 %collective-permute-start.64 = (bf16[3,3,32,192]{3,2,1,0:T(8,128)(2,1)S(1)}, bf16[3,3,32,192]{3,2,1,0:T(8,128)(2,1)S(1)}, u32[]{:S(2)}, u32[]{:S(2)}) collective-permute-start(bf16[3,3,32,192]{3,2,1,0:T(8,128)(2,1)S(1)} %pad_maximum_fusion.14), channel_id=1, source_target_pairs={{0,7},{1,0},{2,1},{3,2},{4,3},{5,4},{6,5},{7,6},{8,15},{9,8},{10,9... | collective-permute-start | bytes 331784 | tf_op jit(solution)/shard_map/ppermute | solution.py:84
  246.8 6.4 %collective-permute-start.63 = (bf16[3,3,32,192]{3,2,1,0:T(8,128)(2,1)S(1)}, bf16[3,3,32,192]{3,2,1,0:T(8,128)(2,1)S(1)}, u32[]{:S(2)}, u32[]{:S(2)}) collective-permute-start(bf16[3,3,32,192]{3,2,1,0:T(8,128)(2,1)S(1)} %pad_maximum_fusion.14), channel_id=1, source_target_pairs={{0,1},{1,2},{2,3},{3,4},{4,5},{5,6},{6,7},{7,0},{8,9},{9,10},{10,1... | collective-permute-start | bytes 331784 | tf_op jit(solution)/shard_map/ppermute | solution.py:84
  254.1 5.0 %collective-permute-start.65 = (bf16[3,32,192]{2,1,0:T(8,128)(2,1)S(1)}, bf16[3,32,192]{2,1,0:T(8,128)(2,1)S(1)}, u32[]{:S(2)}, u32[]{:S(2)}) collective-permute-start(bf16[3,32,192]{2,1,0:T(8,128)(2,1)S(1)} %get-tuple-element.37), channel_id=1, source_target_pairs={{0,8},{8,16},{16,24},{24,0},{1,9},{9,17},{17,25},{25,1},{2,10},{10... | collective-permute-start | bytes 110600 | tf_op jit(solution)/shard_map/ppermute | solution.py:84
  259.7 4.1 %collective-permute-start.68 = (bf16[3,3,32,192]{3,2,1,0:T(8,128)(2,1)S(1)}, bf16[3,3,32,192]{3,2,1,0:T(8,128)(2,1)S(1)}, u32[]{:S(2)}, u32[]{:S(2)}) collective-permute-start(bf16[3,3,32,192]{3,2,1,0:T(8,128)(2,1)S(1)} %pad_maximum_fusion.15), channel_id=1, source_target_pairs={{0,7},{1,0},{2,1},{3,2},{4,3},{5,4},{6,5},{7,6},{8,15},{9,8},{10,9... | collective-permute-start | bytes 331784 | tf_op jit(solution)/shard_map/ppermute | solution.py:84
  260.6 6.4 %collective-permute-start.67 = (bf16[3,3,32,192]{3,2,1,0:T(8,128)(2,1)S(1)}, bf16[3,3,32,192]{3,2,1,0:T(8,128)(2,1)S(1)}, u32[]{:S(2)}, u32[]{:S(2)}) collective-permute-start(bf16[3,3,32,192]{3,2,1,0:T(8,128)(2,1)S(1)} %pad_maximum_fusion.15), channel_id=1, source_target_pairs={{0,1},{1,2},{2,3},{3,4},{4,5},{5,6},{6,7},{7,0},{8,9},{9,10},{10,1... | collective-permute-start | bytes 331784 | tf_op jit(solution)/shard_map/ppermute | solution.py:84
  280.6 4.6 %collective-permute-start.73 = (f32[32,32]{0,1:T(8,128)S(1)}, f32[32,32]{0,1:T(8,128)S(1)}, u32[]{:S(2)}, u32[]{:S(2)}) collective-permute-start(f32[32,32]{0,1:T(8,128)S(1)} %add.332), channel_id=1, source_target_pairs={{0,4},{1,5},{2,6},{3,7},{4,0},{5,1},{6,2},{7,3},{8,12},{9,13},{10,... | collective-permute-start | bytes 12296 | tf_op jit(solution)/shard_map/ppermute | solution.py:52
  (13 other events, 157.6 us)
where the time goes:
time: 293 us
  waiting for transfers between devices  136 us (46%)
  starting transfers between devices  71.1 us (24%)
  matrix products  64.2 us (22%)
  other arithmetic  16.3 us (6%)
  local copies, waits for them, and re-layouts  5.58 us (2%)
    ppermute x64, waiting for transfers between devices, shift(): lax.ppermute(value, axis, [(i, (i + step) % count) for i in range(count)])  107 us
    ppermute x64, starting transfers between devices, shift(): lax.ppermute(value, axis, [(i, (i + step) % count) for i in range(count)])  65.7 us
    dot_general x64, matrix products, part(): jnp.einsum('kvj,tkij->tvi', cells, blocks, preferred_element_type=jnp.flo...  49.3 us
    ppermute x10, waiting for transfers between devices, all_sum(): lax.ppermute(value, axis, [(i, i ^ stride) for i in range(count)])  28.8 us
    dot_general x1, matrix products, dense_coupling(): jnp.einsum('sc,sij->cij', select, matrices, preferred_element_type=jnp.fl...  12.9 us
    another operation x6, other arithmetic, orthonormal(): factor = jnp.linalg.cholesky(gram_matrix)  7.19 us
    another operation x4, other arithmetic, orthonormal(): inverse = jax.scipy.linalg.solve_triangular(factor, identity, lower=True)  6.17 us
  transfers between devices with their start and end apart: 74, of which 71 were waited for; matrix products, arithmetic and copies ran while one was open for 18% of the time, Pallas kernels for 0%

commit v1 on v0

--- a/solution.py
+++ b/solution.py
@@ -36,9 +36,15 @@
     match = (targets[:, None, None] == jnp.arange(depth, dtype=jnp.int32)[None, :, None]) & (
         sources[:, None, None] == jnp.array(order, dtype=jnp.int32)[None, None, :]
     )
-    select = match.reshape(slots, depth * cells).astype(matrices.dtype)
-    blocks = jnp.einsum("sc,sij->cij", select, matrices, preferred_element_type=jnp.float32)
-    return blocks.astype(matrices.dtype).reshape(depth, cells, matrices.shape[1], matrices.shape[2])
+    slot_ids = jnp.arange(slots, dtype=jnp.int32)[:, None, None]
+    index = jnp.sum(jnp.where(match, slot_ids, 0), axis=0)
+    present = jnp.any(match, axis=0)
+    blocks = jnp.take(matrices, index.reshape(-1), axis=0).reshape(
+        depth, cells, matrices.shape[1], matrices.shape[2]
+    )
+    return lax.optimization_barrier(
+        jnp.where(present[:, :, None, None], blocks, jnp.zeros((), matrices.dtype))
+    )
 
 
 def all_sum(value, axes):

time: 293 us -> 290 us (0.990)
  matrix products: 64.2 us -> 51.3 us
  local copies, waits for them, and re-layouts: 5.58 us -> 10.6 us
  other arithmetic: 16.3 us -> 20.9 us
    dot_general x1 -> x0, matrix products: 12.9 us -> none  [dense_coupling(): jnp.einsum('sc,sij->cij', select, matrices, preferred_element_type=jnp.fl...]
    gather x0 -> x1, local copies, waits for them, and re-layouts: none -> 10.3 us  [dense_coupling(): jnp.take(matrices, index.reshape(-1), axis=0)]
    convert_element_type x1 -> x0, local copies, waits for them, and re-layouts: 5.36 us -> none  [dense_coupling(): blocks.astype(matrices.dtype)]
    select_n x0 -> x2, other arithmetic: none -> 4.28 us  [the longest x1 4.28 us: dense_coupling(): jnp.where(present[:, :, None, None], blocks, jnp.zeros((), matrices.dtype))]
where the time goes in v1:
time: 290 us
  waiting for transfers between devices  136 us (47%)
  starting transfers between devices  70.7 us (24%)
  matrix products  51.3 us (18%)
  other arithmetic  20.9 us (7%)
  local copies, waits for them, and re-layouts  10.6 us (4%)
    ppermute x64, waiting for transfers between devices, shift(): lax.ppermute(value, axis, [(i, (i + step) % count) for i in range(count)])  107 us
    ppermute x64, starting transfers between devices, shift(): lax.ppermute(value, axis, [(i, (i + step) % count) for i in range(count)])  65.7 us
    dot_general x64, matrix products, part(): jnp.einsum('kvj,tkij->tvi', cells, blocks, preferred_element_type=jnp.flo...  49.3 us
    ppermute x10, waiting for transfers between devices, all_sum(): lax.ppermute(value, axis, [(i, i ^ stride) for i in range(count)])  29.2 us
    gather x1, local copies, waits for them, and re-layouts, dense_coupling(): jnp.take(matrices, index.reshape(-1), axis=0)  10.3 us
    another operation x6, other arithmetic, orthonormal(): factor = jnp.linalg.cholesky(gram_matrix)  7.19 us
    another operation x4, other arithmetic, orthonormal(): inverse = jax.scipy.linalg.solve_triangular(factor, identity, lower=True)  6.17 us
  transfers between devices with their start and end apart: 74, of which 71 were waited for; matrix products, arithmetic and copies ran while one was open for 18% of the time, Pallas kernels for 0%

profile of v1, /device:TPU:0, one launch (start us, length us, event | category | flops | bytes accessed | tf_op | source)
XLA Modules:
  0.0 289.9 jit_solution(5832817439016611250)
XLA Ops:
  0.9 3.0 %collective-permute-start = (bf16[3,32,192]{2,1,0:T(8,128)(2,1)S(1)}, bf16[3,32,192]{2,1,0:T(8,128)(2,1)S(1)}, u32[]{:S(2)}, u32[]{:S(2)}) collective-permute-start(bf16[3,32,192]{2,1,0:T(8,128)(2,1)S(1)} %get-tuple-element.16), channel_id=1, source_target_pairs={{0,8},{8,16},{16,24},{24,0},{1,9},{9,17},{17,25},{25,1},{2,10},{10... | collective-permute-start | bytes 110600 | tf_op jit(solution)/shard_map/ppermute | solution.py:90
  6.8 10.3 %gather_fusion = bf16[81,192,192]{2,1,0:T(8,128)(2,1)} fusion(bf16[81,192,192]{2,1,0:T(8,128)(2,1)} %bitcast.911, s32[1024]{0:T(1024)S(1)} %pad_clamp_fusion), kind=kCustom, calls=%fused_computation | custom fusion | bytes 11944260 | tf_op jit(solution)/shard_map/jit(_take)/gather | solution.py:42
  17.1 4.3 %select_select_fusion = bf16[3,27,192,192]{3,2,1,0:T(8,128)(2,1)S(1)} fusion(bf16[3,27,192,192]{3,2,1,0:T(8,128)(2,1)} %bitcast.910, pred[3,27]{1,0:T(4,128)(4,1)S(1)} %compare_and_fusion, pred[3,27]{1,0:T(4,128)(4,1)S(1)} %and_reduce_fusion), kind=kLoop, calls=%fused_computation.1 | loop fusion | flops 5971968 | bytes 11944098 | tf_op jit(solution)/shard_map/jit(_where)/select_n | solution.py:46
  21.8 2.9 %collective-permute-start.3 = (bf16[3,3,32,192]{3,2,1,0:T(8,128)(2,1)S(1)}, bf16[3,3,32,192]{3,2,1,0:T(8,128)(2,1)S(1)}, u32[]{:S(2)}, u32[]{:S(2)}) collective-permute-start(bf16[3,3,32,192]{3,2,1,0:T(8,128)(2,1)S(1)} %pad_maximum_fusion), channel_id=1, source_target_pairs={{0,7},{1,0},{2,1},{3,2},{4,3},{5,4},{6,5},{7,6},{8,15},{9,8},{10,9... | collective-permute-start | bytes 331784 | tf_op jit(solution)/shard_map/ppermute | solution.py:90
  25.4 2.3 collective-permute-done.3
  28.5 2.6 collective-permute-done.2
  32.7 2.3 collective-permute-start.5
  35.4 1.7 collective-permute-done.4
  39.5 2.3 collective-permute-done.7
  42.7 2.6 collective-permute-done.6
  49.6 1.7 collective-permute-done.8
  53.2 2.6 collective-permute-done.11
  56.7 2.3 collective-permute-done.10
  66.7 2.7 collective-permute-done.15
  70.3 2.1 collective-permute-done.14
  80.4 2.8 collective-permute-done.19
  84.0 2.1 collective-permute-done.18
  87.1 1.8 collective-permute-start.20
  94.5 2.6 collective-permute-done.23
  98.0 2.3 collective-permute-done.22
  108.4 2.4 collective-permute-done.27
  111.7 2.4 collective-permute-done.26
  116.3 1.8 collective-permute-start.29
  121.8 2.7 collective-permute-done.31
  125.4 2.2 collective-permute-done.30
  130.2 2.4 collective-permute-done.32
  133.7 2.6 collective-permute-done.33
  137.5 3.7 %collective-permute-done.35 = f32[32,32]{0,1:T(8,128)S(1)} collective-permute-done((f32[32,32]{0,1:T(8,128)S(1)}, f32[32,32]{0,1:T(8,128)S(1)}, u32[]{:S(2)}, u32[]{:S(2)}) %collective-permute-start.35) | collective-permute-done | bytes 4128 | tf_op jit(solution)/shard_map/ppermute | solution.py:58
  141.3 4.6 %collective-permute-done.36 = f32[32,32]{0,1:T(8,128)S(1)} collective-permute-done((f32[32,32]{0,1:T(8,128)S(1)}, f32[32,32]{0,1:T(8,128)S(1)}, u32[]{:S(2)}, u32[]{:S(2)}) %collective-permute-start.36) | collective-permute-done | bytes 4128 | tf_op jit(solution)/shard_map/ppermute | solution.py:58
  146.0 2.9 %cholesky.44 = f32[32,32]{1,0:T(8,128)S(1)} custom-call(f32[32,32]{1,0:T(8,128)S(1)} %fusion.162), custom_call_target="Cholesky" | custom-call | tf_op jit(solution)/shard_map/jit(cholesky)/cholesky | solution.py:68
  150.2 2.4 custom-call.6
  159.2 2.1 fusion.98
  162.8 2.6 convolution_bitcast_fusion.14
  166.4 2.2 collective-permute-start.41
  169.8 1.7 collective-permute-done.41
  172.7 2.6 collective-permute-start.44
  176.0 2.1 collective-permute-done.44
  178.9 2.8 collective-permute-done.43
  183.9 1.8 collective-permute-start.46
  186.0 1.7 collective-permute-done.45
  189.2 2.9 %collective-permute-done.48 = bf16[3,3,32,192]{3,2,1,0:T(8,128)(2,1)S(1)} collective-permute-done((bf16[3,3,32,192]{3,2,1,0:T(8,128)(2,1)S(1)}, bf16[3,3,32,192]{3,2,1,0:T(8,128)(2,1)S(1)}, u32[]{:S(2)}, u32[]{:S(2)}) %collective-permute-start.48) | collective-permute-done | bytes 110624 | tf_op jit(solution)/shard_map/ppermute | solution.py:90
  195.4 2.2 collective-permute-start.49
  198.8 1.7 collective-permute-done.49
  203.3 2.6 collective-permute-done.52
  206.8 2.3 collective-permute-done.51
  213.3 1.7 collective-permute-done.53
  216.6 2.9 %collective-permute-done.56 = bf16[3,3,32,192]{3,2,1,0:T(8,128)(2,1)S(1)} collective-permute-done((bf16[3,3,32,192]{3,2,1,0:T(8,128)(2,1)S(1)}, bf16[3,3,32,192]{3,2,1,0:T(8,128)(2,1)S(1)}, u32[]{:S(2)}, u32[]{:S(2)}) %collective-permute-start.56) | collective-permute-done | bytes 110624 | tf_op jit(solution)/shard_map/ppermute | solution.py:90
  220.5 1.8 collective-permute-done.55
  223.2 1.9 collective-permute-start.57
  226.5 1.7 collective-permute-done.57
  230.7 2.6 collective-permute-done.60
  234.2 2.3 collective-permute-done.59
  240.7 1.7 collective-permute-done.61
  244.0 2.9 collective-permute-done.64
  247.8 2.0 collective-permute-done.63
  254.1 1.7 collective-permute-done.65
  258.0 2.6 collective-permute-done.68
  261.4 2.3 collective-permute-done.67
  266.3 2.4 collective-permute-done.69
  269.8 2.6 collective-permute-done.70
  273.6 3.7 %collective-permute-done.72 = f32[32,32]{0,1:T(8,128)S(1)} collective-permute-done((f32[32,32]{0,1:T(8,128)S(1)}, f32[32,32]{0,1:T(8,128)S(1)}, u32[]{:S(2)}, u32[]{:S(2)}) %collective-permute-start.72) | collective-permute-done | bytes 4128 | tf_op jit(solution)/shard_map/ppermute | solution.py:58
  277.4 4.6 %collective-permute-done.73 = f32[32,32]{0,1:T(8,128)S(1)} collective-permute-done((f32[32,32]{0,1:T(8,128)S(1)}, f32[32,32]{0,1:T(8,128)S(1)}, u32[]{:S(2)}, u32[]{:S(2)}) %collective-permute-start.73) | collective-permute-done | bytes 4128 | tf_op jit(solution)/shard_map/ppermute | solution.py:58
  282.1 2.9 %cholesky.55 = f32[32,32]{1,0:T(8,128)S(1)} custom-call(f32[32,32]{1,0:T(8,128)S(1)} %fusion.160), custom_call_target="Cholesky" | custom-call | tf_op jit(solution)/shard_map/jit(cholesky)/cholesky | solution.py:68
  286.3 2.4 custom-call.7
  (215 shorter events, 124.0 us)
Async XLA Ops:
  0.9 20.9 %collective-permute-start = (bf16[3,32,192]{2,1,0:T(8,128)(2,1)S(1)}, bf16[3,32,192]{2,1,0:T(8,128)(2,1)S(1)}, u32[]{:S(2)}, u32[]{:S(2)}) collective-permute-start(bf16[3,32,192]{2,1,0:T(8,128)(2,1)S(1)} %get-tuple-element.16), channel_id=1, source_target_pairs={{0,8},{8,16},{16,24},{24,0},{1,9},{9,17},{17,25},{25,1},{2,10},{10... | collective-permute-start | bytes 110600 | tf_op jit(solution)/shard_map/ppermute | solution.py:90
  3.9 17.9 %collective-permute-start.1 = (bf16[3,32,192]{2,1,0:T(8,128)(2,1)S(1)}, bf16[3,32,192]{2,1,0:T(8,128)(2,1)S(1)}, u32[]{:S(2)}, u32[]{:S(2)}) collective-permute-start(bf16[3,32,192]{2,1,0:T(8,128)(2,1)S(1)} %get-tuple-element.16), channel_id=1, source_target_pairs={{0,24},{8,0},{16,8},{24,16},{1,25},{9,1},{17,9},{25,17},{2,26},{10... | collective-permute-start | bytes 110600 | tf_op jit(solution)/shard_map/ppermute | solution.py:90
  21.8 5.8 %collective-permute-start.3 = (bf16[3,3,32,192]{3,2,1,0:T(8,128)(2,1)S(1)}, bf16[3,3,32,192]{3,2,1,0:T(8,128)(2,1)S(1)}, u32[]{:S(2)}, u32[]{:S(2)}) collective-permute-start(bf16[3,3,32,192]{3,2,1,0:T(8,128)(2,1)S(1)} %pad_maximum_fusion), channel_id=1, source_target_pairs={{0,7},{1,0},{2,1},{3,2},{4,3},{5,4},{6,5},{7,6},{8,15},{9,8},{10,9... | collective-permute-start | bytes 331784 | tf_op jit(solution)/shard_map/ppermute | solution.py:90
  24.8 6.4 %collective-permute-start.2 = (bf16[3,3,32,192]{3,2,1,0:T(8,128)(2,1)S(1)}, bf16[3,3,32,192]{3,2,1,0:T(8,128)(2,1)S(1)}, u32[]{:S(2)}, u32[]{:S(2)}) collective-permute-start(bf16[3,3,32,192]{3,2,1,0:T(8,128)(2,1)S(1)} %pad_maximum_fusion), channel_id=1, source_target_pairs={{0,1},{1,2},{2,3},{3,4},{4,5},{5,6},{6,7},{7,0},{8,9},{9,10},{10,1... | collective-permute-start | bytes 331784 | tf_op jit(solution)/shard_map/ppermute | solution.py:90
  32.1 5.0 %collective-permute-start.4 = (bf16[3,32,192]{2,1,0:T(8,128)(2,1)S(1)}, bf16[3,32,192]{2,1,0:T(8,128)(2,1)S(1)}, u32[]{:S(2)}, u32[]{:S(2)}) collective-permute-start(bf16[3,32,192]{2,1,0:T(8,128)(2,1)S(1)} %get-tuple-element.17), channel_id=1, source_target_pairs={{0,8},{8,16},{16,24},{24,0},{1,9},{9,17},{17,25},{25,1},{2,10},{10... | collective-permute-start | bytes 110600 | tf_op jit(solution)/shard_map/ppermute | solution.py:90
  32.7 5.0 %collective-permute-start.5 = (bf16[3,32,192]{2,1,0:T(8,128)(2,1)S(1)}, bf16[3,32,192]{2,1,0:T(8,128)(2,1)S(1)}, u32[]{:S(2)}, u32[]{:S(2)}) collective-permute-start(bf16[3,32,192]{2,1,0:T(8,128)(2,1)S(1)} %get-tuple-element.17), channel_id=1, source_target_pairs={{0,24},{8,0},{16,8},{24,16},{1,25},{9,1},{17,9},{25,17},{2,26},{10... | collective-permute-start | bytes 110600 | tf_op jit(solution)/shard_map/ppermute | solution.py:90
  37.7 4.1 %collective-permute-start.7 = (bf16[3,3,32,192]{3,2,1,0:T(8,128)(2,1)S(1)}, bf16[3,3,32,192]{3,2,1,0:T(8,128)(2,1)S(1)}, u32[]{:S(2)}, u32[]{:S(2)}) collective-permute-start(bf16[3,3,32,192]{3,2,1,0:T(8,128)(2,1)S(1)} %pad_maximum_fusion.1), channel_id=1, source_target_pairs={{0,7},{1,0},{2,1},{3,2},{4,3},{5,4},{6,5},{7,6},{8,15},{9,8},{10,9... | collective-permute-start | bytes 331784 | tf_op jit(solution)/shard_map/ppermute | solution.py:90
  38.9 6.4 %collective-permute-start.6 = (bf16[3,3,32,192]{3,2,1,0:T(8,128)(2,1)S(1)}, bf16[3,3,32,192]{3,2,1,0:T(8,128)(2,1)S(1)}, u32[]{:S(2)}, u32[]{:S(2)}) collective-permute-start(bf16[3,3,32,192]{3,2,1,0:T(8,128)(2,1)S(1)} %pad_maximum_fusion.1), channel_id=1, source_target_pairs={{0,1},{1,2},{2,3},{3,4},{4,5},{5,6},{6,7},{7,0},{8,9},{9,10},{10,1... | collective-permute-start | bytes 331784 | tf_op jit(solution)/shard_map/ppermute | solution.py:90
  46.2 5.0 %collective-permute-start.8 = (bf16[3,32,192]{2,1,0:T(8,128)(2,1)S(1)}, bf16[3,32,192]{2,1,0:T(8,128)(2,1)S(1)}, u32[]{:S(2)}, u32[]{:S(2)}) collective-permute-start(bf16[3,32,192]{2,1,0:T(8,128)(2,1)S(1)} %get-tuple-element.19), channel_id=1, source_target_pairs={{0,8},{8,16},{16,24},{24,0},{1,9},{9,17},{17,25},{25,1},{2,10},{10... | collective-permute-start | bytes 110600 | tf_op jit(solution)/shard_map/ppermute | solution.py:90
  47.6 4.1 %collective-permute-start.9 = (bf16[3,32,192]{2,1,0:T(8,128)(2,1)S(1)}, bf16[3,32,192]{2,1,0:T(8,128)(2,1)S(1)}, u32[]{:S(2)}, u32[]{:S(2)}) collective-permute-start(bf16[3,32,192]{2,1,0:T(8,128)(2,1)S(1)} %get-tuple-element.19), channel_id=1, source_target_pairs={{0,24},{8,0},{16,8},{24,16},{1,25},{9,1},{17,9},{25,17},{2,26},{10... | collective-permute-start | bytes 110600 | tf_op jit(solution)/shard_map/ppermute | solution.py:90
  51.7 4.1 %collective-permute-start.11 = (bf16[3,3,32,192]{3,2,1,0:T(8,128)(2,1)S(1)}, bf16[3,3,32,192]{3,2,1,0:T(8,128)(2,1)S(1)}, u32[]{:S(2)}, u32[]{:S(2)}) collective-permute-start(bf16[3,3,32,192]{3,2,1,0:T(8,128)(2,1)S(1)} %pad_maximum_fusion.2), channel_id=1, source_target_pairs={{0,7},{1,0},{2,1},{3,2},{4,3},{5,4},{6,5},{7,6},{8,15},{9,8},{10,9... | collective-permute-start | bytes 331784 | tf_op jit(solution)/shard_map/ppermute | solution.py:90
  52.6 6.4 %collective-permute-start.10 = (bf16[3,3,32,192]{3,2,1,0:T(8,128)(2,1)S(1)}, bf16[3,3,32,192]{3,2,1,0:T(8,128)(2,1)S(1)}, u32[]{:S(2)}, u32[]{:S(2)}) collective-permute-start(bf16[3,3,32,192]{3,2,1,0:T(8,128)(2,1)S(1)} %pad_maximum_fusion.2), channel_id=1, source_target_pairs={{0,1},{1,2},{2,3},{3,4},{4,5},{5,6},{6,7},{7,0},{8,9},{9,10},{10,1... | collective-permute-start | bytes 331784 | tf_op jit(solution)/shard_map/ppermute | solution.py:90
  59.9 5.0 %collective-permute-start.12 = (bf16[3,32,192]{2,1,0:T(8,128)(2,1)S(1)}, bf16[3,32,192]{2,1,0:T(8,128)(2,1)S(1)}, u32[]{:S(2)}, u32[]{:S(2)}) collective-permute-start(bf16[3,32,192]{2,1,0:T(8,128)(2,1)S(1)} %get-tuple-element.21), channel_id=1, source_target_pairs={{0,8},{8,16},{16,24},{24,0},{1,9},{9,17},{17,25},{25,1},{2,10},{10... | collective-permute-start | bytes 110600 | tf_op jit(solution)/shard_map/ppermute | solution.py:90
  61.2 4.1 %collective-permute-start.13 = (bf16[3,32,192]{2,1,0:T(8,128)(2,1)S(1)}, bf16[3,32,192]{2,1,0:T(8,128)(2,1)S(1)}, u32[]{:S(2)}, u32[]{:S(2)}) collective-permute-start(bf16[3,32,192]{2,1,0:T(8,128)(2,1)S(1)} %get-tuple-element.21), channel_id=1, source_target_pairs={{0,24},{8,0},{16,8},{24,16},{1,25},{9,1},{17,9},{25,17},{2,26},{10... | collective-permute-start | bytes 110600 | tf_op jit(solution)/shard_map/ppermute | solution.py:90
  65.3 4.1 %collective-permute-start.15 = (bf16[3,3,32,192]{3,2,1,0:T(8,128)(2,1)S(1)}, bf16[3,3,32,192]{3,2,1,0:T(8,128)(2,1)S(1)}, u32[]{:S(2)}, u32[]{:S(2)}) collective-permute-start(bf16[3,3,32,192]{3,2,1,0:T(8,128)(2,1)S(1)} %pad_maximum_fusion.3), channel_id=1, source_target_pairs={{0,7},{1,0},{2,1},{3,2},{4,3},{5,4},{6,5},{7,6},{8,15},{9,8},{10,9... | collective-permute-start | bytes 331784 | tf_op jit(solution)/shard_map/ppermute | solution.py:90
  66.1 6.4 %collective-permute-start.14 = (bf16[3,3,32,192]{3,2,1,0:T(8,128)(2,1)S(1)}, bf16[3,3,32,192]{3,2,1,0:T(8,128)(2,1)S(1)}, u32[]{:S(2)}, u32[]{:S(2)}) collective-permute-start(bf16[3,3,32,192]{3,2,1,0:T(8,128)(2,1)S(1)} %pad_maximum_fusion.3), channel_id=1, source_target_pairs={{0,1},{1,2},{2,3},{3,4},{4,5},{5,6},{6,7},{7,0},{8,9},{9,10},{10,1... | collective-permute-start | bytes 331784 | tf_op jit(solution)/shard_map/ppermute | solution.py:90
  73.4 5.0 %collective-permute-start.16 = (bf16[3,32,192]{2,1,0:T(8,128)(2,1)S(1)}, bf16[3,32,192]{2,1,0:T(8,128)(2,1)S(1)}, u32[]{:S(2)}, u32[]{:S(2)}) collective-permute-start(bf16[3,32,192]{2,1,0:T(8,128)(2,1)S(1)} %get-tuple-element.23), channel_id=1, source_target_pairs={{0,8},{8,16},{16,24},{24,0},{1,9},{9,17},{17,25},{25,1},{2,10},{10... | collective-permute-start | bytes 110600 | tf_op jit(solution)/shard_map/ppermute | solution.py:90
  74.9 4.1 %collective-permute-start.17 = (bf16[3,32,192]{2,1,0:T(8,128)(2,1)S(1)}, bf16[3,32,192]{2,1,0:T(8,128)(2,1)S(1)}, u32[]{:S(2)}, u32[]{:S(2)}) collective-permute-start(bf16[3,32,192]{2,1,0:T(8,128)(2,1)S(1)} %get-tuple-element.23), channel_id=1, source_target_pairs={{0,24},{8,0},{16,8},{24,16},{1,25},{9,1},{17,9},{25,17},{2,26},{10... | collective-permute-start | bytes 110600 | tf_op jit(solution)/shard_map/ppermute | solution.py:90
  79.0 4.1 %collective-permute-start.19 = (bf16[3,3,32,192]{3,2,1,0:T(8,128)(2,1)S(1)}, bf16[3,3,32,192]{3,2,1,0:T(8,128)(2,1)S(1)}, u32[]{:S(2)}, u32[]{:S(2)}) collective-permute-start(bf16[3,3,32,192]{3,2,1,0:T(8,128)(2,1)S(1)} %pad_maximum_fusion.4), channel_id=1, source_target_pairs={{0,7},{1,0},{2,1},{3,2},{4,3},{5,4},{6,5},{7,6},{8,15},{9,8},{10,9... | collective-permute-start | bytes 331784 | tf_op jit(solution)/shard_map/ppermute | solution.py:90
  79.8 6.4 %collective-permute-start.18 = (bf16[3,3,32,192]{3,2,1,0:T(8,128)(2,1)S(1)}, bf16[3,3,32,192]{3,2,1,0:T(8,128)(2,1)S(1)}, u32[]{:S(2)}, u32[]{:S(2)}) collective-permute-start(bf16[3,3,32,192]{3,2,1,0:T(8,128)(2,1)S(1)} %pad_maximum_fusion.4), channel_id=1, source_target_pairs={{0,1},{1,2},{2,3},{3,4},{4,5},{5,6},{6,7},{7,0},{8,9},{9,10},{10,1... | collective-permute-start | bytes 331784 | tf_op jit(solution)/shard_map/ppermute | solution.py:90
  87.1 5.0 %collective-permute-start.20 = (bf16[3,32,192]{2,1,0:T(8,128)(2,1)S(1)}, bf16[3,32,192]{2,1,0:T(8,128)(2,1)S(1)}, u32[]{:S(2)}, u32[]{:S(2)}) collective-permute-start(bf16[3,32,192]{2,1,0:T(8,128)(2,1)S(1)} %get-tuple-element.25), channel_id=1, source_target_pairs={{0,8},{8,16},{16,24},{24,0},{1,9},{9,17},{17,25},{25,1},{2,10},{10... | collective-permute-start | bytes 110600 | tf_op jit(solution)/shard_map/ppermute | solution.py:90
  88.9 4.1 %collective-permute-start.21 = (bf16[3,32,192]{2,1,0:T(8,128)(2,1)S(1)}, bf16[3,32,192]{2,1,0:T(8,128)(2,1)S(1)}, u32[]{:S(2)}, u32[]{:S(2)}) collective-permute-start(bf16[3,32,192]{2,1,0:T(8,128)(2,1)S(1)} %get-tuple-element.25), channel_id=1, source_target_pairs={{0,24},{8,0},{16,8},{24,16},{1,25},{9,1},{17,9},{25,17},{2,26},{10... | collective-permute-start | bytes 110600 | tf_op jit(solution)/shard_map/ppermute | solution.py:90
  93.0 4.1 %collective-permute-start.23 = (bf16[3,3,32,192]{3,2,1,0:T(8,128)(2,1)S(1)}, bf16[3,3,32,192]{3,2,1,0:T(8,128)(2,1)S(1)}, u32[]{:S(2)}, u32[]{:S(2)}) collective-permute-start(bf16[3,3,32,192]{3,2,1,0:T(8,128)(2,1)S(1)} %pad_maximum_fusion.5), channel_id=1, source_target_pairs={{0,7},{1,0},{2,1},{3,2},{4,3},{5,4},{6,5},{7,6},{8,15},{9,8},{10,9... | collective-permute-start | bytes 331784 | tf_op jit(solution)/shard_map/ppermute | solution.py:90
  93.9 6.4 %collective-permute-start.22 = (bf16[3,3,32,192]{3,2,1,0:T(8,128)(2,1)S(1)}, bf16[3,3,32,192]{3,2,1,0:T(8,128)(2,1)S(1)}, u32[]{:S(2)}, u32[]{:S(2)}) collective-permute-start(bf16[3,3,32,192]{3,2,1,0:T(8,128)(2,1)S(1)} %pad_maximum_fusion.5), channel_id=1, source_target_pairs={{0,1},{1,2},{2,3},{3,4},{4,5},{5,6},{6,7},{7,0},{8,9},{9,10},{10,1... | collective-permute-start | bytes 331784 | tf_op jit(solution)/shard_map/ppermute | solution.py:90
  101.2 5.0 %collective-permute-start.24 = (bf16[3,32,192]{2,1,0:T(8,128)(2,1)S(1)}, bf16[3,32,192]{2,1,0:T(8,128)(2,1)S(1)}, u32[]{:S(2)}, u32[]{:S(2)}) collective-permute-start(bf16[3,32,192]{2,1,0:T(8,128)(2,1)S(1)} %get-tuple-element.27), channel_id=1, source_target_pairs={{0,8},{8,16},{16,24},{24,0},{1,9},{9,17},{17,25},{25,1},{2,10},{10... | collective-permute-start | bytes 110600 | tf_op jit(solution)/shard_map/ppermute | solution.py:90
  102.5 4.1 %collective-permute-start.25 = (bf16[3,32,192]{2,1,0:T(8,128)(2,1)S(1)}, bf16[3,32,192]{2,1,0:T(8,128)(2,1)S(1)}, u32[]{:S(2)}, u32[]{:S(2)}) collective-permute-start(bf16[3,32,192]{2,1,0:T(8,128)(2,1)S(1)} %get-tuple-element.27), channel_id=1, source_target_pairs={{0,24},{8,0},{16,8},{24,16},{1,25},{9,1},{17,9},{25,17},{2,26},{10... | collective-permute-start | bytes 110600 | tf_op jit(solution)/shard_map/ppermute | solution.py:90
  106.7 4.1 %collective-permute-start.27 = (bf16[3,3,32,192]{3,2,1,0:T(8,128)(2,1)S(1)}, bf16[3,3,32,192]{3,2,1,0:T(8,128)(2,1)S(1)}, u32[]{:S(2)}, u32[]{:S(2)}) collective-permute-start(bf16[3,3,32,192]{3,2,1,0:T(8,128)(2,1)S(1)} %pad_maximum_fusion.6), channel_id=1, source_target_pairs={{0,7},{1,0},{2,1},{3,2},{4,3},{5,4},{6,5},{7,6},{8,15},{9,8},{10,9... | collective-permute-start | bytes 331784 | tf_op jit(solution)/shard_map/ppermute | solution.py:90
  107.7 6.4 %collective-permute-start.26 = (bf16[3,3,32,192]{3,2,1,0:T(8,128)(2,1)S(1)}, bf16[3,3,32,192]{3,2,1,0:T(8,128)(2,1)S(1)}, u32[]{:S(2)}, u32[]{:S(2)}) collective-permute-start(bf16[3,3,32,192]{3,2,1,0:T(8,128)(2,1)S(1)} %pad_maximum_fusion.6), channel_id=1, source_target_pairs={{0,1},{1,2},{2,3},{3,4},{4,5},{5,6},{6,7},{7,0},{8,9},{9,10},{10,1... | collective-permute-start | bytes 331784 | tf_op jit(solution)/shard_map/ppermute | solution.py:90
  115.0 5.0 %collective-permute-start.28 = (bf16[3,32,192]{2,1,0:T(8,128)(2,1)S(1)}, bf16[3,32,192]{2,1,0:T(8,128)(2,1)S(1)}, u32[]{:S(2)}, u32[]{:S(2)}) collective-permute-start(bf16[3,32,192]{2,1,0:T(8,128)(2,1)S(1)} %get-tuple-element.29), channel_id=1, source_target_pairs={{0,8},{8,16},{16,24},{24,0},{1,9},{9,17},{17,25},{25,1},{2,10},{10... | collective-permute-start | bytes 110600 | tf_op jit(solution)/shard_map/ppermute | solution.py:90
  116.3 4.1 %collective-permute-start.29 = (bf16[3,32,192]{2,1,0:T(8,128)(2,1)S(1)}, bf16[3,32,192]{2,1,0:T(8,128)(2,1)S(1)}, u32[]{:S(2)}, u32[]{:S(2)}) collective-permute-start(bf16[3,32,192]{2,1,0:T(8,128)(2,1)S(1)} %get-tuple-element.29), channel_id=1, source_target_pairs={{0,24},{8,0},{16,8},{24,16},{1,25},{9,1},{17,9},{25,17},{2,26},{10... | collective-permute-start | bytes 110600 | tf_op jit(solution)/shard_map/ppermute | solution.py:90
  120.4 4.1 %collective-permute-start.31 = (bf16[3,3,32,192]{3,2,1,0:T(8,128)(2,1)S(1)}, bf16[3,3,32,192]{3,2,1,0:T(8,128)(2,1)S(1)}, u32[]{:S(2)}, u32[]{:S(2)}) collective-permute-start(bf16[3,3,32,192]{3,2,1,0:T(8,128)(2,1)S(1)} %pad_maximum_fusion.7), channel_id=1, source_target_pairs={{0,7},{1,0},{2,1},{3,2},{4,3},{5,4},{6,5},{7,6},{8,15},{9,8},{10,9... | collective-permute-start | bytes 331784 | tf_op jit(solution)/shard_map/ppermute | solution.py:90
  121.2 6.4 %collective-permute-start.30 = (bf16[3,3,32,192]{3,2,1,0:T(8,128)(2,1)S(1)}, bf16[3,3,32,192]{3,2,1,0:T(8,128)(2,1)S(1)}, u32[]{:S(2)}, u32[]{:S(2)}) collective-permute-start(bf16[3,3,32,192]{3,2,1,0:T(8,128)(2,1)S(1)} %pad_maximum_fusion.7), channel_id=1, source_target_pairs={{0,1},{1,2},{2,3},{3,4},{4,5},{5,6},{6,7},{7,0},{8,9},{9,10},{10,1... | collective-permute-start | bytes 331784 | tf_op jit(solution)/shard_map/ppermute | solution.py:90
  141.2 4.6 %collective-permute-start.36 = (f32[32,32]{0,1:T(8,128)S(1)}, f32[32,32]{0,1:T(8,128)S(1)}, u32[]{:S(2)}, u32[]{:S(2)}) collective-permute-start(f32[32,32]{0,1:T(8,128)S(1)} %add.322), channel_id=1, source_target_pairs={{0,4},{1,5},{2,6},{3,7},{4,0},{5,1},{6,2},{7,3},{8,12},{9,13},{10,... | collective-permute-start | bytes 12296 | tf_op jit(solution)/shard_map/ppermute | solution.py:58
  153.2 5.0 %collective-permute-start.37 = (bf16[3,32,192]{2,1,0:T(8,128)(2,1)S(1)}, bf16[3,32,192]{2,1,0:T(8,128)(2,1)S(1)}, u32[]{:S(2)}, u32[]{:S(2)}) collective-permute-start(bf16[3,32,192]{2,1,0:T(8,128)(2,1)S(1)} %get-tuple-element.14), channel_id=1, source_target_pairs={{0,8},{8,16},{16,24},{24,0},{1,9},{9,17},{17,25},{25,1},{2,10},{10... | collective-permute-start | bytes 110600 | tf_op jit(solution)/shard_map/ppermute | solution.py:90
  154.6 4.1 %collective-permute-start.38 = (bf16[3,32,192]{2,1,0:T(8,128)(2,1)S(1)}, bf16[3,32,192]{2,1,0:T(8,128)(2,1)S(1)}, u32[]{:S(2)}, u32[]{:S(2)}) collective-permute-start(bf16[3,32,192]{2,1,0:T(8,128)(2,1)S(1)} %get-tuple-element.14), channel_id=1, source_target_pairs={{0,24},{8,0},{16,8},{24,16},{1,25},{9,1},{17,9},{25,17},{2,26},{10... | collective-permute-start | bytes 110600 | tf_op jit(solution)/shard_map/ppermute | solution.py:90
  158.7 4.1 %collective-permute-start.40 = (bf16[3,3,32,192]{3,2,1,0:T(8,128)(2,1)S(1)}, bf16[3,3,32,192]{3,2,1,0:T(8,128)(2,1)S(1)}, u32[]{:S(2)}, u32[]{:S(2)}) collective-permute-start(bf16[3,3,32,192]{3,2,1,0:T(8,128)(2,1)S(1)} %pad_maximum_fusion.8), channel_id=1, source_target_pairs={{0,7},{1,0},{2,1},{3,2},{4,3},{5,4},{6,5},{7,6},{8,15},{9,8},{10,9... | collective-permute-start | bytes 331784 | tf_op jit(solution)/shard_map/ppermute | solution.py:90
  158.8 6.7 %collective-permute-start.39 = (bf16[3,3,32,192]{3,2,1,0:T(8,128)(2,1)S(1)}, bf16[3,3,32,192]{3,2,1,0:T(8,128)(2,1)S(1)}, u32[]{:S(2)}, u32[]{:S(2)}) collective-permute-start(bf16[3,3,32,192]{3,2,1,0:T(8,128)(2,1)S(1)} %pad_maximum_fusion.8), channel_id=1, source_target_pairs={{0,1},{1,2},{2,3},{3,4},{4,5},{5,6},{6,7},{7,0},{8,9},{9,10},{10,1... | collective-permute-start | bytes 331784 | tf_op jit(solution)/shard_map/ppermute | solution.py:90
  166.4 5.0 %collective-permute-start.41 = (bf16[3,32,192]{2,1,0:T(8,128)(2,1)S(1)}, bf16[3,32,192]{2,1,0:T(8,128)(2,1)S(1)}, u32[]{:S(2)}, u32[]{:S(2)}) collective-permute-start(bf16[3,32,192]{2,1,0:T(8,128)(2,1)S(1)} %get-tuple-element.12), channel_id=1, source_target_pairs={{0,8},{8,16},{16,24},{24,0},{1,9},{9,17},{17,25},{25,1},{2,10},{10... | collective-permute-start | bytes 110600 | tf_op jit(solution)/shard_map/ppermute | solution.py:90
  168.6 4.1 %collective-permute-start.42 = (bf16[3,32,192]{2,1,0:T(8,128)(2,1)S(1)}, bf16[3,32,192]{2,1,0:T(8,128)(2,1)S(1)}, u32[]{:S(2)}, u32[]{:S(2)}) collective-permute-start(bf16[3,32,192]{2,1,0:T(8,128)(2,1)S(1)} %get-tuple-element.12), channel_id=1, source_target_pairs={{0,24},{8,0},{16,8},{24,16},{1,25},{9,1},{17,9},{25,17},{2,26},{10... | collective-permute-start | bytes 110600 | tf_op jit(solution)/shard_map/ppermute | solution.py:90
  172.7 5.3 %collective-permute-start.44 = (bf16[3,3,32,192]{3,2,1,0:T(8,128)(2,1)S(1)}, bf16[3,3,32,192]{3,2,1,0:T(8,128)(2,1)S(1)}, u32[]{:S(2)}, u32[]{:S(2)}) collective-permute-start(bf16[3,3,32,192]{3,2,1,0:T(8,128)(2,1)S(1)} %pad_maximum_fusion.9), channel_id=1, source_target_pairs={{0,7},{1,0},{2,1},{3,2},{4,3},{5,4},{6,5},{7,6},{8,15},{9,8},{10,9... | collective-permute-start | bytes 331784 | tf_op jit(solution)/shard_map/ppermute | solution.py:90
  175.4 6.4 %collective-permute-start.43 = (bf16[3,3,32,192]{3,2,1,0:T(8,128)(2,1)S(1)}, bf16[3,3,32,192]{3,2,1,0:T(8,128)(2,1)S(1)}, u32[]{:S(2)}, u32[]{:S(2)}) collective-permute-start(bf16[3,3,32,192]{3,2,1,0:T(8,128)(2,1)S(1)} %pad_maximum_fusion.9), channel_id=1, source_target_pairs={{0,1},{1,2},{2,3},{3,4},{4,5},{5,6},{6,7},{7,0},{8,9},{9,10},{10,1... | collective-permute-start | bytes 331784 | tf_op jit(solution)/shard_map/ppermute | solution.py:90
  182.7 5.0 %collective-permute-start.45 = (bf16[3,32,192]{2,1,0:T(8,128)(2,1)S(1)}, bf16[3,32,192]{2,1,0:T(8,128)(2,1)S(1)}, u32[]{:S(2)}, u32[]{:S(2)}) collective-permute-start(bf16[3,32,192]{2,1,0:T(8,128)(2,1)S(1)} %get-tuple-element.10), channel_id=1, source_target_pairs={{0,8},{8,16},{16,24},{24,0},{1,9},{9,17},{17,25},{25,1},{2,10},{10... | collective-permute-start | bytes 110600 | tf_op jit(solution)/shard_map/ppermute | solution.py:90
  183.9 4.1 %collective-permute-start.46 = (bf16[3,32,192]{2,1,0:T(8,128)(2,1)S(1)}, bf16[3,32,192]{2,1,0:T(8,128)(2,1)S(1)}, u32[]{:S(2)}, u32[]{:S(2)}) collective-permute-start(bf16[3,32,192]{2,1,0:T(8,128)(2,1)S(1)} %get-tuple-element.10), channel_id=1, source_target_pairs={{0,24},{8,0},{16,8},{24,16},{1,25},{9,1},{17,9},{25,17},{2,26},{10... | collective-permute-start | bytes 110600 | tf_op jit(solution)/shard_map/ppermute | solution.py:90
  188.0 4.1 %collective-permute-start.48 = (bf16[3,3,32,192]{3,2,1,0:T(8,128)(2,1)S(1)}, bf16[3,3,32,192]{3,2,1,0:T(8,128)(2,1)S(1)}, u32[]{:S(2)}, u32[]{:S(2)}) collective-permute-start(bf16[3,3,32,192]{3,2,1,0:T(8,128)(2,1)S(1)} %pad_maximum_fusion.10), channel_id=1, source_target_pairs={{0,7},{1,0},{2,1},{3,2},{4,3},{5,4},{6,5},{7,6},{8,15},{9,8},{10,9... | collective-permute-start | bytes 331784 | tf_op jit(solution)/shard_map/ppermute | solution.py:90
  188.0 6.4 %collective-permute-start.47 = (bf16[3,3,32,192]{3,2,1,0:T(8,128)(2,1)S(1)}, bf16[3,3,32,192]{3,2,1,0:T(8,128)(2,1)S(1)}, u32[]{:S(2)}, u32[]{:S(2)}) collective-permute-start(bf16[3,3,32,192]{3,2,1,0:T(8,128)(2,1)S(1)} %pad_maximum_fusion.10), channel_id=1, source_target_pairs={{0,1},{1,2},{2,3},{3,4},{4,5},{5,6},{6,7},{7,0},{8,9},{9,10},{10,1... | collective-permute-start | bytes 331784 | tf_op jit(solution)/shard_map/ppermute | solution.py:90
  195.4 5.0 %collective-permute-start.49 = (bf16[3,32,192]{2,1,0:T(8,128)(2,1)S(1)}, bf16[3,32,192]{2,1,0:T(8,128)(2,1)S(1)}, u32[]{:S(2)}, u32[]{:S(2)}) collective-permute-start(bf16[3,32,192]{2,1,0:T(8,128)(2,1)S(1)} %get-tuple-element.8), channel_id=1, source_target_pairs={{0,8},{8,16},{16,24},{24,0},{1,9},{9,17},{17,25},{25,1},{2,10},{10... | collective-permute-start | bytes 110600 | tf_op jit(solution)/shard_map/ppermute | solution.py:90
  197.6 4.1 %collective-permute-start.50 = (bf16[3,32,192]{2,1,0:T(8,128)(2,1)S(1)}, bf16[3,32,192]{2,1,0:T(8,128)(2,1)S(1)}, u32[]{:S(2)}, u32[]{:S(2)}) collective-permute-start(bf16[3,32,192]{2,1,0:T(8,128)(2,1)S(1)} %get-tuple-element.8), channel_id=1, source_target_pairs={{0,24},{8,0},{16,8},{24,16},{1,25},{9,1},{17,9},{25,17},{2,26},{10... | collective-permute-start | bytes 110600 | tf_op jit(solution)/shard_map/ppermute | solution.py:90
  201.8 4.1 %collective-permute-start.52 = (bf16[3,3,32,192]{3,2,1,0:T(8,128)(2,1)S(1)}, bf16[3,3,32,192]{3,2,1,0:T(8,128)(2,1)S(1)}, u32[]{:S(2)}, u32[]{:S(2)}) collective-permute-start(bf16[3,3,32,192]{3,2,1,0:T(8,128)(2,1)S(1)} %pad_maximum_fusion.11), channel_id=1, source_target_pairs={{0,7},{1,0},{2,1},{3,2},{4,3},{5,4},{6,5},{7,6},{8,15},{9,8},{10,9... | collective-permute-start | bytes 331784 | tf_op jit(solution)/shard_map/ppermute | solution.py:90
  202.7 6.4 %collective-permute-start.51 = (bf16[3,3,32,192]{3,2,1,0:T(8,128)(2,1)S(1)}, bf16[3,3,32,192]{3,2,1,0:T(8,128)(2,1)S(1)}, u32[]{:S(2)}, u32[]{:S(2)}) collective-permute-start(bf16[3,3,32,192]{3,2,1,0:T(8,128)(2,1)S(1)} %pad_maximum_fusion.11), channel_id=1, source_target_pairs={{0,1},{1,2},{2,3},{3,4},{4,5},{5,6},{6,7},{7,0},{8,9},{9,10},{10,1... | collective-permute-start | bytes 331784 | tf_op jit(solution)/shard_map/ppermute | solution.py:90
  210.0 5.0 %collective-permute-start.53 = (bf16[3,32,192]{2,1,0:T(8,128)(2,1)S(1)}, bf16[3,32,192]{2,1,0:T(8,128)(2,1)S(1)}, u32[]{:S(2)}, u32[]{:S(2)}) collective-permute-start(bf16[3,32,192]{2,1,0:T(8,128)(2,1)S(1)} %get-tuple-element.31), channel_id=1, source_target_pairs={{0,8},{8,16},{16,24},{24,0},{1,9},{9,17},{17,25},{25,1},{2,10},{10... | collective-permute-start | bytes 110600 | tf_op jit(solution)/shard_map/ppermute | solution.py:90
  211.3 4.1 %collective-permute-start.54 = (bf16[3,32,192]{2,1,0:T(8,128)(2,1)S(1)}, bf16[3,32,192]{2,1,0:T(8,128)(2,1)S(1)}, u32[]{:S(2)}, u32[]{:S(2)}) collective-permute-start(bf16[3,32,192]{2,1,0:T(8,128)(2,1)S(1)} %get-tuple-element.31), channel_id=1, source_target_pairs={{0,24},{8,0},{16,8},{24,16},{1,25},{9,1},{17,9},{25,17},{2,26},{10... | collective-permute-start | bytes 110600 | tf_op jit(solution)/shard_map/ppermute | solution.py:90
  215.5 4.1 %collective-permute-start.56 = (bf16[3,3,32,192]{3,2,1,0:T(8,128)(2,1)S(1)}, bf16[3,3,32,192]{3,2,1,0:T(8,128)(2,1)S(1)}, u32[]{:S(2)}, u32[]{:S(2)}) collective-permute-start(bf16[3,3,32,192]{3,2,1,0:T(8,128)(2,1)S(1)} %pad_maximum_fusion.12), channel_id=1, source_target_pairs={{0,7},{1,0},{2,1},{3,2},{4,3},{5,4},{6,5},{7,6},{8,15},{9,8},{10,9... | collective-permute-start | bytes 331784 | tf_op jit(solution)/shard_map/ppermute | solution.py:90
  215.9 6.4 %collective-permute-start.55 = (bf16[3,3,32,192]{3,2,1,0:T(8,128)(2,1)S(1)}, bf16[3,3,32,192]{3,2,1,0:T(8,128)(2,1)S(1)}, u32[]{:S(2)}, u32[]{:S(2)}) collective-permute-start(bf16[3,3,32,192]{3,2,1,0:T(8,128)(2,1)S(1)} %pad_maximum_fusion.12), channel_id=1, source_target_pairs={{0,1},{1,2},{2,3},{3,4},{4,5},{5,6},{6,7},{7,0},{8,9},{9,10},{10,1... | collective-permute-start | bytes 331784 | tf_op jit(solution)/shard_map/ppermute | solution.py:90
  223.2 5.0 %collective-permute-start.57 = (bf16[3,32,192]{2,1,0:T(8,128)(2,1)S(1)}, bf16[3,32,192]{2,1,0:T(8,128)(2,1)S(1)}, u32[]{:S(2)}, u32[]{:S(2)}) collective-permute-start(bf16[3,32,192]{2,1,0:T(8,128)(2,1)S(1)} %get-tuple-element.33), channel_id=1, source_target_pairs={{0,8},{8,16},{16,24},{24,0},{1,9},{9,17},{17,25},{25,1},{2,10},{10... | collective-permute-start | bytes 110600 | tf_op jit(solution)/shard_map/ppermute | solution.py:90
  229.2 4.1 %collective-permute-start.60 = (bf16[3,3,32,192]{3,2,1,0:T(8,128)(2,1)S(1)}, bf16[3,3,32,192]{3,2,1,0:T(8,128)(2,1)S(1)}, u32[]{:S(2)}, u32[]{:S(2)}) collective-permute-start(bf16[3,3,32,192]{3,2,1,0:T(8,128)(2,1)S(1)} %pad_maximum_fusion.13), channel_id=1, source_target_pairs={{0,7},{1,0},{2,1},{3,2},{4,3},{5,4},{6,5},{7,6},{8,15},{9,8},{10,9... | collective-permute-start | bytes 331784 | tf_op jit(solution)/shard_map/ppermute | solution.py:90
  230.1 6.4 %collective-permute-start.59 = (bf16[3,3,32,192]{3,2,1,0:T(8,128)(2,1)S(1)}, bf16[3,3,32,192]{3,2,1,0:T(8,128)(2,1)S(1)}, u32[]{:S(2)}, u32[]{:S(2)}) collective-permute-start(bf16[3,3,32,192]{3,2,1,0:T(8,128)(2,1)S(1)} %pad_maximum_fusion.13), channel_id=1, source_target_pairs={{0,1},{1,2},{2,3},{3,4},{4,5},{5,6},{6,7},{7,0},{8,9},{9,10},{10,1... | collective-permute-start | bytes 331784 | tf_op jit(solution)/shard_map/ppermute | solution.py:90
  237.4 5.0 %collective-permute-start.61 = (bf16[3,32,192]{2,1,0:T(8,128)(2,1)S(1)}, bf16[3,32,192]{2,1,0:T(8,128)(2,1)S(1)}, u32[]{:S(2)}, u32[]{:S(2)}) collective-permute-start(bf16[3,32,192]{2,1,0:T(8,128)(2,1)S(1)} %get-tuple-element.35), channel_id=1, source_target_pairs={{0,8},{8,16},{16,24},{24,0},{1,9},{9,17},{17,25},{25,1},{2,10},{10... | collective-permute-start | bytes 110600 | tf_op jit(solution)/shard_map/ppermute | solution.py:90
  238.7 4.1 %collective-permute-start.62 = (bf16[3,32,192]{2,1,0:T(8,128)(2,1)S(1)}, bf16[3,32,192]{2,1,0:T(8,128)(2,1)S(1)}, u32[]{:S(2)}, u32[]{:S(2)}) collective-permute-start(bf16[3,32,192]{2,1,0:T(8,128)(2,1)S(1)} %get-tuple-element.35), channel_id=1, source_target_pairs={{0,24},{8,0},{16,8},{24,16},{1,25},{9,1},{17,9},{25,17},{2,26},{10... | collective-permute-start | bytes 110600 | tf_op jit(solution)/shard_map/ppermute | solution.py:90
  242.8 4.1 %collective-permute-start.64 = (bf16[3,3,32,192]{3,2,1,0:T(8,128)(2,1)S(1)}, bf16[3,3,32,192]{3,2,1,0:T(8,128)(2,1)S(1)}, u32[]{:S(2)}, u32[]{:S(2)}) collective-permute-start(bf16[3,3,32,192]{3,2,1,0:T(8,128)(2,1)S(1)} %pad_maximum_fusion.14), channel_id=1, source_target_pairs={{0,7},{1,0},{2,1},{3,2},{4,3},{5,4},{6,5},{7,6},{8,15},{9,8},{10,9... | collective-permute-start | bytes 331784 | tf_op jit(solution)/shard_map/ppermute | solution.py:90
  243.4 6.4 %collective-permute-start.63 = (bf16[3,3,32,192]{3,2,1,0:T(8,128)(2,1)S(1)}, bf16[3,3,32,192]{3,2,1,0:T(8,128)(2,1)S(1)}, u32[]{:S(2)}, u32[]{:S(2)}) collective-permute-start(bf16[3,3,32,192]{3,2,1,0:T(8,128)(2,1)S(1)} %pad_maximum_fusion.14), channel_id=1, source_target_pairs={{0,1},{1,2},{2,3},{3,4},{4,5},{5,6},{6,7},{7,0},{8,9},{9,10},{10,1... | collective-permute-start | bytes 331784 | tf_op jit(solution)/shard_map/ppermute | solution.py:90
  250.7 5.0 %collective-permute-start.65 = (bf16[3,32,192]{2,1,0:T(8,128)(2,1)S(1)}, bf16[3,32,192]{2,1,0:T(8,128)(2,1)S(1)}, u32[]{:S(2)}, u32[]{:S(2)}) collective-permute-start(bf16[3,32,192]{2,1,0:T(8,128)(2,1)S(1)} %get-tuple-element.37), channel_id=1, source_target_pairs={{0,8},{8,16},{16,24},{24,0},{1,9},{9,17},{17,25},{25,1},{2,10},{10... | collective-permute-start | bytes 110600 | tf_op jit(solution)/shard_map/ppermute | solution.py:90
  256.4 4.1 %collective-permute-start.68 = (bf16[3,3,32,192]{3,2,1,0:T(8,128)(2,1)S(1)}, bf16[3,3,32,192]{3,2,1,0:T(8,128)(2,1)S(1)}, u32[]{:S(2)}, u32[]{:S(2)}) collective-permute-start(bf16[3,3,32,192]{3,2,1,0:T(8,128)(2,1)S(1)} %pad_maximum_fusion.15), channel_id=1, source_target_pairs={{0,7},{1,0},{2,1},{3,2},{4,3},{5,4},{6,5},{7,6},{8,15},{9,8},{10,9... | collective-permute-start | bytes 331784 | tf_op jit(solution)/shard_map/ppermute | solution.py:90
  257.3 6.4 %collective-permute-start.67 = (bf16[3,3,32,192]{3,2,1,0:T(8,128)(2,1)S(1)}, bf16[3,3,32,192]{3,2,1,0:T(8,128)(2,1)S(1)}, u32[]{:S(2)}, u32[]{:S(2)}) collective-permute-start(bf16[3,3,32,192]{3,2,1,0:T(8,128)(2,1)S(1)} %pad_maximum_fusion.15), channel_id=1, source_target_pairs={{0,1},{1,2},{2,3},{3,4},{4,5},{5,6},{6,7},{7,0},{8,9},{9,10},{10,1... | collective-permute-start | bytes 331784 | tf_op jit(solution)/shard_map/ppermute | solution.py:90
  277.4 4.6 %collective-permute-start.73 = (f32[32,32]{0,1:T(8,128)S(1)}, f32[32,32]{0,1:T(8,128)S(1)}, u32[]{:S(2)}, u32[]{:S(2)}) collective-permute-start(f32[32,32]{0,1:T(8,128)S(1)} %add.358), channel_id=1, source_target_pairs={{0,4},{1,5},{2,6},{3,7},{4,0},{5,1},{6,2},{7,3},{8,12},{9,13},{10,... | collective-permute-start | bytes 12296 | tf_op jit(solution)/shard_map/ppermute | solution.py:58
  (13 other events, 156.4 us)

commit v2 on v0

--- a/solution.py
+++ b/solution.py
@@ -3,6 +3,8 @@
 import jax
 import jax.numpy as jnp
 from jax import lax
+from jax.experimental import pallas as pl
+from jax.experimental.pallas import tpu as pltpu
 from jax.sharding import PartitionSpec as P
 
 DEGREE = 8
@@ -30,15 +32,56 @@
     return cells
 
 
+def gather_kernel(index_ref, present_ref, cpl_hbm, out_ref, zero, sems):
+    zero[...] = jnp.zeros_like(zero)
+    copies = []
+    for c in range(out_ref.shape[0]):
+        source = cpl_hbm.at[index_ref[c]]
+        live = pltpu.make_async_copy(source, out_ref.at[c], sems.at[c])
+        dead = pltpu.make_async_copy(zero, out_ref.at[c], sems.at[c])
+
+        @pl.when(present_ref[c] != 0)
+        def _():
+            live.start()
+
+        @pl.when(present_ref[c] == 0)
+        def _():
+            dead.start()
+
+        copies.append(live)
+    for cp in copies:
+        cp.wait()
+
+
 def dense_coupling(matrices, targets, sources, depth, order):
-    slots = matrices.shape[0]
+    slots, rows, cols = matrices.shape
     cells = len(order)
     match = (targets[:, None, None] == jnp.arange(depth, dtype=jnp.int32)[None, :, None]) & (
         sources[:, None, None] == jnp.array(order, dtype=jnp.int32)[None, None, :]
     )
-    select = match.reshape(slots, depth * cells).astype(matrices.dtype)
-    blocks = jnp.einsum("sc,sij->cij", select, matrices, preferred_element_type=jnp.float32)
-    return blocks.astype(matrices.dtype).reshape(depth, cells, matrices.shape[1], matrices.shape[2])
+    slot_ids = jnp.arange(slots, dtype=jnp.int32)[:, None, None]
+    index = jnp.clip(jnp.sum(jnp.where(match, slot_ids, 0), axis=0), 0, slots - 1).reshape(-1)
+    present = jnp.any(match, axis=0).astype(jnp.int32).reshape(-1)
+    smem = pltpu.MemorySpace.SMEM
+    blocks = pl.pallas_call(
+        gather_kernel,
+        out_shape=jax.ShapeDtypeStruct((depth * cells, rows, cols), matrices.dtype),
+        in_specs=[
+            pl.BlockSpec(memory_space=smem),
+            pl.BlockSpec(memory_space=smem),
+            pl.BlockSpec(memory_space=pl.ANY),
+        ],
+        out_specs=pl.BlockSpec(memory_space=pltpu.MemorySpace.VMEM),
+        scratch_shapes=[
+            pltpu.VMEM((rows, cols), matrices.dtype),
+            pltpu.SemaphoreType.DMA((depth * cells,)),
+        ],
+        cost_estimate=pl.CostEstimate(
+            flops=0, bytes_accessed=2 * depth * cells * rows * cols * 2, transcendentals=0
+        ),
+        compiler_params=pltpu.CompilerParams(vmem_limit_bytes=24 * 1024 * 1024),
+    )(index, present, matrices)
+    return blocks.reshape(depth, cells, rows, cols)
 
 
 def all_sum(value, axes):

time: 293 us -> 292 us (level)
  starting transfers between devices: 71.1 us -> 56.9 us
  waiting for transfers between devices: 136 us -> 150 us
  matrix products: 64.2 us -> 51.2 us
  Pallas kernels: 0 us -> 12.9 us
    ppermute x64, waiting for transfers between devices: 107 us -> 120 us  [shift(): lax.ppermute(value, axis, [(i, (i + step) % count) for i in range(count)])]
    dot_general x1 -> x0, matrix products: 12.9 us -> none  [dense_coupling(): jnp.einsum('sc,sij->cij', select, matrices, preferred_element_type=jnp.fl...]
    pallas_call x0 -> x1, Pallas kernels: none -> 12.9 us  [dense_coupling(): pl.pallas_call(gather_kernel, out_shape=jax.ShapeDtypeStruct((depth * cel...]
    ppermute x64, starting transfers between devices: 65.7 us -> 52.9 us  [shift(): lax.ppermute(value, axis, [(i, (i + step) % count) for i in range(count)])]
    convert_element_type x1, local copies, waits for them, and re-layouts: 5.36 us -> 0.08 us  [dense_coupling(): present = jnp.any(match, axis=0).astype(jnp.int32).reshape(-1)]
    unnamed x6 -> x8, local copies, waits for them, and re-layouts: 0.05 us -> 3.32 us
  transfers between devices with their start and end apart: 74 -> 74, of which waited for: 71 -> 71; matrix products, arithmetic and copies ran while one was open for 18% -> 12% of each run, Pallas kernels for 0% -> 4%
where the time goes in v2:
time: 292 us
  waiting for transfers between devices  150 us (51%)
  starting transfers between devices  56.9 us (19%)
  matrix products  51.2 us (18%)
  other arithmetic  16.6 us (6%)
  Pallas kernels  12.9 us (4%)
  local copies, waits for them, and re-layouts  3.63 us (1%)
    ppermute x64, waiting for transfers between devices, shift(): lax.ppermute(value, axis, [(i, (i + step) % count) for i in range(count)])  120 us
    ppermute x64, starting transfers between devices, shift(): lax.ppermute(value, axis, [(i, (i + step) % count) for i in range(count)])  52.9 us
    dot_general x64, matrix products, part(): jnp.einsum('kvj,tkij->tvi', cells, blocks, preferred_element_type=jnp.flo...  49.2 us
    ppermute x10, waiting for transfers between devices, all_sum(): lax.ppermute(value, axis, [(i, i ^ stride) for i in range(count)])  30.2 us
    pallas_call x1, Pallas kernels, dense_coupling(): pl.pallas_call(gather_kernel, out_shape=jax.ShapeDtypeStruct((depth * cel...  12.9 us
    another operation x6, other arithmetic, orthonormal(): factor = jnp.linalg.cholesky(gram_matrix)  7.19 us
    another operation x4, other arithmetic, orthonormal(): inverse = jax.scipy.linalg.solve_triangular(factor, identity, lower=True)  6.17 us
  transfers between devices with their start and end apart: 74, of which 71 were waited for; matrix products, arithmetic and copies ran while one was open for 12% of the time, Pallas kernels for 4%

profile of v2, /device:TPU:0, one launch (start us, length us, event | category | flops | bytes accessed | tf_op | source)
XLA Modules:
  0.0 292.1 jit_solution(15683344470049220691)
XLA Ops:
  0.9 3.0 %collective-permute-start = (bf16[3,32,192]{2,1,0:T(8,128)(2,1)S(1)}, bf16[3,32,192]{2,1,0:T(8,128)(2,1)S(1)}, u32[]{:S(2)}, u32[]{:S(2)}) collective-permute-start(bf16[3,32,192]{2,1,0:T(8,128)(2,1)S(1)} %get-tuple-element.16), channel_id=1, source_target_pairs={{0,8},{8,16},{16,24},{24,0},{1,9},{9,17},{17,25},{25,1},{2,10},{10... | collective-permute-start | bytes 110600 | tf_op jit(solution)/shard_map/ppermute | solution.py:127
  6.8 3.3 %copy-done.2 = bf16[1,1,81,192,192]{4,3,2,1,0:T(8,128)(2,1)S(1)} copy-done((bf16[1,1,81,192,192]{4,3,2,1,0:T(8,128)(2,1)S(1)}, bf16[1,1,81,192,192]{4,3,2,1,0:T(8,128)(2,1)}, u32[]{:S(2)}) %copy-start.2) | copy-done | bytes 5971992
  10.1 12.9 %shard_map.55 = bf16[81,192,192]{2,1,0:T(8,128)(2,1)S(1)} custom-call(s32[81]{0:T(128)S(1)} %min.12.index_ref, s32[81]{0:T(128)S(1)} %reshape.224.present_ref, bf16[81,192,192]{2,1,0:T(8,128)(2,1)S(1)} %bitcast.972), custom_call_target="tpu_custom_call" | custom-call | bytes 11943936 | tf_op jit(solution)/shard_map/pallas_call | solution.py:66
  23.4 2.9 %collective-permute-start.3 = (bf16[3,3,32,192]{3,2,1,0:T(8,128)(2,1)S(1)}, bf16[3,3,32,192]{3,2,1,0:T(8,128)(2,1)S(1)}, u32[]{:S(2)}, u32[]{:S(2)}) collective-permute-start(bf16[3,3,32,192]{3,2,1,0:T(8,128)(2,1)S(1)} %pad_maximum_fusion), channel_id=1, source_target_pairs={{0,7},{1,0},{2,1},{3,2},{4,3},{5,4},{6,5},{7,6},{8,15},{9,8},{10,9... | collective-permute-start | bytes 331784 | tf_op jit(solution)/shard_map/ppermute | solution.py:127
  27.0 2.3 collective-permute-done.3
  30.1 2.6 collective-permute-done.2
  36.1 1.7 collective-permute-done.5
  37.8 2.4 collective-permute-done.4
  41.5 2.9 %collective-permute-done.7 = bf16[3,3,32,192]{3,2,1,0:T(8,128)(2,1)S(1)} collective-permute-done((bf16[3,3,32,192]{3,2,1,0:T(8,128)(2,1)S(1)}, bf16[3,3,32,192]{3,2,1,0:T(8,128)(2,1)S(1)}, u32[]{:S(2)}, u32[]{:S(2)}) %collective-permute-start.7) | collective-permute-done | bytes 110624 | tf_op jit(solution)/shard_map/ppermute | solution.py:127
  50.2 1.7 collective-permute-done.9
  54.8 2.7 collective-permute-done.11
  58.4 2.2 collective-permute-done.10
  64.0 1.7 collective-permute-done.13
  68.3 2.9 %collective-permute-done.15 = bf16[3,3,32,192]{3,2,1,0:T(8,128)(2,1)S(1)} collective-permute-done((bf16[3,3,32,192]{3,2,1,0:T(8,128)(2,1)S(1)}, bf16[3,3,32,192]{3,2,1,0:T(8,128)(2,1)S(1)}, u32[]{:S(2)}, u32[]{:S(2)}) %collective-permute-start.15) | collective-permute-done | bytes 110624 | tf_op jit(solution)/shard_map/ppermute | solution.py:127
  72.1 1.9 collective-permute-done.14
  77.4 1.7 collective-permute-done.17
  79.1 2.4 collective-permute-done.16
  82.8 2.9 %collective-permute-done.19 = bf16[3,3,32,192]{3,2,1,0:T(8,128)(2,1)S(1)} collective-permute-done((bf16[3,3,32,192]{3,2,1,0:T(8,128)(2,1)S(1)}, bf16[3,3,32,192]{3,2,1,0:T(8,128)(2,1)S(1)}, u32[]{:S(2)}, u32[]{:S(2)}) %collective-permute-start.19) | collective-permute-done | bytes 110624 | tf_op jit(solution)/shard_map/ppermute | solution.py:127
  91.5 1.7 collective-permute-done.21
  93.1 1.9 collective-permute-done.20
  96.3 2.9 %collective-permute-done.23 = bf16[3,3,32,192]{3,2,1,0:T(8,128)(2,1)S(1)} collective-permute-done((bf16[3,3,32,192]{3,2,1,0:T(8,128)(2,1)S(1)}, bf16[3,3,32,192]{3,2,1,0:T(8,128)(2,1)S(1)}, u32[]{:S(2)}, u32[]{:S(2)}) %collective-permute-start.23) | collective-permute-done | bytes 110624 | tf_op jit(solution)/shard_map/ppermute | solution.py:127
  105.1 1.7 collective-permute-done.25
  106.8 1.9 collective-permute-done.24
  109.8 2.9 %collective-permute-done.27 = bf16[3,3,32,192]{3,2,1,0:T(8,128)(2,1)S(1)} collective-permute-done((bf16[3,3,32,192]{3,2,1,0:T(8,128)(2,1)S(1)}, bf16[3,3,32,192]{3,2,1,0:T(8,128)(2,1)S(1)}, u32[]{:S(2)}, u32[]{:S(2)}) %collective-permute-start.27) | collective-permute-done | bytes 110624 | tf_op jit(solution)/shard_map/ppermute | solution.py:127
  120.3 2.0 collective-permute-done.28
  123.7 2.9 %collective-permute-done.31 = bf16[3,3,32,192]{3,2,1,0:T(8,128)(2,1)S(1)} collective-permute-done((bf16[3,3,32,192]{3,2,1,0:T(8,128)(2,1)S(1)}, bf16[3,3,32,192]{3,2,1,0:T(8,128)(2,1)S(1)}, u32[]{:S(2)}, u32[]{:S(2)}) %collective-permute-start.31) | collective-permute-done | bytes 110624 | tf_op jit(solution)/shard_map/ppermute | solution.py:127
  131.3 2.9 %collective-permute-done.32 = f32[32,32]{0,1:T(8,128)S(1)} collective-permute-done((f32[32,32]{0,1:T(8,128)S(1)}, f32[32,32]{0,1:T(8,128)S(1)}, u32[]{:S(2)}, u32[]{:S(2)}) %collective-permute-start.32) | collective-permute-done | bytes 4128 | tf_op jit(solution)/shard_map/ppermute | solution.py:95
  135.4 2.5 collective-permute-done.33
  139.1 3.7 %collective-permute-done.35 = f32[32,32]{0,1:T(8,128)S(1)} collective-permute-done((f32[32,32]{0,1:T(8,128)S(1)}, f32[32,32]{0,1:T(8,128)S(1)}, u32[]{:S(2)}, u32[]{:S(2)}) %collective-permute-start.35) | collective-permute-done | bytes 4128 | tf_op jit(solution)/shard_map/ppermute | solution.py:95
  142.9 4.6 %collective-permute-done.36 = f32[32,32]{0,1:T(8,128)S(1)} collective-permute-done((f32[32,32]{0,1:T(8,128)S(1)}, f32[32,32]{0,1:T(8,128)S(1)}, u32[]{:S(2)}, u32[]{:S(2)}) %collective-permute-start.36) | collective-permute-done | bytes 4128 | tf_op jit(solution)/shard_map/ppermute | solution.py:95
  147.6 2.9 cholesky.44
  151.9 2.4 custom-call.6
  155.6 2.1 collective-permute-start.38
  160.7 2.1 fusion.98
  164.2 2.6 convolution_bitcast_fusion.14
  167.9 2.5 collective-permute-start.41
  171.2 1.7 collective-permute-done.41
  174.5 2.3 collective-permute-start.44
  177.4 2.1 collective-permute-done.44
  180.3 2.8 collective-permute-done.43
  187.5 1.7 collective-permute-done.45
  190.7 2.9 %collective-permute-done.48 = bf16[3,3,32,192]{3,2,1,0:T(8,128)(2,1)S(1)} collective-permute-done((bf16[3,3,32,192]{3,2,1,0:T(8,128)(2,1)S(1)}, bf16[3,3,32,192]{3,2,1,0:T(8,128)(2,1)S(1)}, u32[]{:S(2)}, u32[]{:S(2)}) %collective-permute-start.48) | collective-permute-done | bytes 110624 | tf_op jit(solution)/shard_map/ppermute | solution.py:127
  197.0 2.0 collective-permute-start.49
  200.3 1.7 collective-permute-done.49
  204.6 2.6 collective-permute-done.52
  208.1 2.3 collective-permute-done.51
  211.3 1.9 collective-permute-start.54
  215.4 2.8 collective-permute-done.53
  219.4 2.9 %collective-permute-done.56 = bf16[3,3,32,192]{3,2,1,0:T(8,128)(2,1)S(1)} collective-permute-done((bf16[3,3,32,192]{3,2,1,0:T(8,128)(2,1)S(1)}, bf16[3,3,32,192]{3,2,1,0:T(8,128)(2,1)S(1)}, u32[]{:S(2)}, u32[]{:S(2)}) %collective-permute-start.56) | collective-permute-done | bytes 110624 | tf_op jit(solution)/shard_map/ppermute | solution.py:127
  228.1 1.7 collective-permute-done.58
  232.6 2.9 collective-permute-done.60
  236.4 2.0 collective-permute-done.59
  241.7 1.7 collective-permute-done.62
  243.4 2.1 collective-permute-done.61
  246.8 2.9 %collective-permute-done.64 = bf16[3,3,32,192]{3,2,1,0:T(8,128)(2,1)S(1)} collective-permute-done((bf16[3,3,32,192]{3,2,1,0:T(8,128)(2,1)S(1)}, bf16[3,3,32,192]{3,2,1,0:T(8,128)(2,1)S(1)}, u32[]{:S(2)}, u32[]{:S(2)}) %collective-permute-start.64) | collective-permute-done | bytes 110624 | tf_op jit(solution)/shard_map/ppermute | solution.py:127
  255.7 1.7 collective-permute-done.66
  257.4 1.8 collective-permute-done.65
  260.4 2.9 %collective-permute-done.68 = bf16[3,3,32,192]{3,2,1,0:T(8,128)(2,1)S(1)} collective-permute-done((bf16[3,3,32,192]{3,2,1,0:T(8,128)(2,1)S(1)}, bf16[3,3,32,192]{3,2,1,0:T(8,128)(2,1)S(1)}, u32[]{:S(2)}, u32[]{:S(2)}) %collective-permute-start.68) | collective-permute-done | bytes 110624 | tf_op jit(solution)/shard_map/ppermute | solution.py:127
  267.9 3.0 %collective-permute-done.69 = f32[32,32]{0,1:T(8,128)S(1)} collective-permute-done((f32[32,32]{0,1:T(8,128)S(1)}, f32[32,32]{0,1:T(8,128)S(1)}, u32[]{:S(2)}, u32[]{:S(2)}) %collective-permute-start.69) | collective-permute-done | bytes 4128 | tf_op jit(solution)/shard_map/ppermute | solution.py:95
  271.9 2.7 collective-permute-done.70
  275.8 3.7 %collective-permute-done.72 = f32[32,32]{0,1:T(8,128)S(1)} collective-permute-done((f32[32,32]{0,1:T(8,128)S(1)}, f32[32,32]{0,1:T(8,128)S(1)}, u32[]{:S(2)}, u32[]{:S(2)}) %collective-permute-start.72) | collective-permute-done | bytes 4128 | tf_op jit(solution)/shard_map/ppermute | solution.py:95
  279.6 4.6 %collective-permute-done.73 = f32[32,32]{0,1:T(8,128)S(1)} collective-permute-done((f32[32,32]{0,1:T(8,128)S(1)}, f32[32,32]{0,1:T(8,128)S(1)}, u32[]{:S(2)}, u32[]{:S(2)}) %collective-permute-start.73) | collective-permute-done | bytes 4128 | tf_op jit(solution)/shard_map/ppermute | solution.py:95
  284.3 2.9 cholesky.55
  288.5 2.4 custom-call.7
  (216 shorter events, 122.2 us)
Async XLA Ops:
  0.9 22.4 %collective-permute-start = (bf16[3,32,192]{2,1,0:T(8,128)(2,1)S(1)}, bf16[3,32,192]{2,1,0:T(8,128)(2,1)S(1)}, u32[]{:S(2)}, u32[]{:S(2)}) collective-permute-start(bf16[3,32,192]{2,1,0:T(8,128)(2,1)S(1)} %get-tuple-element.16), channel_id=1, source_target_pairs={{0,8},{8,16},{16,24},{24,0},{1,9},{9,17},{17,25},{25,1},{2,10},{10... | collective-permute-start | bytes 110600 | tf_op jit(solution)/shard_map/ppermute | solution.py:127
  3.9 19.5 %collective-permute-start.1 = (bf16[3,32,192]{2,1,0:T(8,128)(2,1)S(1)}, bf16[3,32,192]{2,1,0:T(8,128)(2,1)S(1)}, u32[]{:S(2)}, u32[]{:S(2)}) collective-permute-start(bf16[3,32,192]{2,1,0:T(8,128)(2,1)S(1)} %get-tuple-element.16), channel_id=1, source_target_pairs={{0,24},{8,0},{16,8},{24,16},{1,25},{9,1},{17,9},{25,17},{2,26},{10... | collective-permute-start | bytes 110600 | tf_op jit(solution)/shard_map/ppermute | solution.py:127
  23.4 5.8 %collective-permute-start.3 = (bf16[3,3,32,192]{3,2,1,0:T(8,128)(2,1)S(1)}, bf16[3,3,32,192]{3,2,1,0:T(8,128)(2,1)S(1)}, u32[]{:S(2)}, u32[]{:S(2)}) collective-permute-start(bf16[3,3,32,192]{3,2,1,0:T(8,128)(2,1)S(1)} %pad_maximum_fusion), channel_id=1, source_target_pairs={{0,7},{1,0},{2,1},{3,2},{4,3},{5,4},{6,5},{7,6},{8,15},{9,8},{10,9... | collective-permute-start | bytes 331784 | tf_op jit(solution)/shard_map/ppermute | solution.py:127
  26.4 6.4 %collective-permute-start.2 = (bf16[3,3,32,192]{3,2,1,0:T(8,128)(2,1)S(1)}, bf16[3,3,32,192]{3,2,1,0:T(8,128)(2,1)S(1)}, u32[]{:S(2)}, u32[]{:S(2)}) collective-permute-start(bf16[3,3,32,192]{3,2,1,0:T(8,128)(2,1)S(1)} %pad_maximum_fusion), channel_id=1, source_target_pairs={{0,1},{1,2},{2,3},{3,4},{4,5},{5,6},{6,7},{7,0},{8,9},{9,10},{10,1... | collective-permute-start | bytes 331784 | tf_op jit(solution)/shard_map/ppermute | solution.py:127
  33.7 4.1 %collective-permute-start.5 = (bf16[3,32,192]{2,1,0:T(8,128)(2,1)S(1)}, bf16[3,32,192]{2,1,0:T(8,128)(2,1)S(1)}, u32[]{:S(2)}, u32[]{:S(2)}) collective-permute-start(bf16[3,32,192]{2,1,0:T(8,128)(2,1)S(1)} %get-tuple-element.17), channel_id=1, source_target_pairs={{0,24},{8,0},{16,8},{24,16},{1,25},{9,1},{17,9},{25,17},{2,26},{10... | collective-permute-start | bytes 110600 | tf_op jit(solution)/shard_map/ppermute | solution.py:127
  35.3 5.0 %collective-permute-start.4 = (bf16[3,32,192]{2,1,0:T(8,128)(2,1)S(1)}, bf16[3,32,192]{2,1,0:T(8,128)(2,1)S(1)}, u32[]{:S(2)}, u32[]{:S(2)}) collective-permute-start(bf16[3,32,192]{2,1,0:T(8,128)(2,1)S(1)} %get-tuple-element.17), channel_id=1, source_target_pairs={{0,8},{8,16},{16,24},{24,0},{1,9},{9,17},{17,25},{25,1},{2,10},{10... | collective-permute-start | bytes 110600 | tf_op jit(solution)/shard_map/ppermute | solution.py:127
  40.3 4.1 %collective-permute-start.7 = (bf16[3,3,32,192]{3,2,1,0:T(8,128)(2,1)S(1)}, bf16[3,3,32,192]{3,2,1,0:T(8,128)(2,1)S(1)}, u32[]{:S(2)}, u32[]{:S(2)}) collective-permute-start(bf16[3,3,32,192]{3,2,1,0:T(8,128)(2,1)S(1)} %pad_maximum_fusion.1), channel_id=1, source_target_pairs={{0,7},{1,0},{2,1},{3,2},{4,3},{5,4},{6,5},{7,6},{8,15},{9,8},{10,9... | collective-permute-start | bytes 331784 | tf_op jit(solution)/shard_map/ppermute | solution.py:127
  40.3 6.4 %collective-permute-start.6 = (bf16[3,3,32,192]{3,2,1,0:T(8,128)(2,1)S(1)}, bf16[3,3,32,192]{3,2,1,0:T(8,128)(2,1)S(1)}, u32[]{:S(2)}, u32[]{:S(2)}) collective-permute-start(bf16[3,3,32,192]{3,2,1,0:T(8,128)(2,1)S(1)} %pad_maximum_fusion.1), channel_id=1, source_target_pairs={{0,1},{1,2},{2,3},{3,4},{4,5},{5,6},{6,7},{7,0},{8,9},{9,10},{10,1... | collective-permute-start | bytes 331784 | tf_op jit(solution)/shard_map/ppermute | solution.py:127
  47.7 4.1 %collective-permute-start.9 = (bf16[3,32,192]{2,1,0:T(8,128)(2,1)S(1)}, bf16[3,32,192]{2,1,0:T(8,128)(2,1)S(1)}, u32[]{:S(2)}, u32[]{:S(2)}) collective-permute-start(bf16[3,32,192]{2,1,0:T(8,128)(2,1)S(1)} %get-tuple-element.19), channel_id=1, source_target_pairs={{0,24},{8,0},{16,8},{24,16},{1,25},{9,1},{17,9},{25,17},{2,26},{10... | collective-permute-start | bytes 110600 | tf_op jit(solution)/shard_map/ppermute | solution.py:127
  48.4 5.0 %collective-permute-start.8 = (bf16[3,32,192]{2,1,0:T(8,128)(2,1)S(1)}, bf16[3,32,192]{2,1,0:T(8,128)(2,1)S(1)}, u32[]{:S(2)}, u32[]{:S(2)}) collective-permute-start(bf16[3,32,192]{2,1,0:T(8,128)(2,1)S(1)} %get-tuple-element.19), channel_id=1, source_target_pairs={{0,8},{8,16},{16,24},{24,0},{1,9},{9,17},{17,25},{25,1},{2,10},{10... | collective-permute-start | bytes 110600 | tf_op jit(solution)/shard_map/ppermute | solution.py:127
  53.4 4.1 %collective-permute-start.11 = (bf16[3,3,32,192]{3,2,1,0:T(8,128)(2,1)S(1)}, bf16[3,3,32,192]{3,2,1,0:T(8,128)(2,1)S(1)}, u32[]{:S(2)}, u32[]{:S(2)}) collective-permute-start(bf16[3,3,32,192]{3,2,1,0:T(8,128)(2,1)S(1)} %pad_maximum_fusion.2), channel_id=1, source_target_pairs={{0,7},{1,0},{2,1},{3,2},{4,3},{5,4},{6,5},{7,6},{8,15},{9,8},{10,9... | collective-permute-start | bytes 331784 | tf_op jit(solution)/shard_map/ppermute | solution.py:127
  54.2 6.4 %collective-permute-start.10 = (bf16[3,3,32,192]{3,2,1,0:T(8,128)(2,1)S(1)}, bf16[3,3,32,192]{3,2,1,0:T(8,128)(2,1)S(1)}, u32[]{:S(2)}, u32[]{:S(2)}) collective-permute-start(bf16[3,3,32,192]{3,2,1,0:T(8,128)(2,1)S(1)} %pad_maximum_fusion.2), channel_id=1, source_target_pairs={{0,1},{1,2},{2,3},{3,4},{4,5},{5,6},{6,7},{7,0},{8,9},{9,10},{10,1... | collective-permute-start | bytes 331784 | tf_op jit(solution)/shard_map/ppermute | solution.py:127
  61.5 4.1 %collective-permute-start.13 = (bf16[3,32,192]{2,1,0:T(8,128)(2,1)S(1)}, bf16[3,32,192]{2,1,0:T(8,128)(2,1)S(1)}, u32[]{:S(2)}, u32[]{:S(2)}) collective-permute-start(bf16[3,32,192]{2,1,0:T(8,128)(2,1)S(1)} %get-tuple-element.21), channel_id=1, source_target_pairs={{0,24},{8,0},{16,8},{24,16},{1,25},{9,1},{17,9},{25,17},{2,26},{10... | collective-permute-start | bytes 110600 | tf_op jit(solution)/shard_map/ppermute | solution.py:127
  62.1 5.0 %collective-permute-start.12 = (bf16[3,32,192]{2,1,0:T(8,128)(2,1)S(1)}, bf16[3,32,192]{2,1,0:T(8,128)(2,1)S(1)}, u32[]{:S(2)}, u32[]{:S(2)}) collective-permute-start(bf16[3,32,192]{2,1,0:T(8,128)(2,1)S(1)} %get-tuple-element.21), channel_id=1, source_target_pairs={{0,8},{8,16},{16,24},{24,0},{1,9},{9,17},{17,25},{25,1},{2,10},{10... | collective-permute-start | bytes 110600 | tf_op jit(solution)/shard_map/ppermute | solution.py:127
  67.1 4.1 %collective-permute-start.15 = (bf16[3,3,32,192]{3,2,1,0:T(8,128)(2,1)S(1)}, bf16[3,3,32,192]{3,2,1,0:T(8,128)(2,1)S(1)}, u32[]{:S(2)}, u32[]{:S(2)}) collective-permute-start(bf16[3,3,32,192]{3,2,1,0:T(8,128)(2,1)S(1)} %pad_maximum_fusion.3), channel_id=1, source_target_pairs={{0,7},{1,0},{2,1},{3,2},{4,3},{5,4},{6,5},{7,6},{8,15},{9,8},{10,9... | collective-permute-start | bytes 331784 | tf_op jit(solution)/shard_map/ppermute | solution.py:127
  67.7 6.4 %collective-permute-start.14 = (bf16[3,3,32,192]{3,2,1,0:T(8,128)(2,1)S(1)}, bf16[3,3,32,192]{3,2,1,0:T(8,128)(2,1)S(1)}, u32[]{:S(2)}, u32[]{:S(2)}) collective-permute-start(bf16[3,3,32,192]{3,2,1,0:T(8,128)(2,1)S(1)} %pad_maximum_fusion.3), channel_id=1, source_target_pairs={{0,1},{1,2},{2,3},{3,4},{4,5},{5,6},{6,7},{7,0},{8,9},{9,10},{10,1... | collective-permute-start | bytes 331784 | tf_op jit(solution)/shard_map/ppermute | solution.py:127
  75.0 4.1 %collective-permute-start.17 = (bf16[3,32,192]{2,1,0:T(8,128)(2,1)S(1)}, bf16[3,32,192]{2,1,0:T(8,128)(2,1)S(1)}, u32[]{:S(2)}, u32[]{:S(2)}) collective-permute-start(bf16[3,32,192]{2,1,0:T(8,128)(2,1)S(1)} %get-tuple-element.23), channel_id=1, source_target_pairs={{0,24},{8,0},{16,8},{24,16},{1,25},{9,1},{17,9},{25,17},{2,26},{10... | collective-permute-start | bytes 110600 | tf_op jit(solution)/shard_map/ppermute | solution.py:127
  76.6 5.0 %collective-permute-start.16 = (bf16[3,32,192]{2,1,0:T(8,128)(2,1)S(1)}, bf16[3,32,192]{2,1,0:T(8,128)(2,1)S(1)}, u32[]{:S(2)}, u32[]{:S(2)}) collective-permute-start(bf16[3,32,192]{2,1,0:T(8,128)(2,1)S(1)} %get-tuple-element.23), channel_id=1, source_target_pairs={{0,8},{8,16},{16,24},{24,0},{1,9},{9,17},{17,25},{25,1},{2,10},{10... | collective-permute-start | bytes 110600 | tf_op jit(solution)/shard_map/ppermute | solution.py:127
  81.6 4.1 %collective-permute-start.19 = (bf16[3,3,32,192]{3,2,1,0:T(8,128)(2,1)S(1)}, bf16[3,3,32,192]{3,2,1,0:T(8,128)(2,1)S(1)}, u32[]{:S(2)}, u32[]{:S(2)}) collective-permute-start(bf16[3,3,32,192]{3,2,1,0:T(8,128)(2,1)S(1)} %pad_maximum_fusion.4), channel_id=1, source_target_pairs={{0,7},{1,0},{2,1},{3,2},{4,3},{5,4},{6,5},{7,6},{8,15},{9,8},{10,9... | collective-permute-start | bytes 331784 | tf_op jit(solution)/shard_map/ppermute | solution.py:127
  81.6 6.4 %collective-permute-start.18 = (bf16[3,3,32,192]{3,2,1,0:T(8,128)(2,1)S(1)}, bf16[3,3,32,192]{3,2,1,0:T(8,128)(2,1)S(1)}, u32[]{:S(2)}, u32[]{:S(2)}) collective-permute-start(bf16[3,3,32,192]{3,2,1,0:T(8,128)(2,1)S(1)} %pad_maximum_fusion.4), channel_id=1, source_target_pairs={{0,1},{1,2},{2,3},{3,4},{4,5},{5,6},{6,7},{7,0},{8,9},{9,10},{10,1... | collective-permute-start | bytes 331784 | tf_op jit(solution)/shard_map/ppermute | solution.py:127
  89.0 4.1 %collective-permute-start.21 = (bf16[3,32,192]{2,1,0:T(8,128)(2,1)S(1)}, bf16[3,32,192]{2,1,0:T(8,128)(2,1)S(1)}, u32[]{:S(2)}, u32[]{:S(2)}) collective-permute-start(bf16[3,32,192]{2,1,0:T(8,128)(2,1)S(1)} %get-tuple-element.25), channel_id=1, source_target_pairs={{0,24},{8,0},{16,8},{24,16},{1,25},{9,1},{17,9},{25,17},{2,26},{10... | collective-permute-start | bytes 110600 | tf_op jit(solution)/shard_map/ppermute | solution.py:127
  90.1 5.0 %collective-permute-start.20 = (bf16[3,32,192]{2,1,0:T(8,128)(2,1)S(1)}, bf16[3,32,192]{2,1,0:T(8,128)(2,1)S(1)}, u32[]{:S(2)}, u32[]{:S(2)}) collective-permute-start(bf16[3,32,192]{2,1,0:T(8,128)(2,1)S(1)} %get-tuple-element.25), channel_id=1, source_target_pairs={{0,8},{8,16},{16,24},{24,0},{1,9},{9,17},{17,25},{25,1},{2,10},{10... | collective-permute-start | bytes 110600 | tf_op jit(solution)/shard_map/ppermute | solution.py:127
  95.1 4.1 %collective-permute-start.23 = (bf16[3,3,32,192]{3,2,1,0:T(8,128)(2,1)S(1)}, bf16[3,3,32,192]{3,2,1,0:T(8,128)(2,1)S(1)}, u32[]{:S(2)}, u32[]{:S(2)}) collective-permute-start(bf16[3,3,32,192]{3,2,1,0:T(8,128)(2,1)S(1)} %pad_maximum_fusion.5), channel_id=1, source_target_pairs={{0,7},{1,0},{2,1},{3,2},{4,3},{5,4},{6,5},{7,6},{8,15},{9,8},{10,9... | collective-permute-start | bytes 331784 | tf_op jit(solution)/shard_map/ppermute | solution.py:127
  95.3 6.4 %collective-permute-start.22 = (bf16[3,3,32,192]{3,2,1,0:T(8,128)(2,1)S(1)}, bf16[3,3,32,192]{3,2,1,0:T(8,128)(2,1)S(1)}, u32[]{:S(2)}, u32[]{:S(2)}) collective-permute-start(bf16[3,3,32,192]{3,2,1,0:T(8,128)(2,1)S(1)} %pad_maximum_fusion.5), channel_id=1, source_target_pairs={{0,1},{1,2},{2,3},{3,4},{4,5},{5,6},{6,7},{7,0},{8,9},{9,10},{10,1... | collective-permute-start | bytes 331784 | tf_op jit(solution)/shard_map/ppermute | solution.py:127
  102.6 4.1 %collective-permute-start.25 = (bf16[3,32,192]{2,1,0:T(8,128)(2,1)S(1)}, bf16[3,32,192]{2,1,0:T(8,128)(2,1)S(1)}, u32[]{:S(2)}, u32[]{:S(2)}) collective-permute-start(bf16[3,32,192]{2,1,0:T(8,128)(2,1)S(1)} %get-tuple-element.27), channel_id=1, source_target_pairs={{0,24},{8,0},{16,8},{24,16},{1,25},{9,1},{17,9},{25,17},{2,26},{10... | collective-permute-start | bytes 110600 | tf_op jit(solution)/shard_map/ppermute | solution.py:127
  103.6 5.0 %collective-permute-start.24 = (bf16[3,32,192]{2,1,0:T(8,128)(2,1)S(1)}, bf16[3,32,192]{2,1,0:T(8,128)(2,1)S(1)}, u32[]{:S(2)}, u32[]{:S(2)}) collective-permute-start(bf16[3,32,192]{2,1,0:T(8,128)(2,1)S(1)} %get-tuple-element.27), channel_id=1, source_target_pairs={{0,8},{8,16},{16,24},{24,0},{1,9},{9,17},{17,25},{25,1},{2,10},{10... | collective-permute-start | bytes 110600 | tf_op jit(solution)/shard_map/ppermute | solution.py:127
  108.7 4.1 %collective-permute-start.27 = (bf16[3,3,32,192]{3,2,1,0:T(8,128)(2,1)S(1)}, bf16[3,3,32,192]{3,2,1,0:T(8,128)(2,1)S(1)}, u32[]{:S(2)}, u32[]{:S(2)}) collective-permute-start(bf16[3,3,32,192]{3,2,1,0:T(8,128)(2,1)S(1)} %pad_maximum_fusion.6), channel_id=1, source_target_pairs={{0,7},{1,0},{2,1},{3,2},{4,3},{5,4},{6,5},{7,6},{8,15},{9,8},{10,9... | collective-permute-start | bytes 331784 | tf_op jit(solution)/shard_map/ppermute | solution.py:127
  108.9 6.4 %collective-permute-start.26 = (bf16[3,3,32,192]{3,2,1,0:T(8,128)(2,1)S(1)}, bf16[3,3,32,192]{3,2,1,0:T(8,128)(2,1)S(1)}, u32[]{:S(2)}, u32[]{:S(2)}) collective-permute-start(bf16[3,3,32,192]{3,2,1,0:T(8,128)(2,1)S(1)} %pad_maximum_fusion.6), channel_id=1, source_target_pairs={{0,1},{1,2},{2,3},{3,4},{4,5},{5,6},{6,7},{7,0},{8,9},{9,10},{10,1... | collective-permute-start | bytes 331784 | tf_op jit(solution)/shard_map/ppermute | solution.py:127
  116.2 4.1 %collective-permute-start.29 = (bf16[3,32,192]{2,1,0:T(8,128)(2,1)S(1)}, bf16[3,32,192]{2,1,0:T(8,128)(2,1)S(1)}, u32[]{:S(2)}, u32[]{:S(2)}) collective-permute-start(bf16[3,32,192]{2,1,0:T(8,128)(2,1)S(1)} %get-tuple-element.29), channel_id=1, source_target_pairs={{0,24},{8,0},{16,8},{24,16},{1,25},{9,1},{17,9},{25,17},{2,26},{10... | collective-permute-start | bytes 110600 | tf_op jit(solution)/shard_map/ppermute | solution.py:127
  117.4 5.0 %collective-permute-start.28 = (bf16[3,32,192]{2,1,0:T(8,128)(2,1)S(1)}, bf16[3,32,192]{2,1,0:T(8,128)(2,1)S(1)}, u32[]{:S(2)}, u32[]{:S(2)}) collective-permute-start(bf16[3,32,192]{2,1,0:T(8,128)(2,1)S(1)} %get-tuple-element.29), channel_id=1, source_target_pairs={{0,8},{8,16},{16,24},{24,0},{1,9},{9,17},{17,25},{25,1},{2,10},{10... | collective-permute-start | bytes 110600 | tf_op jit(solution)/shard_map/ppermute | solution.py:127
  122.4 4.3 %collective-permute-start.31 = (bf16[3,3,32,192]{3,2,1,0:T(8,128)(2,1)S(1)}, bf16[3,3,32,192]{3,2,1,0:T(8,128)(2,1)S(1)}, u32[]{:S(2)}, u32[]{:S(2)}) collective-permute-start(bf16[3,3,32,192]{3,2,1,0:T(8,128)(2,1)S(1)} %pad_maximum_fusion.7), channel_id=1, source_target_pairs={{0,7},{1,0},{2,1},{3,2},{4,3},{5,4},{6,5},{7,6},{8,15},{9,8},{10,9... | collective-permute-start | bytes 331784 | tf_op jit(solution)/shard_map/ppermute | solution.py:127
  122.8 6.4 %collective-permute-start.30 = (bf16[3,3,32,192]{3,2,1,0:T(8,128)(2,1)S(1)}, bf16[3,3,32,192]{3,2,1,0:T(8,128)(2,1)S(1)}, u32[]{:S(2)}, u32[]{:S(2)}) collective-permute-start(bf16[3,3,32,192]{3,2,1,0:T(8,128)(2,1)S(1)} %pad_maximum_fusion.7), channel_id=1, source_target_pairs={{0,1},{1,2},{2,3},{3,4},{4,5},{5,6},{6,7},{7,0},{8,9},{9,10},{10,1... | collective-permute-start | bytes 331784 | tf_op jit(solution)/shard_map/ppermute | solution.py:127
  142.9 4.6 %collective-permute-start.36 = (f32[32,32]{0,1:T(8,128)S(1)}, f32[32,32]{0,1:T(8,128)S(1)}, u32[]{:S(2)}, u32[]{:S(2)}) collective-permute-start(f32[32,32]{0,1:T(8,128)S(1)} %add.296), channel_id=1, source_target_pairs={{0,4},{1,5},{2,6},{3,7},{4,0},{5,1},{6,2},{7,3},{8,12},{9,13},{10,... | collective-permute-start | bytes 12296 | tf_op jit(solution)/shard_map/ppermute | solution.py:95
  154.8 5.0 %collective-permute-start.37 = (bf16[3,32,192]{2,1,0:T(8,128)(2,1)S(1)}, bf16[3,32,192]{2,1,0:T(8,128)(2,1)S(1)}, u32[]{:S(2)}, u32[]{:S(2)}) collective-permute-start(bf16[3,32,192]{2,1,0:T(8,128)(2,1)S(1)} %get-tuple-element.14), channel_id=1, source_target_pairs={{0,8},{8,16},{16,24},{24,0},{1,9},{9,17},{17,25},{25,1},{2,10},{10... | collective-permute-start | bytes 110600 | tf_op jit(solution)/shard_map/ppermute | solution.py:127
  155.6 4.4 %collective-permute-start.38 = (bf16[3,32,192]{2,1,0:T(8,128)(2,1)S(1)}, bf16[3,32,192]{2,1,0:T(8,128)(2,1)S(1)}, u32[]{:S(2)}, u32[]{:S(2)}) collective-permute-start(bf16[3,32,192]{2,1,0:T(8,128)(2,1)S(1)} %get-tuple-element.14), channel_id=1, source_target_pairs={{0,24},{8,0},{16,8},{24,16},{1,25},{9,1},{17,9},{25,17},{2,26},{10... | collective-permute-start | bytes 110600 | tf_op jit(solution)/shard_map/ppermute | solution.py:127
  160.1 4.1 %collective-permute-start.40 = (bf16[3,3,32,192]{3,2,1,0:T(8,128)(2,1)S(1)}, bf16[3,3,32,192]{3,2,1,0:T(8,128)(2,1)S(1)}, u32[]{:S(2)}, u32[]{:S(2)}) collective-permute-start(bf16[3,3,32,192]{3,2,1,0:T(8,128)(2,1)S(1)} %pad_maximum_fusion.8), channel_id=1, source_target_pairs={{0,7},{1,0},{2,1},{3,2},{4,3},{5,4},{6,5},{7,6},{8,15},{9,8},{10,9... | collective-permute-start | bytes 331784 | tf_op jit(solution)/shard_map/ppermute | solution.py:127
  160.2 6.7 %collective-permute-start.39 = (bf16[3,3,32,192]{3,2,1,0:T(8,128)(2,1)S(1)}, bf16[3,3,32,192]{3,2,1,0:T(8,128)(2,1)S(1)}, u32[]{:S(2)}, u32[]{:S(2)}) collective-permute-start(bf16[3,3,32,192]{3,2,1,0:T(8,128)(2,1)S(1)} %pad_maximum_fusion.8), channel_id=1, source_target_pairs={{0,1},{1,2},{2,3},{3,4},{4,5},{5,6},{6,7},{7,0},{8,9},{9,10},{10,1... | collective-permute-start | bytes 331784 | tf_op jit(solution)/shard_map/ppermute | solution.py:127
  167.9 5.0 %collective-permute-start.41 = (bf16[3,32,192]{2,1,0:T(8,128)(2,1)S(1)}, bf16[3,32,192]{2,1,0:T(8,128)(2,1)S(1)}, u32[]{:S(2)}, u32[]{:S(2)}) collective-permute-start(bf16[3,32,192]{2,1,0:T(8,128)(2,1)S(1)} %get-tuple-element.12), channel_id=1, source_target_pairs={{0,8},{8,16},{16,24},{24,0},{1,9},{9,17},{17,25},{25,1},{2,10},{10... | collective-permute-start | bytes 110600 | tf_op jit(solution)/shard_map/ppermute | solution.py:127
  170.3 4.1 %collective-permute-start.42 = (bf16[3,32,192]{2,1,0:T(8,128)(2,1)S(1)}, bf16[3,32,192]{2,1,0:T(8,128)(2,1)S(1)}, u32[]{:S(2)}, u32[]{:S(2)}) collective-permute-start(bf16[3,32,192]{2,1,0:T(8,128)(2,1)S(1)} %get-tuple-element.12), channel_id=1, source_target_pairs={{0,24},{8,0},{16,8},{24,16},{1,25},{9,1},{17,9},{25,17},{2,26},{10... | collective-permute-start | bytes 110600 | tf_op jit(solution)/shard_map/ppermute | solution.py:127
  174.5 5.0 %collective-permute-start.44 = (bf16[3,3,32,192]{3,2,1,0:T(8,128)(2,1)S(1)}, bf16[3,3,32,192]{3,2,1,0:T(8,128)(2,1)S(1)}, u32[]{:S(2)}, u32[]{:S(2)}) collective-permute-start(bf16[3,3,32,192]{3,2,1,0:T(8,128)(2,1)S(1)} %pad_maximum_fusion.9), channel_id=1, source_target_pairs={{0,7},{1,0},{2,1},{3,2},{4,3},{5,4},{6,5},{7,6},{8,15},{9,8},{10,9... | collective-permute-start | bytes 331784 | tf_op jit(solution)/shard_map/ppermute | solution.py:127
  176.8 6.4 %collective-permute-start.43 = (bf16[3,3,32,192]{3,2,1,0:T(8,128)(2,1)S(1)}, bf16[3,3,32,192]{3,2,1,0:T(8,128)(2,1)S(1)}, u32[]{:S(2)}, u32[]{:S(2)}) collective-permute-start(bf16[3,3,32,192]{3,2,1,0:T(8,128)(2,1)S(1)} %pad_maximum_fusion.9), channel_id=1, source_target_pairs={{0,1},{1,2},{2,3},{3,4},{4,5},{5,6},{6,7},{7,0},{8,9},{9,10},{10,1... | collective-permute-start | bytes 331784 | tf_op jit(solution)/shard_map/ppermute | solution.py:127
  184.1 5.0 %collective-permute-start.45 = (bf16[3,32,192]{2,1,0:T(8,128)(2,1)S(1)}, bf16[3,32,192]{2,1,0:T(8,128)(2,1)S(1)}, u32[]{:S(2)}, u32[]{:S(2)}) collective-permute-start(bf16[3,32,192]{2,1,0:T(8,128)(2,1)S(1)} %get-tuple-element.10), channel_id=1, source_target_pairs={{0,8},{8,16},{16,24},{24,0},{1,9},{9,17},{17,25},{25,1},{2,10},{10... | collective-permute-start | bytes 110600 | tf_op jit(solution)/shard_map/ppermute | solution.py:127
  189.5 4.1 %collective-permute-start.48 = (bf16[3,3,32,192]{3,2,1,0:T(8,128)(2,1)S(1)}, bf16[3,3,32,192]{3,2,1,0:T(8,128)(2,1)S(1)}, u32[]{:S(2)}, u32[]{:S(2)}) collective-permute-start(bf16[3,3,32,192]{3,2,1,0:T(8,128)(2,1)S(1)} %pad_maximum_fusion.10), channel_id=1, source_target_pairs={{0,7},{1,0},{2,1},{3,2},{4,3},{5,4},{6,5},{7,6},{8,15},{9,8},{10,9... | collective-permute-start | bytes 331784 | tf_op jit(solution)/shard_map/ppermute | solution.py:127
  189.6 6.4 %collective-permute-start.47 = (bf16[3,3,32,192]{3,2,1,0:T(8,128)(2,1)S(1)}, bf16[3,3,32,192]{3,2,1,0:T(8,128)(2,1)S(1)}, u32[]{:S(2)}, u32[]{:S(2)}) collective-permute-start(bf16[3,3,32,192]{3,2,1,0:T(8,128)(2,1)S(1)} %pad_maximum_fusion.10), channel_id=1, source_target_pairs={{0,1},{1,2},{2,3},{3,4},{4,5},{5,6},{6,7},{7,0},{8,9},{9,10},{10,1... | collective-permute-start | bytes 331784 | tf_op jit(solution)/shard_map/ppermute | solution.py:127
  197.0 5.0 %collective-permute-start.49 = (bf16[3,32,192]{2,1,0:T(8,128)(2,1)S(1)}, bf16[3,32,192]{2,1,0:T(8,128)(2,1)S(1)}, u32[]{:S(2)}, u32[]{:S(2)}) collective-permute-start(bf16[3,32,192]{2,1,0:T(8,128)(2,1)S(1)} %get-tuple-element.8), channel_id=1, source_target_pairs={{0,8},{8,16},{16,24},{24,0},{1,9},{9,17},{17,25},{25,1},{2,10},{10... | collective-permute-start | bytes 110600 | tf_op jit(solution)/shard_map/ppermute | solution.py:127
  203.1 4.1 %collective-permute-start.52 = (bf16[3,3,32,192]{3,2,1,0:T(8,128)(2,1)S(1)}, bf16[3,3,32,192]{3,2,1,0:T(8,128)(2,1)S(1)}, u32[]{:S(2)}, u32[]{:S(2)}) collective-permute-start(bf16[3,3,32,192]{3,2,1,0:T(8,128)(2,1)S(1)} %pad_maximum_fusion.11), channel_id=1, source_target_pairs={{0,7},{1,0},{2,1},{3,2},{4,3},{5,4},{6,5},{7,6},{8,15},{9,8},{10,9... | collective-permute-start | bytes 331784 | tf_op jit(solution)/shard_map/ppermute | solution.py:127
  204.0 6.4 %collective-permute-start.51 = (bf16[3,3,32,192]{3,2,1,0:T(8,128)(2,1)S(1)}, bf16[3,3,32,192]{3,2,1,0:T(8,128)(2,1)S(1)}, u32[]{:S(2)}, u32[]{:S(2)}) collective-permute-start(bf16[3,3,32,192]{3,2,1,0:T(8,128)(2,1)S(1)} %pad_maximum_fusion.11), channel_id=1, source_target_pairs={{0,1},{1,2},{2,3},{3,4},{4,5},{5,6},{6,7},{7,0},{8,9},{9,10},{10,1... | collective-permute-start | bytes 331784 | tf_op jit(solution)/shard_map/ppermute | solution.py:127
  211.3 4.1 %collective-permute-start.54 = (bf16[3,32,192]{2,1,0:T(8,128)(2,1)S(1)}, bf16[3,32,192]{2,1,0:T(8,128)(2,1)S(1)}, u32[]{:S(2)}, u32[]{:S(2)}) collective-permute-start(bf16[3,32,192]{2,1,0:T(8,128)(2,1)S(1)} %get-tuple-element.31), channel_id=1, source_target_pairs={{0,24},{8,0},{16,8},{24,16},{1,25},{9,1},{17,9},{25,17},{2,26},{10... | collective-permute-start | bytes 110600 | tf_op jit(solution)/shard_map/ppermute | solution.py:127
  213.2 5.0 %collective-permute-start.53 = (bf16[3,32,192]{2,1,0:T(8,128)(2,1)S(1)}, bf16[3,32,192]{2,1,0:T(8,128)(2,1)S(1)}, u32[]{:S(2)}, u32[]{:S(2)}) collective-permute-start(bf16[3,32,192]{2,1,0:T(8,128)(2,1)S(1)} %get-tuple-element.31), channel_id=1, source_target_pairs={{0,8},{8,16},{16,24},{24,0},{1,9},{9,17},{17,25},{25,1},{2,10},{10... | collective-permute-start | bytes 110600 | tf_op jit(solution)/shard_map/ppermute | solution.py:127
  218.2 4.1 %collective-permute-start.56 = (bf16[3,3,32,192]{3,2,1,0:T(8,128)(2,1)S(1)}, bf16[3,3,32,192]{3,2,1,0:T(8,128)(2,1)S(1)}, u32[]{:S(2)}, u32[]{:S(2)}) collective-permute-start(bf16[3,3,32,192]{3,2,1,0:T(8,128)(2,1)S(1)} %pad_maximum_fusion.12), channel_id=1, source_target_pairs={{0,7},{1,0},{2,1},{3,2},{4,3},{5,4},{6,5},{7,6},{8,15},{9,8},{10,9... | collective-permute-start | bytes 331784 | tf_op jit(solution)/shard_map/ppermute | solution.py:127
  218.3 6.4 %collective-permute-start.55 = (bf16[3,3,32,192]{3,2,1,0:T(8,128)(2,1)S(1)}, bf16[3,3,32,192]{3,2,1,0:T(8,128)(2,1)S(1)}, u32[]{:S(2)}, u32[]{:S(2)}) collective-permute-start(bf16[3,3,32,192]{3,2,1,0:T(8,128)(2,1)S(1)} %pad_maximum_fusion.12), channel_id=1, source_target_pairs={{0,1},{1,2},{2,3},{3,4},{4,5},{5,6},{6,7},{7,0},{8,9},{9,10},{10,1... | collective-permute-start | bytes 331784 | tf_op jit(solution)/shard_map/ppermute | solution.py:127
  225.7 4.1 %collective-permute-start.58 = (bf16[3,32,192]{2,1,0:T(8,128)(2,1)S(1)}, bf16[3,32,192]{2,1,0:T(8,128)(2,1)S(1)}, u32[]{:S(2)}, u32[]{:S(2)}) collective-permute-start(bf16[3,32,192]{2,1,0:T(8,128)(2,1)S(1)} %get-tuple-element.33), channel_id=1, source_target_pairs={{0,24},{8,0},{16,8},{24,16},{1,25},{9,1},{17,9},{25,17},{2,26},{10... | collective-permute-start | bytes 110600 | tf_op jit(solution)/shard_map/ppermute | solution.py:127
  226.4 5.0 %collective-permute-start.57 = (bf16[3,32,192]{2,1,0:T(8,128)(2,1)S(1)}, bf16[3,32,192]{2,1,0:T(8,128)(2,1)S(1)}, u32[]{:S(2)}, u32[]{:S(2)}) collective-permute-start(bf16[3,32,192]{2,1,0:T(8,128)(2,1)S(1)} %get-tuple-element.33), channel_id=1, source_target_pairs={{0,8},{8,16},{16,24},{24,0},{1,9},{9,17},{17,25},{25,1},{2,10},{10... | collective-permute-start | bytes 110600 | tf_op jit(solution)/shard_map/ppermute | solution.py:127
  231.4 4.1 %collective-permute-start.60 = (bf16[3,3,32,192]{3,2,1,0:T(8,128)(2,1)S(1)}, bf16[3,3,32,192]{3,2,1,0:T(8,128)(2,1)S(1)}, u32[]{:S(2)}, u32[]{:S(2)}) collective-permute-start(bf16[3,3,32,192]{3,2,1,0:T(8,128)(2,1)S(1)} %pad_maximum_fusion.13), channel_id=1, source_target_pairs={{0,7},{1,0},{2,1},{3,2},{4,3},{5,4},{6,5},{7,6},{8,15},{9,8},{10,9... | collective-permute-start | bytes 331784 | tf_op jit(solution)/shard_map/ppermute | solution.py:127
  232.0 6.4 %collective-permute-start.59 = (bf16[3,3,32,192]{3,2,1,0:T(8,128)(2,1)S(1)}, bf16[3,3,32,192]{3,2,1,0:T(8,128)(2,1)S(1)}, u32[]{:S(2)}, u32[]{:S(2)}) collective-permute-start(bf16[3,3,32,192]{3,2,1,0:T(8,128)(2,1)S(1)} %pad_maximum_fusion.13), channel_id=1, source_target_pairs={{0,1},{1,2},{2,3},{3,4},{4,5},{5,6},{6,7},{7,0},{8,9},{9,10},{10,1... | collective-permute-start | bytes 331784 | tf_op jit(solution)/shard_map/ppermute | solution.py:127
  239.3 4.1 %collective-permute-start.62 = (bf16[3,32,192]{2,1,0:T(8,128)(2,1)S(1)}, bf16[3,32,192]{2,1,0:T(8,128)(2,1)S(1)}, u32[]{:S(2)}, u32[]{:S(2)}) collective-permute-start(bf16[3,32,192]{2,1,0:T(8,128)(2,1)S(1)} %get-tuple-element.35), channel_id=1, source_target_pairs={{0,24},{8,0},{16,8},{24,16},{1,25},{9,1},{17,9},{25,17},{2,26},{10... | collective-permute-start | bytes 110600 | tf_op jit(solution)/shard_map/ppermute | solution.py:127
  240.6 5.0 %collective-permute-start.61 = (bf16[3,32,192]{2,1,0:T(8,128)(2,1)S(1)}, bf16[3,32,192]{2,1,0:T(8,128)(2,1)S(1)}, u32[]{:S(2)}, u32[]{:S(2)}) collective-permute-start(bf16[3,32,192]{2,1,0:T(8,128)(2,1)S(1)} %get-tuple-element.35), channel_id=1, source_target_pairs={{0,8},{8,16},{16,24},{24,0},{1,9},{9,17},{17,25},{25,1},{2,10},{10... | collective-permute-start | bytes 110600 | tf_op jit(solution)/shard_map/ppermute | solution.py:127
  245.6 4.1 %collective-permute-start.64 = (bf16[3,3,32,192]{3,2,1,0:T(8,128)(2,1)S(1)}, bf16[3,3,32,192]{3,2,1,0:T(8,128)(2,1)S(1)}, u32[]{:S(2)}, u32[]{:S(2)}) collective-permute-start(bf16[3,3,32,192]{3,2,1,0:T(8,128)(2,1)S(1)} %pad_maximum_fusion.14), channel_id=1, source_target_pairs={{0,7},{1,0},{2,1},{3,2},{4,3},{5,4},{6,5},{7,6},{8,15},{9,8},{10,9... | collective-permute-start | bytes 331784 | tf_op jit(solution)/shard_map/ppermute | solution.py:127
  245.7 6.4 %collective-permute-start.63 = (bf16[3,3,32,192]{3,2,1,0:T(8,128)(2,1)S(1)}, bf16[3,3,32,192]{3,2,1,0:T(8,128)(2,1)S(1)}, u32[]{:S(2)}, u32[]{:S(2)}) collective-permute-start(bf16[3,3,32,192]{3,2,1,0:T(8,128)(2,1)S(1)} %pad_maximum_fusion.14), channel_id=1, source_target_pairs={{0,1},{1,2},{2,3},{3,4},{4,5},{5,6},{6,7},{7,0},{8,9},{9,10},{10,1... | collective-permute-start | bytes 331784 | tf_op jit(solution)/shard_map/ppermute | solution.py:127
  253.0 4.4 %collective-permute-start.66 = (bf16[3,32,192]{2,1,0:T(8,128)(2,1)S(1)}, bf16[3,32,192]{2,1,0:T(8,128)(2,1)S(1)}, u32[]{:S(2)}, u32[]{:S(2)}) collective-permute-start(bf16[3,32,192]{2,1,0:T(8,128)(2,1)S(1)} %get-tuple-element.37), channel_id=1, source_target_pairs={{0,24},{8,0},{16,8},{24,16},{1,25},{9,1},{17,9},{25,17},{2,26},{10... | collective-permute-start | bytes 110600 | tf_op jit(solution)/shard_map/ppermute | solution.py:127
  254.2 5.0 %collective-permute-start.65 = (bf16[3,32,192]{2,1,0:T(8,128)(2,1)S(1)}, bf16[3,32,192]{2,1,0:T(8,128)(2,1)S(1)}, u32[]{:S(2)}, u32[]{:S(2)}) collective-permute-start(bf16[3,32,192]{2,1,0:T(8,128)(2,1)S(1)} %get-tuple-element.37), channel_id=1, source_target_pairs={{0,8},{8,16},{16,24},{24,0},{1,9},{9,17},{17,25},{25,1},{2,10},{10... | collective-permute-start | bytes 110600 | tf_op jit(solution)/shard_map/ppermute | solution.py:127
  259.2 4.1 %collective-permute-start.68 = (bf16[3,3,32,192]{3,2,1,0:T(8,128)(2,1)S(1)}, bf16[3,3,32,192]{3,2,1,0:T(8,128)(2,1)S(1)}, u32[]{:S(2)}, u32[]{:S(2)}) collective-permute-start(bf16[3,3,32,192]{3,2,1,0:T(8,128)(2,1)S(1)} %pad_maximum_fusion.15), channel_id=1, source_target_pairs={{0,7},{1,0},{2,1},{3,2},{4,3},{5,4},{6,5},{7,6},{8,15},{9,8},{10,9... | collective-permute-start | bytes 331784 | tf_op jit(solution)/shard_map/ppermute | solution.py:127
  259.5 6.4 %collective-permute-start.67 = (bf16[3,3,32,192]{3,2,1,0:T(8,128)(2,1)S(1)}, bf16[3,3,32,192]{3,2,1,0:T(8,128)(2,1)S(1)}, u32[]{:S(2)}, u32[]{:S(2)}) collective-permute-start(bf16[3,3,32,192]{3,2,1,0:T(8,128)(2,1)S(1)} %pad_maximum_fusion.15), channel_id=1, source_target_pairs={{0,1},{1,2},{2,3},{3,4},{4,5},{5,6},{6,7},{7,0},{8,9},{9,10},{10,1... | collective-permute-start | bytes 331784 | tf_op jit(solution)/shard_map/ppermute | solution.py:127
  279.6 4.6 %collective-permute-start.73 = (f32[32,32]{0,1:T(8,128)S(1)}, f32[32,32]{0,1:T(8,128)S(1)}, u32[]{:S(2)}, u32[]{:S(2)}) collective-permute-start(f32[32,32]{0,1:T(8,128)S(1)} %add.332), channel_id=1, source_target_pairs={{0,4},{1,5},{2,6},{3,7},{4,0},{5,1},{6,2},{7,3},{8,12},{9,13},{10,... | collective-permute-start | bytes 12296 | tf_op jit(solution)/shard_map/ppermute | solution.py:95
  (14 other events, 168.2 us)

commit v3 on v1

--- a/solution.py
+++ b/solution.py
@@ -53,10 +53,19 @@
         if count & (count - 1):
             value = lax.psum(value, axis)
             continue
+
+        def swap(v, stride):
+            return lax.ppermute(v, axis, [(i, i ^ stride) for i in range(count)])
+
         stride = 1
         while stride < count:
-            value = value + lax.ppermute(value, axis, [(i, i ^ stride) for i in range(count)])
-            stride *= 2
+            if 4 * stride <= count:
+                near, far, both = swap(value, stride), swap(value, 2 * stride), swap(value, 3 * stride)
+                value = (value + near) + (far + both)
+                stride *= 4
+            else:
+                value = value + swap(value, stride)
+                stride *= 2
     return value
 
 

time: 290 us -> 287 us (0.990)
  waiting for transfers between devices: 136 us -> 124 us
  starting transfers between devices: 70.7 us -> 79.1 us
    ppermute x10 -> x14, waiting for transfers between devices: 29.2 us -> 18.6 us  [swap(): return lax.ppermute(v, axis, [(i, i ^ stride) for i in range(count)])]
    ppermute x10 -> x14, starting transfers between devices: 5.01 us -> 12.9 us  [swap(): return lax.ppermute(v, axis, [(i, i ^ stride) for i in range(count)])]
  transfers between devices with their start and end apart: 74 -> 78, of which waited for: 71 -> 71; matrix products, arithmetic and copies ran while one was open for 18% -> 18% of each run, Pallas kernels for 0% -> 0%
where the time goes in v3:
time: 287 us; the launch traced here: 286 us
  waiting for transfers between devices  124 us (43%)
  starting transfers between devices  79.1 us (28%)
  matrix products  51.3 us (18%)
  other arithmetic  20.9 us (7%)
  local copies, waits for them, and re-layouts  10.6 us (4%)
    ppermute x64, waiting for transfers between devices, shift(): lax.ppermute(value, axis, [(i, (i + step) % count) for i in range(count)])  106 us
    ppermute x64, starting transfers between devices, shift(): lax.ppermute(value, axis, [(i, (i + step) % count) for i in range(count)])  66.2 us
    dot_general x64, matrix products, part(): jnp.einsum('kvj,tkij->tvi', cells, blocks, preferred_element_type=jnp.flo...  49.3 us
    ppermute x14, waiting for transfers between devices, swap(): return lax.ppermute(v, axis, [(i, i ^ stride) for i in range(count)])  18.6 us
    ppermute x14, starting transfers between devices, swap(): return lax.ppermute(v, axis, [(i, i ^ stride) for i in range(count)])  12.9 us
    gather x1, local copies, waits for them, and re-layouts, dense_coupling(): jnp.take(matrices, index.reshape(-1), axis=0)  10.3 us
    another operation x6, other arithmetic, orthonormal(): factor = jnp.linalg.cholesky(gram_matrix)  7.19 us
    another operation x4, other arithmetic, orthonormal(): inverse = jax.scipy.linalg.solve_triangular(factor, identity, lower=True)  6.17 us
  transfers between devices with their start and end apart: 78, of which 71 were waited for; matrix products, arithmetic and copies ran while one was open for 18% of the time, Pallas kernels for 0%

profile of v3, /device:TPU:0, one launch (start us, length us, event | category | flops | bytes accessed | tf_op | source)
XLA Modules:
  0.0 286.5 jit_solution(16693324285831152698)
XLA Ops:
  0.9 3.0 %collective-permute-start = (bf16[3,32,192]{2,1,0:T(8,128)(2,1)S(1)}, bf16[3,32,192]{2,1,0:T(8,128)(2,1)S(1)}, u32[]{:S(2)}, u32[]{:S(2)}) collective-permute-start(bf16[3,32,192]{2,1,0:T(8,128)(2,1)S(1)} %get-tuple-element.16), channel_id=1, source_target_pairs={{0,8},{8,16},{16,24},{24,0},{1,9},{9,17},{17,25},{25,1},{2,10},{10... | collective-permute-start | bytes 110600 | tf_op jit(solution)/shard_map/ppermute | solution.py:99
  6.7 10.3 %gather_fusion = bf16[81,192,192]{2,1,0:T(8,128)(2,1)} fusion(bf16[81,192,192]{2,1,0:T(8,128)(2,1)} %bitcast.915, s32[1024]{0:T(1024)S(1)} %pad_clamp_fusion), kind=kCustom, calls=%fused_computation | custom fusion | bytes 11944260 | tf_op jit(solution)/shard_map/jit(_take)/gather | solution.py:42
  17.1 4.3 %select_select_fusion = bf16[3,27,192,192]{3,2,1,0:T(8,128)(2,1)S(1)} fusion(bf16[3,27,192,192]{3,2,1,0:T(8,128)(2,1)} %bitcast.914, pred[3,27]{1,0:T(4,128)(4,1)S(1)} %compare_and_fusion, pred[3,27]{1,0:T(4,128)(4,1)S(1)} %and_reduce_fusion), kind=kLoop, calls=%fused_computation.1 | loop fusion | flops 5971968 | bytes 11944098 | tf_op jit(solution)/shard_map/jit(_where)/select_n | solution.py:46
  21.8 2.9 %collective-permute-start.3 = (bf16[3,3,32,192]{3,2,1,0:T(8,128)(2,1)S(1)}, bf16[3,3,32,192]{3,2,1,0:T(8,128)(2,1)S(1)}, u32[]{:S(2)}, u32[]{:S(2)}) collective-permute-start(bf16[3,3,32,192]{3,2,1,0:T(8,128)(2,1)S(1)} %pad_maximum_fusion), channel_id=1, source_target_pairs={{0,7},{1,0},{2,1},{3,2},{4,3},{5,4},{6,5},{7,6},{8,15},{9,8},{10,9... | collective-permute-start | bytes 331784 | tf_op jit(solution)/shard_map/ppermute | solution.py:99
  25.4 2.3 collective-permute-done.3
  28.5 2.6 collective-permute-done.2
  32.7 2.4 collective-permute-start.5
  35.4 1.7 collective-permute-done.4
  39.5 2.3 collective-permute-done.7
  42.7 2.6 collective-permute-done.6
  53.2 2.6 collective-permute-done.11
  56.7 2.3 collective-permute-done.10
  63.2 1.7 collective-permute-done.12
  66.7 2.7 collective-permute-done.15
  70.3 2.2 collective-permute-done.14
  80.4 2.7 collective-permute-done.19
  84.0 2.1 collective-permute-done.18
  87.1 1.8 collective-permute-start.20
  94.5 2.6 collective-permute-done.23
  98.0 2.3 collective-permute-done.22
  108.3 2.4 collective-permute-done.27
  111.6 2.4 collective-permute-done.26
  116.2 1.8 collective-permute-start.29
  121.8 2.7 collective-permute-done.31
  125.4 2.2 collective-permute-done.30
  133.9 2.1 collective-permute-done.34
  136.1 1.8 collective-permute-start.37
  137.9 1.9 collective-permute-done.36
  140.9 3.6 %collective-permute-done.38 = f32[32,32]{0,1:T(8,128)S(1)} collective-permute-done((f32[32,32]{0,1:T(8,128)S(1)}, f32[32,32]{0,1:T(8,128)S(1)}, u32[]{:S(2)}, u32[]{:S(2)}) %collective-permute-start.38) | collective-permute-done | bytes 4128 | tf_op jit(solution)/shard_map/ppermute | solution.py:58
  144.7 2.9 %cholesky.44 = f32[32,32]{1,0:T(8,128)S(1)} custom-call(f32[32,32]{1,0:T(8,128)S(1)} %fusion.162), custom_call_target="Cholesky" | custom-call | tf_op jit(solution)/shard_map/jit(cholesky)/cholesky | solution.py:77
  148.9 2.4 custom-call.6
  152.5 2.3 collective-permute-start.40
  157.5 2.1 fusion.98
  160.3 2.6 convolution_bitcast_fusion.14
  164.4 2.3 collective-permute-start.43
  167.8 2.1 collective-permute-done.43
  170.8 1.9 collective-permute-start.46
  173.4 2.1 collective-permute-done.46
  176.3 2.8 collective-permute-done.45
  183.4 1.7 collective-permute-done.47
  187.2 2.6 collective-permute-done.50
  190.7 2.3 collective-permute-done.49
  197.3 1.7 collective-permute-done.51
  200.9 2.6 collective-permute-done.54
  204.4 2.3 collective-permute-done.53
  211.0 1.7 collective-permute-done.55
  214.6 2.6 collective-permute-done.58
  218.1 2.3 collective-permute-done.57
  222.6 1.7 collective-permute-start.60
  224.6 1.7 collective-permute-done.59
  228.3 2.5 collective-permute-done.62
  231.7 2.4 collective-permute-done.61
  238.4 1.7 collective-permute-done.63
  242.1 2.8 collective-permute-done.66
  245.8 2.0 collective-permute-done.65
  252.2 1.7 collective-permute-done.67
  256.0 2.4 collective-permute-done.70
  259.2 2.5 collective-permute-done.69
  267.9 2.1 collective-permute-done.73
  270.1 1.8 collective-permute-start.76
  271.9 1.9 collective-permute-done.75
  274.7 3.9 %collective-permute-done.77 = f32[32,32]{0,1:T(8,128)S(1)} collective-permute-done((f32[32,32]{0,1:T(8,128)S(1)}, f32[32,32]{0,1:T(8,128)S(1)}, u32[]{:S(2)}, u32[]{:S(2)}) %collective-permute-start.77) | collective-permute-done | bytes 4128 | tf_op jit(solution)/shard_map/ppermute | solution.py:58
  278.7 2.9 %cholesky.55 = f32[32,32]{1,0:T(8,128)S(1)} custom-call(f32[32,32]{1,0:T(8,128)S(1)} %fusion.160), custom_call_target="Cholesky" | custom-call | tf_op jit(solution)/shard_map/jit(cholesky)/cholesky | solution.py:77
  282.9 2.4 custom-call.7
  (219 shorter events, 128.2 us)
Async XLA Ops:
  0.9 20.8 %collective-permute-start = (bf16[3,32,192]{2,1,0:T(8,128)(2,1)S(1)}, bf16[3,32,192]{2,1,0:T(8,128)(2,1)S(1)}, u32[]{:S(2)}, u32[]{:S(2)}) collective-permute-start(bf16[3,32,192]{2,1,0:T(8,128)(2,1)S(1)} %get-tuple-element.16), channel_id=1, source_target_pairs={{0,8},{8,16},{16,24},{24,0},{1,9},{9,17},{17,25},{25,1},{2,10},{10... | collective-permute-start | bytes 110600 | tf_op jit(solution)/shard_map/ppermute | solution.py:99
  3.9 17.9 %collective-permute-start.1 = (bf16[3,32,192]{2,1,0:T(8,128)(2,1)S(1)}, bf16[3,32,192]{2,1,0:T(8,128)(2,1)S(1)}, u32[]{:S(2)}, u32[]{:S(2)}) collective-permute-start(bf16[3,32,192]{2,1,0:T(8,128)(2,1)S(1)} %get-tuple-element.16), channel_id=1, source_target_pairs={{0,24},{8,0},{16,8},{24,16},{1,25},{9,1},{17,9},{25,17},{2,26},{10... | collective-permute-start | bytes 110600 | tf_op jit(solution)/shard_map/ppermute | solution.py:99
  21.8 5.8 %collective-permute-start.3 = (bf16[3,3,32,192]{3,2,1,0:T(8,128)(2,1)S(1)}, bf16[3,3,32,192]{3,2,1,0:T(8,128)(2,1)S(1)}, u32[]{:S(2)}, u32[]{:S(2)}) collective-permute-start(bf16[3,3,32,192]{3,2,1,0:T(8,128)(2,1)S(1)} %pad_maximum_fusion), channel_id=1, source_target_pairs={{0,7},{1,0},{2,1},{3,2},{4,3},{5,4},{6,5},{7,6},{8,15},{9,8},{10,9... | collective-permute-start | bytes 331784 | tf_op jit(solution)/shard_map/ppermute | solution.py:99
  24.8 6.4 %collective-permute-start.2 = (bf16[3,3,32,192]{3,2,1,0:T(8,128)(2,1)S(1)}, bf16[3,3,32,192]{3,2,1,0:T(8,128)(2,1)S(1)}, u32[]{:S(2)}, u32[]{:S(2)}) collective-permute-start(bf16[3,3,32,192]{3,2,1,0:T(8,128)(2,1)S(1)} %pad_maximum_fusion), channel_id=1, source_target_pairs={{0,1},{1,2},{2,3},{3,4},{4,5},{5,6},{6,7},{7,0},{8,9},{9,10},{10,1... | collective-permute-start | bytes 331784 | tf_op jit(solution)/shard_map/ppermute | solution.py:99
  32.1 5.0 %collective-permute-start.4 = (bf16[3,32,192]{2,1,0:T(8,128)(2,1)S(1)}, bf16[3,32,192]{2,1,0:T(8,128)(2,1)S(1)}, u32[]{:S(2)}, u32[]{:S(2)}) collective-permute-start(bf16[3,32,192]{2,1,0:T(8,128)(2,1)S(1)} %get-tuple-element.17), channel_id=1, source_target_pairs={{0,8},{8,16},{16,24},{24,0},{1,9},{9,17},{17,25},{25,1},{2,10},{10... | collective-permute-start | bytes 110600 | tf_op jit(solution)/shard_map/ppermute | solution.py:99
  32.7 4.9 %collective-permute-start.5 = (bf16[3,32,192]{2,1,0:T(8,128)(2,1)S(1)}, bf16[3,32,192]{2,1,0:T(8,128)(2,1)S(1)}, u32[]{:S(2)}, u32[]{:S(2)}) collective-permute-start(bf16[3,32,192]{2,1,0:T(8,128)(2,1)S(1)} %get-tuple-element.17), channel_id=1, source_target_pairs={{0,24},{8,0},{16,8},{24,16},{1,25},{9,1},{17,9},{25,17},{2,26},{10... | collective-permute-start | bytes 110600 | tf_op jit(solution)/shard_map/ppermute | solution.py:99
  37.7 4.1 %collective-permute-start.7 = (bf16[3,3,32,192]{3,2,1,0:T(8,128)(2,1)S(1)}, bf16[3,3,32,192]{3,2,1,0:T(8,128)(2,1)S(1)}, u32[]{:S(2)}, u32[]{:S(2)}) collective-permute-start(bf16[3,3,32,192]{3,2,1,0:T(8,128)(2,1)S(1)} %pad_maximum_fusion.1), channel_id=1, source_target_pairs={{0,7},{1,0},{2,1},{3,2},{4,3},{5,4},{6,5},{7,6},{8,15},{9,8},{10,9... | collective-permute-start | bytes 331784 | tf_op jit(solution)/shard_map/ppermute | solution.py:99
  38.9 6.4 %collective-permute-start.6 = (bf16[3,3,32,192]{3,2,1,0:T(8,128)(2,1)S(1)}, bf16[3,3,32,192]{3,2,1,0:T(8,128)(2,1)S(1)}, u32[]{:S(2)}, u32[]{:S(2)}) collective-permute-start(bf16[3,3,32,192]{3,2,1,0:T(8,128)(2,1)S(1)} %pad_maximum_fusion.1), channel_id=1, source_target_pairs={{0,1},{1,2},{2,3},{3,4},{4,5},{5,6},{6,7},{7,0},{8,9},{9,10},{10,1... | collective-permute-start | bytes 331784 | tf_op jit(solution)/shard_map/ppermute | solution.py:99
  46.2 5.0 %collective-permute-start.8 = (bf16[3,32,192]{2,1,0:T(8,128)(2,1)S(1)}, bf16[3,32,192]{2,1,0:T(8,128)(2,1)S(1)}, u32[]{:S(2)}, u32[]{:S(2)}) collective-permute-start(bf16[3,32,192]{2,1,0:T(8,128)(2,1)S(1)} %get-tuple-element.19), channel_id=1, source_target_pairs={{0,8},{8,16},{16,24},{24,0},{1,9},{9,17},{17,25},{25,1},{2,10},{10... | collective-permute-start | bytes 110600 | tf_op jit(solution)/shard_map/ppermute | solution.py:99
  47.5 4.1 %collective-permute-start.9 = (bf16[3,32,192]{2,1,0:T(8,128)(2,1)S(1)}, bf16[3,32,192]{2,1,0:T(8,128)(2,1)S(1)}, u32[]{:S(2)}, u32[]{:S(2)}) collective-permute-start(bf16[3,32,192]{2,1,0:T(8,128)(2,1)S(1)} %get-tuple-element.19), channel_id=1, source_target_pairs={{0,24},{8,0},{16,8},{24,16},{1,25},{9,1},{17,9},{25,17},{2,26},{10... | collective-permute-start | bytes 110600 | tf_op jit(solution)/shard_map/ppermute | solution.py:99
  51.7 4.1 %collective-permute-start.11 = (bf16[3,3,32,192]{3,2,1,0:T(8,128)(2,1)S(1)}, bf16[3,3,32,192]{3,2,1,0:T(8,128)(2,1)S(1)}, u32[]{:S(2)}, u32[]{:S(2)}) collective-permute-start(bf16[3,3,32,192]{3,2,1,0:T(8,128)(2,1)S(1)} %pad_maximum_fusion.2), channel_id=1, source_target_pairs={{0,7},{1,0},{2,1},{3,2},{4,3},{5,4},{6,5},{7,6},{8,15},{9,8},{10,9... | collective-permute-start | bytes 331784 | tf_op jit(solution)/shard_map/ppermute | solution.py:99
  52.6 6.4 %collective-permute-start.10 = (bf16[3,3,32,192]{3,2,1,0:T(8,128)(2,1)S(1)}, bf16[3,3,32,192]{3,2,1,0:T(8,128)(2,1)S(1)}, u32[]{:S(2)}, u32[]{:S(2)}) collective-permute-start(bf16[3,3,32,192]{3,2,1,0:T(8,128)(2,1)S(1)} %pad_maximum_fusion.2), channel_id=1, source_target_pairs={{0,1},{1,2},{2,3},{3,4},{4,5},{5,6},{6,7},{7,0},{8,9},{9,10},{10,1... | collective-permute-start | bytes 331784 | tf_op jit(solution)/shard_map/ppermute | solution.py:99
  59.9 5.0 %collective-permute-start.12 = (bf16[3,32,192]{2,1,0:T(8,128)(2,1)S(1)}, bf16[3,32,192]{2,1,0:T(8,128)(2,1)S(1)}, u32[]{:S(2)}, u32[]{:S(2)}) collective-permute-start(bf16[3,32,192]{2,1,0:T(8,128)(2,1)S(1)} %get-tuple-element.21), channel_id=1, source_target_pairs={{0,8},{8,16},{16,24},{24,0},{1,9},{9,17},{17,25},{25,1},{2,10},{10... | collective-permute-start | bytes 110600 | tf_op jit(solution)/shard_map/ppermute | solution.py:99
  61.2 4.1 %collective-permute-start.13 = (bf16[3,32,192]{2,1,0:T(8,128)(2,1)S(1)}, bf16[3,32,192]{2,1,0:T(8,128)(2,1)S(1)}, u32[]{:S(2)}, u32[]{:S(2)}) collective-permute-start(bf16[3,32,192]{2,1,0:T(8,128)(2,1)S(1)} %get-tuple-element.21), channel_id=1, source_target_pairs={{0,24},{8,0},{16,8},{24,16},{1,25},{9,1},{17,9},{25,17},{2,26},{10... | collective-permute-start | bytes 110600 | tf_op jit(solution)/shard_map/ppermute | solution.py:99
  65.3 4.1 %collective-permute-start.15 = (bf16[3,3,32,192]{3,2,1,0:T(8,128)(2,1)S(1)}, bf16[3,3,32,192]{3,2,1,0:T(8,128)(2,1)S(1)}, u32[]{:S(2)}, u32[]{:S(2)}) collective-permute-start(bf16[3,3,32,192]{3,2,1,0:T(8,128)(2,1)S(1)} %pad_maximum_fusion.3), channel_id=1, source_target_pairs={{0,7},{1,0},{2,1},{3,2},{4,3},{5,4},{6,5},{7,6},{8,15},{9,8},{10,9... | collective-permute-start | bytes 331784 | tf_op jit(solution)/shard_map/ppermute | solution.py:99
  66.1 6.4 %collective-permute-start.14 = (bf16[3,3,32,192]{3,2,1,0:T(8,128)(2,1)S(1)}, bf16[3,3,32,192]{3,2,1,0:T(8,128)(2,1)S(1)}, u32[]{:S(2)}, u32[]{:S(2)}) collective-permute-start(bf16[3,3,32,192]{3,2,1,0:T(8,128)(2,1)S(1)} %pad_maximum_fusion.3), channel_id=1, source_target_pairs={{0,1},{1,2},{2,3},{3,4},{4,5},{5,6},{6,7},{7,0},{8,9},{9,10},{10,1... | collective-permute-start | bytes 331784 | tf_op jit(solution)/shard_map/ppermute | solution.py:99
  73.4 5.0 %collective-permute-start.16 = (bf16[3,32,192]{2,1,0:T(8,128)(2,1)S(1)}, bf16[3,32,192]{2,1,0:T(8,128)(2,1)S(1)}, u32[]{:S(2)}, u32[]{:S(2)}) collective-permute-start(bf16[3,32,192]{2,1,0:T(8,128)(2,1)S(1)} %get-tuple-element.23), channel_id=1, source_target_pairs={{0,8},{8,16},{16,24},{24,0},{1,9},{9,17},{17,25},{25,1},{2,10},{10... | collective-permute-start | bytes 110600 | tf_op jit(solution)/shard_map/ppermute | solution.py:99
  74.9 4.1 %collective-permute-start.17 = (bf16[3,32,192]{2,1,0:T(8,128)(2,1)S(1)}, bf16[3,32,192]{2,1,0:T(8,128)(2,1)S(1)}, u32[]{:S(2)}, u32[]{:S(2)}) collective-permute-start(bf16[3,32,192]{2,1,0:T(8,128)(2,1)S(1)} %get-tuple-element.23), channel_id=1, source_target_pairs={{0,24},{8,0},{16,8},{24,16},{1,25},{9,1},{17,9},{25,17},{2,26},{10... | collective-permute-start | bytes 110600 | tf_op jit(solution)/shard_map/ppermute | solution.py:99
  79.0 4.1 %collective-permute-start.19 = (bf16[3,3,32,192]{3,2,1,0:T(8,128)(2,1)S(1)}, bf16[3,3,32,192]{3,2,1,0:T(8,128)(2,1)S(1)}, u32[]{:S(2)}, u32[]{:S(2)}) collective-permute-start(bf16[3,3,32,192]{3,2,1,0:T(8,128)(2,1)S(1)} %pad_maximum_fusion.4), channel_id=1, source_target_pairs={{0,7},{1,0},{2,1},{3,2},{4,3},{5,4},{6,5},{7,6},{8,15},{9,8},{10,9... | collective-permute-start | bytes 331784 | tf_op jit(solution)/shard_map/ppermute | solution.py:99
  79.8 6.4 %collective-permute-start.18 = (bf16[3,3,32,192]{3,2,1,0:T(8,128)(2,1)S(1)}, bf16[3,3,32,192]{3,2,1,0:T(8,128)(2,1)S(1)}, u32[]{:S(2)}, u32[]{:S(2)}) collective-permute-start(bf16[3,3,32,192]{3,2,1,0:T(8,128)(2,1)S(1)} %pad_maximum_fusion.4), channel_id=1, source_target_pairs={{0,1},{1,2},{2,3},{3,4},{4,5},{5,6},{6,7},{7,0},{8,9},{9,10},{10,1... | collective-permute-start | bytes 331784 | tf_op jit(solution)/shard_map/ppermute | solution.py:99
  87.1 5.0 %collective-permute-start.20 = (bf16[3,32,192]{2,1,0:T(8,128)(2,1)S(1)}, bf16[3,32,192]{2,1,0:T(8,128)(2,1)S(1)}, u32[]{:S(2)}, u32[]{:S(2)}) collective-permute-start(bf16[3,32,192]{2,1,0:T(8,128)(2,1)S(1)} %get-tuple-element.25), channel_id=1, source_target_pairs={{0,8},{8,16},{16,24},{24,0},{1,9},{9,17},{17,25},{25,1},{2,10},{10... | collective-permute-start | bytes 110600 | tf_op jit(solution)/shard_map/ppermute | solution.py:99
  88.9 4.1 %collective-permute-start.21 = (bf16[3,32,192]{2,1,0:T(8,128)(2,1)S(1)}, bf16[3,32,192]{2,1,0:T(8,128)(2,1)S(1)}, u32[]{:S(2)}, u32[]{:S(2)}) collective-permute-start(bf16[3,32,192]{2,1,0:T(8,128)(2,1)S(1)} %get-tuple-element.25), channel_id=1, source_target_pairs={{0,24},{8,0},{16,8},{24,16},{1,25},{9,1},{17,9},{25,17},{2,26},{10... | collective-permute-start | bytes 110600 | tf_op jit(solution)/shard_map/ppermute | solution.py:99
  93.0 4.1 %collective-permute-start.23 = (bf16[3,3,32,192]{3,2,1,0:T(8,128)(2,1)S(1)}, bf16[3,3,32,192]{3,2,1,0:T(8,128)(2,1)S(1)}, u32[]{:S(2)}, u32[]{:S(2)}) collective-permute-start(bf16[3,3,32,192]{3,2,1,0:T(8,128)(2,1)S(1)} %pad_maximum_fusion.5), channel_id=1, source_target_pairs={{0,7},{1,0},{2,1},{3,2},{4,3},{5,4},{6,5},{7,6},{8,15},{9,8},{10,9... | collective-permute-start | bytes 331784 | tf_op jit(solution)/shard_map/ppermute | solution.py:99
  93.9 6.4 %collective-permute-start.22 = (bf16[3,3,32,192]{3,2,1,0:T(8,128)(2,1)S(1)}, bf16[3,3,32,192]{3,2,1,0:T(8,128)(2,1)S(1)}, u32[]{:S(2)}, u32[]{:S(2)}) collective-permute-start(bf16[3,3,32,192]{3,2,1,0:T(8,128)(2,1)S(1)} %pad_maximum_fusion.5), channel_id=1, source_target_pairs={{0,1},{1,2},{2,3},{3,4},{4,5},{5,6},{6,7},{7,0},{8,9},{9,10},{10,1... | collective-permute-start | bytes 331784 | tf_op jit(solution)/shard_map/ppermute | solution.py:99
  101.2 5.0 %collective-permute-start.24 = (bf16[3,32,192]{2,1,0:T(8,128)(2,1)S(1)}, bf16[3,32,192]{2,1,0:T(8,128)(2,1)S(1)}, u32[]{:S(2)}, u32[]{:S(2)}) collective-permute-start(bf16[3,32,192]{2,1,0:T(8,128)(2,1)S(1)} %get-tuple-element.27), channel_id=1, source_target_pairs={{0,8},{8,16},{16,24},{24,0},{1,9},{9,17},{17,25},{25,1},{2,10},{10... | collective-permute-start | bytes 110600 | tf_op jit(solution)/shard_map/ppermute | solution.py:99
  102.5 4.1 %collective-permute-start.25 = (bf16[3,32,192]{2,1,0:T(8,128)(2,1)S(1)}, bf16[3,32,192]{2,1,0:T(8,128)(2,1)S(1)}, u32[]{:S(2)}, u32[]{:S(2)}) collective-permute-start(bf16[3,32,192]{2,1,0:T(8,128)(2,1)S(1)} %get-tuple-element.27), channel_id=1, source_target_pairs={{0,24},{8,0},{16,8},{24,16},{1,25},{9,1},{17,9},{25,17},{2,26},{10... | collective-permute-start | bytes 110600 | tf_op jit(solution)/shard_map/ppermute | solution.py:99
  106.6 4.1 %collective-permute-start.27 = (bf16[3,3,32,192]{3,2,1,0:T(8,128)(2,1)S(1)}, bf16[3,3,32,192]{3,2,1,0:T(8,128)(2,1)S(1)}, u32[]{:S(2)}, u32[]{:S(2)}) collective-permute-start(bf16[3,3,32,192]{3,2,1,0:T(8,128)(2,1)S(1)} %pad_maximum_fusion.6), channel_id=1, source_target_pairs={{0,7},{1,0},{2,1},{3,2},{4,3},{5,4},{6,5},{7,6},{8,15},{9,8},{10,9... | collective-permute-start | bytes 331784 | tf_op jit(solution)/shard_map/ppermute | solution.py:99
  107.7 6.4 %collective-permute-start.26 = (bf16[3,3,32,192]{3,2,1,0:T(8,128)(2,1)S(1)}, bf16[3,3,32,192]{3,2,1,0:T(8,128)(2,1)S(1)}, u32[]{:S(2)}, u32[]{:S(2)}) collective-permute-start(bf16[3,3,32,192]{3,2,1,0:T(8,128)(2,1)S(1)} %pad_maximum_fusion.6), channel_id=1, source_target_pairs={{0,1},{1,2},{2,3},{3,4},{4,5},{5,6},{6,7},{7,0},{8,9},{9,10},{10,1... | collective-permute-start | bytes 331784 | tf_op jit(solution)/shard_map/ppermute | solution.py:99
  115.0 5.0 %collective-permute-start.28 = (bf16[3,32,192]{2,1,0:T(8,128)(2,1)S(1)}, bf16[3,32,192]{2,1,0:T(8,128)(2,1)S(1)}, u32[]{:S(2)}, u32[]{:S(2)}) collective-permute-start(bf16[3,32,192]{2,1,0:T(8,128)(2,1)S(1)} %get-tuple-element.29), channel_id=1, source_target_pairs={{0,8},{8,16},{16,24},{24,0},{1,9},{9,17},{17,25},{25,1},{2,10},{10... | collective-permute-start | bytes 110600 | tf_op jit(solution)/shard_map/ppermute | solution.py:99
  116.2 4.1 %collective-permute-start.29 = (bf16[3,32,192]{2,1,0:T(8,128)(2,1)S(1)}, bf16[3,32,192]{2,1,0:T(8,128)(2,1)S(1)}, u32[]{:S(2)}, u32[]{:S(2)}) collective-permute-start(bf16[3,32,192]{2,1,0:T(8,128)(2,1)S(1)} %get-tuple-element.29), channel_id=1, source_target_pairs={{0,24},{8,0},{16,8},{24,16},{1,25},{9,1},{17,9},{25,17},{2,26},{10... | collective-permute-start | bytes 110600 | tf_op jit(solution)/shard_map/ppermute | solution.py:99
  120.4 4.1 %collective-permute-start.31 = (bf16[3,3,32,192]{3,2,1,0:T(8,128)(2,1)S(1)}, bf16[3,3,32,192]{3,2,1,0:T(8,128)(2,1)S(1)}, u32[]{:S(2)}, u32[]{:S(2)}) collective-permute-start(bf16[3,3,32,192]{3,2,1,0:T(8,128)(2,1)S(1)} %pad_maximum_fusion.7), channel_id=1, source_target_pairs={{0,7},{1,0},{2,1},{3,2},{4,3},{5,4},{6,5},{7,6},{8,15},{9,8},{10,9... | collective-permute-start | bytes 331784 | tf_op jit(solution)/shard_map/ppermute | solution.py:99
  121.2 6.4 %collective-permute-start.30 = (bf16[3,3,32,192]{3,2,1,0:T(8,128)(2,1)S(1)}, bf16[3,3,32,192]{3,2,1,0:T(8,128)(2,1)S(1)}, u32[]{:S(2)}, u32[]{:S(2)}) collective-permute-start(bf16[3,3,32,192]{3,2,1,0:T(8,128)(2,1)S(1)} %pad_maximum_fusion.7), channel_id=1, source_target_pairs={{0,1},{1,2},{2,3},{3,4},{4,5},{5,6},{6,7},{7,0},{8,9},{9,10},{10,1... | collective-permute-start | bytes 331784 | tf_op jit(solution)/shard_map/ppermute | solution.py:99
  131.3 4.6 %collective-permute-start.34 = (f32[32,32]{0,1:T(8,128)S(1)}, f32[32,32]{0,1:T(8,128)S(1)}, u32[]{:S(2)}, u32[]{:S(2)}) collective-permute-start(f32[32,32]{0,1:T(8,128)S(1)} %convolution_bitcast_fusion.67), channel_id=1, source_target_pairs={{0,24},{8,16},{16,8},{24,0},{1,25},{9,17},{17,9},{25,1},{2,26},{10... | collective-permute-start | bytes 12296 | tf_op jit(solution)/shard_map/ppermute | solution.py:58
  139.9 4.7 %collective-permute-start.38 = (f32[32,32]{0,1:T(8,128)S(1)}, f32[32,32]{0,1:T(8,128)S(1)}, u32[]{:S(2)}, u32[]{:S(2)}) collective-permute-start(f32[32,32]{0,1:T(8,128)S(1)} %add_add_fusion.2), channel_id=1, source_target_pairs={{0,4},{1,5},{2,6},{3,7},{4,0},{5,1},{6,2},{7,3},{8,12},{9,13},{10,... | collective-permute-start | bytes 12296 | tf_op jit(solution)/shard_map/ppermute | solution.py:58
  151.9 5.0 %collective-permute-start.39 = (bf16[3,32,192]{2,1,0:T(8,128)(2,1)S(1)}, bf16[3,32,192]{2,1,0:T(8,128)(2,1)S(1)}, u32[]{:S(2)}, u32[]{:S(2)}) collective-permute-start(bf16[3,32,192]{2,1,0:T(8,128)(2,1)S(1)} %get-tuple-element.14), channel_id=1, source_target_pairs={{0,8},{8,16},{16,24},{24,0},{1,9},{9,17},{17,25},{25,1},{2,10},{10... | collective-permute-start | bytes 110600 | tf_op jit(solution)/shard_map/ppermute | solution.py:99
  152.5 4.4 %collective-permute-start.40 = (bf16[3,32,192]{2,1,0:T(8,128)(2,1)S(1)}, bf16[3,32,192]{2,1,0:T(8,128)(2,1)S(1)}, u32[]{:S(2)}, u32[]{:S(2)}) collective-permute-start(bf16[3,32,192]{2,1,0:T(8,128)(2,1)S(1)} %get-tuple-element.14), channel_id=1, source_target_pairs={{0,24},{8,0},{16,8},{24,16},{1,25},{9,1},{17,9},{25,17},{2,26},{10... | collective-permute-start | bytes 110600 | tf_op jit(solution)/shard_map/ppermute | solution.py:99
  157.0 6.4 %collective-permute-start.41 = (bf16[3,3,32,192]{3,2,1,0:T(8,128)(2,1)S(1)}, bf16[3,3,32,192]{3,2,1,0:T(8,128)(2,1)S(1)}, u32[]{:S(2)}, u32[]{:S(2)}) collective-permute-start(bf16[3,3,32,192]{3,2,1,0:T(8,128)(2,1)S(1)} %pad_maximum_fusion.8), channel_id=1, source_target_pairs={{0,1},{1,2},{2,3},{3,4},{4,5},{5,6},{6,7},{7,0},{8,9},{9,10},{10,1... | collective-permute-start | bytes 331784 | tf_op jit(solution)/shard_map/ppermute | solution.py:99
  164.4 5.5 %collective-permute-start.43 = (bf16[3,32,192]{2,1,0:T(8,128)(2,1)S(1)}, bf16[3,32,192]{2,1,0:T(8,128)(2,1)S(1)}, u32[]{:S(2)}, u32[]{:S(2)}) collective-permute-start(bf16[3,32,192]{2,1,0:T(8,128)(2,1)S(1)} %get-tuple-element.12), channel_id=1, source_target_pairs={{0,8},{8,16},{16,24},{24,0},{1,9},{9,17},{17,25},{25,1},{2,10},{10... | collective-permute-start | bytes 110600 | tf_op jit(solution)/shard_map/ppermute | solution.py:99
  166.7 4.1 %collective-permute-start.44 = (bf16[3,32,192]{2,1,0:T(8,128)(2,1)S(1)}, bf16[3,32,192]{2,1,0:T(8,128)(2,1)S(1)}, u32[]{:S(2)}, u32[]{:S(2)}) collective-permute-start(bf16[3,32,192]{2,1,0:T(8,128)(2,1)S(1)} %get-tuple-element.12), channel_id=1, source_target_pairs={{0,24},{8,0},{16,8},{24,16},{1,25},{9,1},{17,9},{25,17},{2,26},{10... | collective-permute-start | bytes 110600 | tf_op jit(solution)/shard_map/ppermute | solution.py:99
  170.8 4.6 %collective-permute-start.46 = (bf16[3,3,32,192]{3,2,1,0:T(8,128)(2,1)S(1)}, bf16[3,3,32,192]{3,2,1,0:T(8,128)(2,1)S(1)}, u32[]{:S(2)}, u32[]{:S(2)}) collective-permute-start(bf16[3,3,32,192]{3,2,1,0:T(8,128)(2,1)S(1)} %pad_maximum_fusion.9), channel_id=1, source_target_pairs={{0,7},{1,0},{2,1},{3,2},{4,3},{5,4},{6,5},{7,6},{8,15},{9,8},{10,9... | collective-permute-start | bytes 331784 | tf_op jit(solution)/shard_map/ppermute | solution.py:99
  172.8 6.4 %collective-permute-start.45 = (bf16[3,3,32,192]{3,2,1,0:T(8,128)(2,1)S(1)}, bf16[3,3,32,192]{3,2,1,0:T(8,128)(2,1)S(1)}, u32[]{:S(2)}, u32[]{:S(2)}) collective-permute-start(bf16[3,3,32,192]{3,2,1,0:T(8,128)(2,1)S(1)} %pad_maximum_fusion.9), channel_id=1, source_target_pairs={{0,1},{1,2},{2,3},{3,4},{4,5},{5,6},{6,7},{7,0},{8,9},{9,10},{10,1... | collective-permute-start | bytes 331784 | tf_op jit(solution)/shard_map/ppermute | solution.py:99
  180.1 5.0 %collective-permute-start.47 = (bf16[3,32,192]{2,1,0:T(8,128)(2,1)S(1)}, bf16[3,32,192]{2,1,0:T(8,128)(2,1)S(1)}, u32[]{:S(2)}, u32[]{:S(2)}) collective-permute-start(bf16[3,32,192]{2,1,0:T(8,128)(2,1)S(1)} %get-tuple-element.10), channel_id=1, source_target_pairs={{0,8},{8,16},{16,24},{24,0},{1,9},{9,17},{17,25},{25,1},{2,10},{10... | collective-permute-start | bytes 110600 | tf_op jit(solution)/shard_map/ppermute | solution.py:99
  181.6 4.1 %collective-permute-start.48 = (bf16[3,32,192]{2,1,0:T(8,128)(2,1)S(1)}, bf16[3,32,192]{2,1,0:T(8,128)(2,1)S(1)}, u32[]{:S(2)}, u32[]{:S(2)}) collective-permute-start(bf16[3,32,192]{2,1,0:T(8,128)(2,1)S(1)} %get-tuple-element.10), channel_id=1, source_target_pairs={{0,24},{8,0},{16,8},{24,16},{1,25},{9,1},{17,9},{25,17},{2,26},{10... | collective-permute-start | bytes 110600 | tf_op jit(solution)/shard_map/ppermute | solution.py:99
  185.7 4.1 %collective-permute-start.50 = (bf16[3,3,32,192]{3,2,1,0:T(8,128)(2,1)S(1)}, bf16[3,3,32,192]{3,2,1,0:T(8,128)(2,1)S(1)}, u32[]{:S(2)}, u32[]{:S(2)}) collective-permute-start(bf16[3,3,32,192]{3,2,1,0:T(8,128)(2,1)S(1)} %pad_maximum_fusion.10), channel_id=1, source_target_pairs={{0,7},{1,0},{2,1},{3,2},{4,3},{5,4},{6,5},{7,6},{8,15},{9,8},{10,9... | collective-permute-start | bytes 331784 | tf_op jit(solution)/shard_map/ppermute | solution.py:99
  186.6 6.4 %collective-permute-start.49 = (bf16[3,3,32,192]{3,2,1,0:T(8,128)(2,1)S(1)}, bf16[3,3,32,192]{3,2,1,0:T(8,128)(2,1)S(1)}, u32[]{:S(2)}, u32[]{:S(2)}) collective-permute-start(bf16[3,3,32,192]{3,2,1,0:T(8,128)(2,1)S(1)} %pad_maximum_fusion.10), channel_id=1, source_target_pairs={{0,1},{1,2},{2,3},{3,4},{4,5},{5,6},{6,7},{7,0},{8,9},{9,10},{10,1... | collective-permute-start | bytes 331784 | tf_op jit(solution)/shard_map/ppermute | solution.py:99
  193.9 5.0 %collective-permute-start.51 = (bf16[3,32,192]{2,1,0:T(8,128)(2,1)S(1)}, bf16[3,32,192]{2,1,0:T(8,128)(2,1)S(1)}, u32[]{:S(2)}, u32[]{:S(2)}) collective-permute-start(bf16[3,32,192]{2,1,0:T(8,128)(2,1)S(1)} %get-tuple-element.8), channel_id=1, source_target_pairs={{0,8},{8,16},{16,24},{24,0},{1,9},{9,17},{17,25},{25,1},{2,10},{10... | collective-permute-start | bytes 110600 | tf_op jit(solution)/shard_map/ppermute | solution.py:99
  195.3 4.1 %collective-permute-start.52 = (bf16[3,32,192]{2,1,0:T(8,128)(2,1)S(1)}, bf16[3,32,192]{2,1,0:T(8,128)(2,1)S(1)}, u32[]{:S(2)}, u32[]{:S(2)}) collective-permute-start(bf16[3,32,192]{2,1,0:T(8,128)(2,1)S(1)} %get-tuple-element.8), channel_id=1, source_target_pairs={{0,24},{8,0},{16,8},{24,16},{1,25},{9,1},{17,9},{25,17},{2,26},{10... | collective-permute-start | bytes 110600 | tf_op jit(solution)/shard_map/ppermute | solution.py:99
  199.4 4.1 %collective-permute-start.54 = (bf16[3,3,32,192]{3,2,1,0:T(8,128)(2,1)S(1)}, bf16[3,3,32,192]{3,2,1,0:T(8,128)(2,1)S(1)}, u32[]{:S(2)}, u32[]{:S(2)}) collective-permute-start(bf16[3,3,32,192]{3,2,1,0:T(8,128)(2,1)S(1)} %pad_maximum_fusion.11), channel_id=1, source_target_pairs={{0,7},{1,0},{2,1},{3,2},{4,3},{5,4},{6,5},{7,6},{8,15},{9,8},{10,9... | collective-permute-start | bytes 331784 | tf_op jit(solution)/shard_map/ppermute | solution.py:99
  200.3 6.4 %collective-permute-start.53 = (bf16[3,3,32,192]{3,2,1,0:T(8,128)(2,1)S(1)}, bf16[3,3,32,192]{3,2,1,0:T(8,128)(2,1)S(1)}, u32[]{:S(2)}, u32[]{:S(2)}) collective-permute-start(bf16[3,3,32,192]{3,2,1,0:T(8,128)(2,1)S(1)} %pad_maximum_fusion.11), channel_id=1, source_target_pairs={{0,1},{1,2},{2,3},{3,4},{4,5},{5,6},{6,7},{7,0},{8,9},{9,10},{10,1... | collective-permute-start | bytes 331784 | tf_op jit(solution)/shard_map/ppermute | solution.py:99
  207.6 5.0 %collective-permute-start.55 = (bf16[3,32,192]{2,1,0:T(8,128)(2,1)S(1)}, bf16[3,32,192]{2,1,0:T(8,128)(2,1)S(1)}, u32[]{:S(2)}, u32[]{:S(2)}) collective-permute-start(bf16[3,32,192]{2,1,0:T(8,128)(2,1)S(1)} %get-tuple-element.31), channel_id=1, source_target_pairs={{0,8},{8,16},{16,24},{24,0},{1,9},{9,17},{17,25},{25,1},{2,10},{10... | collective-permute-start | bytes 110600 | tf_op jit(solution)/shard_map/ppermute | solution.py:99
  208.9 4.1 %collective-permute-start.56 = (bf16[3,32,192]{2,1,0:T(8,128)(2,1)S(1)}, bf16[3,32,192]{2,1,0:T(8,128)(2,1)S(1)}, u32[]{:S(2)}, u32[]{:S(2)}) collective-permute-start(bf16[3,32,192]{2,1,0:T(8,128)(2,1)S(1)} %get-tuple-element.31), channel_id=1, source_target_pairs={{0,24},{8,0},{16,8},{24,16},{1,25},{9,1},{17,9},{25,17},{2,26},{10... | collective-permute-start | bytes 110600 | tf_op jit(solution)/shard_map/ppermute | solution.py:99
  213.1 4.1 %collective-permute-start.58 = (bf16[3,3,32,192]{3,2,1,0:T(8,128)(2,1)S(1)}, bf16[3,3,32,192]{3,2,1,0:T(8,128)(2,1)S(1)}, u32[]{:S(2)}, u32[]{:S(2)}) collective-permute-start(bf16[3,3,32,192]{3,2,1,0:T(8,128)(2,1)S(1)} %pad_maximum_fusion.12), channel_id=1, source_target_pairs={{0,7},{1,0},{2,1},{3,2},{4,3},{5,4},{6,5},{7,6},{8,15},{9,8},{10,9... | collective-permute-start | bytes 331784 | tf_op jit(solution)/shard_map/ppermute | solution.py:99
  214.0 6.4 %collective-permute-start.57 = (bf16[3,3,32,192]{3,2,1,0:T(8,128)(2,1)S(1)}, bf16[3,3,32,192]{3,2,1,0:T(8,128)(2,1)S(1)}, u32[]{:S(2)}, u32[]{:S(2)}) collective-permute-start(bf16[3,3,32,192]{3,2,1,0:T(8,128)(2,1)S(1)} %pad_maximum_fusion.12), channel_id=1, source_target_pairs={{0,1},{1,2},{2,3},{3,4},{4,5},{5,6},{6,7},{7,0},{8,9},{9,10},{10,1... | collective-permute-start | bytes 331784 | tf_op jit(solution)/shard_map/ppermute | solution.py:99
  221.3 5.0 %collective-permute-start.59 = (bf16[3,32,192]{2,1,0:T(8,128)(2,1)S(1)}, bf16[3,32,192]{2,1,0:T(8,128)(2,1)S(1)}, u32[]{:S(2)}, u32[]{:S(2)}) collective-permute-start(bf16[3,32,192]{2,1,0:T(8,128)(2,1)S(1)} %get-tuple-element.33), channel_id=1, source_target_pairs={{0,8},{8,16},{16,24},{24,0},{1,9},{9,17},{17,25},{25,1},{2,10},{10... | collective-permute-start | bytes 110600 | tf_op jit(solution)/shard_map/ppermute | solution.py:99
  226.7 4.1 %collective-permute-start.62 = (bf16[3,3,32,192]{3,2,1,0:T(8,128)(2,1)S(1)}, bf16[3,3,32,192]{3,2,1,0:T(8,128)(2,1)S(1)}, u32[]{:S(2)}, u32[]{:S(2)}) collective-permute-start(bf16[3,3,32,192]{3,2,1,0:T(8,128)(2,1)S(1)} %pad_maximum_fusion.13), channel_id=1, source_target_pairs={{0,7},{1,0},{2,1},{3,2},{4,3},{5,4},{6,5},{7,6},{8,15},{9,8},{10,9... | collective-permute-start | bytes 331784 | tf_op jit(solution)/shard_map/ppermute | solution.py:99
  227.7 6.4 %collective-permute-start.61 = (bf16[3,3,32,192]{3,2,1,0:T(8,128)(2,1)S(1)}, bf16[3,3,32,192]{3,2,1,0:T(8,128)(2,1)S(1)}, u32[]{:S(2)}, u32[]{:S(2)}) collective-permute-start(bf16[3,3,32,192]{3,2,1,0:T(8,128)(2,1)S(1)} %pad_maximum_fusion.13), channel_id=1, source_target_pairs={{0,1},{1,2},{2,3},{3,4},{4,5},{5,6},{6,7},{7,0},{8,9},{9,10},{10,1... | collective-permute-start | bytes 331784 | tf_op jit(solution)/shard_map/ppermute | solution.py:99
  235.0 5.0 %collective-permute-start.63 = (bf16[3,32,192]{2,1,0:T(8,128)(2,1)S(1)}, bf16[3,32,192]{2,1,0:T(8,128)(2,1)S(1)}, u32[]{:S(2)}, u32[]{:S(2)}) collective-permute-start(bf16[3,32,192]{2,1,0:T(8,128)(2,1)S(1)} %get-tuple-element.35), channel_id=1, source_target_pairs={{0,8},{8,16},{16,24},{24,0},{1,9},{9,17},{17,25},{25,1},{2,10},{10... | collective-permute-start | bytes 110600 | tf_op jit(solution)/shard_map/ppermute | solution.py:99
  240.8 4.1 %collective-permute-start.66 = (bf16[3,3,32,192]{3,2,1,0:T(8,128)(2,1)S(1)}, bf16[3,3,32,192]{3,2,1,0:T(8,128)(2,1)S(1)}, u32[]{:S(2)}, u32[]{:S(2)}) collective-permute-start(bf16[3,3,32,192]{3,2,1,0:T(8,128)(2,1)S(1)} %pad_maximum_fusion.14), channel_id=1, source_target_pairs={{0,7},{1,0},{2,1},{3,2},{4,3},{5,4},{6,5},{7,6},{8,15},{9,8},{10,9... | collective-permute-start | bytes 331784 | tf_op jit(solution)/shard_map/ppermute | solution.py:99
  241.5 6.4 %collective-permute-start.65 = (bf16[3,3,32,192]{3,2,1,0:T(8,128)(2,1)S(1)}, bf16[3,3,32,192]{3,2,1,0:T(8,128)(2,1)S(1)}, u32[]{:S(2)}, u32[]{:S(2)}) collective-permute-start(bf16[3,3,32,192]{3,2,1,0:T(8,128)(2,1)S(1)} %pad_maximum_fusion.14), channel_id=1, source_target_pairs={{0,1},{1,2},{2,3},{3,4},{4,5},{5,6},{6,7},{7,0},{8,9},{9,10},{10,1... | collective-permute-start | bytes 331784 | tf_op jit(solution)/shard_map/ppermute | solution.py:99
  248.8 5.0 %collective-permute-start.67 = (bf16[3,32,192]{2,1,0:T(8,128)(2,1)S(1)}, bf16[3,32,192]{2,1,0:T(8,128)(2,1)S(1)}, u32[]{:S(2)}, u32[]{:S(2)}) collective-permute-start(bf16[3,32,192]{2,1,0:T(8,128)(2,1)S(1)} %get-tuple-element.37), channel_id=1, source_target_pairs={{0,8},{8,16},{16,24},{24,0},{1,9},{9,17},{17,25},{25,1},{2,10},{10... | collective-permute-start | bytes 110600 | tf_op jit(solution)/shard_map/ppermute | solution.py:99
  254.2 4.1 %collective-permute-start.70 = (bf16[3,3,32,192]{3,2,1,0:T(8,128)(2,1)S(1)}, bf16[3,3,32,192]{3,2,1,0:T(8,128)(2,1)S(1)}, u32[]{:S(2)}, u32[]{:S(2)}) collective-permute-start(bf16[3,3,32,192]{3,2,1,0:T(8,128)(2,1)S(1)} %pad_maximum_fusion.15), channel_id=1, source_target_pairs={{0,7},{1,0},{2,1},{3,2},{4,3},{5,4},{6,5},{7,6},{8,15},{9,8},{10,9... | collective-permute-start | bytes 331784 | tf_op jit(solution)/shard_map/ppermute | solution.py:99
  255.3 6.4 %collective-permute-start.69 = (bf16[3,3,32,192]{3,2,1,0:T(8,128)(2,1)S(1)}, bf16[3,3,32,192]{3,2,1,0:T(8,128)(2,1)S(1)}, u32[]{:S(2)}, u32[]{:S(2)}) collective-permute-start(bf16[3,3,32,192]{3,2,1,0:T(8,128)(2,1)S(1)} %pad_maximum_fusion.15), channel_id=1, source_target_pairs={{0,1},{1,2},{2,3},{3,4},{4,5},{5,6},{6,7},{7,0},{8,9},{9,10},{10,1... | collective-permute-start | bytes 331784 | tf_op jit(solution)/shard_map/ppermute | solution.py:99
  265.3 4.6 %collective-permute-start.73 = (f32[32,32]{0,1:T(8,128)S(1)}, f32[32,32]{0,1:T(8,128)S(1)}, u32[]{:S(2)}, u32[]{:S(2)}) collective-permute-start(f32[32,32]{0,1:T(8,128)S(1)} %convolution_bitcast_fusion.65), channel_id=1, source_target_pairs={{0,24},{8,16},{16,8},{24,0},{1,25},{9,17},{17,9},{25,1},{2,26},{10... | collective-permute-start | bytes 12296 | tf_op jit(solution)/shard_map/ppermute | solution.py:58
  273.9 4.7 %collective-permute-start.77 = (f32[32,32]{0,1:T(8,128)S(1)}, f32[32,32]{0,1:T(8,128)S(1)}, u32[]{:S(2)}, u32[]{:S(2)}) collective-permute-start(f32[32,32]{0,1:T(8,128)S(1)} %add_add_fusion), channel_id=1, source_target_pairs={{0,4},{1,5},{2,6},{3,7},{4,0},{5,1},{6,2},{7,3},{8,12},{9,13},{10,... | collective-permute-start | bytes 12296 | tf_op jit(solution)/shard_map/ppermute | solution.py:58
  (17 other events, 172.3 us)

commit v4 on v3

--- a/solution.py
+++ b/solution.py
@@ -3,6 +3,7 @@
 import jax
 import jax.numpy as jnp
 from jax import lax
+from jax.experimental import pallas as pl
 from jax.sharding import PartitionSpec as P
 
 DEGREE = 8
@@ -69,14 +70,48 @@
     return value
 
 
+def chol_inv_kernel(g_ref, out_ref):
+    a = g_ref[...]
+    n = a.shape[0]
+    rows = lax.broadcasted_iota(jnp.int32, (n, n), 0)
+    lanes = lax.broadcasted_iota(jnp.int32, (n, n), 1)
+    row_ids = lax.broadcasted_iota(jnp.int32, (n, 1), 0)
+    lane_ids = lax.broadcasted_iota(jnp.int32, (1, n), 1)
+    lower = jnp.zeros_like(a)
+    upper = jnp.zeros_like(a)
+    for j in range(n):
+        col = jnp.sum(jnp.where(lanes == j, a, 0.0), axis=1, keepdims=True)
+        row = jnp.sum(jnp.where(rows == j, a, 0.0), axis=0, keepdims=True)
+        pivot = jnp.sqrt(jnp.sum(jnp.where(row_ids == j, col, 0.0), axis=0, keepdims=True))
+        col = jnp.where(row_ids >= j, col / pivot, 0.0)
+        row = jnp.where(lane_ids >= j, row / pivot, 0.0)
+        lower = jnp.where(lanes == j, col, lower)
+        upper = jnp.where(rows == j, row, upper)
+        a = a - col * row
+    inv = jnp.zeros_like(a)
+    for i in range(n):
+        coeff = jnp.sum(jnp.where(lanes == i, upper, 0.0), axis=1, keepdims=True)
+        diag = jnp.sum(jnp.where(row_ids == i, coeff, 0.0), axis=0, keepdims=True)
+        t = jnp.sum(coeff * inv, axis=0, keepdims=True)
+        new = (jnp.where(lane_ids == i, 1.0, 0.0) - t) / diag
+        inv = jnp.where(rows == i, new, inv)
+    out_ref[...] = inv
+
+def chol_inv(g):
+    n = g.shape[0]
+    return pl.pallas_call(
+        chol_inv_kernel,
+        out_shape=jax.ShapeDtypeStruct(g.shape, jnp.float32),
+        cost_estimate=pl.CostEstimate(flops=4 * n * n * n, bytes_accessed=8 * n * n, transcendentals=n),
+    )(g)
+
+
 def orthonormal(filtered, rows_total):
     partial_gram = jnp.einsum(
         "zvd,zwd->vw", filtered, filtered, precision=lax.Precision.HIGHEST
     )
     gram_matrix = all_sum(partial_gram, ("gx", "gy"))
-    factor = jnp.linalg.cholesky(gram_matrix)
-    identity = jnp.eye(filtered.shape[1], dtype=jnp.float32)
-    inverse = jax.scipy.linalg.solve_triangular(factor, identity, lower=True)
+    inverse = chol_inv(gram_matrix)
     result = jnp.einsum("vw,zwd->zvd", inverse, filtered, precision=lax.Precision.HIGHEST)
     return result * math.sqrt(rows_total)
 

time: 287 us -> 286 us (level)
  other arithmetic: 20.9 us -> 8.71 us
  Pallas kernels: 0 us -> 10.4 us
    another operation x10 -> x0, other arithmetic: 13.4 us -> none  [the longest x6 7.19 us: orthonormal(): factor = jnp.linalg.cholesky(gram_matrix)]
    pallas_call x0 -> x2, Pallas kernels: none -> 10.4 us  [chol_inv(): pl.pallas_call(chol_inv_kernel, out_shape=jax.ShapeDtypeStruct(g.shape, j...]
where the time goes in v4:
time: 286 us
  waiting for transfers between devices  124 us (43%)
  starting transfers between devices  78.9 us (28%)
  matrix products  52.4 us (18%)
  local copies, waits for them, and re-layouts  10.4 us (4%)
  Pallas kernels  10.4 us (4%)
  other arithmetic  8.71 us (3%)
    ppermute x64, waiting for transfers between devices, shift(): lax.ppermute(value, axis, [(i, (i + step) % count) for i in range(count)])  106 us
    ppermute x64, starting transfers between devices, shift(): lax.ppermute(value, axis, [(i, (i + step) % count) for i in range(count)])  66 us
    dot_general x64, matrix products, part(): jnp.einsum('kvj,tkij->tvi', cells, blocks, preferred_element_type=jnp.flo...  49.3 us
    ppermute x14, waiting for transfers between devices, swap(): return lax.ppermute(v, axis, [(i, i ^ stride) for i in range(count)])  18.7 us
    ppermute x14, starting transfers between devices, swap(): return lax.ppermute(v, axis, [(i, i ^ stride) for i in range(count)])  12.9 us
    pallas_call x2, Pallas kernels, chol_inv(): pl.pallas_call(chol_inv_kernel, out_shape=jax.ShapeDtypeStruct(g.shape, j...  10.4 us
    gather x1, local copies, waits for them, and re-layouts, dense_coupling(): jnp.take(matrices, index.reshape(-1), axis=0)  10.3 us
  transfers between devices with their start and end apart: 78, of which 71 were waited for; matrix products, arithmetic and copies ran while one was open for 18% of the time, Pallas kernels for 0%

profile of v4, /device:TPU:0, one launch (start us, length us, event | category | flops | bytes accessed | tf_op | source)
XLA Modules:
  0.0 285.7 jit_solution(4016827037430906243)
XLA Ops:
  0.9 3.0 %collective-permute-start = (bf16[3,32,192]{2,1,0:T(8,128)(2,1)S(1)}, bf16[3,32,192]{2,1,0:T(8,128)(2,1)S(1)}, u32[]{:S(2)}, u32[]{:S(2)}) collective-permute-start(bf16[3,32,192]{2,1,0:T(8,128)(2,1)S(1)} %get-tuple-element.14), channel_id=1, source_target_pairs={{0,8},{8,16},{16,24},{24,0},{1,9},{9,17},{17,25},{25,1},{2,10},{10... | collective-permute-start | bytes 110600 | tf_op jit(solution)/shard_map/ppermute | solution.py:134
  6.7 10.3 %gather_fusion = bf16[81,192,192]{2,1,0:T(8,128)(2,1)} fusion(bf16[81,192,192]{2,1,0:T(8,128)(2,1)} %bitcast.889, s32[1024]{0:T(1024)S(1)} %pad_clamp_fusion), kind=kCustom, calls=%fused_computation | custom fusion | bytes 11944260 | tf_op jit(solution)/shard_map/jit(_take)/gather | solution.py:43
  17.1 4.3 %select_select_fusion = bf16[3,27,192,192]{3,2,1,0:T(8,128)(2,1)S(1)} fusion(bf16[3,27,192,192]{3,2,1,0:T(8,128)(2,1)} %bitcast.888, pred[3,27]{1,0:T(4,128)(4,1)S(1)} %compare_and_fusion, pred[3,27]{1,0:T(4,128)(4,1)S(1)} %and_reduce_fusion), kind=kLoop, calls=%fused_computation.1 | loop fusion | flops 5971968 | bytes 11944098 | tf_op jit(solution)/shard_map/jit(_where)/select_n | solution.py:47
  21.8 2.9 %collective-permute-start.3 = (bf16[3,3,32,192]{3,2,1,0:T(8,128)(2,1)S(1)}, bf16[3,3,32,192]{3,2,1,0:T(8,128)(2,1)S(1)}, u32[]{:S(2)}, u32[]{:S(2)}) collective-permute-start(bf16[3,3,32,192]{3,2,1,0:T(8,128)(2,1)S(1)} %pad_maximum_fusion), channel_id=1, source_target_pairs={{0,7},{1,0},{2,1},{3,2},{4,3},{5,4},{6,5},{7,6},{8,15},{9,8},{10,9... | collective-permute-start | bytes 331784 | tf_op jit(solution)/shard_map/ppermute | solution.py:134
  25.4 2.3 collective-permute-done.3
  28.5 2.6 collective-permute-done.2
  32.7 2.3 collective-permute-start.5
  35.4 1.7 collective-permute-done.4
  39.5 2.3 collective-permute-done.7
  42.7 2.6 collective-permute-done.6
  49.6 1.7 collective-permute-done.8
  53.2 2.6 collective-permute-done.11
  56.7 2.3 collective-permute-done.10
  66.7 2.7 collective-permute-done.15
  70.3 2.1 collective-permute-done.14
  76.8 1.7 collective-permute-done.16
  80.4 2.8 collective-permute-done.19
  84.0 2.1 collective-permute-done.18
  87.1 1.8 collective-permute-start.20
  94.5 2.6 collective-permute-done.23
  98.0 2.3 collective-permute-done.22
  108.4 2.4 collective-permute-done.27
  111.7 2.5 collective-permute-done.26
  116.2 1.8 collective-permute-start.29
  121.8 2.7 collective-permute-done.31
  125.4 2.2 collective-permute-done.30
  133.9 2.1 collective-permute-done.34
  136.2 1.8 collective-permute-start.37
  138.0 1.9 collective-permute-done.36
  141.0 3.6 %collective-permute-done.38 = f32[32,32]{1,0:T(8,128)S(1)} collective-permute-done((f32[32,32]{1,0:T(8,128)S(1)}, f32[32,32]{1,0:T(8,128)S(1)}, u32[]{:S(2)}, u32[]{:S(2)}) %collective-permute-start.38) | collective-permute-done | bytes 4128 | tf_op jit(solution)/shard_map/ppermute | solution.py:59
  145.2 5.2 %shard_map.55 = f32[32,32]{1,0:T(8,128)} custom-call(f32[32,32]{1,0:T(8,128)} %add.328.g_ref), custom_call_target="tpu_custom_call" | custom-call | flops 131072 | bytes 8192 | tf_op jit(solution)/shard_map/pallas_call | solution.py:102
  152.2 2.3 collective-permute-start.40
  157.2 2.1 fusion.98
  160.0 2.6 convolution_bitcast_fusion.14
  164.1 2.3 collective-permute-start.43
  167.5 2.1 collective-permute-done.43
  170.5 1.9 collective-permute-start.46
  173.1 2.1 collective-permute-done.46
  176.0 2.8 collective-permute-done.45
  183.1 1.7 collective-permute-done.47
  186.8 2.7 collective-permute-done.50
  190.4 2.2 collective-permute-done.49
  196.9 1.7 collective-permute-done.51
  200.6 2.6 collective-permute-done.54
  204.1 2.3 collective-permute-done.53
  210.7 1.7 collective-permute-done.55
  214.4 2.5 collective-permute-done.58
  217.7 2.4 collective-permute-done.57
  222.2 1.9 collective-permute-start.60
  224.4 1.7 collective-permute-done.59
  227.9 2.5 collective-permute-done.62
  231.3 2.3 collective-permute-done.61
  234.6 1.8 collective-permute-start.63
  237.9 1.7 collective-permute-done.63
  241.8 2.8 collective-permute-done.66
  245.5 2.0 collective-permute-done.65
  251.9 1.7 collective-permute-done.67
  255.6 2.4 collective-permute-done.70
  258.9 2.4 collective-permute-done.69
  267.6 2.0 collective-permute-done.73
  269.8 1.8 collective-permute-start.76
  271.6 1.9 collective-permute-done.75
  274.4 3.9 %collective-permute-done.77 = f32[32,32]{1,0:T(8,128)S(1)} collective-permute-done((f32[32,32]{1,0:T(8,128)S(1)}, f32[32,32]{1,0:T(8,128)S(1)}, u32[]{:S(2)}, u32[]{:S(2)}) %collective-permute-start.77) | collective-permute-done | bytes 4128 | tf_op jit(solution)/shard_map/ppermute | solution.py:59
  278.9 5.2 %shard_map.56 = f32[32,32]{1,0:T(8,128)} custom-call(f32[32,32]{1,0:T(8,128)} %add.366.g_ref), custom_call_target="tpu_custom_call" | custom-call | flops 131072 | bytes 8192 | tf_op jit(solution)/shard_map/pallas_call | solution.py:102
  (205 shorter events, 124.0 us)
Async XLA Ops:
  0.9 20.8 %collective-permute-start = (bf16[3,32,192]{2,1,0:T(8,128)(2,1)S(1)}, bf16[3,32,192]{2,1,0:T(8,128)(2,1)S(1)}, u32[]{:S(2)}, u32[]{:S(2)}) collective-permute-start(bf16[3,32,192]{2,1,0:T(8,128)(2,1)S(1)} %get-tuple-element.14), channel_id=1, source_target_pairs={{0,8},{8,16},{16,24},{24,0},{1,9},{9,17},{17,25},{25,1},{2,10},{10... | collective-permute-start | bytes 110600 | tf_op jit(solution)/shard_map/ppermute | solution.py:134
  3.9 17.9 %collective-permute-start.1 = (bf16[3,32,192]{2,1,0:T(8,128)(2,1)S(1)}, bf16[3,32,192]{2,1,0:T(8,128)(2,1)S(1)}, u32[]{:S(2)}, u32[]{:S(2)}) collective-permute-start(bf16[3,32,192]{2,1,0:T(8,128)(2,1)S(1)} %get-tuple-element.14), channel_id=1, source_target_pairs={{0,24},{8,0},{16,8},{24,16},{1,25},{9,1},{17,9},{25,17},{2,26},{10... | collective-permute-start | bytes 110600 | tf_op jit(solution)/shard_map/ppermute | solution.py:134
  21.8 5.8 %collective-permute-start.3 = (bf16[3,3,32,192]{3,2,1,0:T(8,128)(2,1)S(1)}, bf16[3,3,32,192]{3,2,1,0:T(8,128)(2,1)S(1)}, u32[]{:S(2)}, u32[]{:S(2)}) collective-permute-start(bf16[3,3,32,192]{3,2,1,0:T(8,128)(2,1)S(1)} %pad_maximum_fusion), channel_id=1, source_target_pairs={{0,7},{1,0},{2,1},{3,2},{4,3},{5,4},{6,5},{7,6},{8,15},{9,8},{10,9... | collective-permute-start | bytes 331784 | tf_op jit(solution)/shard_map/ppermute | solution.py:134
  24.8 6.4 %collective-permute-start.2 = (bf16[3,3,32,192]{3,2,1,0:T(8,128)(2,1)S(1)}, bf16[3,3,32,192]{3,2,1,0:T(8,128)(2,1)S(1)}, u32[]{:S(2)}, u32[]{:S(2)}) collective-permute-start(bf16[3,3,32,192]{3,2,1,0:T(8,128)(2,1)S(1)} %pad_maximum_fusion), channel_id=1, source_target_pairs={{0,1},{1,2},{2,3},{3,4},{4,5},{5,6},{6,7},{7,0},{8,9},{9,10},{10,1... | collective-permute-start | bytes 331784 | tf_op jit(solution)/shard_map/ppermute | solution.py:134
  32.1 5.0 %collective-permute-start.4 = (bf16[3,32,192]{2,1,0:T(8,128)(2,1)S(1)}, bf16[3,32,192]{2,1,0:T(8,128)(2,1)S(1)}, u32[]{:S(2)}, u32[]{:S(2)}) collective-permute-start(bf16[3,32,192]{2,1,0:T(8,128)(2,1)S(1)} %get-tuple-element.15), channel_id=1, source_target_pairs={{0,8},{8,16},{16,24},{24,0},{1,9},{9,17},{17,25},{25,1},{2,10},{10... | collective-permute-start | bytes 110600 | tf_op jit(solution)/shard_map/ppermute | solution.py:134
  32.7 5.0 %collective-permute-start.5 = (bf16[3,32,192]{2,1,0:T(8,128)(2,1)S(1)}, bf16[3,32,192]{2,1,0:T(8,128)(2,1)S(1)}, u32[]{:S(2)}, u32[]{:S(2)}) collective-permute-start(bf16[3,32,192]{2,1,0:T(8,128)(2,1)S(1)} %get-tuple-element.15), channel_id=1, source_target_pairs={{0,24},{8,0},{16,8},{24,16},{1,25},{9,1},{17,9},{25,17},{2,26},{10... | collective-permute-start | bytes 110600 | tf_op jit(solution)/shard_map/ppermute | solution.py:134
  37.7 4.1 %collective-permute-start.7 = (bf16[3,3,32,192]{3,2,1,0:T(8,128)(2,1)S(1)}, bf16[3,3,32,192]{3,2,1,0:T(8,128)(2,1)S(1)}, u32[]{:S(2)}, u32[]{:S(2)}) collective-permute-start(bf16[3,3,32,192]{3,2,1,0:T(8,128)(2,1)S(1)} %pad_maximum_fusion.1), channel_id=1, source_target_pairs={{0,7},{1,0},{2,1},{3,2},{4,3},{5,4},{6,5},{7,6},{8,15},{9,8},{10,9... | collective-permute-start | bytes 331784 | tf_op jit(solution)/shard_map/ppermute | solution.py:134
  38.9 6.4 %collective-permute-start.6 = (bf16[3,3,32,192]{3,2,1,0:T(8,128)(2,1)S(1)}, bf16[3,3,32,192]{3,2,1,0:T(8,128)(2,1)S(1)}, u32[]{:S(2)}, u32[]{:S(2)}) collective-permute-start(bf16[3,3,32,192]{3,2,1,0:T(8,128)(2,1)S(1)} %pad_maximum_fusion.1), channel_id=1, source_target_pairs={{0,1},{1,2},{2,3},{3,4},{4,5},{5,6},{6,7},{7,0},{8,9},{9,10},{10,1... | collective-permute-start | bytes 331784 | tf_op jit(solution)/shard_map/ppermute | solution.py:134
  46.2 5.0 %collective-permute-start.8 = (bf16[3,32,192]{2,1,0:T(8,128)(2,1)S(1)}, bf16[3,32,192]{2,1,0:T(8,128)(2,1)S(1)}, u32[]{:S(2)}, u32[]{:S(2)}) collective-permute-start(bf16[3,32,192]{2,1,0:T(8,128)(2,1)S(1)} %get-tuple-element.17), channel_id=1, source_target_pairs={{0,8},{8,16},{16,24},{24,0},{1,9},{9,17},{17,25},{25,1},{2,10},{10... | collective-permute-start | bytes 110600 | tf_op jit(solution)/shard_map/ppermute | solution.py:134
  47.6 4.1 %collective-permute-start.9 = (bf16[3,32,192]{2,1,0:T(8,128)(2,1)S(1)}, bf16[3,32,192]{2,1,0:T(8,128)(2,1)S(1)}, u32[]{:S(2)}, u32[]{:S(2)}) collective-permute-start(bf16[3,32,192]{2,1,0:T(8,128)(2,1)S(1)} %get-tuple-element.17), channel_id=1, source_target_pairs={{0,24},{8,0},{16,8},{24,16},{1,25},{9,1},{17,9},{25,17},{2,26},{10... | collective-permute-start | bytes 110600 | tf_op jit(solution)/shard_map/ppermute | solution.py:134
  51.7 4.1 %collective-permute-start.11 = (bf16[3,3,32,192]{3,2,1,0:T(8,128)(2,1)S(1)}, bf16[3,3,32,192]{3,2,1,0:T(8,128)(2,1)S(1)}, u32[]{:S(2)}, u32[]{:S(2)}) collective-permute-start(bf16[3,3,32,192]{3,2,1,0:T(8,128)(2,1)S(1)} %pad_maximum_fusion.2), channel_id=1, source_target_pairs={{0,7},{1,0},{2,1},{3,2},{4,3},{5,4},{6,5},{7,6},{8,15},{9,8},{10,9... | collective-permute-start | bytes 331784 | tf_op jit(solution)/shard_map/ppermute | solution.py:134
  52.6 6.4 %collective-permute-start.10 = (bf16[3,3,32,192]{3,2,1,0:T(8,128)(2,1)S(1)}, bf16[3,3,32,192]{3,2,1,0:T(8,128)(2,1)S(1)}, u32[]{:S(2)}, u32[]{:S(2)}) collective-permute-start(bf16[3,3,32,192]{3,2,1,0:T(8,128)(2,1)S(1)} %pad_maximum_fusion.2), channel_id=1, source_target_pairs={{0,1},{1,2},{2,3},{3,4},{4,5},{5,6},{6,7},{7,0},{8,9},{9,10},{10,1... | collective-permute-start | bytes 331784 | tf_op jit(solution)/shard_map/ppermute | solution.py:134
  59.9 5.0 %collective-permute-start.12 = (bf16[3,32,192]{2,1,0:T(8,128)(2,1)S(1)}, bf16[3,32,192]{2,1,0:T(8,128)(2,1)S(1)}, u32[]{:S(2)}, u32[]{:S(2)}) collective-permute-start(bf16[3,32,192]{2,1,0:T(8,128)(2,1)S(1)} %get-tuple-element.19), channel_id=1, source_target_pairs={{0,8},{8,16},{16,24},{24,0},{1,9},{9,17},{17,25},{25,1},{2,10},{10... | collective-permute-start | bytes 110600 | tf_op jit(solution)/shard_map/ppermute | solution.py:134
  61.2 4.1 %collective-permute-start.13 = (bf16[3,32,192]{2,1,0:T(8,128)(2,1)S(1)}, bf16[3,32,192]{2,1,0:T(8,128)(2,1)S(1)}, u32[]{:S(2)}, u32[]{:S(2)}) collective-permute-start(bf16[3,32,192]{2,1,0:T(8,128)(2,1)S(1)} %get-tuple-element.19), channel_id=1, source_target_pairs={{0,24},{8,0},{16,8},{24,16},{1,25},{9,1},{17,9},{25,17},{2,26},{10... | collective-permute-start | bytes 110600 | tf_op jit(solution)/shard_map/ppermute | solution.py:134
  65.3 4.1 %collective-permute-start.15 = (bf16[3,3,32,192]{3,2,1,0:T(8,128)(2,1)S(1)}, bf16[3,3,32,192]{3,2,1,0:T(8,128)(2,1)S(1)}, u32[]{:S(2)}, u32[]{:S(2)}) collective-permute-start(bf16[3,3,32,192]{3,2,1,0:T(8,128)(2,1)S(1)} %pad_maximum_fusion.3), channel_id=1, source_target_pairs={{0,7},{1,0},{2,1},{3,2},{4,3},{5,4},{6,5},{7,6},{8,15},{9,8},{10,9... | collective-permute-start | bytes 331784 | tf_op jit(solution)/shard_map/ppermute | solution.py:134
  66.1 6.4 %collective-permute-start.14 = (bf16[3,3,32,192]{3,2,1,0:T(8,128)(2,1)S(1)}, bf16[3,3,32,192]{3,2,1,0:T(8,128)(2,1)S(1)}, u32[]{:S(2)}, u32[]{:S(2)}) collective-permute-start(bf16[3,3,32,192]{3,2,1,0:T(8,128)(2,1)S(1)} %pad_maximum_fusion.3), channel_id=1, source_target_pairs={{0,1},{1,2},{2,3},{3,4},{4,5},{5,6},{6,7},{7,0},{8,9},{9,10},{10,1... | collective-permute-start | bytes 331784 | tf_op jit(solution)/shard_map/ppermute | solution.py:134
  73.4 5.0 %collective-permute-start.16 = (bf16[3,32,192]{2,1,0:T(8,128)(2,1)S(1)}, bf16[3,32,192]{2,1,0:T(8,128)(2,1)S(1)}, u32[]{:S(2)}, u32[]{:S(2)}) collective-permute-start(bf16[3,32,192]{2,1,0:T(8,128)(2,1)S(1)} %get-tuple-element.21), channel_id=1, source_target_pairs={{0,8},{8,16},{16,24},{24,0},{1,9},{9,17},{17,25},{25,1},{2,10},{10... | collective-permute-start | bytes 110600 | tf_op jit(solution)/shard_map/ppermute | solution.py:134
  74.9 4.1 %collective-permute-start.17 = (bf16[3,32,192]{2,1,0:T(8,128)(2,1)S(1)}, bf16[3,32,192]{2,1,0:T(8,128)(2,1)S(1)}, u32[]{:S(2)}, u32[]{:S(2)}) collective-permute-start(bf16[3,32,192]{2,1,0:T(8,128)(2,1)S(1)} %get-tuple-element.21), channel_id=1, source_target_pairs={{0,24},{8,0},{16,8},{24,16},{1,25},{9,1},{17,9},{25,17},{2,26},{10... | collective-permute-start | bytes 110600 | tf_op jit(solution)/shard_map/ppermute | solution.py:134
  79.0 4.1 %collective-permute-start.19 = (bf16[3,3,32,192]{3,2,1,0:T(8,128)(2,1)S(1)}, bf16[3,3,32,192]{3,2,1,0:T(8,128)(2,1)S(1)}, u32[]{:S(2)}, u32[]{:S(2)}) collective-permute-start(bf16[3,3,32,192]{3,2,1,0:T(8,128)(2,1)S(1)} %pad_maximum_fusion.4), channel_id=1, source_target_pairs={{0,7},{1,0},{2,1},{3,2},{4,3},{5,4},{6,5},{7,6},{8,15},{9,8},{10,9... | collective-permute-start | bytes 331784 | tf_op jit(solution)/shard_map/ppermute | solution.py:134
  79.8 6.4 %collective-permute-start.18 = (bf16[3,3,32,192]{3,2,1,0:T(8,128)(2,1)S(1)}, bf16[3,3,32,192]{3,2,1,0:T(8,128)(2,1)S(1)}, u32[]{:S(2)}, u32[]{:S(2)}) collective-permute-start(bf16[3,3,32,192]{3,2,1,0:T(8,128)(2,1)S(1)} %pad_maximum_fusion.4), channel_id=1, source_target_pairs={{0,1},{1,2},{2,3},{3,4},{4,5},{5,6},{6,7},{7,0},{8,9},{9,10},{10,1... | collective-permute-start | bytes 331784 | tf_op jit(solution)/shard_map/ppermute | solution.py:134
  87.1 5.0 %collective-permute-start.20 = (bf16[3,32,192]{2,1,0:T(8,128)(2,1)S(1)}, bf16[3,32,192]{2,1,0:T(8,128)(2,1)S(1)}, u32[]{:S(2)}, u32[]{:S(2)}) collective-permute-start(bf16[3,32,192]{2,1,0:T(8,128)(2,1)S(1)} %get-tuple-element.23), channel_id=1, source_target_pairs={{0,8},{8,16},{16,24},{24,0},{1,9},{9,17},{17,25},{25,1},{2,10},{10... | collective-permute-start | bytes 110600 | tf_op jit(solution)/shard_map/ppermute | solution.py:134
  88.9 4.1 %collective-permute-start.21 = (bf16[3,32,192]{2,1,0:T(8,128)(2,1)S(1)}, bf16[3,32,192]{2,1,0:T(8,128)(2,1)S(1)}, u32[]{:S(2)}, u32[]{:S(2)}) collective-permute-start(bf16[3,32,192]{2,1,0:T(8,128)(2,1)S(1)} %get-tuple-element.23), channel_id=1, source_target_pairs={{0,24},{8,0},{16,8},{24,16},{1,25},{9,1},{17,9},{25,17},{2,26},{10... | collective-permute-start | bytes 110600 | tf_op jit(solution)/shard_map/ppermute | solution.py:134
  93.0 4.1 %collective-permute-start.23 = (bf16[3,3,32,192]{3,2,1,0:T(8,128)(2,1)S(1)}, bf16[3,3,32,192]{3,2,1,0:T(8,128)(2,1)S(1)}, u32[]{:S(2)}, u32[]{:S(2)}) collective-permute-start(bf16[3,3,32,192]{3,2,1,0:T(8,128)(2,1)S(1)} %pad_maximum_fusion.5), channel_id=1, source_target_pairs={{0,7},{1,0},{2,1},{3,2},{4,3},{5,4},{6,5},{7,6},{8,15},{9,8},{10,9... | collective-permute-start | bytes 331784 | tf_op jit(solution)/shard_map/ppermute | solution.py:134
  93.9 6.4 %collective-permute-start.22 = (bf16[3,3,32,192]{3,2,1,0:T(8,128)(2,1)S(1)}, bf16[3,3,32,192]{3,2,1,0:T(8,128)(2,1)S(1)}, u32[]{:S(2)}, u32[]{:S(2)}) collective-permute-start(bf16[3,3,32,192]{3,2,1,0:T(8,128)(2,1)S(1)} %pad_maximum_fusion.5), channel_id=1, source_target_pairs={{0,1},{1,2},{2,3},{3,4},{4,5},{5,6},{6,7},{7,0},{8,9},{9,10},{10,1... | collective-permute-start | bytes 331784 | tf_op jit(solution)/shard_map/ppermute | solution.py:134
  101.2 5.0 %collective-permute-start.24 = (bf16[3,32,192]{2,1,0:T(8,128)(2,1)S(1)}, bf16[3,32,192]{2,1,0:T(8,128)(2,1)S(1)}, u32[]{:S(2)}, u32[]{:S(2)}) collective-permute-start(bf16[3,32,192]{2,1,0:T(8,128)(2,1)S(1)} %get-tuple-element.25), channel_id=1, source_target_pairs={{0,8},{8,16},{16,24},{24,0},{1,9},{9,17},{17,25},{25,1},{2,10},{10... | collective-permute-start | bytes 110600 | tf_op jit(solution)/shard_map/ppermute | solution.py:134
  102.5 4.1 %collective-permute-start.25 = (bf16[3,32,192]{2,1,0:T(8,128)(2,1)S(1)}, bf16[3,32,192]{2,1,0:T(8,128)(2,1)S(1)}, u32[]{:S(2)}, u32[]{:S(2)}) collective-permute-start(bf16[3,32,192]{2,1,0:T(8,128)(2,1)S(1)} %get-tuple-element.25), channel_id=1, source_target_pairs={{0,24},{8,0},{16,8},{24,16},{1,25},{9,1},{17,9},{25,17},{2,26},{10... | collective-permute-start | bytes 110600 | tf_op jit(solution)/shard_map/ppermute | solution.py:134
  106.7 4.1 %collective-permute-start.27 = (bf16[3,3,32,192]{3,2,1,0:T(8,128)(2,1)S(1)}, bf16[3,3,32,192]{3,2,1,0:T(8,128)(2,1)S(1)}, u32[]{:S(2)}, u32[]{:S(2)}) collective-permute-start(bf16[3,3,32,192]{3,2,1,0:T(8,128)(2,1)S(1)} %pad_maximum_fusion.6), channel_id=1, source_target_pairs={{0,7},{1,0},{2,1},{3,2},{4,3},{5,4},{6,5},{7,6},{8,15},{9,8},{10,9... | collective-permute-start | bytes 331784 | tf_op jit(solution)/shard_map/ppermute | solution.py:134
  107.8 6.4 %collective-permute-start.26 = (bf16[3,3,32,192]{3,2,1,0:T(8,128)(2,1)S(1)}, bf16[3,3,32,192]{3,2,1,0:T(8,128)(2,1)S(1)}, u32[]{:S(2)}, u32[]{:S(2)}) collective-permute-start(bf16[3,3,32,192]{3,2,1,0:T(8,128)(2,1)S(1)} %pad_maximum_fusion.6), channel_id=1, source_target_pairs={{0,1},{1,2},{2,3},{3,4},{4,5},{5,6},{6,7},{7,0},{8,9},{9,10},{10,1... | collective-permute-start | bytes 331784 | tf_op jit(solution)/shard_map/ppermute | solution.py:134
  115.1 5.0 %collective-permute-start.28 = (bf16[3,32,192]{2,1,0:T(8,128)(2,1)S(1)}, bf16[3,32,192]{2,1,0:T(8,128)(2,1)S(1)}, u32[]{:S(2)}, u32[]{:S(2)}) collective-permute-start(bf16[3,32,192]{2,1,0:T(8,128)(2,1)S(1)} %get-tuple-element.27), channel_id=1, source_target_pairs={{0,8},{8,16},{16,24},{24,0},{1,9},{9,17},{17,25},{25,1},{2,10},{10... | collective-permute-start | bytes 110600 | tf_op jit(solution)/shard_map/ppermute | solution.py:134
  116.2 4.1 %collective-permute-start.29 = (bf16[3,32,192]{2,1,0:T(8,128)(2,1)S(1)}, bf16[3,32,192]{2,1,0:T(8,128)(2,1)S(1)}, u32[]{:S(2)}, u32[]{:S(2)}) collective-permute-start(bf16[3,32,192]{2,1,0:T(8,128)(2,1)S(1)} %get-tuple-element.27), channel_id=1, source_target_pairs={{0,24},{8,0},{16,8},{24,16},{1,25},{9,1},{17,9},{25,17},{2,26},{10... | collective-permute-start | bytes 110600 | tf_op jit(solution)/shard_map/ppermute | solution.py:134
  120.4 4.1 %collective-permute-start.31 = (bf16[3,3,32,192]{3,2,1,0:T(8,128)(2,1)S(1)}, bf16[3,3,32,192]{3,2,1,0:T(8,128)(2,1)S(1)}, u32[]{:S(2)}, u32[]{:S(2)}) collective-permute-start(bf16[3,3,32,192]{3,2,1,0:T(8,128)(2,1)S(1)} %pad_maximum_fusion.7), channel_id=1, source_target_pairs={{0,7},{1,0},{2,1},{3,2},{4,3},{5,4},{6,5},{7,6},{8,15},{9,8},{10,9... | collective-permute-start | bytes 331784 | tf_op jit(solution)/shard_map/ppermute | solution.py:134
  121.2 6.4 %collective-permute-start.30 = (bf16[3,3,32,192]{3,2,1,0:T(8,128)(2,1)S(1)}, bf16[3,3,32,192]{3,2,1,0:T(8,128)(2,1)S(1)}, u32[]{:S(2)}, u32[]{:S(2)}) collective-permute-start(bf16[3,3,32,192]{3,2,1,0:T(8,128)(2,1)S(1)} %pad_maximum_fusion.7), channel_id=1, source_target_pairs={{0,1},{1,2},{2,3},{3,4},{4,5},{5,6},{6,7},{7,0},{8,9},{9,10},{10,1... | collective-permute-start | bytes 331784 | tf_op jit(solution)/shard_map/ppermute | solution.py:134
  131.4 4.6 %collective-permute-start.34 = (f32[32,32]{1,0:T(8,128)S(1)}, f32[32,32]{1,0:T(8,128)S(1)}, u32[]{:S(2)}, u32[]{:S(2)}) collective-permute-start(f32[32,32]{1,0:T(8,128)S(1)} %convolution_bitcast_fusion.65), channel_id=1, source_target_pairs={{0,24},{8,16},{16,8},{24,0},{1,25},{9,17},{17,9},{25,1},{2,26},{10... | collective-permute-start | bytes 12296 | tf_op jit(solution)/shard_map/ppermute | solution.py:59
  139.9 4.7 %collective-permute-start.38 = (f32[32,32]{1,0:T(8,128)S(1)}, f32[32,32]{1,0:T(8,128)S(1)}, u32[]{:S(2)}, u32[]{:S(2)}) collective-permute-start(f32[32,32]{1,0:T(8,128)S(1)} %add_add_fusion.2), channel_id=1, source_target_pairs={{0,4},{1,5},{2,6},{3,7},{4,0},{5,1},{6,2},{7,3},{8,12},{9,13},{10,... | collective-permute-start | bytes 12296 | tf_op jit(solution)/shard_map/ppermute | solution.py:59
  151.6 5.0 %collective-permute-start.39 = (bf16[3,32,192]{2,1,0:T(8,128)(2,1)S(1)}, bf16[3,32,192]{2,1,0:T(8,128)(2,1)S(1)}, u32[]{:S(2)}, u32[]{:S(2)}) collective-permute-start(bf16[3,32,192]{2,1,0:T(8,128)(2,1)S(1)} %get-tuple-element.12), channel_id=1, source_target_pairs={{0,8},{8,16},{16,24},{24,0},{1,9},{9,17},{17,25},{25,1},{2,10},{10... | collective-permute-start | bytes 110600 | tf_op jit(solution)/shard_map/ppermute | solution.py:134
  152.2 4.4 %collective-permute-start.40 = (bf16[3,32,192]{2,1,0:T(8,128)(2,1)S(1)}, bf16[3,32,192]{2,1,0:T(8,128)(2,1)S(1)}, u32[]{:S(2)}, u32[]{:S(2)}) collective-permute-start(bf16[3,32,192]{2,1,0:T(8,128)(2,1)S(1)} %get-tuple-element.12), channel_id=1, source_target_pairs={{0,24},{8,0},{16,8},{24,16},{1,25},{9,1},{17,9},{25,17},{2,26},{10... | collective-permute-start | bytes 110600 | tf_op jit(solution)/shard_map/ppermute | solution.py:134
  156.7 6.4 %collective-permute-start.41 = (bf16[3,3,32,192]{3,2,1,0:T(8,128)(2,1)S(1)}, bf16[3,3,32,192]{3,2,1,0:T(8,128)(2,1)S(1)}, u32[]{:S(2)}, u32[]{:S(2)}) collective-permute-start(bf16[3,3,32,192]{3,2,1,0:T(8,128)(2,1)S(1)} %pad_maximum_fusion.8), channel_id=1, source_target_pairs={{0,1},{1,2},{2,3},{3,4},{4,5},{5,6},{6,7},{7,0},{8,9},{9,10},{10,1... | collective-permute-start | bytes 331784 | tf_op jit(solution)/shard_map/ppermute | solution.py:134
  164.1 5.5 %collective-permute-start.43 = (bf16[3,32,192]{2,1,0:T(8,128)(2,1)S(1)}, bf16[3,32,192]{2,1,0:T(8,128)(2,1)S(1)}, u32[]{:S(2)}, u32[]{:S(2)}) collective-permute-start(bf16[3,32,192]{2,1,0:T(8,128)(2,1)S(1)} %get-tuple-element.10), channel_id=1, source_target_pairs={{0,8},{8,16},{16,24},{24,0},{1,9},{9,17},{17,25},{25,1},{2,10},{10... | collective-permute-start | bytes 110600 | tf_op jit(solution)/shard_map/ppermute | solution.py:134
  166.4 4.1 %collective-permute-start.44 = (bf16[3,32,192]{2,1,0:T(8,128)(2,1)S(1)}, bf16[3,32,192]{2,1,0:T(8,128)(2,1)S(1)}, u32[]{:S(2)}, u32[]{:S(2)}) collective-permute-start(bf16[3,32,192]{2,1,0:T(8,128)(2,1)S(1)} %get-tuple-element.10), channel_id=1, source_target_pairs={{0,24},{8,0},{16,8},{24,16},{1,25},{9,1},{17,9},{25,17},{2,26},{10... | collective-permute-start | bytes 110600 | tf_op jit(solution)/shard_map/ppermute | solution.py:134
  170.5 4.6 %collective-permute-start.46 = (bf16[3,3,32,192]{3,2,1,0:T(8,128)(2,1)S(1)}, bf16[3,3,32,192]{3,2,1,0:T(8,128)(2,1)S(1)}, u32[]{:S(2)}, u32[]{:S(2)}) collective-permute-start(bf16[3,3,32,192]{3,2,1,0:T(8,128)(2,1)S(1)} %pad_maximum_fusion.9), channel_id=1, source_target_pairs={{0,7},{1,0},{2,1},{3,2},{4,3},{5,4},{6,5},{7,6},{8,15},{9,8},{10,9... | collective-permute-start | bytes 331784 | tf_op jit(solution)/shard_map/ppermute | solution.py:134
  172.5 6.4 %collective-permute-start.45 = (bf16[3,3,32,192]{3,2,1,0:T(8,128)(2,1)S(1)}, bf16[3,3,32,192]{3,2,1,0:T(8,128)(2,1)S(1)}, u32[]{:S(2)}, u32[]{:S(2)}) collective-permute-start(bf16[3,3,32,192]{3,2,1,0:T(8,128)(2,1)S(1)} %pad_maximum_fusion.9), channel_id=1, source_target_pairs={{0,1},{1,2},{2,3},{3,4},{4,5},{5,6},{6,7},{7,0},{8,9},{9,10},{10,1... | collective-permute-start | bytes 331784 | tf_op jit(solution)/shard_map/ppermute | solution.py:134
  179.8 5.0 %collective-permute-start.47 = (bf16[3,32,192]{2,1,0:T(8,128)(2,1)S(1)}, bf16[3,32,192]{2,1,0:T(8,128)(2,1)S(1)}, u32[]{:S(2)}, u32[]{:S(2)}) collective-permute-start(bf16[3,32,192]{2,1,0:T(8,128)(2,1)S(1)} %get-tuple-element.8), channel_id=1, source_target_pairs={{0,8},{8,16},{16,24},{24,0},{1,9},{9,17},{17,25},{25,1},{2,10},{10... | collective-permute-start | bytes 110600 | tf_op jit(solution)/shard_map/ppermute | solution.py:134
  181.3 4.1 %collective-permute-start.48 = (bf16[3,32,192]{2,1,0:T(8,128)(2,1)S(1)}, bf16[3,32,192]{2,1,0:T(8,128)(2,1)S(1)}, u32[]{:S(2)}, u32[]{:S(2)}) collective-permute-start(bf16[3,32,192]{2,1,0:T(8,128)(2,1)S(1)} %get-tuple-element.8), channel_id=1, source_target_pairs={{0,24},{8,0},{16,8},{24,16},{1,25},{9,1},{17,9},{25,17},{2,26},{10... | collective-permute-start | bytes 110600 | tf_op jit(solution)/shard_map/ppermute | solution.py:134
  185.4 4.1 %collective-permute-start.50 = (bf16[3,3,32,192]{3,2,1,0:T(8,128)(2,1)S(1)}, bf16[3,3,32,192]{3,2,1,0:T(8,128)(2,1)S(1)}, u32[]{:S(2)}, u32[]{:S(2)}) collective-permute-start(bf16[3,3,32,192]{3,2,1,0:T(8,128)(2,1)S(1)} %pad_maximum_fusion.10), channel_id=1, source_target_pairs={{0,7},{1,0},{2,1},{3,2},{4,3},{5,4},{6,5},{7,6},{8,15},{9,8},{10,9... | collective-permute-start | bytes 331784 | tf_op jit(solution)/shard_map/ppermute | solution.py:134
  186.2 6.4 %collective-permute-start.49 = (bf16[3,3,32,192]{3,2,1,0:T(8,128)(2,1)S(1)}, bf16[3,3,32,192]{3,2,1,0:T(8,128)(2,1)S(1)}, u32[]{:S(2)}, u32[]{:S(2)}) collective-permute-start(bf16[3,3,32,192]{3,2,1,0:T(8,128)(2,1)S(1)} %pad_maximum_fusion.10), channel_id=1, source_target_pairs={{0,1},{1,2},{2,3},{3,4},{4,5},{5,6},{6,7},{7,0},{8,9},{9,10},{10,1... | collective-permute-start | bytes 331784 | tf_op jit(solution)/shard_map/ppermute | solution.py:134
  193.5 5.0 %collective-permute-start.51 = (bf16[3,32,192]{2,1,0:T(8,128)(2,1)S(1)}, bf16[3,32,192]{2,1,0:T(8,128)(2,1)S(1)}, u32[]{:S(2)}, u32[]{:S(2)}) collective-permute-start(bf16[3,32,192]{2,1,0:T(8,128)(2,1)S(1)} %get-tuple-element.6), channel_id=1, source_target_pairs={{0,8},{8,16},{16,24},{24,0},{1,9},{9,17},{17,25},{25,1},{2,10},{10... | collective-permute-start | bytes 110600 | tf_op jit(solution)/shard_map/ppermute | solution.py:134
  195.0 4.1 %collective-permute-start.52 = (bf16[3,32,192]{2,1,0:T(8,128)(2,1)S(1)}, bf16[3,32,192]{2,1,0:T(8,128)(2,1)S(1)}, u32[]{:S(2)}, u32[]{:S(2)}) collective-permute-start(bf16[3,32,192]{2,1,0:T(8,128)(2,1)S(1)} %get-tuple-element.6), channel_id=1, source_target_pairs={{0,24},{8,0},{16,8},{24,16},{1,25},{9,1},{17,9},{25,17},{2,26},{10... | collective-permute-start | bytes 110600 | tf_op jit(solution)/shard_map/ppermute | solution.py:134
  199.1 4.1 %collective-permute-start.54 = (bf16[3,3,32,192]{3,2,1,0:T(8,128)(2,1)S(1)}, bf16[3,3,32,192]{3,2,1,0:T(8,128)(2,1)S(1)}, u32[]{:S(2)}, u32[]{:S(2)}) collective-permute-start(bf16[3,3,32,192]{3,2,1,0:T(8,128)(2,1)S(1)} %pad_maximum_fusion.11), channel_id=1, source_target_pairs={{0,7},{1,0},{2,1},{3,2},{4,3},{5,4},{6,5},{7,6},{8,15},{9,8},{10,9... | collective-permute-start | bytes 331784 | tf_op jit(solution)/shard_map/ppermute | solution.py:134
  200.0 6.4 %collective-permute-start.53 = (bf16[3,3,32,192]{3,2,1,0:T(8,128)(2,1)S(1)}, bf16[3,3,32,192]{3,2,1,0:T(8,128)(2,1)S(1)}, u32[]{:S(2)}, u32[]{:S(2)}) collective-permute-start(bf16[3,3,32,192]{3,2,1,0:T(8,128)(2,1)S(1)} %pad_maximum_fusion.11), channel_id=1, source_target_pairs={{0,1},{1,2},{2,3},{3,4},{4,5},{5,6},{6,7},{7,0},{8,9},{9,10},{10,1... | collective-permute-start | bytes 331784 | tf_op jit(solution)/shard_map/ppermute | solution.py:134
  207.3 5.0 %collective-permute-start.55 = (bf16[3,32,192]{2,1,0:T(8,128)(2,1)S(1)}, bf16[3,32,192]{2,1,0:T(8,128)(2,1)S(1)}, u32[]{:S(2)}, u32[]{:S(2)}) collective-permute-start(bf16[3,32,192]{2,1,0:T(8,128)(2,1)S(1)} %get-tuple-element.29), channel_id=1, source_target_pairs={{0,8},{8,16},{16,24},{24,0},{1,9},{9,17},{17,25},{25,1},{2,10},{10... | collective-permute-start | bytes 110600 | tf_op jit(solution)/shard_map/ppermute | solution.py:134
  212.7 4.1 %collective-permute-start.58 = (bf16[3,3,32,192]{3,2,1,0:T(8,128)(2,1)S(1)}, bf16[3,3,32,192]{3,2,1,0:T(8,128)(2,1)S(1)}, u32[]{:S(2)}, u32[]{:S(2)}) collective-permute-start(bf16[3,3,32,192]{3,2,1,0:T(8,128)(2,1)S(1)} %pad_maximum_fusion.12), channel_id=1, source_target_pairs={{0,7},{1,0},{2,1},{3,2},{4,3},{5,4},{6,5},{7,6},{8,15},{9,8},{10,9... | collective-permute-start | bytes 331784 | tf_op jit(solution)/shard_map/ppermute | solution.py:134
  213.8 6.4 %collective-permute-start.57 = (bf16[3,3,32,192]{3,2,1,0:T(8,128)(2,1)S(1)}, bf16[3,3,32,192]{3,2,1,0:T(8,128)(2,1)S(1)}, u32[]{:S(2)}, u32[]{:S(2)}) collective-permute-start(bf16[3,3,32,192]{3,2,1,0:T(8,128)(2,1)S(1)} %pad_maximum_fusion.12), channel_id=1, source_target_pairs={{0,1},{1,2},{2,3},{3,4},{4,5},{5,6},{6,7},{7,0},{8,9},{9,10},{10,1... | collective-permute-start | bytes 331784 | tf_op jit(solution)/shard_map/ppermute | solution.py:134
  221.1 5.0 %collective-permute-start.59 = (bf16[3,32,192]{2,1,0:T(8,128)(2,1)S(1)}, bf16[3,32,192]{2,1,0:T(8,128)(2,1)S(1)}, u32[]{:S(2)}, u32[]{:S(2)}) collective-permute-start(bf16[3,32,192]{2,1,0:T(8,128)(2,1)S(1)} %get-tuple-element.31), channel_id=1, source_target_pairs={{0,8},{8,16},{16,24},{24,0},{1,9},{9,17},{17,25},{25,1},{2,10},{10... | collective-permute-start | bytes 110600 | tf_op jit(solution)/shard_map/ppermute | solution.py:134
  222.2 4.1 %collective-permute-start.60 = (bf16[3,32,192]{2,1,0:T(8,128)(2,1)S(1)}, bf16[3,32,192]{2,1,0:T(8,128)(2,1)S(1)}, u32[]{:S(2)}, u32[]{:S(2)}) collective-permute-start(bf16[3,32,192]{2,1,0:T(8,128)(2,1)S(1)} %get-tuple-element.31), channel_id=1, source_target_pairs={{0,24},{8,0},{16,8},{24,16},{1,25},{9,1},{17,9},{25,17},{2,26},{10... | collective-permute-start | bytes 110600 | tf_op jit(solution)/shard_map/ppermute | solution.py:134
  226.3 4.1 %collective-permute-start.62 = (bf16[3,3,32,192]{3,2,1,0:T(8,128)(2,1)S(1)}, bf16[3,3,32,192]{3,2,1,0:T(8,128)(2,1)S(1)}, u32[]{:S(2)}, u32[]{:S(2)}) collective-permute-start(bf16[3,3,32,192]{3,2,1,0:T(8,128)(2,1)S(1)} %pad_maximum_fusion.13), channel_id=1, source_target_pairs={{0,7},{1,0},{2,1},{3,2},{4,3},{5,4},{6,5},{7,6},{8,15},{9,8},{10,9... | collective-permute-start | bytes 331784 | tf_op jit(solution)/shard_map/ppermute | solution.py:134
  227.3 6.4 %collective-permute-start.61 = (bf16[3,3,32,192]{3,2,1,0:T(8,128)(2,1)S(1)}, bf16[3,3,32,192]{3,2,1,0:T(8,128)(2,1)S(1)}, u32[]{:S(2)}, u32[]{:S(2)}) collective-permute-start(bf16[3,3,32,192]{3,2,1,0:T(8,128)(2,1)S(1)} %pad_maximum_fusion.13), channel_id=1, source_target_pairs={{0,1},{1,2},{2,3},{3,4},{4,5},{5,6},{6,7},{7,0},{8,9},{9,10},{10,1... | collective-permute-start | bytes 331784 | tf_op jit(solution)/shard_map/ppermute | solution.py:134
  234.6 5.0 %collective-permute-start.63 = (bf16[3,32,192]{2,1,0:T(8,128)(2,1)S(1)}, bf16[3,32,192]{2,1,0:T(8,128)(2,1)S(1)}, u32[]{:S(2)}, u32[]{:S(2)}) collective-permute-start(bf16[3,32,192]{2,1,0:T(8,128)(2,1)S(1)} %get-tuple-element.33), channel_id=1, source_target_pairs={{0,8},{8,16},{16,24},{24,0},{1,9},{9,17},{17,25},{25,1},{2,10},{10... | collective-permute-start | bytes 110600 | tf_op jit(solution)/shard_map/ppermute | solution.py:134
  240.5 4.1 %collective-permute-start.66 = (bf16[3,3,32,192]{3,2,1,0:T(8,128)(2,1)S(1)}, bf16[3,3,32,192]{3,2,1,0:T(8,128)(2,1)S(1)}, u32[]{:S(2)}, u32[]{:S(2)}) collective-permute-start(bf16[3,3,32,192]{3,2,1,0:T(8,128)(2,1)S(1)} %pad_maximum_fusion.14), channel_id=1, source_target_pairs={{0,7},{1,0},{2,1},{3,2},{4,3},{5,4},{6,5},{7,6},{8,15},{9,8},{10,9... | collective-permute-start | bytes 331784 | tf_op jit(solution)/shard_map/ppermute | solution.py:134
  241.2 6.4 %collective-permute-start.65 = (bf16[3,3,32,192]{3,2,1,0:T(8,128)(2,1)S(1)}, bf16[3,3,32,192]{3,2,1,0:T(8,128)(2,1)S(1)}, u32[]{:S(2)}, u32[]{:S(2)}) collective-permute-start(bf16[3,3,32,192]{3,2,1,0:T(8,128)(2,1)S(1)} %pad_maximum_fusion.14), channel_id=1, source_target_pairs={{0,1},{1,2},{2,3},{3,4},{4,5},{5,6},{6,7},{7,0},{8,9},{9,10},{10,1... | collective-permute-start | bytes 331784 | tf_op jit(solution)/shard_map/ppermute | solution.py:134
  248.5 5.0 %collective-permute-start.67 = (bf16[3,32,192]{2,1,0:T(8,128)(2,1)S(1)}, bf16[3,32,192]{2,1,0:T(8,128)(2,1)S(1)}, u32[]{:S(2)}, u32[]{:S(2)}) collective-permute-start(bf16[3,32,192]{2,1,0:T(8,128)(2,1)S(1)} %get-tuple-element.35), channel_id=1, source_target_pairs={{0,8},{8,16},{16,24},{24,0},{1,9},{9,17},{17,25},{25,1},{2,10},{10... | collective-permute-start | bytes 110600 | tf_op jit(solution)/shard_map/ppermute | solution.py:134
  253.9 4.1 %collective-permute-start.70 = (bf16[3,3,32,192]{3,2,1,0:T(8,128)(2,1)S(1)}, bf16[3,3,32,192]{3,2,1,0:T(8,128)(2,1)S(1)}, u32[]{:S(2)}, u32[]{:S(2)}) collective-permute-start(bf16[3,3,32,192]{3,2,1,0:T(8,128)(2,1)S(1)} %pad_maximum_fusion.15), channel_id=1, source_target_pairs={{0,7},{1,0},{2,1},{3,2},{4,3},{5,4},{6,5},{7,6},{8,15},{9,8},{10,9... | collective-permute-start | bytes 331784 | tf_op jit(solution)/shard_map/ppermute | solution.py:134
  255.0 6.4 %collective-permute-start.69 = (bf16[3,3,32,192]{3,2,1,0:T(8,128)(2,1)S(1)}, bf16[3,3,32,192]{3,2,1,0:T(8,128)(2,1)S(1)}, u32[]{:S(2)}, u32[]{:S(2)}) collective-permute-start(bf16[3,3,32,192]{3,2,1,0:T(8,128)(2,1)S(1)} %pad_maximum_fusion.15), channel_id=1, source_target_pairs={{0,1},{1,2},{2,3},{3,4},{4,5},{5,6},{6,7},{7,0},{8,9},{9,10},{10,1... | collective-permute-start | bytes 331784 | tf_op jit(solution)/shard_map/ppermute | solution.py:134
  265.0 4.6 %collective-permute-start.73 = (f32[32,32]{1,0:T(8,128)S(1)}, f32[32,32]{1,0:T(8,128)S(1)}, u32[]{:S(2)}, u32[]{:S(2)}) collective-permute-start(f32[32,32]{1,0:T(8,128)S(1)} %convolution_bitcast_fusion.64), channel_id=1, source_target_pairs={{0,24},{8,16},{16,8},{24,0},{1,25},{9,17},{17,9},{25,1},{2,26},{10... | collective-permute-start | bytes 12296 | tf_op jit(solution)/shard_map/ppermute | solution.py:59
  273.5 4.7 %collective-permute-start.77 = (f32[32,32]{1,0:T(8,128)S(1)}, f32[32,32]{1,0:T(8,128)S(1)}, u32[]{:S(2)}, u32[]{:S(2)}) collective-permute-start(f32[32,32]{1,0:T(8,128)S(1)} %add_add_fusion), channel_id=1, source_target_pairs={{0,4},{1,5},{2,6},{3,7},{4,0},{5,1},{6,2},{7,3},{8,12},{9,13},{10,... | collective-permute-start | bytes 12296 | tf_op jit(solution)/shard_map/ppermute | solution.py:59
  (17 other events, 172.8 us)

commit v5 on v3

--- a/solution.py
+++ b/solution.py
@@ -39,12 +39,16 @@
     slot_ids = jnp.arange(slots, dtype=jnp.int32)[:, None, None]
     index = jnp.sum(jnp.where(match, slot_ids, 0), axis=0)
     present = jnp.any(match, axis=0)
-    blocks = jnp.take(matrices, index.reshape(-1), axis=0).reshape(
-        depth, cells, matrices.shape[1], matrices.shape[2]
-    )
-    return lax.optimization_barrier(
-        jnp.where(present[:, :, None, None], blocks, jnp.zeros((), matrices.dtype))
-    )
+    flat_index = index.reshape(-1)
+    flat_present = present.reshape(-1)
+    zero = jnp.zeros(matrices.shape[1:], matrices.dtype)
+    blocks = jnp.stack(
+        [
+            jnp.where(flat_present[c], lax.dynamic_index_in_dim(matrices, flat_index[c], keepdims=False), zero)
+            for c in range(depth * cells)
+        ]
+    ).reshape(depth, cells, matrices.shape[1], matrices.shape[2])
+    return lax.optimization_barrier(blocks)
 
 
 def all_sum(value, axes):

time: 287 us -> 523 us (1.82)
  between operations: 0.43 us -> 152 us
  other arithmetic: 20.9 us -> 105 us
    unnamed x0 -> x80, other arithmetic: none -> 87.8 us
    gather x1 -> x0, local copies, waits for them, and re-layouts: 10.3 us -> none  [dense_coupling(): jnp.take(matrices, index.reshape(-1), axis=0)]
    slice x0 -> x10, local copies, waits for them, and re-layouts: none -> 7.2 us  [the longest x5 3.6 us: dense_coupling(): flat_index[c]]
  transfers between devices with their start and end apart: 78 -> 78, of which waited for: 71 -> 71; matrix products, arithmetic and copies ran while one was open for 18% -> 25% of each run, Pallas kernels for 0% -> 0%
where the time goes in v5:
time: 523 us; the launch traced here: 519 us
  between operations  152 us (29%)
  waiting for transfers between devices  124 us (24%)
  other arithmetic  105 us (20%)
  starting transfers between devices  79.1 us (15%)
  matrix products  51.2 us (10%)
  local copies, waits for them, and re-layouts  7.53 us (1%)
    ppermute x64, waiting for transfers between devices, shift(): lax.ppermute(value, axis, [(i, (i + step) % count) for i in range(count)])  106 us
    unnamed x80, other arithmetic  87.8 us
    ppermute x64, starting transfers between devices, shift(): lax.ppermute(value, axis, [(i, (i + step) % count) for i in range(count)])  66.1 us
    dot_general x64, matrix products, part(): jnp.einsum('kvj,tkij->tvi', cells, blocks, preferred_element_type=jnp.flo...  49.2 us
    ppermute x14, waiting for transfers between devices, swap(): return lax.ppermute(v, axis, [(i, i ^ stride) for i in range(count)])  18.3 us
    ppermute x14, starting transfers between devices, swap(): return lax.ppermute(v, axis, [(i, i ^ stride) for i in range(count)])  13.1 us
  transfers between devices with their start and end apart: 78, of which 71 were waited for; matrix products, arithmetic and copies ran while one was open for 25% of the time, Pallas kernels for 0%

profile of v5, /device:TPU:0, one launch (start us, length us, event | category | flops | bytes accessed | tf_op | source)
XLA Modules:
  0.0 518.7 jit_solution(2554694633129342860)
XLA Ops:
  0.9 3.0 collective-permute-start
  164.9 1.7 constant_dynamic-update-slice_fusion.80
  166.6 1.8 constant_dynamic-update-slice_fusion.79
  254.2 2.9 collective-permute-start.3
  257.8 2.3 collective-permute-done.3
  261.0 2.6 collective-permute-done.2
  265.1 2.3 collective-permute-start.5
  272.0 2.3 collective-permute-done.7
  275.1 2.6 collective-permute-done.6
  282.0 1.7 collective-permute-done.8
  285.6 2.6 collective-permute-done.11
  289.1 2.3 collective-permute-done.10
  295.7 1.7 collective-permute-done.12
  299.1 2.8 collective-permute-done.15
  302.8 2.1 collective-permute-done.14
  309.2 1.7 collective-permute-done.16
  312.8 2.8 collective-permute-done.19
  316.5 2.1 collective-permute-done.18
  319.5 1.9 collective-permute-start.20
  326.9 2.6 collective-permute-done.23
  330.4 2.3 collective-permute-done.22
  337.0 1.7 collective-permute-done.24
  340.8 2.6 collective-permute-done.27
  344.2 2.3 collective-permute-done.26
  348.5 2.0 collective-permute-start.29
  350.8 1.7 collective-permute-done.28
  354.1 2.6 collective-permute-done.31
  357.6 2.3 collective-permute-done.30
  366.3 2.1 collective-permute-done.34
  368.5 1.8 collective-permute-start.37
  370.3 1.9 collective-permute-done.36
  373.4 3.6 collective-permute-done.38
  377.1 2.9 cholesky.44
  381.3 2.4 custom-call.6
  384.9 2.3 collective-permute-start.40
  389.9 2.1 fusion.98
  392.8 2.6 convolution_bitcast_fusion.14
  396.8 2.3 collective-permute-start.43
  400.2 2.1 collective-permute-done.43
  403.3 1.9 collective-permute-start.46
  405.8 2.1 collective-permute-done.46
  408.7 2.8 collective-permute-done.45
  415.9 1.7 collective-permute-done.47
  419.6 2.6 collective-permute-done.50
  423.1 2.3 collective-permute-done.49
  429.7 1.7 collective-permute-done.51
  433.4 2.6 collective-permute-done.54
  436.9 2.3 collective-permute-done.53
  447.1 2.5 collective-permute-done.58
  450.5 2.4 collective-permute-done.57
  457.2 1.7 collective-permute-done.59
  460.8 2.6 collective-permute-done.62
  464.2 2.3 collective-permute-done.61
  470.8 1.7 collective-permute-done.63
  474.6 2.6 collective-permute-done.66
  478.1 2.3 collective-permute-done.65
  488.4 2.5 collective-permute-done.70
  491.8 2.4 collective-permute-done.69
  500.2 2.0 collective-permute-done.73
  502.3 1.8 collective-permute-start.76
  504.1 1.9 collective-permute-done.75
  507.1 3.6 collective-permute-done.77
  510.9 2.9 cholesky.55
  515.1 2.4 custom-call.7
  (308 shorter events, 220.2 us)
Async XLA Ops:
  0.9 253.3 %collective-permute-start = (bf16[3,32,192]{2,1,0:T(8,128)(2,1)S(1)}, bf16[3,32,192]{2,1,0:T(8,128)(2,1)S(1)}, u32[]{:S(2)}, u32[]{:S(2)}) collective-permute-start(bf16[3,32,192]{2,1,0:T(8,128)(2,1)S(1)} %get-tuple-element.16), channel_id=1, source_target_pairs={{0,8},{8,16},{16,24},{24,0},{1,9},{9,17},{17,25},{25,1},{2,10},{10... | collective-permute-start | bytes 110600 | tf_op jit(solution)/shard_map/ppermute | solution.py:103
  3.9 250.3 %collective-permute-start.1 = (bf16[3,32,192]{2,1,0:T(8,128)(2,1)S(1)}, bf16[3,32,192]{2,1,0:T(8,128)(2,1)S(1)}, u32[]{:S(2)}, u32[]{:S(2)}) collective-permute-start(bf16[3,32,192]{2,1,0:T(8,128)(2,1)S(1)} %get-tuple-element.16), channel_id=1, source_target_pairs={{0,24},{8,0},{16,8},{24,16},{1,25},{9,1},{17,9},{25,17},{2,26},{10... | collective-permute-start | bytes 110600 | tf_op jit(solution)/shard_map/ppermute | solution.py:103
  254.2 5.8 %collective-permute-start.3 = (bf16[3,3,32,192]{3,2,1,0:T(8,128)(2,1)S(1)}, bf16[3,3,32,192]{3,2,1,0:T(8,128)(2,1)S(1)}, u32[]{:S(2)}, u32[]{:S(2)}) collective-permute-start(bf16[3,3,32,192]{3,2,1,0:T(8,128)(2,1)S(1)} %pad_maximum_fusion), channel_id=1, source_target_pairs={{0,7},{1,0},{2,1},{3,2},{4,3},{5,4},{6,5},{7,6},{8,15},{9,8},{10,9... | collective-permute-start | bytes 331784 | tf_op jit(solution)/shard_map/ppermute | solution.py:103
  257.2 6.4 %collective-permute-start.2 = (bf16[3,3,32,192]{3,2,1,0:T(8,128)(2,1)S(1)}, bf16[3,3,32,192]{3,2,1,0:T(8,128)(2,1)S(1)}, u32[]{:S(2)}, u32[]{:S(2)}) collective-permute-start(bf16[3,3,32,192]{3,2,1,0:T(8,128)(2,1)S(1)} %pad_maximum_fusion), channel_id=1, source_target_pairs={{0,1},{1,2},{2,3},{3,4},{4,5},{5,6},{6,7},{7,0},{8,9},{9,10},{10,1... | collective-permute-start | bytes 331784 | tf_op jit(solution)/shard_map/ppermute | solution.py:103
  264.5 5.0 collective-permute-start.4
  265.1 5.0 collective-permute-start.5
  270.1 4.1 collective-permute-start.7
  271.4 6.4 %collective-permute-start.6 = (bf16[3,3,32,192]{3,2,1,0:T(8,128)(2,1)S(1)}, bf16[3,3,32,192]{3,2,1,0:T(8,128)(2,1)S(1)}, u32[]{:S(2)}, u32[]{:S(2)}) collective-permute-start(bf16[3,3,32,192]{3,2,1,0:T(8,128)(2,1)S(1)} %pad_maximum_fusion.1), channel_id=1, source_target_pairs={{0,1},{1,2},{2,3},{3,4},{4,5},{5,6},{6,7},{7,0},{8,9},{9,10},{10,1... | collective-permute-start | bytes 331784 | tf_op jit(solution)/shard_map/ppermute | solution.py:103
  278.7 5.0 collective-permute-start.8
  280.0 4.1 collective-permute-start.9
  284.1 4.1 collective-permute-start.11
  285.0 6.4 %collective-permute-start.10 = (bf16[3,3,32,192]{3,2,1,0:T(8,128)(2,1)S(1)}, bf16[3,3,32,192]{3,2,1,0:T(8,128)(2,1)S(1)}, u32[]{:S(2)}, u32[]{:S(2)}) collective-permute-start(bf16[3,3,32,192]{3,2,1,0:T(8,128)(2,1)S(1)} %pad_maximum_fusion.2), channel_id=1, source_target_pairs={{0,1},{1,2},{2,3},{3,4},{4,5},{5,6},{6,7},{7,0},{8,9},{9,10},{10,1... | collective-permute-start | bytes 331784 | tf_op jit(solution)/shard_map/ppermute | solution.py:103
  292.3 5.0 collective-permute-start.12
  293.6 4.1 collective-permute-start.13
  297.8 4.1 collective-permute-start.15
  298.5 6.4 %collective-permute-start.14 = (bf16[3,3,32,192]{3,2,1,0:T(8,128)(2,1)S(1)}, bf16[3,3,32,192]{3,2,1,0:T(8,128)(2,1)S(1)}, u32[]{:S(2)}, u32[]{:S(2)}) collective-permute-start(bf16[3,3,32,192]{3,2,1,0:T(8,128)(2,1)S(1)} %pad_maximum_fusion.3), channel_id=1, source_target_pairs={{0,1},{1,2},{2,3},{3,4},{4,5},{5,6},{6,7},{7,0},{8,9},{9,10},{10,1... | collective-permute-start | bytes 331784 | tf_op jit(solution)/shard_map/ppermute | solution.py:103
  305.8 5.0 collective-permute-start.16
  307.3 4.1 collective-permute-start.17
  311.5 4.1 collective-permute-start.19
  312.2 6.4 %collective-permute-start.18 = (bf16[3,3,32,192]{3,2,1,0:T(8,128)(2,1)S(1)}, bf16[3,3,32,192]{3,2,1,0:T(8,128)(2,1)S(1)}, u32[]{:S(2)}, u32[]{:S(2)}) collective-permute-start(bf16[3,3,32,192]{3,2,1,0:T(8,128)(2,1)S(1)} %pad_maximum_fusion.4), channel_id=1, source_target_pairs={{0,1},{1,2},{2,3},{3,4},{4,5},{5,6},{6,7},{7,0},{8,9},{9,10},{10,1... | collective-permute-start | bytes 331784 | tf_op jit(solution)/shard_map/ppermute | solution.py:103
  319.5 5.0 collective-permute-start.20
  321.3 4.1 collective-permute-start.21
  325.4 4.1 collective-permute-start.23
  326.3 6.4 %collective-permute-start.22 = (bf16[3,3,32,192]{3,2,1,0:T(8,128)(2,1)S(1)}, bf16[3,3,32,192]{3,2,1,0:T(8,128)(2,1)S(1)}, u32[]{:S(2)}, u32[]{:S(2)}) collective-permute-start(bf16[3,3,32,192]{3,2,1,0:T(8,128)(2,1)S(1)} %pad_maximum_fusion.5), channel_id=1, source_target_pairs={{0,1},{1,2},{2,3},{3,4},{4,5},{5,6},{6,7},{7,0},{8,9},{9,10},{10,1... | collective-permute-start | bytes 331784 | tf_op jit(solution)/shard_map/ppermute | solution.py:103
  333.6 5.0 collective-permute-start.24
  335.1 4.1 collective-permute-start.25
  339.2 4.1 collective-permute-start.27
  340.2 6.4 %collective-permute-start.26 = (bf16[3,3,32,192]{3,2,1,0:T(8,128)(2,1)S(1)}, bf16[3,3,32,192]{3,2,1,0:T(8,128)(2,1)S(1)}, u32[]{:S(2)}, u32[]{:S(2)}) collective-permute-start(bf16[3,3,32,192]{3,2,1,0:T(8,128)(2,1)S(1)} %pad_maximum_fusion.6), channel_id=1, source_target_pairs={{0,1},{1,2},{2,3},{3,4},{4,5},{5,6},{6,7},{7,0},{8,9},{9,10},{10,1... | collective-permute-start | bytes 331784 | tf_op jit(solution)/shard_map/ppermute | solution.py:103
  347.5 5.0 collective-permute-start.28
  348.5 4.1 collective-permute-start.29
  352.6 4.1 collective-permute-start.31
  353.5 6.4 %collective-permute-start.30 = (bf16[3,3,32,192]{3,2,1,0:T(8,128)(2,1)S(1)}, bf16[3,3,32,192]{3,2,1,0:T(8,128)(2,1)S(1)}, u32[]{:S(2)}, u32[]{:S(2)}) collective-permute-start(bf16[3,3,32,192]{3,2,1,0:T(8,128)(2,1)S(1)} %pad_maximum_fusion.7), channel_id=1, source_target_pairs={{0,1},{1,2},{2,3},{3,4},{4,5},{5,6},{6,7},{7,0},{8,9},{9,10},{10,1... | collective-permute-start | bytes 331784 | tf_op jit(solution)/shard_map/ppermute | solution.py:103
  363.7 4.6 collective-permute-start.34
  372.3 4.7 collective-permute-start.38
  384.3 5.0 collective-permute-start.39
  384.9 4.4 collective-permute-start.40
  389.4 6.4 %collective-permute-start.41 = (bf16[3,3,32,192]{3,2,1,0:T(8,128)(2,1)S(1)}, bf16[3,3,32,192]{3,2,1,0:T(8,128)(2,1)S(1)}, u32[]{:S(2)}, u32[]{:S(2)}) collective-permute-start(bf16[3,3,32,192]{3,2,1,0:T(8,128)(2,1)S(1)} %pad_maximum_fusion.8), channel_id=1, source_target_pairs={{0,1},{1,2},{2,3},{3,4},{4,5},{5,6},{6,7},{7,0},{8,9},{9,10},{10,1... | collective-permute-start | bytes 331784 | tf_op jit(solution)/shard_map/ppermute | solution.py:103
  396.8 5.5 %collective-permute-start.43 = (bf16[3,32,192]{2,1,0:T(8,128)(2,1)S(1)}, bf16[3,32,192]{2,1,0:T(8,128)(2,1)S(1)}, u32[]{:S(2)}, u32[]{:S(2)}) collective-permute-start(bf16[3,32,192]{2,1,0:T(8,128)(2,1)S(1)} %get-tuple-element.12), channel_id=1, source_target_pairs={{0,8},{8,16},{16,24},{24,0},{1,9},{9,17},{17,25},{25,1},{2,10},{10... | collective-permute-start | bytes 110600 | tf_op jit(solution)/shard_map/ppermute | solution.py:103
  399.1 4.1 collective-permute-start.44
  403.3 4.6 collective-permute-start.46
  405.2 6.4 %collective-permute-start.45 = (bf16[3,3,32,192]{3,2,1,0:T(8,128)(2,1)S(1)}, bf16[3,3,32,192]{3,2,1,0:T(8,128)(2,1)S(1)}, u32[]{:S(2)}, u32[]{:S(2)}) collective-permute-start(bf16[3,3,32,192]{3,2,1,0:T(8,128)(2,1)S(1)} %pad_maximum_fusion.9), channel_id=1, source_target_pairs={{0,1},{1,2},{2,3},{3,4},{4,5},{5,6},{6,7},{7,0},{8,9},{9,10},{10,1... | collective-permute-start | bytes 331784 | tf_op jit(solution)/shard_map/ppermute | solution.py:103
  412.5 5.0 collective-permute-start.47
  414.0 4.1 collective-permute-start.48
  418.1 4.1 collective-permute-start.50
  419.0 6.4 %collective-permute-start.49 = (bf16[3,3,32,192]{3,2,1,0:T(8,128)(2,1)S(1)}, bf16[3,3,32,192]{3,2,1,0:T(8,128)(2,1)S(1)}, u32[]{:S(2)}, u32[]{:S(2)}) collective-permute-start(bf16[3,3,32,192]{3,2,1,0:T(8,128)(2,1)S(1)} %pad_maximum_fusion.10), channel_id=1, source_target_pairs={{0,1},{1,2},{2,3},{3,4},{4,5},{5,6},{6,7},{7,0},{8,9},{9,10},{10,1... | collective-permute-start | bytes 331784 | tf_op jit(solution)/shard_map/ppermute | solution.py:103
  426.3 5.0 collective-permute-start.51
  427.7 4.1 collective-permute-start.52
  431.9 4.1 collective-permute-start.54
  432.8 6.4 %collective-permute-start.53 = (bf16[3,3,32,192]{3,2,1,0:T(8,128)(2,1)S(1)}, bf16[3,3,32,192]{3,2,1,0:T(8,128)(2,1)S(1)}, u32[]{:S(2)}, u32[]{:S(2)}) collective-permute-start(bf16[3,3,32,192]{3,2,1,0:T(8,128)(2,1)S(1)} %pad_maximum_fusion.11), channel_id=1, source_target_pairs={{0,1},{1,2},{2,3},{3,4},{4,5},{5,6},{6,7},{7,0},{8,9},{9,10},{10,1... | collective-permute-start | bytes 331784 | tf_op jit(solution)/shard_map/ppermute | solution.py:103
  440.1 5.0 collective-permute-start.55
  441.4 4.1 collective-permute-start.56
  445.5 4.1 collective-permute-start.58
  446.5 6.4 %collective-permute-start.57 = (bf16[3,3,32,192]{3,2,1,0:T(8,128)(2,1)S(1)}, bf16[3,3,32,192]{3,2,1,0:T(8,128)(2,1)S(1)}, u32[]{:S(2)}, u32[]{:S(2)}) collective-permute-start(bf16[3,3,32,192]{3,2,1,0:T(8,128)(2,1)S(1)} %pad_maximum_fusion.12), channel_id=1, source_target_pairs={{0,1},{1,2},{2,3},{3,4},{4,5},{5,6},{6,7},{7,0},{8,9},{9,10},{10,1... | collective-permute-start | bytes 331784 | tf_op jit(solution)/shard_map/ppermute | solution.py:103
  453.8 5.0 collective-permute-start.59
  459.2 4.1 collective-permute-start.62
  460.2 6.4 %collective-permute-start.61 = (bf16[3,3,32,192]{3,2,1,0:T(8,128)(2,1)S(1)}, bf16[3,3,32,192]{3,2,1,0:T(8,128)(2,1)S(1)}, u32[]{:S(2)}, u32[]{:S(2)}) collective-permute-start(bf16[3,3,32,192]{3,2,1,0:T(8,128)(2,1)S(1)} %pad_maximum_fusion.13), channel_id=1, source_target_pairs={{0,1},{1,2},{2,3},{3,4},{4,5},{5,6},{6,7},{7,0},{8,9},{9,10},{10,1... | collective-permute-start | bytes 331784 | tf_op jit(solution)/shard_map/ppermute | solution.py:103
  467.5 5.0 collective-permute-start.63
  473.1 4.1 collective-permute-start.66
  473.9 6.4 %collective-permute-start.65 = (bf16[3,3,32,192]{3,2,1,0:T(8,128)(2,1)S(1)}, bf16[3,3,32,192]{3,2,1,0:T(8,128)(2,1)S(1)}, u32[]{:S(2)}, u32[]{:S(2)}) collective-permute-start(bf16[3,3,32,192]{3,2,1,0:T(8,128)(2,1)S(1)} %pad_maximum_fusion.14), channel_id=1, source_target_pairs={{0,1},{1,2},{2,3},{3,4},{4,5},{5,6},{6,7},{7,0},{8,9},{9,10},{10,1... | collective-permute-start | bytes 331784 | tf_op jit(solution)/shard_map/ppermute | solution.py:103
  481.2 5.0 collective-permute-start.67
  486.8 4.1 collective-permute-start.70
  487.8 6.4 %collective-permute-start.69 = (bf16[3,3,32,192]{3,2,1,0:T(8,128)(2,1)S(1)}, bf16[3,3,32,192]{3,2,1,0:T(8,128)(2,1)S(1)}, u32[]{:S(2)}, u32[]{:S(2)}) collective-permute-start(bf16[3,3,32,192]{3,2,1,0:T(8,128)(2,1)S(1)} %pad_maximum_fusion.15), channel_id=1, source_target_pairs={{0,1},{1,2},{2,3},{3,4},{4,5},{5,6},{6,7},{7,0},{8,9},{9,10},{10,1... | collective-permute-start | bytes 331784 | tf_op jit(solution)/shard_map/ppermute | solution.py:103
  497.5 4.6 collective-permute-start.73
  506.1 4.7 collective-permute-start.77
  (18 other events, 315.3 us)

commit v6 on v3

--- a/solution.py
+++ b/solution.py
@@ -88,11 +88,7 @@
     rows_total = lax.axis_size("gx") * lax.axis_size("gy") * column_depth * block_rows
     columns = [(1, 1), (0, 1), (2, 1)] + [(dx, 0) for dx in range(3)] + [(dx, 2) for dx in range(3)]
     order = [(3 * dx + dy) * column_depth + z for dx, dy in columns for z in range(column_depth)]
-    dense = dense_coupling(coupling[0, 0], cpl_dst[0, 0], cpl_src[0, 0], column_depth, order)
-    dense_own = dense[:, :column_depth]
-    dense_side = dense[:, column_depth:3 * column_depth]
-    dense_low = dense[:, 3 * column_depth:6 * column_depth]
-    dense_high = dense[:, 6 * column_depth:]
+    dense = {}
 
     def shift(value, axis, step):
         count = lax.axis_size(axis)
@@ -105,13 +101,20 @@
         rounded = current.astype(jnp.bfloat16)
         left = shift(rounded, "gx", 1)
         right = shift(rounded, "gx", -1)
-        image = part(rounded, dense_own)
         strip = jnp.stack([left, rounded, right])
         low = shift(strip, "gy", 1)
         high = shift(strip, "gy", -1)
-        image = image + part(jnp.concatenate([left, right]), dense_side)
-        image = image + part(low.reshape(3 * column_depth, vector_count, block_rows), dense_low)
-        return image + part(high.reshape(3 * column_depth, vector_count, block_rows), dense_high)
+        if not dense:
+            matrices = lax.optimization_barrier((coupling[0, 0], left, right))[0]
+            full = dense_coupling(matrices, cpl_dst[0, 0], cpl_src[0, 0], column_depth, order)
+            dense["own"] = full[:, :column_depth]
+            dense["side"] = full[:, column_depth:3 * column_depth]
+            dense["low"] = full[:, 3 * column_depth:6 * column_depth]
+            dense["high"] = full[:, 6 * column_depth:]
+        image = part(rounded, dense["own"])
+        image = image + part(jnp.concatenate([left, right]), dense["side"])
+        image = image + part(low.reshape(3 * column_depth, vector_count, block_rows), dense["low"])
+        return image + part(high.reshape(3 * column_depth, vector_count, block_rows), dense["high"])
 
     sigma_one = HALF / (LOWEST - CENTER)
     current_basis = basis[0, 0]

time: 287 us -> 286 us (level)
  no operation moved by 1% of the time
where the time goes in v6:
time: 286 us
  waiting for transfers between devices  122 us (43%)
  starting transfers between devices  78.3 us (27%)
  matrix products  52.5 us (18%)
  other arithmetic  21.5 us (8%)
  local copies, waits for them, and re-layouts  10.6 us (4%)
    ppermute x64, waiting for transfers between devices, shift(): lax.ppermute(value, axis, [(i, (i + step) % count) for i in range(count)])  103 us
    ppermute x64, starting transfers between devices, shift(): lax.ppermute(value, axis, [(i, (i + step) % count) for i in range(count)])  65.6 us
    dot_general x64, matrix products, part(): jnp.einsum('kvj,tkij->tvi', cells, blocks, preferred_element_type=jnp.flo...  50.5 us
    ppermute x14, waiting for transfers between devices, swap(): return lax.ppermute(v, axis, [(i, i ^ stride) for i in range(count)])  18.9 us
    ppermute x14, starting transfers between devices, swap(): return lax.ppermute(v, axis, [(i, i ^ stride) for i in range(count)])  12.7 us
    gather x1, local copies, waits for them, and re-layouts, dense_coupling(): jnp.take(matrices, index.reshape(-1), axis=0)  10.3 us
    another operation x6, other arithmetic, orthonormal(): factor = jnp.linalg.cholesky(gram_matrix)  7.19 us
    another operation x4, other arithmetic, orthonormal(): inverse = jax.scipy.linalg.solve_triangular(factor, identity, lower=True)  6.17 us
  transfers between devices with their start and end apart: 78, of which 71 were waited for; matrix products, arithmetic and copies ran while one was open for 18% of the time, Pallas kernels for 0%

profile of v6, /device:TPU:0, one launch (start us, length us, event | category | flops | bytes accessed | tf_op | source)
XLA Modules:
  0.0 285.7 jit_solution(11709952081758404679)
XLA Ops:
  0.9 3.0 %collective-permute-start = (bf16[3,32,192]{2,1,0:T(8,128)(2,1)S(1)}, bf16[3,32,192]{2,1,0:T(8,128)(2,1)S(1)}, u32[]{:S(2)}, u32[]{:S(2)}) collective-permute-start(bf16[3,32,192]{2,1,0:T(8,128)(2,1)S(1)} %get-tuple-element.18), channel_id=1, source_target_pairs={{0,8},{8,16},{16,24},{24,0},{1,9},{9,17},{17,25},{25,1},{2,10},{10... | collective-permute-start | bytes 110600 | tf_op jit(solution)/shard_map/ppermute | solution.py:95
  8.7 1.9 collective-permute-start.3
  10.6 10.3 %gather_fusion = bf16[81,192,192]{2,1,0:T(8,128)(2,1)} fusion(bf16[81,192,192]{2,1,0:T(8,128)(2,1)} %bitcast.915, s32[1024]{0:T(1024)S(1)} %pad_clamp_fusion), kind=kCustom, calls=%fused_computation | custom fusion | bytes 11944260 | tf_op jit(solution)/shard_map/jit(_take)/gather | solution.py:42
  20.9 4.3 %select_select_fusion = bf16[3,27,192,192]{3,2,1,0:T(8,128)(2,1)S(1)} fusion(bf16[3,27,192,192]{3,2,1,0:T(8,128)(2,1)} %bitcast.914, pred[3,27]{1,0:T(4,128)(4,1)S(1)} %compare_and_fusion, pred[3,27]{1,0:T(4,128)(4,1)S(1)} %and_reduce_fusion), kind=kLoop, calls=%fused_computation.1 | loop fusion | flops 5971968 | bytes 11944098 | tf_op jit(solution)/shard_map/jit(_where)/select_n | solution.py:46
  26.3 2.0 convolution_bitcast_fusion.30
  29.2 2.7 collective-permute-start.4
  32.6 2.2 collective-permute-done.4
  36.0 2.2 collective-permute-start.7
  38.8 2.1 collective-permute-done.7
  41.8 2.8 collective-permute-done.6
  52.5 2.9 %collective-permute-done.11 = bf16[3,3,32,192]{3,2,1,0:T(8,128)(2,1)S(1)} collective-permute-done((bf16[3,3,32,192]{3,2,1,0:T(8,128)(2,1)S(1)}, bf16[3,3,32,192]{3,2,1,0:T(8,128)(2,1)S(1)}, u32[]{:S(2)}, u32[]{:S(2)}) %collective-permute-start.11) | collective-permute-done | bytes 110624 | tf_op jit(solution)/shard_map/ppermute | solution.py:95
  62.1 1.7 collective-permute-done.12
  66.1 2.3 collective-permute-done.15
  69.3 2.6 collective-permute-done.14
  76.2 1.7 collective-permute-done.16
  79.5 2.9 %collective-permute-done.19 = bf16[3,3,32,192]{3,2,1,0:T(8,128)(2,1)S(1)} collective-permute-done((bf16[3,3,32,192]{3,2,1,0:T(8,128)(2,1)S(1)}, bf16[3,3,32,192]{3,2,1,0:T(8,128)(2,1)S(1)}, u32[]{:S(2)}, u32[]{:S(2)}) %collective-permute-start.19) | collective-permute-done | bytes 110624 | tf_op jit(solution)/shard_map/ppermute | solution.py:95
  83.4 1.8 collective-permute-done.18
  86.1 2.1 collective-permute-start.20
  93.8 2.6 collective-permute-done.23
  97.3 2.3 collective-permute-done.22
  107.3 2.8 collective-permute-done.27
  111.0 2.1 collective-permute-done.26
  120.8 2.8 collective-permute-done.31
  124.5 2.1 collective-permute-done.30
  127.8 1.7 collective-permute-start.32
  133.2 1.9 collective-permute-done.34
  135.3 1.8 collective-permute-start.37
  137.1 1.9 collective-permute-done.36
  139.9 3.8 %collective-permute-done.38 = f32[32,32]{0,1:T(8,128)S(1)} collective-permute-done((f32[32,32]{0,1:T(8,128)S(1)}, f32[32,32]{0,1:T(8,128)S(1)}, u32[]{:S(2)}, u32[]{:S(2)}) %collective-permute-start.38) | collective-permute-done | bytes 4128 | tf_op jit(solution)/shard_map/ppermute | solution.py:58
  143.9 2.9 %cholesky.44 = f32[32,32]{1,0:T(8,128)S(1)} custom-call(f32[32,32]{1,0:T(8,128)S(1)} %fusion.162), custom_call_target="Cholesky" | custom-call | tf_op jit(solution)/shard_map/jit(cholesky)/cholesky | solution.py:77
  148.1 2.4 custom-call.6
  151.8 2.2 collective-permute-start.40
  156.7 2.1 fusion.98
  159.6 2.6 convolution_bitcast_fusion.14
  163.6 2.5 collective-permute-start.43
  167.0 2.1 collective-permute-done.43
  170.2 1.9 collective-permute-start.46
  172.7 2.1 collective-permute-done.46
  175.7 2.8 collective-permute-done.45
  182.8 1.7 collective-permute-done.47
  186.4 2.6 collective-permute-done.50
  189.9 2.3 collective-permute-done.49
  196.5 1.7 collective-permute-done.51
  200.1 2.6 collective-permute-done.54
  203.6 2.3 collective-permute-done.53
  210.2 1.7 collective-permute-done.55
  213.9 2.4 collective-permute-done.58
  217.3 2.4 collective-permute-done.57
  221.8 1.8 collective-permute-start.60
  224.0 1.7 collective-permute-done.59
  227.5 2.5 collective-permute-done.62
  230.9 2.4 collective-permute-done.61
  237.6 1.7 collective-permute-done.63
  241.3 2.8 collective-permute-done.66
  245.0 2.0 collective-permute-done.65
  251.4 1.7 collective-permute-done.67
  255.2 2.4 collective-permute-done.70
  258.4 2.5 collective-permute-done.69
  267.2 2.0 collective-permute-done.73
  269.3 1.8 collective-permute-start.76
  271.1 1.9 collective-permute-done.75
  273.9 3.9 %collective-permute-done.77 = f32[32,32]{0,1:T(8,128)S(1)} collective-permute-done((f32[32,32]{0,1:T(8,128)S(1)}, f32[32,32]{0,1:T(8,128)S(1)}, u32[]{:S(2)}, u32[]{:S(2)}) %collective-permute-start.77) | collective-permute-done | bytes 4128 | tf_op jit(solution)/shard_map/ppermute | solution.py:58
  277.9 2.9 %cholesky.55 = f32[32,32]{1,0:T(8,128)S(1)} custom-call(f32[32,32]{1,0:T(8,128)S(1)} %fusion.160), custom_call_target="Cholesky" | custom-call | tf_op jit(solution)/shard_map/jit(cholesky)/cholesky | solution.py:77
  282.1 2.4 custom-call.7
  (219 shorter events, 128.5 us)
Async XLA Ops:
  0.9 6.0 %collective-permute-start = (bf16[3,32,192]{2,1,0:T(8,128)(2,1)S(1)}, bf16[3,32,192]{2,1,0:T(8,128)(2,1)S(1)}, u32[]{:S(2)}, u32[]{:S(2)}) collective-permute-start(bf16[3,32,192]{2,1,0:T(8,128)(2,1)S(1)} %get-tuple-element.18), channel_id=1, source_target_pairs={{0,8},{8,16},{16,24},{24,0},{1,9},{9,17},{17,25},{25,1},{2,10},{10... | collective-permute-start | bytes 110600 | tf_op jit(solution)/shard_map/ppermute | solution.py:95
  3.9 4.1 %collective-permute-start.1 = (bf16[3,32,192]{2,1,0:T(8,128)(2,1)S(1)}, bf16[3,32,192]{2,1,0:T(8,128)(2,1)S(1)}, u32[]{:S(2)}, u32[]{:S(2)}) collective-permute-start(bf16[3,32,192]{2,1,0:T(8,128)(2,1)S(1)} %get-tuple-element.18), channel_id=1, source_target_pairs={{0,24},{8,0},{16,8},{24,16},{1,25},{9,1},{17,9},{25,17},{2,26},{10... | collective-permute-start | bytes 110600 | tf_op jit(solution)/shard_map/ppermute | solution.py:95
  8.7 17.6 %collective-permute-start.3 = (bf16[3,3,32,192]{3,2,1,0:T(8,128)(2,1)}, bf16[3,3,32,192]{3,2,1,0:T(8,128)(2,1)}, u32[]{:S(2)}, u32[]{:S(2)}) collective-permute-start(bf16[3,3,32,192]{3,2,1,0:T(8,128)(2,1)} %pad_maximum_fusion), channel_id=1, source_target_pairs={{0,7},{1,0},{2,1},{3,2},{4,3},{5,4},{6,5},{7,6},{8,15},{9,8},{10,9... | collective-permute-start | bytes 331784 | tf_op jit(solution)/shard_map/ppermute | solution.py:95
  10.6 17.7 %collective-permute-start.2 = (bf16[3,3,32,192]{3,2,1,0:T(8,128)(2,1)}, bf16[3,3,32,192]{3,2,1,0:T(8,128)(2,1)S(1)}, u32[]{:S(2)}, u32[]{:S(2)}) collective-permute-start(bf16[3,3,32,192]{3,2,1,0:T(8,128)(2,1)} %pad_maximum_fusion), channel_id=1, source_target_pairs={{0,1},{1,2},{2,3},{3,4},{4,5},{5,6},{6,7},{7,0},{8,9},{9,10},{10,1... | collective-permute-start | bytes 331784 | tf_op jit(solution)/shard_map/ppermute | solution.py:95
  29.2 5.5 %collective-permute-start.4 = (bf16[3,32,192]{2,1,0:T(8,128)(2,1)S(1)}, bf16[3,32,192]{2,1,0:T(8,128)(2,1)S(1)}, u32[]{:S(2)}, u32[]{:S(2)}) collective-permute-start(bf16[3,32,192]{2,1,0:T(8,128)(2,1)S(1)} %get-tuple-element.19), channel_id=1, source_target_pairs={{0,8},{8,16},{16,24},{24,0},{1,9},{9,17},{17,25},{25,1},{2,10},{10... | collective-permute-start | bytes 110600 | tf_op jit(solution)/shard_map/ppermute | solution.py:95
  31.9 4.1 %collective-permute-start.5 = (bf16[3,32,192]{2,1,0:T(8,128)(2,1)S(1)}, bf16[3,32,192]{2,1,0:T(8,128)(2,1)S(1)}, u32[]{:S(2)}, u32[]{:S(2)}) collective-permute-start(bf16[3,32,192]{2,1,0:T(8,128)(2,1)S(1)} %get-tuple-element.19), channel_id=1, source_target_pairs={{0,24},{8,0},{16,8},{24,16},{1,25},{9,1},{17,9},{25,17},{2,26},{10... | collective-permute-start | bytes 110600 | tf_op jit(solution)/shard_map/ppermute | solution.py:95
  36.0 4.9 %collective-permute-start.7 = (bf16[3,3,32,192]{3,2,1,0:T(8,128)(2,1)S(1)}, bf16[3,3,32,192]{3,2,1,0:T(8,128)(2,1)S(1)}, u32[]{:S(2)}, u32[]{:S(2)}) collective-permute-start(bf16[3,3,32,192]{3,2,1,0:T(8,128)(2,1)S(1)} %pad_maximum_fusion.1), channel_id=1, source_target_pairs={{0,7},{1,0},{2,1},{3,2},{4,3},{5,4},{6,5},{7,6},{8,15},{9,8},{10,9... | collective-permute-start | bytes 331784 | tf_op jit(solution)/shard_map/ppermute | solution.py:95
  38.2 6.4 %collective-permute-start.6 = (bf16[3,3,32,192]{3,2,1,0:T(8,128)(2,1)S(1)}, bf16[3,3,32,192]{3,2,1,0:T(8,128)(2,1)S(1)}, u32[]{:S(2)}, u32[]{:S(2)}) collective-permute-start(bf16[3,3,32,192]{3,2,1,0:T(8,128)(2,1)S(1)} %pad_maximum_fusion.1), channel_id=1, source_target_pairs={{0,1},{1,2},{2,3},{3,4},{4,5},{5,6},{6,7},{7,0},{8,9},{9,10},{10,1... | collective-permute-start | bytes 331784 | tf_op jit(solution)/shard_map/ppermute | solution.py:95
  45.5 5.0 %collective-permute-start.8 = (bf16[3,32,192]{2,1,0:T(8,128)(2,1)S(1)}, bf16[3,32,192]{2,1,0:T(8,128)(2,1)S(1)}, u32[]{:S(2)}, u32[]{:S(2)}) collective-permute-start(bf16[3,32,192]{2,1,0:T(8,128)(2,1)S(1)} %get-tuple-element.21), channel_id=1, source_target_pairs={{0,8},{8,16},{16,24},{24,0},{1,9},{9,17},{17,25},{25,1},{2,10},{10... | collective-permute-start | bytes 110600 | tf_op jit(solution)/shard_map/ppermute | solution.py:95
  47.2 4.1 %collective-permute-start.9 = (bf16[3,32,192]{2,1,0:T(8,128)(2,1)S(1)}, bf16[3,32,192]{2,1,0:T(8,128)(2,1)S(1)}, u32[]{:S(2)}, u32[]{:S(2)}) collective-permute-start(bf16[3,32,192]{2,1,0:T(8,128)(2,1)S(1)} %get-tuple-element.21), channel_id=1, source_target_pairs={{0,24},{8,0},{16,8},{24,16},{1,25},{9,1},{17,9},{25,17},{2,26},{10... | collective-permute-start | bytes 110600 | tf_op jit(solution)/shard_map/ppermute | solution.py:95
  51.3 4.1 %collective-permute-start.11 = (bf16[3,3,32,192]{3,2,1,0:T(8,128)(2,1)S(1)}, bf16[3,3,32,192]{3,2,1,0:T(8,128)(2,1)S(1)}, u32[]{:S(2)}, u32[]{:S(2)}) collective-permute-start(bf16[3,3,32,192]{3,2,1,0:T(8,128)(2,1)S(1)} %pad_maximum_fusion.2), channel_id=1, source_target_pairs={{0,7},{1,0},{2,1},{3,2},{4,3},{5,4},{6,5},{7,6},{8,15},{9,8},{10,9... | collective-permute-start | bytes 331784 | tf_op jit(solution)/shard_map/ppermute | solution.py:95
  51.4 6.4 %collective-permute-start.10 = (bf16[3,3,32,192]{3,2,1,0:T(8,128)(2,1)S(1)}, bf16[3,3,32,192]{3,2,1,0:T(8,128)(2,1)S(1)}, u32[]{:S(2)}, u32[]{:S(2)}) collective-permute-start(bf16[3,3,32,192]{3,2,1,0:T(8,128)(2,1)S(1)} %pad_maximum_fusion.2), channel_id=1, source_target_pairs={{0,1},{1,2},{2,3},{3,4},{4,5},{5,6},{6,7},{7,0},{8,9},{9,10},{10,1... | collective-permute-start | bytes 331784 | tf_op jit(solution)/shard_map/ppermute | solution.py:95
  58.7 5.0 %collective-permute-start.12 = (bf16[3,32,192]{2,1,0:T(8,128)(2,1)S(1)}, bf16[3,32,192]{2,1,0:T(8,128)(2,1)S(1)}, u32[]{:S(2)}, u32[]{:S(2)}) collective-permute-start(bf16[3,32,192]{2,1,0:T(8,128)(2,1)S(1)} %get-tuple-element.23), channel_id=1, source_target_pairs={{0,8},{8,16},{16,24},{24,0},{1,9},{9,17},{17,25},{25,1},{2,10},{10... | collective-permute-start | bytes 110600 | tf_op jit(solution)/shard_map/ppermute | solution.py:95
  60.2 4.1 %collective-permute-start.13 = (bf16[3,32,192]{2,1,0:T(8,128)(2,1)S(1)}, bf16[3,32,192]{2,1,0:T(8,128)(2,1)S(1)}, u32[]{:S(2)}, u32[]{:S(2)}) collective-permute-start(bf16[3,32,192]{2,1,0:T(8,128)(2,1)S(1)} %get-tuple-element.23), channel_id=1, source_target_pairs={{0,24},{8,0},{16,8},{24,16},{1,25},{9,1},{17,9},{25,17},{2,26},{10... | collective-permute-start | bytes 110600 | tf_op jit(solution)/shard_map/ppermute | solution.py:95
  64.3 4.1 %collective-permute-start.15 = (bf16[3,3,32,192]{3,2,1,0:T(8,128)(2,1)S(1)}, bf16[3,3,32,192]{3,2,1,0:T(8,128)(2,1)S(1)}, u32[]{:S(2)}, u32[]{:S(2)}) collective-permute-start(bf16[3,3,32,192]{3,2,1,0:T(8,128)(2,1)S(1)} %pad_maximum_fusion.3), channel_id=1, source_target_pairs={{0,7},{1,0},{2,1},{3,2},{4,3},{5,4},{6,5},{7,6},{8,15},{9,8},{10,9... | collective-permute-start | bytes 331784 | tf_op jit(solution)/shard_map/ppermute | solution.py:95
  65.5 6.4 %collective-permute-start.14 = (bf16[3,3,32,192]{3,2,1,0:T(8,128)(2,1)S(1)}, bf16[3,3,32,192]{3,2,1,0:T(8,128)(2,1)S(1)}, u32[]{:S(2)}, u32[]{:S(2)}) collective-permute-start(bf16[3,3,32,192]{3,2,1,0:T(8,128)(2,1)S(1)} %pad_maximum_fusion.3), channel_id=1, source_target_pairs={{0,1},{1,2},{2,3},{3,4},{4,5},{5,6},{6,7},{7,0},{8,9},{9,10},{10,1... | collective-permute-start | bytes 331784 | tf_op jit(solution)/shard_map/ppermute | solution.py:95
  72.8 5.0 %collective-permute-start.16 = (bf16[3,32,192]{2,1,0:T(8,128)(2,1)S(1)}, bf16[3,32,192]{2,1,0:T(8,128)(2,1)S(1)}, u32[]{:S(2)}, u32[]{:S(2)}) collective-permute-start(bf16[3,32,192]{2,1,0:T(8,128)(2,1)S(1)} %get-tuple-element.25), channel_id=1, source_target_pairs={{0,8},{8,16},{16,24},{24,0},{1,9},{9,17},{17,25},{25,1},{2,10},{10... | collective-permute-start | bytes 110600 | tf_op jit(solution)/shard_map/ppermute | solution.py:95
  74.2 4.1 %collective-permute-start.17 = (bf16[3,32,192]{2,1,0:T(8,128)(2,1)S(1)}, bf16[3,32,192]{2,1,0:T(8,128)(2,1)S(1)}, u32[]{:S(2)}, u32[]{:S(2)}) collective-permute-start(bf16[3,32,192]{2,1,0:T(8,128)(2,1)S(1)} %get-tuple-element.25), channel_id=1, source_target_pairs={{0,24},{8,0},{16,8},{24,16},{1,25},{9,1},{17,9},{25,17},{2,26},{10... | collective-permute-start | bytes 110600 | tf_op jit(solution)/shard_map/ppermute | solution.py:95
  78.4 4.1 %collective-permute-start.19 = (bf16[3,3,32,192]{3,2,1,0:T(8,128)(2,1)S(1)}, bf16[3,3,32,192]{3,2,1,0:T(8,128)(2,1)S(1)}, u32[]{:S(2)}, u32[]{:S(2)}) collective-permute-start(bf16[3,3,32,192]{3,2,1,0:T(8,128)(2,1)S(1)} %pad_maximum_fusion.4), channel_id=1, source_target_pairs={{0,7},{1,0},{2,1},{3,2},{4,3},{5,4},{6,5},{7,6},{8,15},{9,8},{10,9... | collective-permute-start | bytes 331784 | tf_op jit(solution)/shard_map/ppermute | solution.py:95
  78.8 6.4 %collective-permute-start.18 = (bf16[3,3,32,192]{3,2,1,0:T(8,128)(2,1)S(1)}, bf16[3,3,32,192]{3,2,1,0:T(8,128)(2,1)S(1)}, u32[]{:S(2)}, u32[]{:S(2)}) collective-permute-start(bf16[3,3,32,192]{3,2,1,0:T(8,128)(2,1)S(1)} %pad_maximum_fusion.4), channel_id=1, source_target_pairs={{0,1},{1,2},{2,3},{3,4},{4,5},{5,6},{6,7},{7,0},{8,9},{9,10},{10,1... | collective-permute-start | bytes 331784 | tf_op jit(solution)/shard_map/ppermute | solution.py:95
  86.1 5.0 %collective-permute-start.20 = (bf16[3,32,192]{2,1,0:T(8,128)(2,1)S(1)}, bf16[3,32,192]{2,1,0:T(8,128)(2,1)S(1)}, u32[]{:S(2)}, u32[]{:S(2)}) collective-permute-start(bf16[3,32,192]{2,1,0:T(8,128)(2,1)S(1)} %get-tuple-element.27), channel_id=1, source_target_pairs={{0,8},{8,16},{16,24},{24,0},{1,9},{9,17},{17,25},{25,1},{2,10},{10... | collective-permute-start | bytes 110600 | tf_op jit(solution)/shard_map/ppermute | solution.py:95
  88.2 4.1 %collective-permute-start.21 = (bf16[3,32,192]{2,1,0:T(8,128)(2,1)S(1)}, bf16[3,32,192]{2,1,0:T(8,128)(2,1)S(1)}, u32[]{:S(2)}, u32[]{:S(2)}) collective-permute-start(bf16[3,32,192]{2,1,0:T(8,128)(2,1)S(1)} %get-tuple-element.27), channel_id=1, source_target_pairs={{0,24},{8,0},{16,8},{24,16},{1,25},{9,1},{17,9},{25,17},{2,26},{10... | collective-permute-start | bytes 110600 | tf_op jit(solution)/shard_map/ppermute | solution.py:95
  92.3 4.1 %collective-permute-start.23 = (bf16[3,3,32,192]{3,2,1,0:T(8,128)(2,1)S(1)}, bf16[3,3,32,192]{3,2,1,0:T(8,128)(2,1)S(1)}, u32[]{:S(2)}, u32[]{:S(2)}) collective-permute-start(bf16[3,3,32,192]{3,2,1,0:T(8,128)(2,1)S(1)} %pad_maximum_fusion.5), channel_id=1, source_target_pairs={{0,7},{1,0},{2,1},{3,2},{4,3},{5,4},{6,5},{7,6},{8,15},{9,8},{10,9... | collective-permute-start | bytes 331784 | tf_op jit(solution)/shard_map/ppermute | solution.py:95
  93.2 6.4 %collective-permute-start.22 = (bf16[3,3,32,192]{3,2,1,0:T(8,128)(2,1)S(1)}, bf16[3,3,32,192]{3,2,1,0:T(8,128)(2,1)S(1)}, u32[]{:S(2)}, u32[]{:S(2)}) collective-permute-start(bf16[3,3,32,192]{3,2,1,0:T(8,128)(2,1)S(1)} %pad_maximum_fusion.5), channel_id=1, source_target_pairs={{0,1},{1,2},{2,3},{3,4},{4,5},{5,6},{6,7},{7,0},{8,9},{9,10},{10,1... | collective-permute-start | bytes 331784 | tf_op jit(solution)/shard_map/ppermute | solution.py:95
  100.5 5.0 %collective-permute-start.24 = (bf16[3,32,192]{2,1,0:T(8,128)(2,1)S(1)}, bf16[3,32,192]{2,1,0:T(8,128)(2,1)S(1)}, u32[]{:S(2)}, u32[]{:S(2)}) collective-permute-start(bf16[3,32,192]{2,1,0:T(8,128)(2,1)S(1)} %get-tuple-element.29), channel_id=1, source_target_pairs={{0,8},{8,16},{16,24},{24,0},{1,9},{9,17},{17,25},{25,1},{2,10},{10... | collective-permute-start | bytes 110600 | tf_op jit(solution)/shard_map/ppermute | solution.py:95
  101.9 4.1 %collective-permute-start.25 = (bf16[3,32,192]{2,1,0:T(8,128)(2,1)S(1)}, bf16[3,32,192]{2,1,0:T(8,128)(2,1)S(1)}, u32[]{:S(2)}, u32[]{:S(2)}) collective-permute-start(bf16[3,32,192]{2,1,0:T(8,128)(2,1)S(1)} %get-tuple-element.29), channel_id=1, source_target_pairs={{0,24},{8,0},{16,8},{24,16},{1,25},{9,1},{17,9},{25,17},{2,26},{10... | collective-permute-start | bytes 110600 | tf_op jit(solution)/shard_map/ppermute | solution.py:95
  106.0 4.1 %collective-permute-start.27 = (bf16[3,3,32,192]{3,2,1,0:T(8,128)(2,1)S(1)}, bf16[3,3,32,192]{3,2,1,0:T(8,128)(2,1)S(1)}, u32[]{:S(2)}, u32[]{:S(2)}) collective-permute-start(bf16[3,3,32,192]{3,2,1,0:T(8,128)(2,1)S(1)} %pad_maximum_fusion.6), channel_id=1, source_target_pairs={{0,7},{1,0},{2,1},{3,2},{4,3},{5,4},{6,5},{7,6},{8,15},{9,8},{10,9... | collective-permute-start | bytes 331784 | tf_op jit(solution)/shard_map/ppermute | solution.py:95
  106.7 6.4 %collective-permute-start.26 = (bf16[3,3,32,192]{3,2,1,0:T(8,128)(2,1)S(1)}, bf16[3,3,32,192]{3,2,1,0:T(8,128)(2,1)S(1)}, u32[]{:S(2)}, u32[]{:S(2)}) collective-permute-start(bf16[3,3,32,192]{3,2,1,0:T(8,128)(2,1)S(1)} %pad_maximum_fusion.6), channel_id=1, source_target_pairs={{0,1},{1,2},{2,3},{3,4},{4,5},{5,6},{6,7},{7,0},{8,9},{9,10},{10,1... | collective-permute-start | bytes 331784 | tf_op jit(solution)/shard_map/ppermute | solution.py:95
  114.0 5.0 %collective-permute-start.28 = (bf16[3,32,192]{2,1,0:T(8,128)(2,1)S(1)}, bf16[3,32,192]{2,1,0:T(8,128)(2,1)S(1)}, u32[]{:S(2)}, u32[]{:S(2)}) collective-permute-start(bf16[3,32,192]{2,1,0:T(8,128)(2,1)S(1)} %get-tuple-element.31), channel_id=1, source_target_pairs={{0,8},{8,16},{16,24},{24,0},{1,9},{9,17},{17,25},{25,1},{2,10},{10... | collective-permute-start | bytes 110600 | tf_op jit(solution)/shard_map/ppermute | solution.py:95
  115.4 4.1 %collective-permute-start.29 = (bf16[3,32,192]{2,1,0:T(8,128)(2,1)S(1)}, bf16[3,32,192]{2,1,0:T(8,128)(2,1)S(1)}, u32[]{:S(2)}, u32[]{:S(2)}) collective-permute-start(bf16[3,32,192]{2,1,0:T(8,128)(2,1)S(1)} %get-tuple-element.31), channel_id=1, source_target_pairs={{0,24},{8,0},{16,8},{24,16},{1,25},{9,1},{17,9},{25,17},{2,26},{10... | collective-permute-start | bytes 110600 | tf_op jit(solution)/shard_map/ppermute | solution.py:95
  119.5 4.1 %collective-permute-start.31 = (bf16[3,3,32,192]{3,2,1,0:T(8,128)(2,1)S(1)}, bf16[3,3,32,192]{3,2,1,0:T(8,128)(2,1)S(1)}, u32[]{:S(2)}, u32[]{:S(2)}) collective-permute-start(bf16[3,3,32,192]{3,2,1,0:T(8,128)(2,1)S(1)} %pad_maximum_fusion.7), channel_id=1, source_target_pairs={{0,7},{1,0},{2,1},{3,2},{4,3},{5,4},{6,5},{7,6},{8,15},{9,8},{10,9... | collective-permute-start | bytes 331784 | tf_op jit(solution)/shard_map/ppermute | solution.py:95
  120.2 6.4 %collective-permute-start.30 = (bf16[3,3,32,192]{3,2,1,0:T(8,128)(2,1)S(1)}, bf16[3,3,32,192]{3,2,1,0:T(8,128)(2,1)S(1)}, u32[]{:S(2)}, u32[]{:S(2)}) collective-permute-start(bf16[3,3,32,192]{3,2,1,0:T(8,128)(2,1)S(1)} %pad_maximum_fusion.7), channel_id=1, source_target_pairs={{0,1},{1,2},{2,3},{3,4},{4,5},{5,6},{6,7},{7,0},{8,9},{9,10},{10,1... | collective-permute-start | bytes 331784 | tf_op jit(solution)/shard_map/ppermute | solution.py:95
  130.5 4.6 %collective-permute-start.34 = (f32[32,32]{0,1:T(8,128)S(1)}, f32[32,32]{0,1:T(8,128)S(1)}, u32[]{:S(2)}, u32[]{:S(2)}) collective-permute-start(f32[32,32]{0,1:T(8,128)S(1)} %convolution_bitcast_fusion.67), channel_id=1, source_target_pairs={{0,24},{8,16},{16,8},{24,0},{1,25},{9,17},{17,9},{25,1},{2,26},{10... | collective-permute-start | bytes 12296 | tf_op jit(solution)/shard_map/ppermute | solution.py:58
  139.1 4.7 %collective-permute-start.38 = (f32[32,32]{0,1:T(8,128)S(1)}, f32[32,32]{0,1:T(8,128)S(1)}, u32[]{:S(2)}, u32[]{:S(2)}) collective-permute-start(f32[32,32]{0,1:T(8,128)S(1)} %add_add_fusion.2), channel_id=1, source_target_pairs={{0,4},{1,5},{2,6},{3,7},{4,0},{5,1},{6,2},{7,3},{8,12},{9,13},{10,... | collective-permute-start | bytes 12296 | tf_op jit(solution)/shard_map/ppermute | solution.py:58
  151.1 5.0 %collective-permute-start.39 = (bf16[3,32,192]{2,1,0:T(8,128)(2,1)S(1)}, bf16[3,32,192]{2,1,0:T(8,128)(2,1)S(1)}, u32[]{:S(2)}, u32[]{:S(2)}) collective-permute-start(bf16[3,32,192]{2,1,0:T(8,128)(2,1)S(1)} %get-tuple-element.16), channel_id=1, source_target_pairs={{0,8},{8,16},{16,24},{24,0},{1,9},{9,17},{17,25},{25,1},{2,10},{10... | collective-permute-start | bytes 110600 | tf_op jit(solution)/shard_map/ppermute | solution.py:95
  151.8 4.3 %collective-permute-start.40 = (bf16[3,32,192]{2,1,0:T(8,128)(2,1)S(1)}, bf16[3,32,192]{2,1,0:T(8,128)(2,1)S(1)}, u32[]{:S(2)}, u32[]{:S(2)}) collective-permute-start(bf16[3,32,192]{2,1,0:T(8,128)(2,1)S(1)} %get-tuple-element.16), channel_id=1, source_target_pairs={{0,24},{8,0},{16,8},{24,16},{1,25},{9,1},{17,9},{25,17},{2,26},{10... | collective-permute-start | bytes 110600 | tf_op jit(solution)/shard_map/ppermute | solution.py:95
  156.2 6.4 %collective-permute-start.41 = (bf16[3,3,32,192]{3,2,1,0:T(8,128)(2,1)S(1)}, bf16[3,3,32,192]{3,2,1,0:T(8,128)(2,1)S(1)}, u32[]{:S(2)}, u32[]{:S(2)}) collective-permute-start(bf16[3,3,32,192]{3,2,1,0:T(8,128)(2,1)S(1)} %pad_maximum_fusion.8), channel_id=1, source_target_pairs={{0,1},{1,2},{2,3},{3,4},{4,5},{5,6},{6,7},{7,0},{8,9},{9,10},{10,1... | collective-permute-start | bytes 331784 | tf_op jit(solution)/shard_map/ppermute | solution.py:95
  163.6 5.5 %collective-permute-start.43 = (bf16[3,32,192]{2,1,0:T(8,128)(2,1)S(1)}, bf16[3,32,192]{2,1,0:T(8,128)(2,1)S(1)}, u32[]{:S(2)}, u32[]{:S(2)}) collective-permute-start(bf16[3,32,192]{2,1,0:T(8,128)(2,1)S(1)} %get-tuple-element.14), channel_id=1, source_target_pairs={{0,8},{8,16},{16,24},{24,0},{1,9},{9,17},{17,25},{25,1},{2,10},{10... | collective-permute-start | bytes 110600 | tf_op jit(solution)/shard_map/ppermute | solution.py:95
  166.1 4.1 %collective-permute-start.44 = (bf16[3,32,192]{2,1,0:T(8,128)(2,1)S(1)}, bf16[3,32,192]{2,1,0:T(8,128)(2,1)S(1)}, u32[]{:S(2)}, u32[]{:S(2)}) collective-permute-start(bf16[3,32,192]{2,1,0:T(8,128)(2,1)S(1)} %get-tuple-element.14), channel_id=1, source_target_pairs={{0,24},{8,0},{16,8},{24,16},{1,25},{9,1},{17,9},{25,17},{2,26},{10... | collective-permute-start | bytes 110600 | tf_op jit(solution)/shard_map/ppermute | solution.py:95
  170.2 4.6 %collective-permute-start.46 = (bf16[3,3,32,192]{3,2,1,0:T(8,128)(2,1)S(1)}, bf16[3,3,32,192]{3,2,1,0:T(8,128)(2,1)S(1)}, u32[]{:S(2)}, u32[]{:S(2)}) collective-permute-start(bf16[3,3,32,192]{3,2,1,0:T(8,128)(2,1)S(1)} %pad_maximum_fusion.9), channel_id=1, source_target_pairs={{0,7},{1,0},{2,1},{3,2},{4,3},{5,4},{6,5},{7,6},{8,15},{9,8},{10,9... | collective-permute-start | bytes 331784 | tf_op jit(solution)/shard_map/ppermute | solution.py:95
  172.1 6.4 %collective-permute-start.45 = (bf16[3,3,32,192]{3,2,1,0:T(8,128)(2,1)S(1)}, bf16[3,3,32,192]{3,2,1,0:T(8,128)(2,1)S(1)}, u32[]{:S(2)}, u32[]{:S(2)}) collective-permute-start(bf16[3,3,32,192]{3,2,1,0:T(8,128)(2,1)S(1)} %pad_maximum_fusion.9), channel_id=1, source_target_pairs={{0,1},{1,2},{2,3},{3,4},{4,5},{5,6},{6,7},{7,0},{8,9},{9,10},{10,1... | collective-permute-start | bytes 331784 | tf_op jit(solution)/shard_map/ppermute | solution.py:95
  179.4 5.0 %collective-permute-start.47 = (bf16[3,32,192]{2,1,0:T(8,128)(2,1)S(1)}, bf16[3,32,192]{2,1,0:T(8,128)(2,1)S(1)}, u32[]{:S(2)}, u32[]{:S(2)}) collective-permute-start(bf16[3,32,192]{2,1,0:T(8,128)(2,1)S(1)} %get-tuple-element.12), channel_id=1, source_target_pairs={{0,8},{8,16},{16,24},{24,0},{1,9},{9,17},{17,25},{25,1},{2,10},{10... | collective-permute-start | bytes 110600 | tf_op jit(solution)/shard_map/ppermute | solution.py:95
  180.8 4.1 %collective-permute-start.48 = (bf16[3,32,192]{2,1,0:T(8,128)(2,1)S(1)}, bf16[3,32,192]{2,1,0:T(8,128)(2,1)S(1)}, u32[]{:S(2)}, u32[]{:S(2)}) collective-permute-start(bf16[3,32,192]{2,1,0:T(8,128)(2,1)S(1)} %get-tuple-element.12), channel_id=1, source_target_pairs={{0,24},{8,0},{16,8},{24,16},{1,25},{9,1},{17,9},{25,17},{2,26},{10... | collective-permute-start | bytes 110600 | tf_op jit(solution)/shard_map/ppermute | solution.py:95
  184.9 4.1 %collective-permute-start.50 = (bf16[3,3,32,192]{3,2,1,0:T(8,128)(2,1)S(1)}, bf16[3,3,32,192]{3,2,1,0:T(8,128)(2,1)S(1)}, u32[]{:S(2)}, u32[]{:S(2)}) collective-permute-start(bf16[3,3,32,192]{3,2,1,0:T(8,128)(2,1)S(1)} %pad_maximum_fusion.10), channel_id=1, source_target_pairs={{0,7},{1,0},{2,1},{3,2},{4,3},{5,4},{6,5},{7,6},{8,15},{9,8},{10,9... | collective-permute-start | bytes 331784 | tf_op jit(solution)/shard_map/ppermute | solution.py:95
  185.8 6.4 %collective-permute-start.49 = (bf16[3,3,32,192]{3,2,1,0:T(8,128)(2,1)S(1)}, bf16[3,3,32,192]{3,2,1,0:T(8,128)(2,1)S(1)}, u32[]{:S(2)}, u32[]{:S(2)}) collective-permute-start(bf16[3,3,32,192]{3,2,1,0:T(8,128)(2,1)S(1)} %pad_maximum_fusion.10), channel_id=1, source_target_pairs={{0,1},{1,2},{2,3},{3,4},{4,5},{5,6},{6,7},{7,0},{8,9},{9,10},{10,1... | collective-permute-start | bytes 331784 | tf_op jit(solution)/shard_map/ppermute | solution.py:95
  193.1 5.0 %collective-permute-start.51 = (bf16[3,32,192]{2,1,0:T(8,128)(2,1)S(1)}, bf16[3,32,192]{2,1,0:T(8,128)(2,1)S(1)}, u32[]{:S(2)}, u32[]{:S(2)}) collective-permute-start(bf16[3,32,192]{2,1,0:T(8,128)(2,1)S(1)} %get-tuple-element.10), channel_id=1, source_target_pairs={{0,8},{8,16},{16,24},{24,0},{1,9},{9,17},{17,25},{25,1},{2,10},{10... | collective-permute-start | bytes 110600 | tf_op jit(solution)/shard_map/ppermute | solution.py:95
  194.5 4.1 %collective-permute-start.52 = (bf16[3,32,192]{2,1,0:T(8,128)(2,1)S(1)}, bf16[3,32,192]{2,1,0:T(8,128)(2,1)S(1)}, u32[]{:S(2)}, u32[]{:S(2)}) collective-permute-start(bf16[3,32,192]{2,1,0:T(8,128)(2,1)S(1)} %get-tuple-element.10), channel_id=1, source_target_pairs={{0,24},{8,0},{16,8},{24,16},{1,25},{9,1},{17,9},{25,17},{2,26},{10... | collective-permute-start | bytes 110600 | tf_op jit(solution)/shard_map/ppermute | solution.py:95
  198.6 4.1 %collective-permute-start.54 = (bf16[3,3,32,192]{3,2,1,0:T(8,128)(2,1)S(1)}, bf16[3,3,32,192]{3,2,1,0:T(8,128)(2,1)S(1)}, u32[]{:S(2)}, u32[]{:S(2)}) collective-permute-start(bf16[3,3,32,192]{3,2,1,0:T(8,128)(2,1)S(1)} %pad_maximum_fusion.11), channel_id=1, source_target_pairs={{0,7},{1,0},{2,1},{3,2},{4,3},{5,4},{6,5},{7,6},{8,15},{9,8},{10,9... | collective-permute-start | bytes 331784 | tf_op jit(solution)/shard_map/ppermute | solution.py:95
  199.5 6.4 %collective-permute-start.53 = (bf16[3,3,32,192]{3,2,1,0:T(8,128)(2,1)S(1)}, bf16[3,3,32,192]{3,2,1,0:T(8,128)(2,1)S(1)}, u32[]{:S(2)}, u32[]{:S(2)}) collective-permute-start(bf16[3,3,32,192]{3,2,1,0:T(8,128)(2,1)S(1)} %pad_maximum_fusion.11), channel_id=1, source_target_pairs={{0,1},{1,2},{2,3},{3,4},{4,5},{5,6},{6,7},{7,0},{8,9},{9,10},{10,1... | collective-permute-start | bytes 331784 | tf_op jit(solution)/shard_map/ppermute | solution.py:95
  206.8 5.0 %collective-permute-start.55 = (bf16[3,32,192]{2,1,0:T(8,128)(2,1)S(1)}, bf16[3,32,192]{2,1,0:T(8,128)(2,1)S(1)}, u32[]{:S(2)}, u32[]{:S(2)}) collective-permute-start(bf16[3,32,192]{2,1,0:T(8,128)(2,1)S(1)} %get-tuple-element.33), channel_id=1, source_target_pairs={{0,8},{8,16},{16,24},{24,0},{1,9},{9,17},{17,25},{25,1},{2,10},{10... | collective-permute-start | bytes 110600 | tf_op jit(solution)/shard_map/ppermute | solution.py:95
  208.1 4.1 %collective-permute-start.56 = (bf16[3,32,192]{2,1,0:T(8,128)(2,1)S(1)}, bf16[3,32,192]{2,1,0:T(8,128)(2,1)S(1)}, u32[]{:S(2)}, u32[]{:S(2)}) collective-permute-start(bf16[3,32,192]{2,1,0:T(8,128)(2,1)S(1)} %get-tuple-element.33), channel_id=1, source_target_pairs={{0,24},{8,0},{16,8},{24,16},{1,25},{9,1},{17,9},{25,17},{2,26},{10... | collective-permute-start | bytes 110600 | tf_op jit(solution)/shard_map/ppermute | solution.py:95
  212.3 4.1 %collective-permute-start.58 = (bf16[3,3,32,192]{3,2,1,0:T(8,128)(2,1)S(1)}, bf16[3,3,32,192]{3,2,1,0:T(8,128)(2,1)S(1)}, u32[]{:S(2)}, u32[]{:S(2)}) collective-permute-start(bf16[3,3,32,192]{3,2,1,0:T(8,128)(2,1)S(1)} %pad_maximum_fusion.12), channel_id=1, source_target_pairs={{0,7},{1,0},{2,1},{3,2},{4,3},{5,4},{6,5},{7,6},{8,15},{9,8},{10,9... | collective-permute-start | bytes 331784 | tf_op jit(solution)/shard_map/ppermute | solution.py:95
  213.3 6.4 %collective-permute-start.57 = (bf16[3,3,32,192]{3,2,1,0:T(8,128)(2,1)S(1)}, bf16[3,3,32,192]{3,2,1,0:T(8,128)(2,1)S(1)}, u32[]{:S(2)}, u32[]{:S(2)}) collective-permute-start(bf16[3,3,32,192]{3,2,1,0:T(8,128)(2,1)S(1)} %pad_maximum_fusion.12), channel_id=1, source_target_pairs={{0,1},{1,2},{2,3},{3,4},{4,5},{5,6},{6,7},{7,0},{8,9},{9,10},{10,1... | collective-permute-start | bytes 331784 | tf_op jit(solution)/shard_map/ppermute | solution.py:95
  220.6 5.0 %collective-permute-start.59 = (bf16[3,32,192]{2,1,0:T(8,128)(2,1)S(1)}, bf16[3,32,192]{2,1,0:T(8,128)(2,1)S(1)}, u32[]{:S(2)}, u32[]{:S(2)}) collective-permute-start(bf16[3,32,192]{2,1,0:T(8,128)(2,1)S(1)} %get-tuple-element.35), channel_id=1, source_target_pairs={{0,8},{8,16},{16,24},{24,0},{1,9},{9,17},{17,25},{25,1},{2,10},{10... | collective-permute-start | bytes 110600 | tf_op jit(solution)/shard_map/ppermute | solution.py:95
  225.9 4.1 %collective-permute-start.62 = (bf16[3,3,32,192]{3,2,1,0:T(8,128)(2,1)S(1)}, bf16[3,3,32,192]{3,2,1,0:T(8,128)(2,1)S(1)}, u32[]{:S(2)}, u32[]{:S(2)}) collective-permute-start(bf16[3,3,32,192]{3,2,1,0:T(8,128)(2,1)S(1)} %pad_maximum_fusion.13), channel_id=1, source_target_pairs={{0,7},{1,0},{2,1},{3,2},{4,3},{5,4},{6,5},{7,6},{8,15},{9,8},{10,9... | collective-permute-start | bytes 331784 | tf_op jit(solution)/shard_map/ppermute | solution.py:95
  226.9 6.4 %collective-permute-start.61 = (bf16[3,3,32,192]{3,2,1,0:T(8,128)(2,1)S(1)}, bf16[3,3,32,192]{3,2,1,0:T(8,128)(2,1)S(1)}, u32[]{:S(2)}, u32[]{:S(2)}) collective-permute-start(bf16[3,3,32,192]{3,2,1,0:T(8,128)(2,1)S(1)} %pad_maximum_fusion.13), channel_id=1, source_target_pairs={{0,1},{1,2},{2,3},{3,4},{4,5},{5,6},{6,7},{7,0},{8,9},{9,10},{10,1... | collective-permute-start | bytes 331784 | tf_op jit(solution)/shard_map/ppermute | solution.py:95
  234.2 5.0 %collective-permute-start.63 = (bf16[3,32,192]{2,1,0:T(8,128)(2,1)S(1)}, bf16[3,32,192]{2,1,0:T(8,128)(2,1)S(1)}, u32[]{:S(2)}, u32[]{:S(2)}) collective-permute-start(bf16[3,32,192]{2,1,0:T(8,128)(2,1)S(1)} %get-tuple-element.37), channel_id=1, source_target_pairs={{0,8},{8,16},{16,24},{24,0},{1,9},{9,17},{17,25},{25,1},{2,10},{10... | collective-permute-start | bytes 110600 | tf_op jit(solution)/shard_map/ppermute | solution.py:95
  240.0 4.1 %collective-permute-start.66 = (bf16[3,3,32,192]{3,2,1,0:T(8,128)(2,1)S(1)}, bf16[3,3,32,192]{3,2,1,0:T(8,128)(2,1)S(1)}, u32[]{:S(2)}, u32[]{:S(2)}) collective-permute-start(bf16[3,3,32,192]{3,2,1,0:T(8,128)(2,1)S(1)} %pad_maximum_fusion.14), channel_id=1, source_target_pairs={{0,7},{1,0},{2,1},{3,2},{4,3},{5,4},{6,5},{7,6},{8,15},{9,8},{10,9... | collective-permute-start | bytes 331784 | tf_op jit(solution)/shard_map/ppermute | solution.py:95
  240.7 6.4 %collective-permute-start.65 = (bf16[3,3,32,192]{3,2,1,0:T(8,128)(2,1)S(1)}, bf16[3,3,32,192]{3,2,1,0:T(8,128)(2,1)S(1)}, u32[]{:S(2)}, u32[]{:S(2)}) collective-permute-start(bf16[3,3,32,192]{3,2,1,0:T(8,128)(2,1)S(1)} %pad_maximum_fusion.14), channel_id=1, source_target_pairs={{0,1},{1,2},{2,3},{3,4},{4,5},{5,6},{6,7},{7,0},{8,9},{9,10},{10,1... | collective-permute-start | bytes 331784 | tf_op jit(solution)/shard_map/ppermute | solution.py:95
  248.0 5.0 %collective-permute-start.67 = (bf16[3,32,192]{2,1,0:T(8,128)(2,1)S(1)}, bf16[3,32,192]{2,1,0:T(8,128)(2,1)S(1)}, u32[]{:S(2)}, u32[]{:S(2)}) collective-permute-start(bf16[3,32,192]{2,1,0:T(8,128)(2,1)S(1)} %get-tuple-element.39), channel_id=1, source_target_pairs={{0,8},{8,16},{16,24},{24,0},{1,9},{9,17},{17,25},{25,1},{2,10},{10... | collective-permute-start | bytes 110600 | tf_op jit(solution)/shard_map/ppermute | solution.py:95
  253.4 4.1 %collective-permute-start.70 = (bf16[3,3,32,192]{3,2,1,0:T(8,128)(2,1)S(1)}, bf16[3,3,32,192]{3,2,1,0:T(8,128)(2,1)S(1)}, u32[]{:S(2)}, u32[]{:S(2)}) collective-permute-start(bf16[3,3,32,192]{3,2,1,0:T(8,128)(2,1)S(1)} %pad_maximum_fusion.15), channel_id=1, source_target_pairs={{0,7},{1,0},{2,1},{3,2},{4,3},{5,4},{6,5},{7,6},{8,15},{9,8},{10,9... | collective-permute-start | bytes 331784 | tf_op jit(solution)/shard_map/ppermute | solution.py:95
  254.5 6.4 %collective-permute-start.69 = (bf16[3,3,32,192]{3,2,1,0:T(8,128)(2,1)S(1)}, bf16[3,3,32,192]{3,2,1,0:T(8,128)(2,1)S(1)}, u32[]{:S(2)}, u32[]{:S(2)}) collective-permute-start(bf16[3,3,32,192]{3,2,1,0:T(8,128)(2,1)S(1)} %pad_maximum_fusion.15), channel_id=1, source_target_pairs={{0,1},{1,2},{2,3},{3,4},{4,5},{5,6},{6,7},{7,0},{8,9},{9,10},{10,1... | collective-permute-start | bytes 331784 | tf_op jit(solution)/shard_map/ppermute | solution.py:95
  264.5 4.6 %collective-permute-start.73 = (f32[32,32]{0,1:T(8,128)S(1)}, f32[32,32]{0,1:T(8,128)S(1)}, u32[]{:S(2)}, u32[]{:S(2)}) collective-permute-start(f32[32,32]{0,1:T(8,128)S(1)} %convolution_bitcast_fusion.65), channel_id=1, source_target_pairs={{0,24},{8,16},{16,8},{24,0},{1,25},{9,17},{17,9},{25,1},{2,26},{10... | collective-permute-start | bytes 12296 | tf_op jit(solution)/shard_map/ppermute | solution.py:58
  273.1 4.7 %collective-permute-start.77 = (f32[32,32]{0,1:T(8,128)S(1)}, f32[32,32]{0,1:T(8,128)S(1)}, u32[]{:S(2)}, u32[]{:S(2)}) collective-permute-start(f32[32,32]{0,1:T(8,128)S(1)} %add_add_fusion), channel_id=1, source_target_pairs={{0,4},{1,5},{2,6},{3,7},{4,0},{5,1},{6,2},{7,3},{8,12},{9,13},{10,... | collective-permute-start | bytes 12296 | tf_op jit(solution)/shard_map/ppermute | solution.py:58
  (17 other events, 167.5 us)

commit v7 on v6

--- a/solution.py
+++ b/solution.py
@@ -86,7 +86,7 @@
     vector_count = basis.shape[3]
     block_rows = basis.shape[4]
     rows_total = lax.axis_size("gx") * lax.axis_size("gy") * column_depth * block_rows
-    columns = [(1, 1), (0, 1), (2, 1)] + [(dx, 0) for dx in range(3)] + [(dx, 2) for dx in range(3)]
+    columns = [(1, 1), (1, 0), (1, 2)] + [(0, dy) for dy in range(3)] + [(2, dy) for dy in range(3)]
     order = [(3 * dx + dy) * column_depth + z for dx, dy in columns for z in range(column_depth)]
     dense = {}
 
@@ -99,11 +99,11 @@
 
     def apply_operator(current):
         rounded = current.astype(jnp.bfloat16)
-        left = shift(rounded, "gx", 1)
-        right = shift(rounded, "gx", -1)
+        left = shift(rounded, "gy", 1)
+        right = shift(rounded, "gy", -1)
         strip = jnp.stack([left, rounded, right])
-        low = shift(strip, "gy", 1)
-        high = shift(strip, "gy", -1)
+        low = shift(strip, "gx", 1)
+        high = shift(strip, "gx", -1)
         if not dense:
             matrices = lax.optimization_barrier((coupling[0, 0], left, right))[0]
             full = dense_coupling(matrices, cpl_dst[0, 0], cpl_src[0, 0], column_depth, order)

time: 286 us -> 292 us (1.021)
  starting transfers between devices: 78.3 us -> 106 us
  waiting for transfers between devices: 122 us -> 100 us
    ppermute x64, starting transfers between devices: 65.6 us -> 93.8 us  [shift(): lax.ppermute(value, axis, [(i, (i + step) % count) for i in range(count)])]
    ppermute x64, waiting for transfers between devices: 103 us -> 82.1 us  [shift(): lax.ppermute(value, axis, [(i, (i + step) % count) for i in range(count)])]
  transfers between devices with their start and end apart: 78 -> 78, of which waited for: 71 -> 55; matrix products, arithmetic and copies ran while one was open for 18% -> 18% of each run, Pallas kernels for 0% -> 0%
where the time goes in v7:
time: 292 us; the launch traced here: 291 us
  starting transfers between devices  106 us (36%)
  waiting for transfers between devices  100 us (34%)
  matrix products  52.5 us (18%)
  other arithmetic  21.5 us (7%)
  local copies, waits for them, and re-layouts  10.6 us (4%)
    ppermute x64, starting transfers between devices, shift(): lax.ppermute(value, axis, [(i, (i + step) % count) for i in range(count)])  93.8 us
    ppermute x64, waiting for transfers between devices, shift(): lax.ppermute(value, axis, [(i, (i + step) % count) for i in range(count)])  82.1 us
    dot_general x64, matrix products, part(): jnp.einsum('kvj,tkij->tvi', cells, blocks, preferred_element_type=jnp.flo...  50.5 us
    ppermute x14, waiting for transfers between devices, swap(): return lax.ppermute(v, axis, [(i, i ^ stride) for i in range(count)])  18.2 us
    ppermute x14, starting transfers between devices, swap(): return lax.ppermute(v, axis, [(i, i ^ stride) for i in range(count)])  12 us
    gather x1, local copies, waits for them, and re-layouts, dense_coupling(): jnp.take(matrices, index.reshape(-1), axis=0)  10.3 us
    another operation x6, other arithmetic, orthonormal(): factor = jnp.linalg.cholesky(gram_matrix)  7.19 us
    another operation x4, other arithmetic, orthonormal(): inverse = jax.scipy.linalg.solve_triangular(factor, identity, lower=True)  6.17 us
  transfers between devices with their start and end apart: 78, of which 55 were waited for; matrix products, arithmetic and copies ran while one was open for 18% of the time, Pallas kernels for 0%

profile of v7, /device:TPU:0, one launch (start us, length us, event | category | flops | bytes accessed | tf_op | source)
XLA Modules:
  0.0 291.3 jit_solution(405551438062330527)
XLA Ops:
  1.4 4.1 %collective-permute-start.1 = (bf16[3,32,192]{2,1,0:T(8,128)(2,1)S(1)}, bf16[3,32,192]{2,1,0:T(8,128)(2,1)S(1)}, u32[]{:S(2)}, u32[]{:S(2)}) collective-permute-start(bf16[3,32,192]{2,1,0:T(8,128)(2,1)S(1)} %get-tuple-element.18), channel_id=1, source_target_pairs={{0,7},{1,0},{2,1},{3,2},{4,3},{5,4},{6,5},{7,6},{8,15},{9,8},{10,9... | collective-permute-start | bytes 110600 | tf_op jit(solution)/shard_map/ppermute | solution.py:95
  8.1 2.9 collective-permute-start.3
  11.0 10.3 %gather_fusion = bf16[81,192,192]{2,1,0:T(8,128)(2,1)} fusion(bf16[81,192,192]{2,1,0:T(8,128)(2,1)} %bitcast.915, s32[1024]{0:T(1024)S(1)} %pad_clamp_fusion), kind=kCustom, calls=%fused_computation | custom fusion | bytes 11944260 | tf_op jit(solution)/shard_map/jit(_take)/gather | solution.py:42
  21.3 4.3 %select_select_fusion = bf16[3,27,192,192]{3,2,1,0:T(8,128)(2,1)S(1)} fusion(bf16[3,27,192,192]{3,2,1,0:T(8,128)(2,1)} %bitcast.914, pred[3,27]{1,0:T(4,128)(4,1)S(1)} %compare_and_fusion, pred[3,27]{1,0:T(4,128)(4,1)S(1)} %and_reduce_fusion), kind=kLoop, calls=%fused_computation.1 | loop fusion | flops 5971968 | bytes 11944098 | tf_op jit(solution)/shard_map/jit(_where)/select_n | solution.py:46
  26.6 2.0 convolution_bitcast_fusion.30
  29.6 3.5 %collective-permute-start.5 = (bf16[3,32,192]{2,1,0:T(8,128)(2,1)S(1)}, bf16[3,32,192]{2,1,0:T(8,128)(2,1)S(1)}, u32[]{:S(2)}, u32[]{:S(2)}) collective-permute-start(bf16[3,32,192]{2,1,0:T(8,128)(2,1)S(1)} %get-tuple-element.19), channel_id=1, source_target_pairs={{0,7},{1,0},{2,1},{3,2},{4,3},{5,4},{6,5},{7,6},{8,15},{9,8},{10,9... | collective-permute-start | bytes 110600 | tf_op jit(solution)/shard_map/ppermute | solution.py:95
  33.6 1.6 collective-permute-done.4
  35.2 3.0 %collective-permute-start.7 = (bf16[3,3,32,192]{3,2,1,0:T(8,128)(2,1)S(1)}, bf16[3,3,32,192]{3,2,1,0:T(8,128)(2,1)S(1)}, u32[]{:S(2)}, u32[]{:S(2)}) collective-permute-start(bf16[3,3,32,192]{3,2,1,0:T(8,128)(2,1)S(1)} %pad_maximum_fusion.1), channel_id=1, source_target_pairs={{0,24},{8,0},{16,8},{24,16},{1,25},{9,1},{17,9},{25,17},{2,26},{10... | collective-permute-start | bytes 331784 | tf_op jit(solution)/shard_map/ppermute | solution.py:95
  38.8 2.9 collective-permute-done.7
  42.6 1.7 collective-permute-done.6
  45.2 3.5 %collective-permute-start.9 = (bf16[3,32,192]{2,1,0:T(8,128)(2,1)S(1)}, bf16[3,32,192]{2,1,0:T(8,128)(2,1)S(1)}, u32[]{:S(2)}, u32[]{:S(2)}) collective-permute-start(bf16[3,32,192]{2,1,0:T(8,128)(2,1)S(1)} %get-tuple-element.21), channel_id=1, source_target_pairs={{0,7},{1,0},{2,1},{3,2},{4,3},{5,4},{6,5},{7,6},{8,15},{9,8},{10,9... | collective-permute-start | bytes 110600 | tf_op jit(solution)/shard_map/ppermute | solution.py:95
  49.2 1.5 collective-permute-done.8
  53.4 3.3 %collective-permute-done.11 = bf16[3,3,32,192]{3,2,1,0:T(8,128)(2,1)S(1)} collective-permute-done((bf16[3,3,32,192]{3,2,1,0:T(8,128)(2,1)S(1)}, bf16[3,3,32,192]{3,2,1,0:T(8,128)(2,1)S(1)}, u32[]{:S(2)}, u32[]{:S(2)}) %collective-permute-start.11) | collective-permute-done | bytes 110624 | tf_op jit(solution)/shard_map/ppermute | solution.py:95
  59.3 3.5 %collective-permute-start.13 = (bf16[3,32,192]{2,1,0:T(8,128)(2,1)S(1)}, bf16[3,32,192]{2,1,0:T(8,128)(2,1)S(1)}, u32[]{:S(2)}, u32[]{:S(2)}) collective-permute-start(bf16[3,32,192]{2,1,0:T(8,128)(2,1)S(1)} %get-tuple-element.23), channel_id=1, source_target_pairs={{0,7},{1,0},{2,1},{3,2},{4,3},{5,4},{6,5},{7,6},{8,15},{9,8},{10,9... | collective-permute-start | bytes 110600 | tf_op jit(solution)/shard_map/ppermute | solution.py:95
  64.6 2.0 collective-permute-start.15
  67.3 3.8 %collective-permute-done.15 = bf16[3,3,32,192]{3,2,1,0:T(8,128)(2,1)S(1)} collective-permute-done((bf16[3,3,32,192]{3,2,1,0:T(8,128)(2,1)S(1)}, bf16[3,3,32,192]{3,2,1,0:T(8,128)(2,1)S(1)}, u32[]{:S(2)}, u32[]{:S(2)}) %collective-permute-start.15) | collective-permute-done | bytes 110624 | tf_op jit(solution)/shard_map/ppermute | solution.py:95
  72.0 1.9 collective-permute-done.14
  74.9 3.5 %collective-permute-start.17 = (bf16[3,32,192]{2,1,0:T(8,128)(2,1)S(1)}, bf16[3,32,192]{2,1,0:T(8,128)(2,1)S(1)}, u32[]{:S(2)}, u32[]{:S(2)}) collective-permute-start(bf16[3,32,192]{2,1,0:T(8,128)(2,1)S(1)} %get-tuple-element.25), channel_id=1, source_target_pairs={{0,7},{1,0},{2,1},{3,2},{4,3},{5,4},{6,5},{7,6},{8,15},{9,8},{10,9... | collective-permute-start | bytes 110600 | tf_op jit(solution)/shard_map/ppermute | solution.py:95
  83.0 3.4 %collective-permute-done.19 = bf16[3,3,32,192]{3,2,1,0:T(8,128)(2,1)S(1)} collective-permute-done((bf16[3,3,32,192]{3,2,1,0:T(8,128)(2,1)S(1)}, bf16[3,3,32,192]{3,2,1,0:T(8,128)(2,1)S(1)}, u32[]{:S(2)}, u32[]{:S(2)}) %collective-permute-start.19) | collective-permute-done | bytes 110624 | tf_op jit(solution)/shard_map/ppermute | solution.py:95
  89.0 3.5 %collective-permute-start.21 = (bf16[3,32,192]{2,1,0:T(8,128)(2,1)S(1)}, bf16[3,32,192]{2,1,0:T(8,128)(2,1)S(1)}, u32[]{:S(2)}, u32[]{:S(2)}) collective-permute-start(bf16[3,32,192]{2,1,0:T(8,128)(2,1)S(1)} %get-tuple-element.27), channel_id=1, source_target_pairs={{0,7},{1,0},{2,1},{3,2},{4,3},{5,4},{6,5},{7,6},{8,15},{9,8},{10,9... | collective-permute-start | bytes 110600 | tf_op jit(solution)/shard_map/ppermute | solution.py:95
  94.3 1.9 collective-permute-start.23
  97.0 3.1 %collective-permute-done.23 = bf16[3,3,32,192]{3,2,1,0:T(8,128)(2,1)S(1)} collective-permute-done((bf16[3,3,32,192]{3,2,1,0:T(8,128)(2,1)S(1)}, bf16[3,3,32,192]{3,2,1,0:T(8,128)(2,1)S(1)}, u32[]{:S(2)}, u32[]{:S(2)}) %collective-permute-start.23) | collective-permute-done | bytes 110624 | tf_op jit(solution)/shard_map/ppermute | solution.py:95
  100.9 1.5 collective-permute-done.22
  103.5 3.5 %collective-permute-start.25 = (bf16[3,32,192]{2,1,0:T(8,128)(2,1)S(1)}, bf16[3,32,192]{2,1,0:T(8,128)(2,1)S(1)}, u32[]{:S(2)}, u32[]{:S(2)}) collective-permute-start(bf16[3,32,192]{2,1,0:T(8,128)(2,1)S(1)} %get-tuple-element.29), channel_id=1, source_target_pairs={{0,7},{1,0},{2,1},{3,2},{4,3},{5,4},{6,5},{7,6},{8,15},{9,8},{10,9... | collective-permute-start | bytes 110600 | tf_op jit(solution)/shard_map/ppermute | solution.py:95
  111.5 3.2 %collective-permute-done.27 = bf16[3,3,32,192]{3,2,1,0:T(8,128)(2,1)S(1)} collective-permute-done((bf16[3,3,32,192]{3,2,1,0:T(8,128)(2,1)S(1)}, bf16[3,3,32,192]{3,2,1,0:T(8,128)(2,1)S(1)}, u32[]{:S(2)}, u32[]{:S(2)}) %collective-permute-start.27) | collective-permute-done | bytes 110624 | tf_op jit(solution)/shard_map/ppermute | solution.py:95
  117.6 3.5 %collective-permute-start.29 = (bf16[3,32,192]{2,1,0:T(8,128)(2,1)S(1)}, bf16[3,32,192]{2,1,0:T(8,128)(2,1)S(1)}, u32[]{:S(2)}, u32[]{:S(2)}) collective-permute-start(bf16[3,32,192]{2,1,0:T(8,128)(2,1)S(1)} %get-tuple-element.31), channel_id=1, source_target_pairs={{0,7},{1,0},{2,1},{3,2},{4,3},{5,4},{6,5},{7,6},{8,15},{9,8},{10,9... | collective-permute-start | bytes 110600 | tf_op jit(solution)/shard_map/ppermute | solution.py:95
  122.9 1.7 collective-permute-start.31
  125.6 4.0 %collective-permute-done.31 = bf16[3,3,32,192]{3,2,1,0:T(8,128)(2,1)S(1)} collective-permute-done((bf16[3,3,32,192]{3,2,1,0:T(8,128)(2,1)S(1)}, bf16[3,3,32,192]{3,2,1,0:T(8,128)(2,1)S(1)}, u32[]{:S(2)}, u32[]{:S(2)}) %collective-permute-start.31) | collective-permute-done | bytes 110624 | tf_op jit(solution)/shard_map/ppermute | solution.py:95
  134.8 1.7 collective-permute-start.34
  137.7 1.7 collective-permute-done.34
  141.4 2.1 collective-permute-done.36
  143.5 4.8 %collective-permute-done.38 = f32[32,32]{0,1:T(8,128)S(1)} collective-permute-done((f32[32,32]{0,1:T(8,128)S(1)}, f32[32,32]{0,1:T(8,128)S(1)}, u32[]{:S(2)}, u32[]{:S(2)}) %collective-permute-start.38) | collective-permute-done | bytes 4128 | tf_op jit(solution)/shard_map/ppermute | solution.py:58
  148.4 2.9 %cholesky.44 = f32[32,32]{1,0:T(8,128)S(1)} custom-call(f32[32,32]{1,0:T(8,128)S(1)} %fusion.162), custom_call_target="Cholesky" | custom-call | tf_op jit(solution)/shard_map/jit(cholesky)/cholesky | solution.py:77
  152.7 2.4 custom-call.6
  155.7 3.5 %collective-permute-start.40 = (bf16[3,32,192]{2,1,0:T(8,128)(2,1)S(1)}, bf16[3,32,192]{2,1,0:T(8,128)(2,1)S(1)}, u32[]{:S(2)}, u32[]{:S(2)}) collective-permute-start(bf16[3,32,192]{2,1,0:T(8,128)(2,1)S(1)} %get-tuple-element.16), channel_id=1, source_target_pairs={{0,7},{1,0},{2,1},{3,2},{4,3},{5,4},{6,5},{7,6},{8,15},{9,8},{10,9... | collective-permute-start | bytes 110600 | tf_op jit(solution)/shard_map/ppermute | solution.py:95
  159.2 1.5 convolution_bitcast_fusion.47
  161.1 1.8 collective-permute-start.42
  163.2 2.1 fusion.98
  165.3 2.6 collective-permute-done.42
  167.9 2.6 convolution_bitcast_fusion.14
  171.7 3.5 %collective-permute-start.44 = (bf16[3,32,192]{2,1,0:T(8,128)(2,1)S(1)}, bf16[3,32,192]{2,1,0:T(8,128)(2,1)S(1)}, u32[]{:S(2)}, u32[]{:S(2)}) collective-permute-start(bf16[3,32,192]{2,1,0:T(8,128)(2,1)S(1)} %get-tuple-element.14), channel_id=1, source_target_pairs={{0,7},{1,0},{2,1},{3,2},{4,3},{5,4},{6,5},{7,6},{8,15},{9,8},{10,9... | collective-permute-start | bytes 110600 | tf_op jit(solution)/shard_map/ppermute | solution.py:95
  177.1 2.5 collective-permute-start.46
  180.2 2.8 collective-permute-done.46
  183.8 1.8 collective-permute-done.45
  186.6 3.5 %collective-permute-start.48 = (bf16[3,32,192]{2,1,0:T(8,128)(2,1)S(1)}, bf16[3,32,192]{2,1,0:T(8,128)(2,1)S(1)}, u32[]{:S(2)}, u32[]{:S(2)}) collective-permute-start(bf16[3,32,192]{2,1,0:T(8,128)(2,1)S(1)} %get-tuple-element.12), channel_id=1, source_target_pairs={{0,7},{1,0},{2,1},{3,2},{4,3},{5,4},{6,5},{7,6},{8,15},{9,8},{10,9... | collective-permute-start | bytes 110600 | tf_op jit(solution)/shard_map/ppermute | solution.py:95
  194.7 2.5 collective-permute-done.50
  200.1 3.5 %collective-permute-start.52 = (bf16[3,32,192]{2,1,0:T(8,128)(2,1)S(1)}, bf16[3,32,192]{2,1,0:T(8,128)(2,1)S(1)}, u32[]{:S(2)}, u32[]{:S(2)}) collective-permute-start(bf16[3,32,192]{2,1,0:T(8,128)(2,1)S(1)} %get-tuple-element.10), channel_id=1, source_target_pairs={{0,7},{1,0},{2,1},{3,2},{4,3},{5,4},{6,5},{7,6},{8,15},{9,8},{10,9... | collective-permute-start | bytes 110600 | tf_op jit(solution)/shard_map/ppermute | solution.py:95
  208.1 2.5 collective-permute-done.54
  213.8 3.5 %collective-permute-start.56 = (bf16[3,32,192]{2,1,0:T(8,128)(2,1)S(1)}, bf16[3,32,192]{2,1,0:T(8,128)(2,1)S(1)}, u32[]{:S(2)}, u32[]{:S(2)}) collective-permute-start(bf16[3,32,192]{2,1,0:T(8,128)(2,1)S(1)} %get-tuple-element.33), channel_id=1, source_target_pairs={{0,7},{1,0},{2,1},{3,2},{4,3},{5,4},{6,5},{7,6},{8,15},{9,8},{10,9... | collective-permute-start | bytes 110600 | tf_op jit(solution)/shard_map/ppermute | solution.py:95
  217.8 1.5 collective-permute-done.55
  221.9 2.5 collective-permute-done.58
  227.3 3.5 %collective-permute-start.60 = (bf16[3,32,192]{2,1,0:T(8,128)(2,1)S(1)}, bf16[3,32,192]{2,1,0:T(8,128)(2,1)S(1)}, u32[]{:S(2)}, u32[]{:S(2)}) collective-permute-start(bf16[3,32,192]{2,1,0:T(8,128)(2,1)S(1)} %get-tuple-element.35), channel_id=1, source_target_pairs={{0,7},{1,0},{2,1},{3,2},{4,3},{5,4},{6,5},{7,6},{8,15},{9,8},{10,9... | collective-permute-start | bytes 110600 | tf_op jit(solution)/shard_map/ppermute | solution.py:95
  235.3 2.5 collective-permute-done.62
  241.0 3.5 %collective-permute-start.64 = (bf16[3,32,192]{2,1,0:T(8,128)(2,1)S(1)}, bf16[3,32,192]{2,1,0:T(8,128)(2,1)S(1)}, u32[]{:S(2)}, u32[]{:S(2)}) collective-permute-start(bf16[3,32,192]{2,1,0:T(8,128)(2,1)S(1)} %get-tuple-element.37), channel_id=1, source_target_pairs={{0,7},{1,0},{2,1},{3,2},{4,3},{5,4},{6,5},{7,6},{8,15},{9,8},{10,9... | collective-permute-start | bytes 110600 | tf_op jit(solution)/shard_map/ppermute | solution.py:95
  249.1 2.5 collective-permute-done.66
  254.5 3.5 %collective-permute-start.68 = (bf16[3,32,192]{2,1,0:T(8,128)(2,1)S(1)}, bf16[3,32,192]{2,1,0:T(8,128)(2,1)S(1)}, u32[]{:S(2)}, u32[]{:S(2)}) collective-permute-start(bf16[3,32,192]{2,1,0:T(8,128)(2,1)S(1)} %get-tuple-element.39), channel_id=1, source_target_pairs={{0,7},{1,0},{2,1},{3,2},{4,3},{5,4},{6,5},{7,6},{8,15},{9,8},{10,9... | collective-permute-start | bytes 110600 | tf_op jit(solution)/shard_map/ppermute | solution.py:95
  262.5 2.5 collective-permute-done.70
  270.1 1.8 collective-permute-start.73
  273.1 1.7 collective-permute-done.73
  274.9 1.8 collective-permute-start.76
  276.7 1.9 collective-permute-done.75
  279.7 3.7 %collective-permute-done.77 = f32[32,32]{0,1:T(8,128)S(1)} collective-permute-done((f32[32,32]{0,1:T(8,128)S(1)}, f32[32,32]{0,1:T(8,128)S(1)}, u32[]{:S(2)}, u32[]{:S(2)}) %collective-permute-start.77) | collective-permute-done | bytes 4128 | tf_op jit(solution)/shard_map/ppermute | solution.py:58
  283.5 2.9 %cholesky.55 = f32[32,32]{1,0:T(8,128)S(1)} custom-call(f32[32,32]{1,0:T(8,128)S(1)} %fusion.160), custom_call_target="Cholesky" | custom-call | tf_op jit(solution)/shard_map/jit(cholesky)/cholesky | solution.py:77
  287.7 2.4 custom-call.7
  (219 shorter events, 107.6 us)
Async XLA Ops:
  0.9 6.4 %collective-permute-start = (bf16[3,32,192]{2,1,0:T(8,128)(2,1)S(1)}, bf16[3,32,192]{2,1,0:T(8,128)(2,1)S(1)}, u32[]{:S(2)}, u32[]{:S(2)}) collective-permute-start(bf16[3,32,192]{2,1,0:T(8,128)(2,1)S(1)} %get-tuple-element.18), channel_id=1, source_target_pairs={{0,1},{1,2},{2,3},{3,4},{4,5},{5,6},{6,7},{7,0},{8,9},{9,10},{10,1... | collective-permute-start | bytes 110600 | tf_op jit(solution)/shard_map/ppermute | solution.py:95
  1.4 5.9 %collective-permute-start.1 = (bf16[3,32,192]{2,1,0:T(8,128)(2,1)S(1)}, bf16[3,32,192]{2,1,0:T(8,128)(2,1)S(1)}, u32[]{:S(2)}, u32[]{:S(2)}) collective-permute-start(bf16[3,32,192]{2,1,0:T(8,128)(2,1)S(1)} %get-tuple-element.18), channel_id=1, source_target_pairs={{0,7},{1,0},{2,1},{3,2},{4,3},{5,4},{6,5},{7,6},{8,15},{9,8},{10,9... | collective-permute-start | bytes 110600 | tf_op jit(solution)/shard_map/ppermute | solution.py:95
  8.1 18.6 %collective-permute-start.3 = (bf16[3,3,32,192]{3,2,1,0:T(8,128)(2,1)}, bf16[3,3,32,192]{3,2,1,0:T(8,128)(2,1)}, u32[]{:S(2)}, u32[]{:S(2)}) collective-permute-start(bf16[3,3,32,192]{3,2,1,0:T(8,128)(2,1)} %pad_maximum_fusion), channel_id=1, source_target_pairs={{0,24},{8,0},{16,8},{24,16},{1,25},{9,1},{17,9},{25,17},{2,26},{10... | collective-permute-start | bytes 331784 | tf_op jit(solution)/shard_map/ppermute | solution.py:95
  10.9 17.7 %collective-permute-start.2 = (bf16[3,3,32,192]{3,2,1,0:T(8,128)(2,1)}, bf16[3,3,32,192]{3,2,1,0:T(8,128)(2,1)S(1)}, u32[]{:S(2)}, u32[]{:S(2)}) collective-permute-start(bf16[3,3,32,192]{3,2,1,0:T(8,128)(2,1)} %pad_maximum_fusion), channel_id=1, source_target_pairs={{0,8},{8,16},{16,24},{24,0},{1,9},{9,17},{17,25},{25,1},{2,10},{10... | collective-permute-start | bytes 331784 | tf_op jit(solution)/shard_map/ppermute | solution.py:95
  29.6 5.5 %collective-permute-start.4 = (bf16[3,32,192]{2,1,0:T(8,128)(2,1)S(1)}, bf16[3,32,192]{2,1,0:T(8,128)(2,1)S(1)}, u32[]{:S(2)}, u32[]{:S(2)}) collective-permute-start(bf16[3,32,192]{2,1,0:T(8,128)(2,1)S(1)} %get-tuple-element.19), channel_id=1, source_target_pairs={{0,1},{1,2},{2,3},{3,4},{4,5},{5,6},{6,7},{7,0},{8,9},{9,10},{10,1... | collective-permute-start | bytes 110600 | tf_op jit(solution)/shard_map/ppermute | solution.py:95
  29.6 5.5 %collective-permute-start.5 = (bf16[3,32,192]{2,1,0:T(8,128)(2,1)S(1)}, bf16[3,32,192]{2,1,0:T(8,128)(2,1)S(1)}, u32[]{:S(2)}, u32[]{:S(2)}) collective-permute-start(bf16[3,32,192]{2,1,0:T(8,128)(2,1)S(1)} %get-tuple-element.19), channel_id=1, source_target_pairs={{0,7},{1,0},{2,1},{3,2},{4,3},{5,4},{6,5},{7,6},{8,15},{9,8},{10,9... | collective-permute-start | bytes 110600 | tf_op jit(solution)/shard_map/ppermute | solution.py:95
  35.2 6.5 %collective-permute-start.7 = (bf16[3,3,32,192]{3,2,1,0:T(8,128)(2,1)S(1)}, bf16[3,3,32,192]{3,2,1,0:T(8,128)(2,1)S(1)}, u32[]{:S(2)}, u32[]{:S(2)}) collective-permute-start(bf16[3,3,32,192]{3,2,1,0:T(8,128)(2,1)S(1)} %pad_maximum_fusion.1), channel_id=1, source_target_pairs={{0,24},{8,0},{16,8},{24,16},{1,25},{9,1},{17,9},{25,17},{2,26},{10... | collective-permute-start | bytes 331784 | tf_op jit(solution)/shard_map/ppermute | solution.py:95
  38.2 6.1 %collective-permute-start.6 = (bf16[3,3,32,192]{3,2,1,0:T(8,128)(2,1)S(1)}, bf16[3,3,32,192]{3,2,1,0:T(8,128)(2,1)S(1)}, u32[]{:S(2)}, u32[]{:S(2)}) collective-permute-start(bf16[3,3,32,192]{3,2,1,0:T(8,128)(2,1)S(1)} %pad_maximum_fusion.1), channel_id=1, source_target_pairs={{0,8},{8,16},{16,24},{24,0},{1,9},{9,17},{17,25},{25,1},{2,10},{10... | collective-permute-start | bytes 331784 | tf_op jit(solution)/shard_map/ppermute | solution.py:95
  45.2 5.5 %collective-permute-start.8 = (bf16[3,32,192]{2,1,0:T(8,128)(2,1)S(1)}, bf16[3,32,192]{2,1,0:T(8,128)(2,1)S(1)}, u32[]{:S(2)}, u32[]{:S(2)}) collective-permute-start(bf16[3,32,192]{2,1,0:T(8,128)(2,1)S(1)} %get-tuple-element.21), channel_id=1, source_target_pairs={{0,1},{1,2},{2,3},{3,4},{4,5},{5,6},{6,7},{7,0},{8,9},{9,10},{10,1... | collective-permute-start | bytes 110600 | tf_op jit(solution)/shard_map/ppermute | solution.py:95
  45.2 5.5 %collective-permute-start.9 = (bf16[3,32,192]{2,1,0:T(8,128)(2,1)S(1)}, bf16[3,32,192]{2,1,0:T(8,128)(2,1)S(1)}, u32[]{:S(2)}, u32[]{:S(2)}) collective-permute-start(bf16[3,32,192]{2,1,0:T(8,128)(2,1)S(1)} %get-tuple-element.21), channel_id=1, source_target_pairs={{0,7},{1,0},{2,1},{3,2},{4,3},{5,4},{6,5},{7,6},{8,15},{9,8},{10,9... | collective-permute-start | bytes 110600 | tf_op jit(solution)/shard_map/ppermute | solution.py:95
  50.7 6.0 %collective-permute-start.11 = (bf16[3,3,32,192]{3,2,1,0:T(8,128)(2,1)S(1)}, bf16[3,3,32,192]{3,2,1,0:T(8,128)(2,1)S(1)}, u32[]{:S(2)}, u32[]{:S(2)}) collective-permute-start(bf16[3,3,32,192]{3,2,1,0:T(8,128)(2,1)S(1)} %pad_maximum_fusion.2), channel_id=1, source_target_pairs={{0,24},{8,0},{16,8},{24,16},{1,25},{9,1},{17,9},{25,17},{2,26},{10... | collective-permute-start | bytes 331784 | tf_op jit(solution)/shard_map/ppermute | solution.py:95
  51.9 6.4 %collective-permute-start.10 = (bf16[3,3,32,192]{3,2,1,0:T(8,128)(2,1)S(1)}, bf16[3,3,32,192]{3,2,1,0:T(8,128)(2,1)S(1)}, u32[]{:S(2)}, u32[]{:S(2)}) collective-permute-start(bf16[3,3,32,192]{3,2,1,0:T(8,128)(2,1)S(1)} %pad_maximum_fusion.2), channel_id=1, source_target_pairs={{0,8},{8,16},{16,24},{24,0},{1,9},{9,17},{17,25},{25,1},{2,10},{10... | collective-permute-start | bytes 331784 | tf_op jit(solution)/shard_map/ppermute | solution.py:95
  59.2 5.4 %collective-permute-start.12 = (bf16[3,32,192]{2,1,0:T(8,128)(2,1)S(1)}, bf16[3,32,192]{2,1,0:T(8,128)(2,1)S(1)}, u32[]{:S(2)}, u32[]{:S(2)}) collective-permute-start(bf16[3,32,192]{2,1,0:T(8,128)(2,1)S(1)} %get-tuple-element.23), channel_id=1, source_target_pairs={{0,1},{1,2},{2,3},{3,4},{4,5},{5,6},{6,7},{7,0},{8,9},{9,10},{10,1... | collective-permute-start | bytes 110600 | tf_op jit(solution)/shard_map/ppermute | solution.py:95
  59.3 5.3 %collective-permute-start.13 = (bf16[3,32,192]{2,1,0:T(8,128)(2,1)S(1)}, bf16[3,32,192]{2,1,0:T(8,128)(2,1)S(1)}, u32[]{:S(2)}, u32[]{:S(2)}) collective-permute-start(bf16[3,32,192]{2,1,0:T(8,128)(2,1)S(1)} %get-tuple-element.23), channel_id=1, source_target_pairs={{0,7},{1,0},{2,1},{3,2},{4,3},{5,4},{6,5},{7,6},{8,15},{9,8},{10,9... | collective-permute-start | bytes 110600 | tf_op jit(solution)/shard_map/ppermute | solution.py:95
  64.6 6.5 %collective-permute-start.15 = (bf16[3,3,32,192]{3,2,1,0:T(8,128)(2,1)S(1)}, bf16[3,3,32,192]{3,2,1,0:T(8,128)(2,1)S(1)}, u32[]{:S(2)}, u32[]{:S(2)}) collective-permute-start(bf16[3,3,32,192]{3,2,1,0:T(8,128)(2,1)S(1)} %pad_maximum_fusion.3), channel_id=1, source_target_pairs={{0,24},{8,0},{16,8},{24,16},{1,25},{9,1},{17,9},{25,17},{2,26},{10... | collective-permute-start | bytes 331784 | tf_op jit(solution)/shard_map/ppermute | solution.py:95
  66.6 7.3 %collective-permute-start.14 = (bf16[3,3,32,192]{3,2,1,0:T(8,128)(2,1)S(1)}, bf16[3,3,32,192]{3,2,1,0:T(8,128)(2,1)S(1)}, u32[]{:S(2)}, u32[]{:S(2)}) collective-permute-start(bf16[3,3,32,192]{3,2,1,0:T(8,128)(2,1)S(1)} %pad_maximum_fusion.3), channel_id=1, source_target_pairs={{0,8},{8,16},{16,24},{24,0},{1,9},{9,17},{17,25},{25,1},{2,10},{10... | collective-permute-start | bytes 331784 | tf_op jit(solution)/shard_map/ppermute | solution.py:95
  74.9 5.4 %collective-permute-start.16 = (bf16[3,32,192]{2,1,0:T(8,128)(2,1)S(1)}, bf16[3,32,192]{2,1,0:T(8,128)(2,1)S(1)}, u32[]{:S(2)}, u32[]{:S(2)}) collective-permute-start(bf16[3,32,192]{2,1,0:T(8,128)(2,1)S(1)} %get-tuple-element.25), channel_id=1, source_target_pairs={{0,1},{1,2},{2,3},{3,4},{4,5},{5,6},{6,7},{7,0},{8,9},{9,10},{10,1... | collective-permute-start | bytes 110600 | tf_op jit(solution)/shard_map/ppermute | solution.py:95
  74.9 5.3 %collective-permute-start.17 = (bf16[3,32,192]{2,1,0:T(8,128)(2,1)S(1)}, bf16[3,32,192]{2,1,0:T(8,128)(2,1)S(1)}, u32[]{:S(2)}, u32[]{:S(2)}) collective-permute-start(bf16[3,32,192]{2,1,0:T(8,128)(2,1)S(1)} %get-tuple-element.25), channel_id=1, source_target_pairs={{0,7},{1,0},{2,1},{3,2},{4,3},{5,4},{6,5},{7,6},{8,15},{9,8},{10,9... | collective-permute-start | bytes 110600 | tf_op jit(solution)/shard_map/ppermute | solution.py:95
  80.3 6.1 %collective-permute-start.19 = (bf16[3,3,32,192]{3,2,1,0:T(8,128)(2,1)S(1)}, bf16[3,3,32,192]{3,2,1,0:T(8,128)(2,1)S(1)}, u32[]{:S(2)}, u32[]{:S(2)}) collective-permute-start(bf16[3,3,32,192]{3,2,1,0:T(8,128)(2,1)S(1)} %pad_maximum_fusion.4), channel_id=1, source_target_pairs={{0,24},{8,0},{16,8},{24,16},{1,25},{9,1},{17,9},{25,17},{2,26},{10... | collective-permute-start | bytes 331784 | tf_op jit(solution)/shard_map/ppermute | solution.py:95
  81.5 6.4 %collective-permute-start.18 = (bf16[3,3,32,192]{3,2,1,0:T(8,128)(2,1)S(1)}, bf16[3,3,32,192]{3,2,1,0:T(8,128)(2,1)S(1)}, u32[]{:S(2)}, u32[]{:S(2)}) collective-permute-start(bf16[3,3,32,192]{3,2,1,0:T(8,128)(2,1)S(1)} %pad_maximum_fusion.4), channel_id=1, source_target_pairs={{0,8},{8,16},{16,24},{24,0},{1,9},{9,17},{17,25},{25,1},{2,10},{10... | collective-permute-start | bytes 331784 | tf_op jit(solution)/shard_map/ppermute | solution.py:95
  88.9 5.4 %collective-permute-start.20 = (bf16[3,32,192]{2,1,0:T(8,128)(2,1)S(1)}, bf16[3,32,192]{2,1,0:T(8,128)(2,1)S(1)}, u32[]{:S(2)}, u32[]{:S(2)}) collective-permute-start(bf16[3,32,192]{2,1,0:T(8,128)(2,1)S(1)} %get-tuple-element.27), channel_id=1, source_target_pairs={{0,1},{1,2},{2,3},{3,4},{4,5},{5,6},{6,7},{7,0},{8,9},{9,10},{10,1... | collective-permute-start | bytes 110600 | tf_op jit(solution)/shard_map/ppermute | solution.py:95
  89.0 5.3 %collective-permute-start.21 = (bf16[3,32,192]{2,1,0:T(8,128)(2,1)S(1)}, bf16[3,32,192]{2,1,0:T(8,128)(2,1)S(1)}, u32[]{:S(2)}, u32[]{:S(2)}) collective-permute-start(bf16[3,32,192]{2,1,0:T(8,128)(2,1)S(1)} %get-tuple-element.27), channel_id=1, source_target_pairs={{0,7},{1,0},{2,1},{3,2},{4,3},{5,4},{6,5},{7,6},{8,15},{9,8},{10,9... | collective-permute-start | bytes 110600 | tf_op jit(solution)/shard_map/ppermute | solution.py:95
  94.3 5.8 %collective-permute-start.23 = (bf16[3,3,32,192]{3,2,1,0:T(8,128)(2,1)S(1)}, bf16[3,3,32,192]{3,2,1,0:T(8,128)(2,1)S(1)}, u32[]{:S(2)}, u32[]{:S(2)}) collective-permute-start(bf16[3,3,32,192]{3,2,1,0:T(8,128)(2,1)S(1)} %pad_maximum_fusion.5), channel_id=1, source_target_pairs={{0,24},{8,0},{16,8},{24,16},{1,25},{9,1},{17,9},{25,17},{2,26},{10... | collective-permute-start | bytes 331784 | tf_op jit(solution)/shard_map/ppermute | solution.py:95
  96.2 6.3 %collective-permute-start.22 = (bf16[3,3,32,192]{3,2,1,0:T(8,128)(2,1)S(1)}, bf16[3,3,32,192]{3,2,1,0:T(8,128)(2,1)S(1)}, u32[]{:S(2)}, u32[]{:S(2)}) collective-permute-start(bf16[3,3,32,192]{3,2,1,0:T(8,128)(2,1)S(1)} %pad_maximum_fusion.5), channel_id=1, source_target_pairs={{0,8},{8,16},{16,24},{24,0},{1,9},{9,17},{17,25},{25,1},{2,10},{10... | collective-permute-start | bytes 331784 | tf_op jit(solution)/shard_map/ppermute | solution.py:95
  103.4 5.4 %collective-permute-start.24 = (bf16[3,32,192]{2,1,0:T(8,128)(2,1)S(1)}, bf16[3,32,192]{2,1,0:T(8,128)(2,1)S(1)}, u32[]{:S(2)}, u32[]{:S(2)}) collective-permute-start(bf16[3,32,192]{2,1,0:T(8,128)(2,1)S(1)} %get-tuple-element.29), channel_id=1, source_target_pairs={{0,1},{1,2},{2,3},{3,4},{4,5},{5,6},{6,7},{7,0},{8,9},{9,10},{10,1... | collective-permute-start | bytes 110600 | tf_op jit(solution)/shard_map/ppermute | solution.py:95
  103.5 5.3 %collective-permute-start.25 = (bf16[3,32,192]{2,1,0:T(8,128)(2,1)S(1)}, bf16[3,32,192]{2,1,0:T(8,128)(2,1)S(1)}, u32[]{:S(2)}, u32[]{:S(2)}) collective-permute-start(bf16[3,32,192]{2,1,0:T(8,128)(2,1)S(1)} %get-tuple-element.29), channel_id=1, source_target_pairs={{0,7},{1,0},{2,1},{3,2},{4,3},{5,4},{6,5},{7,6},{8,15},{9,8},{10,9... | collective-permute-start | bytes 110600 | tf_op jit(solution)/shard_map/ppermute | solution.py:95
  108.8 5.9 %collective-permute-start.27 = (bf16[3,3,32,192]{3,2,1,0:T(8,128)(2,1)S(1)}, bf16[3,3,32,192]{3,2,1,0:T(8,128)(2,1)S(1)}, u32[]{:S(2)}, u32[]{:S(2)}) collective-permute-start(bf16[3,3,32,192]{3,2,1,0:T(8,128)(2,1)S(1)} %pad_maximum_fusion.6), channel_id=1, source_target_pairs={{0,24},{8,0},{16,8},{24,16},{1,25},{9,1},{17,9},{25,17},{2,26},{10... | collective-permute-start | bytes 331784 | tf_op jit(solution)/shard_map/ppermute | solution.py:95
  110.1 6.5 %collective-permute-start.26 = (bf16[3,3,32,192]{3,2,1,0:T(8,128)(2,1)S(1)}, bf16[3,3,32,192]{3,2,1,0:T(8,128)(2,1)S(1)}, u32[]{:S(2)}, u32[]{:S(2)}) collective-permute-start(bf16[3,3,32,192]{3,2,1,0:T(8,128)(2,1)S(1)} %pad_maximum_fusion.6), channel_id=1, source_target_pairs={{0,8},{8,16},{16,24},{24,0},{1,9},{9,17},{17,25},{25,1},{2,10},{10... | collective-permute-start | bytes 331784 | tf_op jit(solution)/shard_map/ppermute | solution.py:95
  117.5 5.4 %collective-permute-start.28 = (bf16[3,32,192]{2,1,0:T(8,128)(2,1)S(1)}, bf16[3,32,192]{2,1,0:T(8,128)(2,1)S(1)}, u32[]{:S(2)}, u32[]{:S(2)}) collective-permute-start(bf16[3,32,192]{2,1,0:T(8,128)(2,1)S(1)} %get-tuple-element.31), channel_id=1, source_target_pairs={{0,1},{1,2},{2,3},{3,4},{4,5},{5,6},{6,7},{7,0},{8,9},{9,10},{10,1... | collective-permute-start | bytes 110600 | tf_op jit(solution)/shard_map/ppermute | solution.py:95
  117.6 5.3 %collective-permute-start.29 = (bf16[3,32,192]{2,1,0:T(8,128)(2,1)S(1)}, bf16[3,32,192]{2,1,0:T(8,128)(2,1)S(1)}, u32[]{:S(2)}, u32[]{:S(2)}) collective-permute-start(bf16[3,32,192]{2,1,0:T(8,128)(2,1)S(1)} %get-tuple-element.31), channel_id=1, source_target_pairs={{0,7},{1,0},{2,1},{3,2},{4,3},{5,4},{6,5},{7,6},{8,15},{9,8},{10,9... | collective-permute-start | bytes 110600 | tf_op jit(solution)/shard_map/ppermute | solution.py:95
  122.9 6.7 %collective-permute-start.31 = (bf16[3,3,32,192]{3,2,1,0:T(8,128)(2,1)S(1)}, bf16[3,3,32,192]{3,2,1,0:T(8,128)(2,1)S(1)}, u32[]{:S(2)}, u32[]{:S(2)}) collective-permute-start(bf16[3,3,32,192]{3,2,1,0:T(8,128)(2,1)S(1)} %pad_maximum_fusion.7), channel_id=1, source_target_pairs={{0,24},{8,0},{16,8},{24,16},{1,25},{9,1},{17,9},{25,17},{2,26},{10... | collective-permute-start | bytes 331784 | tf_op jit(solution)/shard_map/ppermute | solution.py:95
  124.6 7.2 %collective-permute-start.30 = (bf16[3,3,32,192]{3,2,1,0:T(8,128)(2,1)S(1)}, bf16[3,3,32,192]{3,2,1,0:T(8,128)(2,1)S(1)}, u32[]{:S(2)}, u32[]{:S(2)}) collective-permute-start(bf16[3,3,32,192]{3,2,1,0:T(8,128)(2,1)S(1)} %pad_maximum_fusion.7), channel_id=1, source_target_pairs={{0,8},{8,16},{16,24},{24,0},{1,9},{9,17},{17,25},{25,1},{2,10},{10... | collective-permute-start | bytes 331784 | tf_op jit(solution)/shard_map/ppermute | solution.py:95
  155.6 5.5 %collective-permute-start.39 = (bf16[3,32,192]{2,1,0:T(8,128)(2,1)S(1)}, bf16[3,32,192]{2,1,0:T(8,128)(2,1)S(1)}, u32[]{:S(2)}, u32[]{:S(2)}) collective-permute-start(bf16[3,32,192]{2,1,0:T(8,128)(2,1)S(1)} %get-tuple-element.16), channel_id=1, source_target_pairs={{0,1},{1,2},{2,3},{3,4},{4,5},{5,6},{6,7},{7,0},{8,9},{9,10},{10,1... | collective-permute-start | bytes 110600 | tf_op jit(solution)/shard_map/ppermute | solution.py:95
  155.7 5.4 %collective-permute-start.40 = (bf16[3,32,192]{2,1,0:T(8,128)(2,1)S(1)}, bf16[3,32,192]{2,1,0:T(8,128)(2,1)S(1)}, u32[]{:S(2)}, u32[]{:S(2)}) collective-permute-start(bf16[3,32,192]{2,1,0:T(8,128)(2,1)S(1)} %get-tuple-element.16), channel_id=1, source_target_pairs={{0,7},{1,0},{2,1},{3,2},{4,3},{5,4},{6,5},{7,6},{8,15},{9,8},{10,9... | collective-permute-start | bytes 110600 | tf_op jit(solution)/shard_map/ppermute | solution.py:95
  161.1 6.8 %collective-permute-start.42 = (bf16[3,3,32,192]{3,2,1,0:T(8,128)(2,1)S(1)}, bf16[3,3,32,192]{3,2,1,0:T(8,128)(2,1)S(1)}, u32[]{:S(2)}, u32[]{:S(2)}) collective-permute-start(bf16[3,3,32,192]{3,2,1,0:T(8,128)(2,1)S(1)} %pad_maximum_fusion.8), channel_id=1, source_target_pairs={{0,24},{8,0},{16,8},{24,16},{1,25},{9,1},{17,9},{25,17},{2,26},{10... | collective-permute-start | bytes 331784 | tf_op jit(solution)/shard_map/ppermute | solution.py:95
  162.9 7.8 %collective-permute-start.41 = (bf16[3,3,32,192]{3,2,1,0:T(8,128)(2,1)S(1)}, bf16[3,3,32,192]{3,2,1,0:T(8,128)(2,1)S(1)}, u32[]{:S(2)}, u32[]{:S(2)}) collective-permute-start(bf16[3,3,32,192]{3,2,1,0:T(8,128)(2,1)S(1)} %pad_maximum_fusion.8), channel_id=1, source_target_pairs={{0,8},{8,16},{16,24},{24,0},{1,9},{9,17},{17,25},{25,1},{2,10},{10... | collective-permute-start | bytes 331784 | tf_op jit(solution)/shard_map/ppermute | solution.py:95
  171.7 5.4 %collective-permute-start.43 = (bf16[3,32,192]{2,1,0:T(8,128)(2,1)S(1)}, bf16[3,32,192]{2,1,0:T(8,128)(2,1)S(1)}, u32[]{:S(2)}, u32[]{:S(2)}) collective-permute-start(bf16[3,32,192]{2,1,0:T(8,128)(2,1)S(1)} %get-tuple-element.14), channel_id=1, source_target_pairs={{0,1},{1,2},{2,3},{3,4},{4,5},{5,6},{6,7},{7,0},{8,9},{9,10},{10,1... | collective-permute-start | bytes 110600 | tf_op jit(solution)/shard_map/ppermute | solution.py:95
  171.7 5.3 %collective-permute-start.44 = (bf16[3,32,192]{2,1,0:T(8,128)(2,1)S(1)}, bf16[3,32,192]{2,1,0:T(8,128)(2,1)S(1)}, u32[]{:S(2)}, u32[]{:S(2)}) collective-permute-start(bf16[3,32,192]{2,1,0:T(8,128)(2,1)S(1)} %get-tuple-element.14), channel_id=1, source_target_pairs={{0,7},{1,0},{2,1},{3,2},{4,3},{5,4},{6,5},{7,6},{8,15},{9,8},{10,9... | collective-permute-start | bytes 110600 | tf_op jit(solution)/shard_map/ppermute | solution.py:95
  177.1 5.9 %collective-permute-start.46 = (bf16[3,3,32,192]{3,2,1,0:T(8,128)(2,1)S(1)}, bf16[3,3,32,192]{3,2,1,0:T(8,128)(2,1)S(1)}, u32[]{:S(2)}, u32[]{:S(2)}) collective-permute-start(bf16[3,3,32,192]{3,2,1,0:T(8,128)(2,1)S(1)} %pad_maximum_fusion.9), channel_id=1, source_target_pairs={{0,24},{8,0},{16,8},{24,16},{1,25},{9,1},{17,9},{25,17},{2,26},{10... | collective-permute-start | bytes 331784 | tf_op jit(solution)/shard_map/ppermute | solution.py:95
  179.6 6.0 %collective-permute-start.45 = (bf16[3,3,32,192]{3,2,1,0:T(8,128)(2,1)S(1)}, bf16[3,3,32,192]{3,2,1,0:T(8,128)(2,1)S(1)}, u32[]{:S(2)}, u32[]{:S(2)}) collective-permute-start(bf16[3,3,32,192]{3,2,1,0:T(8,128)(2,1)S(1)} %pad_maximum_fusion.9), channel_id=1, source_target_pairs={{0,8},{8,16},{16,24},{24,0},{1,9},{9,17},{17,25},{25,1},{2,10},{10... | collective-permute-start | bytes 331784 | tf_op jit(solution)/shard_map/ppermute | solution.py:95
  186.6 5.4 %collective-permute-start.47 = (bf16[3,32,192]{2,1,0:T(8,128)(2,1)S(1)}, bf16[3,32,192]{2,1,0:T(8,128)(2,1)S(1)}, u32[]{:S(2)}, u32[]{:S(2)}) collective-permute-start(bf16[3,32,192]{2,1,0:T(8,128)(2,1)S(1)} %get-tuple-element.12), channel_id=1, source_target_pairs={{0,1},{1,2},{2,3},{3,4},{4,5},{5,6},{6,7},{7,0},{8,9},{9,10},{10,1... | collective-permute-start | bytes 110600 | tf_op jit(solution)/shard_map/ppermute | solution.py:95
  186.6 5.3 %collective-permute-start.48 = (bf16[3,32,192]{2,1,0:T(8,128)(2,1)S(1)}, bf16[3,32,192]{2,1,0:T(8,128)(2,1)S(1)}, u32[]{:S(2)}, u32[]{:S(2)}) collective-permute-start(bf16[3,32,192]{2,1,0:T(8,128)(2,1)S(1)} %get-tuple-element.12), channel_id=1, source_target_pairs={{0,7},{1,0},{2,1},{3,2},{4,3},{5,4},{6,5},{7,6},{8,15},{9,8},{10,9... | collective-permute-start | bytes 110600 | tf_op jit(solution)/shard_map/ppermute | solution.py:95
  192.0 5.2 %collective-permute-start.50 = (bf16[3,3,32,192]{3,2,1,0:T(8,128)(2,1)S(1)}, bf16[3,3,32,192]{3,2,1,0:T(8,128)(2,1)S(1)}, u32[]{:S(2)}, u32[]{:S(2)}) collective-permute-start(bf16[3,3,32,192]{3,2,1,0:T(8,128)(2,1)S(1)} %pad_maximum_fusion.10), channel_id=1, source_target_pairs={{0,24},{8,0},{16,8},{24,16},{1,25},{9,1},{17,9},{25,17},{2,26},{10... | collective-permute-start | bytes 331784 | tf_op jit(solution)/shard_map/ppermute | solution.py:95
  193.0 6.0 %collective-permute-start.49 = (bf16[3,3,32,192]{3,2,1,0:T(8,128)(2,1)S(1)}, bf16[3,3,32,192]{3,2,1,0:T(8,128)(2,1)S(1)}, u32[]{:S(2)}, u32[]{:S(2)}) collective-permute-start(bf16[3,3,32,192]{3,2,1,0:T(8,128)(2,1)S(1)} %pad_maximum_fusion.10), channel_id=1, source_target_pairs={{0,8},{8,16},{16,24},{24,0},{1,9},{9,17},{17,25},{25,1},{2,10},{10... | collective-permute-start | bytes 331784 | tf_op jit(solution)/shard_map/ppermute | solution.py:95
  200.0 5.4 %collective-permute-start.51 = (bf16[3,32,192]{2,1,0:T(8,128)(2,1)S(1)}, bf16[3,32,192]{2,1,0:T(8,128)(2,1)S(1)}, u32[]{:S(2)}, u32[]{:S(2)}) collective-permute-start(bf16[3,32,192]{2,1,0:T(8,128)(2,1)S(1)} %get-tuple-element.10), channel_id=1, source_target_pairs={{0,1},{1,2},{2,3},{3,4},{4,5},{5,6},{6,7},{7,0},{8,9},{9,10},{10,1... | collective-permute-start | bytes 110600 | tf_op jit(solution)/shard_map/ppermute | solution.py:95
  200.1 5.3 %collective-permute-start.52 = (bf16[3,32,192]{2,1,0:T(8,128)(2,1)S(1)}, bf16[3,32,192]{2,1,0:T(8,128)(2,1)S(1)}, u32[]{:S(2)}, u32[]{:S(2)}) collective-permute-start(bf16[3,32,192]{2,1,0:T(8,128)(2,1)S(1)} %get-tuple-element.10), channel_id=1, source_target_pairs={{0,7},{1,0},{2,1},{3,2},{4,3},{5,4},{6,5},{7,6},{8,15},{9,8},{10,9... | collective-permute-start | bytes 110600 | tf_op jit(solution)/shard_map/ppermute | solution.py:95
  205.4 5.2 %collective-permute-start.54 = (bf16[3,3,32,192]{3,2,1,0:T(8,128)(2,1)S(1)}, bf16[3,3,32,192]{3,2,1,0:T(8,128)(2,1)S(1)}, u32[]{:S(2)}, u32[]{:S(2)}) collective-permute-start(bf16[3,3,32,192]{3,2,1,0:T(8,128)(2,1)S(1)} %pad_maximum_fusion.11), channel_id=1, source_target_pairs={{0,24},{8,0},{16,8},{24,16},{1,25},{9,1},{17,9},{25,17},{2,26},{10... | collective-permute-start | bytes 331784 | tf_op jit(solution)/shard_map/ppermute | solution.py:95
  206.8 6.0 %collective-permute-start.53 = (bf16[3,3,32,192]{3,2,1,0:T(8,128)(2,1)S(1)}, bf16[3,3,32,192]{3,2,1,0:T(8,128)(2,1)S(1)}, u32[]{:S(2)}, u32[]{:S(2)}) collective-permute-start(bf16[3,3,32,192]{3,2,1,0:T(8,128)(2,1)S(1)} %pad_maximum_fusion.11), channel_id=1, source_target_pairs={{0,8},{8,16},{16,24},{24,0},{1,9},{9,17},{17,25},{25,1},{2,10},{10... | collective-permute-start | bytes 331784 | tf_op jit(solution)/shard_map/ppermute | solution.py:95
  213.8 5.4 %collective-permute-start.55 = (bf16[3,32,192]{2,1,0:T(8,128)(2,1)S(1)}, bf16[3,32,192]{2,1,0:T(8,128)(2,1)S(1)}, u32[]{:S(2)}, u32[]{:S(2)}) collective-permute-start(bf16[3,32,192]{2,1,0:T(8,128)(2,1)S(1)} %get-tuple-element.33), channel_id=1, source_target_pairs={{0,1},{1,2},{2,3},{3,4},{4,5},{5,6},{6,7},{7,0},{8,9},{9,10},{10,1... | collective-permute-start | bytes 110600 | tf_op jit(solution)/shard_map/ppermute | solution.py:95
  213.8 5.4 %collective-permute-start.56 = (bf16[3,32,192]{2,1,0:T(8,128)(2,1)S(1)}, bf16[3,32,192]{2,1,0:T(8,128)(2,1)S(1)}, u32[]{:S(2)}, u32[]{:S(2)}) collective-permute-start(bf16[3,32,192]{2,1,0:T(8,128)(2,1)S(1)} %get-tuple-element.33), channel_id=1, source_target_pairs={{0,7},{1,0},{2,1},{3,2},{4,3},{5,4},{6,5},{7,6},{8,15},{9,8},{10,9... | collective-permute-start | bytes 110600 | tf_op jit(solution)/shard_map/ppermute | solution.py:95
  219.2 5.2 %collective-permute-start.58 = (bf16[3,3,32,192]{3,2,1,0:T(8,128)(2,1)S(1)}, bf16[3,3,32,192]{3,2,1,0:T(8,128)(2,1)S(1)}, u32[]{:S(2)}, u32[]{:S(2)}) collective-permute-start(bf16[3,3,32,192]{3,2,1,0:T(8,128)(2,1)S(1)} %pad_maximum_fusion.12), channel_id=1, source_target_pairs={{0,24},{8,0},{16,8},{24,16},{1,25},{9,1},{17,9},{25,17},{2,26},{10... | collective-permute-start | bytes 331784 | tf_op jit(solution)/shard_map/ppermute | solution.py:95
  220.2 6.0 %collective-permute-start.57 = (bf16[3,3,32,192]{3,2,1,0:T(8,128)(2,1)S(1)}, bf16[3,3,32,192]{3,2,1,0:T(8,128)(2,1)S(1)}, u32[]{:S(2)}, u32[]{:S(2)}) collective-permute-start(bf16[3,3,32,192]{3,2,1,0:T(8,128)(2,1)S(1)} %pad_maximum_fusion.12), channel_id=1, source_target_pairs={{0,8},{8,16},{16,24},{24,0},{1,9},{9,17},{17,25},{25,1},{2,10},{10... | collective-permute-start | bytes 331784 | tf_op jit(solution)/shard_map/ppermute | solution.py:95
  227.2 5.4 %collective-permute-start.59 = (bf16[3,32,192]{2,1,0:T(8,128)(2,1)S(1)}, bf16[3,32,192]{2,1,0:T(8,128)(2,1)S(1)}, u32[]{:S(2)}, u32[]{:S(2)}) collective-permute-start(bf16[3,32,192]{2,1,0:T(8,128)(2,1)S(1)} %get-tuple-element.35), channel_id=1, source_target_pairs={{0,1},{1,2},{2,3},{3,4},{4,5},{5,6},{6,7},{7,0},{8,9},{9,10},{10,1... | collective-permute-start | bytes 110600 | tf_op jit(solution)/shard_map/ppermute | solution.py:95
  227.3 5.3 %collective-permute-start.60 = (bf16[3,32,192]{2,1,0:T(8,128)(2,1)S(1)}, bf16[3,32,192]{2,1,0:T(8,128)(2,1)S(1)}, u32[]{:S(2)}, u32[]{:S(2)}) collective-permute-start(bf16[3,32,192]{2,1,0:T(8,128)(2,1)S(1)} %get-tuple-element.35), channel_id=1, source_target_pairs={{0,7},{1,0},{2,1},{3,2},{4,3},{5,4},{6,5},{7,6},{8,15},{9,8},{10,9... | collective-permute-start | bytes 110600 | tf_op jit(solution)/shard_map/ppermute | solution.py:95
  232.6 5.2 %collective-permute-start.62 = (bf16[3,3,32,192]{3,2,1,0:T(8,128)(2,1)S(1)}, bf16[3,3,32,192]{3,2,1,0:T(8,128)(2,1)S(1)}, u32[]{:S(2)}, u32[]{:S(2)}) collective-permute-start(bf16[3,3,32,192]{3,2,1,0:T(8,128)(2,1)S(1)} %pad_maximum_fusion.13), channel_id=1, source_target_pairs={{0,24},{8,0},{16,8},{24,16},{1,25},{9,1},{17,9},{25,17},{2,26},{10... | collective-permute-start | bytes 331784 | tf_op jit(solution)/shard_map/ppermute | solution.py:95
  234.0 6.0 %collective-permute-start.61 = (bf16[3,3,32,192]{3,2,1,0:T(8,128)(2,1)S(1)}, bf16[3,3,32,192]{3,2,1,0:T(8,128)(2,1)S(1)}, u32[]{:S(2)}, u32[]{:S(2)}) collective-permute-start(bf16[3,3,32,192]{3,2,1,0:T(8,128)(2,1)S(1)} %pad_maximum_fusion.13), channel_id=1, source_target_pairs={{0,8},{8,16},{16,24},{24,0},{1,9},{9,17},{17,25},{25,1},{2,10},{10... | collective-permute-start | bytes 331784 | tf_op jit(solution)/shard_map/ppermute | solution.py:95
  241.0 5.4 %collective-permute-start.63 = (bf16[3,32,192]{2,1,0:T(8,128)(2,1)S(1)}, bf16[3,32,192]{2,1,0:T(8,128)(2,1)S(1)}, u32[]{:S(2)}, u32[]{:S(2)}) collective-permute-start(bf16[3,32,192]{2,1,0:T(8,128)(2,1)S(1)} %get-tuple-element.37), channel_id=1, source_target_pairs={{0,1},{1,2},{2,3},{3,4},{4,5},{5,6},{6,7},{7,0},{8,9},{9,10},{10,1... | collective-permute-start | bytes 110600 | tf_op jit(solution)/shard_map/ppermute | solution.py:95
  241.0 5.4 %collective-permute-start.64 = (bf16[3,32,192]{2,1,0:T(8,128)(2,1)S(1)}, bf16[3,32,192]{2,1,0:T(8,128)(2,1)S(1)}, u32[]{:S(2)}, u32[]{:S(2)}) collective-permute-start(bf16[3,32,192]{2,1,0:T(8,128)(2,1)S(1)} %get-tuple-element.37), channel_id=1, source_target_pairs={{0,7},{1,0},{2,1},{3,2},{4,3},{5,4},{6,5},{7,6},{8,15},{9,8},{10,9... | collective-permute-start | bytes 110600 | tf_op jit(solution)/shard_map/ppermute | solution.py:95
  246.4 5.2 %collective-permute-start.66 = (bf16[3,3,32,192]{3,2,1,0:T(8,128)(2,1)S(1)}, bf16[3,3,32,192]{3,2,1,0:T(8,128)(2,1)S(1)}, u32[]{:S(2)}, u32[]{:S(2)}) collective-permute-start(bf16[3,3,32,192]{3,2,1,0:T(8,128)(2,1)S(1)} %pad_maximum_fusion.14), channel_id=1, source_target_pairs={{0,24},{8,0},{16,8},{24,16},{1,25},{9,1},{17,9},{25,17},{2,26},{10... | collective-permute-start | bytes 331784 | tf_op jit(solution)/shard_map/ppermute | solution.py:95
  247.4 6.0 %collective-permute-start.65 = (bf16[3,3,32,192]{3,2,1,0:T(8,128)(2,1)S(1)}, bf16[3,3,32,192]{3,2,1,0:T(8,128)(2,1)S(1)}, u32[]{:S(2)}, u32[]{:S(2)}) collective-permute-start(bf16[3,3,32,192]{3,2,1,0:T(8,128)(2,1)S(1)} %pad_maximum_fusion.14), channel_id=1, source_target_pairs={{0,8},{8,16},{16,24},{24,0},{1,9},{9,17},{17,25},{25,1},{2,10},{10... | collective-permute-start | bytes 331784 | tf_op jit(solution)/shard_map/ppermute | solution.py:95
  254.4 5.4 %collective-permute-start.67 = (bf16[3,32,192]{2,1,0:T(8,128)(2,1)S(1)}, bf16[3,32,192]{2,1,0:T(8,128)(2,1)S(1)}, u32[]{:S(2)}, u32[]{:S(2)}) collective-permute-start(bf16[3,32,192]{2,1,0:T(8,128)(2,1)S(1)} %get-tuple-element.39), channel_id=1, source_target_pairs={{0,1},{1,2},{2,3},{3,4},{4,5},{5,6},{6,7},{7,0},{8,9},{9,10},{10,1... | collective-permute-start | bytes 110600 | tf_op jit(solution)/shard_map/ppermute | solution.py:95
  254.5 5.3 %collective-permute-start.68 = (bf16[3,32,192]{2,1,0:T(8,128)(2,1)S(1)}, bf16[3,32,192]{2,1,0:T(8,128)(2,1)S(1)}, u32[]{:S(2)}, u32[]{:S(2)}) collective-permute-start(bf16[3,32,192]{2,1,0:T(8,128)(2,1)S(1)} %get-tuple-element.39), channel_id=1, source_target_pairs={{0,7},{1,0},{2,1},{3,2},{4,3},{5,4},{6,5},{7,6},{8,15},{9,8},{10,9... | collective-permute-start | bytes 110600 | tf_op jit(solution)/shard_map/ppermute | solution.py:95
  259.8 5.2 %collective-permute-start.70 = (bf16[3,3,32,192]{3,2,1,0:T(8,128)(2,1)S(1)}, bf16[3,3,32,192]{3,2,1,0:T(8,128)(2,1)S(1)}, u32[]{:S(2)}, u32[]{:S(2)}) collective-permute-start(bf16[3,3,32,192]{3,2,1,0:T(8,128)(2,1)S(1)} %pad_maximum_fusion.15), channel_id=1, source_target_pairs={{0,24},{8,0},{16,8},{24,16},{1,25},{9,1},{17,9},{25,17},{2,26},{10... | collective-permute-start | bytes 331784 | tf_op jit(solution)/shard_map/ppermute | solution.py:95
  261.2 6.1 %collective-permute-start.69 = (bf16[3,3,32,192]{3,2,1,0:T(8,128)(2,1)S(1)}, bf16[3,3,32,192]{3,2,1,0:T(8,128)(2,1)S(1)}, u32[]{:S(2)}, u32[]{:S(2)}) collective-permute-start(bf16[3,3,32,192]{3,2,1,0:T(8,128)(2,1)S(1)} %pad_maximum_fusion.15), channel_id=1, source_target_pairs={{0,8},{8,16},{16,24},{24,0},{1,9},{9,17},{17,25},{25,1},{2,10},{10... | collective-permute-start | bytes 331784 | tf_op jit(solution)/shard_map/ppermute | solution.py:95
  (17 other events, 178.7 us)

commit v8 on v6

--- a/solution.py
+++ b/solution.py
@@ -99,11 +99,15 @@
 
     def apply_operator(current):
         rounded = current.astype(jnp.bfloat16)
-        left = shift(rounded, "gx", 1)
-        right = shift(rounded, "gx", -1)
-        strip = jnp.stack([left, rounded, right])
-        low = shift(strip, "gy", 1)
-        high = shift(strip, "gy", -1)
+        dense_rows = (column_depth, vector_count * block_rows // 128, 128)
+        flat = rounded.reshape(dense_rows)
+        left_flat = shift(flat, "gx", 1)
+        right_flat = shift(flat, "gx", -1)
+        strip = jnp.stack([left_flat, flat, right_flat])
+        low = shift(strip, "gy", 1).reshape(3, column_depth, vector_count, block_rows)
+        high = shift(strip, "gy", -1).reshape(3, column_depth, vector_count, block_rows)
+        left = left_flat.reshape(rounded.shape)
+        right = right_flat.reshape(rounded.shape)
         if not dense:
             matrices = lax.optimization_barrier((coupling[0, 0], left, right))[0]
             full = dense_coupling(matrices, cpl_dst[0, 0], cpl_src[0, 0], column_depth, order)

time: 286 us -> 328 us (1.15)
  matrix products: 52.5 us -> 143 us
  waiting for transfers between devices: 122 us -> 47 us
  local copies, waits for them, and re-layouts: 10.6 us -> 26.5 us
  starting transfers between devices: 78.3 us -> 87.7 us
    dot_general x64, matrix products: 50.5 us -> 141 us  [part(): jnp.einsum('kvj,tkij->tvi', cells, blocks, preferred_element_type=jnp.flo...]
    ppermute x64, waiting for transfers between devices: 103 us -> 28.9 us  [shift(): lax.ppermute(value, axis, [(i, (i + step) % count) for i in range(count)])]
    another operation x0 -> x47, local copies, waits for them, and re-layouts: none -> 7.99 us  [the longest x16 2.92 us: apply_operator(): low.reshape(3 * column_depth, vector_count, block_rows)]
    ppermute x64, starting transfers between devices: 65.6 us -> 73.5 us  [shift(): lax.ppermute(value, axis, [(i, (i + step) % count) for i in range(count)])]
    reshape x0 -> x47, local copies, waits for them, and re-layouts: none -> 4.95 us  [the longest x15 1.82 us: apply_operator(): flat = rounded.reshape(dense_rows)]
  transfers between devices with their start and end apart: 78 -> 78, of which waited for: 71 -> 56; matrix products, arithmetic and copies ran while one was open for 18% -> 38% of each run, Pallas kernels for 0% -> 0%
where the time goes in v8:
time: 328 us; the launch traced here: 326 us
  matrix products  143 us (44%)
  starting transfers between devices  87.7 us (27%)
  waiting for transfers between devices  47 us (14%)
  local copies, waits for them, and re-layouts  26.5 us (8%)
  other arithmetic  21.2 us (6%)
    dot_general x64, matrix products, part(): jnp.einsum('kvj,tkij->tvi', cells, blocks, preferred_element_type=jnp.flo...  141 us
    ppermute x64, starting transfers between devices, shift(): lax.ppermute(value, axis, [(i, (i + step) % count) for i in range(count)])  73.5 us
    ppermute x64, waiting for transfers between devices, shift(): lax.ppermute(value, axis, [(i, (i + step) % count) for i in range(count)])  28.9 us
    ppermute x14, waiting for transfers between devices, swap(): return lax.ppermute(v, axis, [(i, i ^ stride) for i in range(count)])  18 us
    ppermute x14, starting transfers between devices, swap(): return lax.ppermute(v, axis, [(i, i ^ stride) for i in range(count)])  14.2 us
    gather x1, local copies, waits for them, and re-layouts, dense_coupling(): jnp.take(matrices, index.reshape(-1), axis=0)  10.3 us
    another operation x6, other arithmetic, orthonormal(): factor = jnp.linalg.cholesky(gram_matrix)  7.19 us
  transfers between devices with their start and end apart: 78, of which 56 were waited for; matrix products, arithmetic and copies ran while one was open for 38% of the time, Pallas kernels for 0%

profile of v8, /device:TPU:0, one launch (start us, length us, event | category | flops | bytes accessed | tf_op | source)
XLA Modules:
  0.0 326.0 jit_solution(12766097305726316011)
XLA Ops:
  1.0 3.0 collective-permute-start
  10.8 10.3 %gather_fusion = bf16[81,192,192]{2,1,0:T(8,128)(2,1)} fusion(bf16[81,192,192]{2,1,0:T(8,128)(2,1)} %bitcast.861, s32[1024]{0:T(1024)S(1)} %pad_clamp_fusion), kind=kCustom, calls=%fused_computation | custom fusion | bytes 11944260 | tf_op jit(solution)/shard_map/jit(_take)/gather | solution.py:42
  21.1 4.2 %select_select_fusion = bf16[3,27,192,192]{3,2,1,0:T(8,128)(2,1)S(1)} fusion(bf16[3,27,192,192]{3,2,1,0:T(8,128)(2,1)} %bitcast.860, pred[3,27]{1,0:T(4,128)(4,1)S(1)} %compare_and_fusion, pred[3,27]{1,0:T(4,128)(4,1)S(1)} %and_reduce_fusion), kind=kLoop, calls=%fused_computation.1 | loop fusion | flops 5971968 | bytes 11944098 | tf_op jit(solution)/shard_map/jit(_where)/select_n | solution.py:46
  25.7 2.8 copy-done
  30.2 2.6 convolution_bitcast_fusion.30
  33.9 2.7 multiply_convert_fusion.2
  36.7 2.5 collective-permute-start.4
  43.2 2.2 collective-permute-start.7
  45.5 2.1 fusion.91
  47.8 2.6 convolution_bitcast_fusion.28
  51.5 2.7 fusion.186
  63.8 2.6 convolution_bitcast_fusion.26
  67.4 2.7 fusion.187
  77.5 2.1 fusion.93
  79.7 2.6 convolution_bitcast_fusion.24
  83.4 2.7 fusion.188
  95.7 2.6 convolution_bitcast_fusion.22
  99.3 2.7 fusion.189
  102.1 2.1 collective-permute-start.20
  109.9 2.1 fusion.95
  112.1 2.6 convolution_bitcast_fusion.20
  115.8 2.7 fusion.190
  125.8 2.1 fusion.96
  128.1 2.6 convolution_bitcast_fusion.18
  131.7 2.7 fusion.191
  141.8 2.1 fusion.97
  144.0 2.6 convolution_bitcast_fusion.16
  147.7 2.7 fusion.46
  156.0 2.2 collective-permute-done.34
  163.7 3.1 collective-permute-done.38
  166.8 2.9 cholesky.44
  171.1 2.4 custom-call.6
  174.7 2.5 collective-permute-start.40
  179.9 2.1 fusion.98
  182.1 2.6 convolution_bitcast_fusion.14
  185.3 2.7 fusion.49
  188.1 2.3 collective-permute-start.43
  196.2 2.1 fusion.99
  198.5 2.6 convolution_bitcast_fusion.12
  202.1 2.7 fusion.54
  210.4 2.3 collective-permute-start.50
  212.8 2.1 fusion.100
  215.1 2.6 convolution_bitcast_fusion.10
  218.7 2.7 fusion.59
  228.8 2.1 fusion.101
  231.1 2.6 convolution_bitcast_fusion.8
  234.7 2.7 fusion.192
  244.8 2.1 fusion.102
  247.0 2.6 convolution_bitcast_fusion.6
  250.7 2.7 fusion.193
  260.7 2.1 fusion.103
  263.0 2.6 convolution_bitcast_fusion.4
  266.6 2.7 fusion.194
  269.4 2.1 collective-permute-start.63
  277.2 2.1 fusion.104
  279.4 2.6 convolution_bitcast_fusion.2
  283.1 2.7 fusion.195
  293.1 2.1 fusion.105
  295.4 2.6 convolution_bitcast_fusion
  299.0 2.7 fusion.89
  307.3 2.2 collective-permute-done.73
  315.0 3.1 collective-permute-done.77
  318.2 2.9 cholesky.55
  322.5 2.4 custom-call.7
  (313 shorter events, 155.4 us)
Async XLA Ops:
  1.0 6.0 %collective-permute-start = (bf16[3,48,128]{2,1,0:T(8,128)(2,1)S(1)}, bf16[3,48,128]{2,1,0:T(8,128)(2,1)S(1)}, u32[]{:S(2)}, u32[]{:S(2)}) collective-permute-start(bf16[3,48,128]{2,1,0:T(8,128)(2,1)S(1)} %convert_element_type.75), channel_id=1, source_target_pairs={{0,8},{8,16},{16,24},{24,0},{1,9},{9,17},{17,25},{25,1},{2,10},{10... | collective-permute-start | bytes 110600 | tf_op jit(solution)/shard_map/ppermute | solution.py:95
  4.0 4.0 %collective-permute-start.1 = (bf16[3,48,128]{2,1,0:T(8,128)(2,1)S(1)}, bf16[3,48,128]{2,1,0:T(8,128)(2,1)S(1)}, u32[]{:S(2)}, u32[]{:S(2)}) collective-permute-start(bf16[3,48,128]{2,1,0:T(8,128)(2,1)S(1)} %convert_element_type.75), channel_id=1, source_target_pairs={{0,24},{8,0},{16,8},{24,16},{1,25},{9,1},{17,9},{25,17},{2,26},{10... | collective-permute-start | bytes 110600 | tf_op jit(solution)/shard_map/ppermute | solution.py:95
  8.6 20.5 %collective-permute-start.3 = (bf16[3,3,48,128]{3,2,1,0:T(8,128)(2,1)}, bf16[3,3,48,128]{3,2,1,0:T(8,128)(2,1)}, u32[]{:S(2)}, u32[]{:S(2)}) collective-permute-start(bf16[3,3,48,128]{3,2,1,0:T(8,128)(2,1)} %pad_maximum_fusion), channel_id=1, source_target_pairs={{0,7},{1,0},{2,1},{3,2},{4,3},{5,4},{6,5},{7,6},{8,15},{9,8},{10,9... | collective-permute-start | bytes 331784 | tf_op jit(solution)/shard_map/ppermute | solution.py:95
  10.6 22.2 %collective-permute-start.2 = (bf16[3,3,48,128]{3,2,1,0:T(8,128)(2,1)}, bf16[3,3,48,128]{3,2,1,0:T(8,128)(2,1)}, u32[]{:S(2)}, u32[]{:S(2)}) collective-permute-start(bf16[3,3,48,128]{3,2,1,0:T(8,128)(2,1)} %pad_maximum_fusion), channel_id=1, source_target_pairs={{0,1},{1,2},{2,3},{3,4},{4,5},{5,6},{6,7},{7,0},{8,9},{9,10},{10,1... | collective-permute-start | bytes 331784 | tf_op jit(solution)/shard_map/ppermute | solution.py:95
  36.7 5.2 %collective-permute-start.4 = (bf16[3,48,128]{2,1,0:T(8,128)(2,1)S(1)}, bf16[3,48,128]{2,1,0:T(8,128)(2,1)S(1)}, u32[]{:S(2)}, u32[]{:S(2)}) collective-permute-start(bf16[3,48,128]{2,1,0:T(8,128)(2,1)S(1)} %reshape.271), channel_id=1, source_target_pairs={{0,8},{8,16},{16,24},{24,0},{1,9},{9,17},{17,25},{25,1},{2,10},{10... | collective-permute-start | bytes 110600 | tf_op jit(solution)/shard_map/ppermute | solution.py:95
  39.2 4.0 %collective-permute-start.5 = (bf16[3,48,128]{2,1,0:T(8,128)(2,1)S(1)}, bf16[3,48,128]{2,1,0:T(8,128)(2,1)S(1)}, u32[]{:S(2)}, u32[]{:S(2)}) collective-permute-start(bf16[3,48,128]{2,1,0:T(8,128)(2,1)S(1)} %reshape.271), channel_id=1, source_target_pairs={{0,24},{8,0},{16,8},{24,16},{1,25},{9,1},{17,9},{25,17},{2,26},{10... | collective-permute-start | bytes 110600 | tf_op jit(solution)/shard_map/ppermute | solution.py:95
  43.2 4.5 %collective-permute-start.7 = (bf16[3,3,48,128]{3,2,1,0:T(8,128)(2,1)S(1)}, bf16[3,3,48,128]{3,2,1,0:T(8,128)(2,1)S(1)}, u32[]{:S(2)}, u32[]{:S(2)}) collective-permute-start(bf16[3,3,48,128]{3,2,1,0:T(8,128)(2,1)S(1)} %pad_maximum_fusion.1), channel_id=1, source_target_pairs={{0,7},{1,0},{2,1},{3,2},{4,3},{5,4},{6,5},{7,6},{8,15},{9,8},{10,9... | collective-permute-start | bytes 331784 | tf_op jit(solution)/shard_map/ppermute | solution.py:95
  45.3 6.0 %collective-permute-start.6 = (bf16[3,3,48,128]{3,2,1,0:T(8,128)(2,1)S(1)}, bf16[3,3,48,128]{3,2,1,0:T(8,128)(2,1)S(1)}, u32[]{:S(2)}, u32[]{:S(2)}) collective-permute-start(bf16[3,3,48,128]{3,2,1,0:T(8,128)(2,1)S(1)} %pad_maximum_fusion.1), channel_id=1, source_target_pairs={{0,1},{1,2},{2,3},{3,4},{4,5},{5,6},{6,7},{7,0},{8,9},{9,10},{10,1... | collective-permute-start | bytes 331784 | tf_op jit(solution)/shard_map/ppermute | solution.py:95
  54.3 4.9 %collective-permute-start.8 = (bf16[3,48,128]{2,1,0:T(8,128)(2,1)S(1)}, bf16[3,48,128]{2,1,0:T(8,128)(2,1)S(1)}, u32[]{:S(2)}, u32[]{:S(2)}) collective-permute-start(bf16[3,48,128]{2,1,0:T(8,128)(2,1)S(1)} %reshape.274), channel_id=1, source_target_pairs={{0,8},{8,16},{16,24},{24,0},{1,9},{9,17},{17,25},{25,1},{2,10},{10... | collective-permute-start | bytes 110600 | tf_op jit(solution)/shard_map/ppermute | solution.py:95
  55.7 4.0 %collective-permute-start.9 = (bf16[3,48,128]{2,1,0:T(8,128)(2,1)S(1)}, bf16[3,48,128]{2,1,0:T(8,128)(2,1)S(1)}, u32[]{:S(2)}, u32[]{:S(2)}) collective-permute-start(bf16[3,48,128]{2,1,0:T(8,128)(2,1)S(1)} %reshape.274), channel_id=1, source_target_pairs={{0,24},{8,0},{16,8},{24,16},{1,25},{9,1},{17,9},{25,17},{2,26},{10... | collective-permute-start | bytes 110600 | tf_op jit(solution)/shard_map/ppermute | solution.py:95
  59.7 3.9 %collective-permute-start.11 = (bf16[3,3,48,128]{3,2,1,0:T(8,128)(2,1)S(1)}, bf16[3,3,48,128]{3,2,1,0:T(8,128)(2,1)S(1)}, u32[]{:S(2)}, u32[]{:S(2)}) collective-permute-start(bf16[3,3,48,128]{3,2,1,0:T(8,128)(2,1)S(1)} %pad_maximum_fusion.2), channel_id=1, source_target_pairs={{0,7},{1,0},{2,1},{3,2},{4,3},{5,4},{6,5},{7,6},{8,15},{9,8},{10,9... | collective-permute-start | bytes 331784 | tf_op jit(solution)/shard_map/ppermute | solution.py:95
  61.3 6.0 %collective-permute-start.10 = (bf16[3,3,48,128]{3,2,1,0:T(8,128)(2,1)S(1)}, bf16[3,3,48,128]{3,2,1,0:T(8,128)(2,1)S(1)}, u32[]{:S(2)}, u32[]{:S(2)}) collective-permute-start(bf16[3,3,48,128]{3,2,1,0:T(8,128)(2,1)S(1)} %pad_maximum_fusion.2), channel_id=1, source_target_pairs={{0,1},{1,2},{2,3},{3,4},{4,5},{5,6},{6,7},{7,0},{8,9},{9,10},{10,1... | collective-permute-start | bytes 331784 | tf_op jit(solution)/shard_map/ppermute | solution.py:95
  70.2 4.9 %collective-permute-start.12 = (bf16[3,48,128]{2,1,0:T(8,128)(2,1)S(1)}, bf16[3,48,128]{2,1,0:T(8,128)(2,1)S(1)}, u32[]{:S(2)}, u32[]{:S(2)}) collective-permute-start(bf16[3,48,128]{2,1,0:T(8,128)(2,1)S(1)} %reshape.277), channel_id=1, source_target_pairs={{0,8},{8,16},{16,24},{24,0},{1,9},{9,17},{17,25},{25,1},{2,10},{10... | collective-permute-start | bytes 110600 | tf_op jit(solution)/shard_map/ppermute | solution.py:95
  71.7 4.0 %collective-permute-start.13 = (bf16[3,48,128]{2,1,0:T(8,128)(2,1)S(1)}, bf16[3,48,128]{2,1,0:T(8,128)(2,1)S(1)}, u32[]{:S(2)}, u32[]{:S(2)}) collective-permute-start(bf16[3,48,128]{2,1,0:T(8,128)(2,1)S(1)} %reshape.277), channel_id=1, source_target_pairs={{0,24},{8,0},{16,8},{24,16},{1,25},{9,1},{17,9},{25,17},{2,26},{10... | collective-permute-start | bytes 110600 | tf_op jit(solution)/shard_map/ppermute | solution.py:95
  75.7 3.9 %collective-permute-start.15 = (bf16[3,3,48,128]{3,2,1,0:T(8,128)(2,1)S(1)}, bf16[3,3,48,128]{3,2,1,0:T(8,128)(2,1)S(1)}, u32[]{:S(2)}, u32[]{:S(2)}) collective-permute-start(bf16[3,3,48,128]{3,2,1,0:T(8,128)(2,1)S(1)} %pad_maximum_fusion.3), channel_id=1, source_target_pairs={{0,7},{1,0},{2,1},{3,2},{4,3},{5,4},{6,5},{7,6},{8,15},{9,8},{10,9... | collective-permute-start | bytes 331784 | tf_op jit(solution)/shard_map/ppermute | solution.py:95
  77.3 6.0 %collective-permute-start.14 = (bf16[3,3,48,128]{3,2,1,0:T(8,128)(2,1)S(1)}, bf16[3,3,48,128]{3,2,1,0:T(8,128)(2,1)S(1)}, u32[]{:S(2)}, u32[]{:S(2)}) collective-permute-start(bf16[3,3,48,128]{3,2,1,0:T(8,128)(2,1)S(1)} %pad_maximum_fusion.3), channel_id=1, source_target_pairs={{0,1},{1,2},{2,3},{3,4},{4,5},{5,6},{6,7},{7,0},{8,9},{9,10},{10,1... | collective-permute-start | bytes 331784 | tf_op jit(solution)/shard_map/ppermute | solution.py:95
  86.2 4.9 %collective-permute-start.16 = (bf16[3,48,128]{2,1,0:T(8,128)(2,1)S(1)}, bf16[3,48,128]{2,1,0:T(8,128)(2,1)S(1)}, u32[]{:S(2)}, u32[]{:S(2)}) collective-permute-start(bf16[3,48,128]{2,1,0:T(8,128)(2,1)S(1)} %reshape.280), channel_id=1, source_target_pairs={{0,8},{8,16},{16,24},{24,0},{1,9},{9,17},{17,25},{25,1},{2,10},{10... | collective-permute-start | bytes 110600 | tf_op jit(solution)/shard_map/ppermute | solution.py:95
  87.7 4.0 %collective-permute-start.17 = (bf16[3,48,128]{2,1,0:T(8,128)(2,1)S(1)}, bf16[3,48,128]{2,1,0:T(8,128)(2,1)S(1)}, u32[]{:S(2)}, u32[]{:S(2)}) collective-permute-start(bf16[3,48,128]{2,1,0:T(8,128)(2,1)S(1)} %reshape.280), channel_id=1, source_target_pairs={{0,24},{8,0},{16,8},{24,16},{1,25},{9,1},{17,9},{25,17},{2,26},{10... | collective-permute-start | bytes 110600 | tf_op jit(solution)/shard_map/ppermute | solution.py:95
  91.7 3.8 %collective-permute-start.19 = (bf16[3,3,48,128]{3,2,1,0:T(8,128)(2,1)S(1)}, bf16[3,3,48,128]{3,2,1,0:T(8,128)(2,1)S(1)}, u32[]{:S(2)}, u32[]{:S(2)}) collective-permute-start(bf16[3,3,48,128]{3,2,1,0:T(8,128)(2,1)S(1)} %pad_maximum_fusion.4), channel_id=1, source_target_pairs={{0,7},{1,0},{2,1},{3,2},{4,3},{5,4},{6,5},{7,6},{8,15},{9,8},{10,9... | collective-permute-start | bytes 331784 | tf_op jit(solution)/shard_map/ppermute | solution.py:95
  93.2 6.0 %collective-permute-start.18 = (bf16[3,3,48,128]{3,2,1,0:T(8,128)(2,1)S(1)}, bf16[3,3,48,128]{3,2,1,0:T(8,128)(2,1)S(1)}, u32[]{:S(2)}, u32[]{:S(2)}) collective-permute-start(bf16[3,3,48,128]{3,2,1,0:T(8,128)(2,1)S(1)} %pad_maximum_fusion.4), channel_id=1, source_target_pairs={{0,1},{1,2},{2,3},{3,4},{4,5},{5,6},{6,7},{7,0},{8,9},{9,10},{10,1... | collective-permute-start | bytes 331784 | tf_op jit(solution)/shard_map/ppermute | solution.py:95
  102.1 4.9 %collective-permute-start.20 = (bf16[3,48,128]{2,1,0:T(8,128)(2,1)S(1)}, bf16[3,48,128]{2,1,0:T(8,128)(2,1)S(1)}, u32[]{:S(2)}, u32[]{:S(2)}) collective-permute-start(bf16[3,48,128]{2,1,0:T(8,128)(2,1)S(1)} %reshape.283), channel_id=1, source_target_pairs={{0,8},{8,16},{16,24},{24,0},{1,9},{9,17},{17,25},{25,1},{2,10},{10... | collective-permute-start | bytes 110600 | tf_op jit(solution)/shard_map/ppermute | solution.py:95
  104.3 4.0 %collective-permute-start.21 = (bf16[3,48,128]{2,1,0:T(8,128)(2,1)S(1)}, bf16[3,48,128]{2,1,0:T(8,128)(2,1)S(1)}, u32[]{:S(2)}, u32[]{:S(2)}) collective-permute-start(bf16[3,48,128]{2,1,0:T(8,128)(2,1)S(1)} %reshape.283), channel_id=1, source_target_pairs={{0,24},{8,0},{16,8},{24,16},{1,25},{9,1},{17,9},{25,17},{2,26},{10... | collective-permute-start | bytes 110600 | tf_op jit(solution)/shard_map/ppermute | solution.py:95
  109.7 6.0 %collective-permute-start.22 = (bf16[3,3,48,128]{3,2,1,0:T(8,128)(2,1)S(1)}, bf16[3,3,48,128]{3,2,1,0:T(8,128)(2,1)S(1)}, u32[]{:S(2)}, u32[]{:S(2)}) collective-permute-start(bf16[3,3,48,128]{3,2,1,0:T(8,128)(2,1)S(1)} %pad_maximum_fusion.5), channel_id=1, source_target_pairs={{0,1},{1,2},{2,3},{3,4},{4,5},{5,6},{6,7},{7,0},{8,9},{9,10},{10,1... | collective-permute-start | bytes 331784 | tf_op jit(solution)/shard_map/ppermute | solution.py:95
  118.6 4.9 %collective-permute-start.24 = (bf16[3,48,128]{2,1,0:T(8,128)(2,1)S(1)}, bf16[3,48,128]{2,1,0:T(8,128)(2,1)S(1)}, u32[]{:S(2)}, u32[]{:S(2)}) collective-permute-start(bf16[3,48,128]{2,1,0:T(8,128)(2,1)S(1)} %reshape.286), channel_id=1, source_target_pairs={{0,8},{8,16},{16,24},{24,0},{1,9},{9,17},{17,25},{25,1},{2,10},{10... | collective-permute-start | bytes 110600 | tf_op jit(solution)/shard_map/ppermute | solution.py:95
  120.2 4.0 %collective-permute-start.25 = (bf16[3,48,128]{2,1,0:T(8,128)(2,1)S(1)}, bf16[3,48,128]{2,1,0:T(8,128)(2,1)S(1)}, u32[]{:S(2)}, u32[]{:S(2)}) collective-permute-start(bf16[3,48,128]{2,1,0:T(8,128)(2,1)S(1)} %reshape.286), channel_id=1, source_target_pairs={{0,24},{8,0},{16,8},{24,16},{1,25},{9,1},{17,9},{25,17},{2,26},{10... | collective-permute-start | bytes 110600 | tf_op jit(solution)/shard_map/ppermute | solution.py:95
  125.6 6.0 %collective-permute-start.26 = (bf16[3,3,48,128]{3,2,1,0:T(8,128)(2,1)S(1)}, bf16[3,3,48,128]{3,2,1,0:T(8,128)(2,1)S(1)}, u32[]{:S(2)}, u32[]{:S(2)}) collective-permute-start(bf16[3,3,48,128]{3,2,1,0:T(8,128)(2,1)S(1)} %pad_maximum_fusion.6), channel_id=1, source_target_pairs={{0,1},{1,2},{2,3},{3,4},{4,5},{5,6},{6,7},{7,0},{8,9},{9,10},{10,1... | collective-permute-start | bytes 331784 | tf_op jit(solution)/shard_map/ppermute | solution.py:95
  134.5 4.9 %collective-permute-start.28 = (bf16[3,48,128]{2,1,0:T(8,128)(2,1)S(1)}, bf16[3,48,128]{2,1,0:T(8,128)(2,1)S(1)}, u32[]{:S(2)}, u32[]{:S(2)}) collective-permute-start(bf16[3,48,128]{2,1,0:T(8,128)(2,1)S(1)} %reshape.289), channel_id=1, source_target_pairs={{0,8},{8,16},{16,24},{24,0},{1,9},{9,17},{17,25},{25,1},{2,10},{10... | collective-permute-start | bytes 110600 | tf_op jit(solution)/shard_map/ppermute | solution.py:95
  136.2 4.0 %collective-permute-start.29 = (bf16[3,48,128]{2,1,0:T(8,128)(2,1)S(1)}, bf16[3,48,128]{2,1,0:T(8,128)(2,1)S(1)}, u32[]{:S(2)}, u32[]{:S(2)}) collective-permute-start(bf16[3,48,128]{2,1,0:T(8,128)(2,1)S(1)} %reshape.289), channel_id=1, source_target_pairs={{0,24},{8,0},{16,8},{24,16},{1,25},{9,1},{17,9},{25,17},{2,26},{10... | collective-permute-start | bytes 110600 | tf_op jit(solution)/shard_map/ppermute | solution.py:95
  141.6 6.0 %collective-permute-start.30 = (bf16[3,3,48,128]{3,2,1,0:T(8,128)(2,1)S(1)}, bf16[3,3,48,128]{3,2,1,0:T(8,128)(2,1)S(1)}, u32[]{:S(2)}, u32[]{:S(2)}) collective-permute-start(bf16[3,3,48,128]{3,2,1,0:T(8,128)(2,1)S(1)} %pad_maximum_fusion.7), channel_id=1, source_target_pairs={{0,1},{1,2},{2,3},{3,4},{4,5},{5,6},{6,7},{7,0},{8,9},{9,10},{10,1... | collective-permute-start | bytes 331784 | tf_op jit(solution)/shard_map/ppermute | solution.py:95
  150.6 3.8 %collective-permute-start.32 = (f32[32,32]{0,1:T(8,128)S(1)}, f32[32,32]{0,1:T(8,128)S(1)}, u32[]{:S(2)}, u32[]{:S(2)}) collective-permute-start(f32[32,32]{0,1:T(8,128)S(1)} %convolution_bitcast_fusion.67), channel_id=1, source_target_pairs={{0,8},{8,0},{16,24},{24,16},{1,9},{9,1},{17,25},{25,17},{2,10},{10... | collective-permute-start | bytes 12296 | tf_op jit(solution)/shard_map/ppermute | solution.py:58
  153.5 4.6 %collective-permute-start.34 = (f32[32,32]{0,1:T(8,128)S(1)}, f32[32,32]{0,1:T(8,128)S(1)}, u32[]{:S(2)}, u32[]{:S(2)}) collective-permute-start(f32[32,32]{0,1:T(8,128)S(1)} %convolution_bitcast_fusion.67), channel_id=1, source_target_pairs={{0,24},{8,16},{16,8},{24,0},{1,25},{9,17},{17,9},{25,1},{2,26},{10... | collective-permute-start | bytes 12296 | tf_op jit(solution)/shard_map/ppermute | solution.py:58
  158.2 3.8 %collective-permute-start.36 = (f32[32,32]{0,1:T(8,128)S(1)}, f32[32,32]{0,1:T(8,128)S(1)}, u32[]{:S(2)}, u32[]{:S(2)}) collective-permute-start(f32[32,32]{0,1:T(8,128)S(1)} %add_add_fusion.3), channel_id=1, source_target_pairs={{0,2},{1,3},{2,0},{3,1},{4,6},{5,7},{6,4},{7,5},{8,10},{9,11},{10,... | collective-permute-start | bytes 12296 | tf_op jit(solution)/shard_map/ppermute | solution.py:58
  162.0 4.7 %collective-permute-start.38 = (f32[32,32]{0,1:T(8,128)S(1)}, f32[32,32]{0,1:T(8,128)S(1)}, u32[]{:S(2)}, u32[]{:S(2)}) collective-permute-start(f32[32,32]{0,1:T(8,128)S(1)} %add_add_fusion.2), channel_id=1, source_target_pairs={{0,4},{1,5},{2,6},{3,7},{4,0},{5,1},{6,2},{7,3},{8,12},{9,13},{10,... | collective-permute-start | bytes 12296 | tf_op jit(solution)/shard_map/ppermute | solution.py:58
  174.2 4.9 %collective-permute-start.39 = (bf16[3,48,128]{2,1,0:T(8,128)(2,1)S(1)}, bf16[3,48,128]{2,1,0:T(8,128)(2,1)S(1)}, u32[]{:S(2)}, u32[]{:S(2)}) collective-permute-start(bf16[3,48,128]{2,1,0:T(8,128)(2,1)S(1)} %reshape.292), channel_id=1, source_target_pairs={{0,8},{8,16},{16,24},{24,0},{1,9},{9,17},{17,25},{25,1},{2,10},{10... | collective-permute-start | bytes 110600 | tf_op jit(solution)/shard_map/ppermute | solution.py:95
  174.7 4.4 %collective-permute-start.40 = (bf16[3,48,128]{2,1,0:T(8,128)(2,1)S(1)}, bf16[3,48,128]{2,1,0:T(8,128)(2,1)S(1)}, u32[]{:S(2)}, u32[]{:S(2)}) collective-permute-start(bf16[3,48,128]{2,1,0:T(8,128)(2,1)S(1)} %reshape.292), channel_id=1, source_target_pairs={{0,24},{8,0},{16,8},{24,16},{1,25},{9,1},{17,9},{25,17},{2,26},{10... | collective-permute-start | bytes 110600 | tf_op jit(solution)/shard_map/ppermute | solution.py:95
  179.2 6.0 %collective-permute-start.41 = (bf16[3,3,48,128]{3,2,1,0:T(8,128)(2,1)S(1)}, bf16[3,3,48,128]{3,2,1,0:T(8,128)(2,1)S(1)}, u32[]{:S(2)}, u32[]{:S(2)}) collective-permute-start(bf16[3,3,48,128]{3,2,1,0:T(8,128)(2,1)S(1)} %pad_maximum_fusion.8), channel_id=1, source_target_pairs={{0,1},{1,2},{2,3},{3,4},{4,5},{5,6},{6,7},{7,0},{8,9},{9,10},{10,1... | collective-permute-start | bytes 331784 | tf_op jit(solution)/shard_map/ppermute | solution.py:95
  188.1 5.2 %collective-permute-start.43 = (bf16[3,48,128]{2,1,0:T(8,128)(2,1)S(1)}, bf16[3,48,128]{2,1,0:T(8,128)(2,1)S(1)}, u32[]{:S(2)}, u32[]{:S(2)}) collective-permute-start(bf16[3,48,128]{2,1,0:T(8,128)(2,1)S(1)} %reshape.295), channel_id=1, source_target_pairs={{0,8},{8,16},{16,24},{24,0},{1,9},{9,17},{17,25},{25,1},{2,10},{10... | collective-permute-start | bytes 110600 | tf_op jit(solution)/shard_map/ppermute | solution.py:95
  190.4 4.0 %collective-permute-start.44 = (bf16[3,48,128]{2,1,0:T(8,128)(2,1)S(1)}, bf16[3,48,128]{2,1,0:T(8,128)(2,1)S(1)}, u32[]{:S(2)}, u32[]{:S(2)}) collective-permute-start(bf16[3,48,128]{2,1,0:T(8,128)(2,1)S(1)} %reshape.295), channel_id=1, source_target_pairs={{0,24},{8,0},{16,8},{24,16},{1,25},{9,1},{17,9},{25,17},{2,26},{10... | collective-permute-start | bytes 110600 | tf_op jit(solution)/shard_map/ppermute | solution.py:95
  194.4 4.0 %collective-permute-start.46 = (bf16[3,3,48,128]{3,2,1,0:T(8,128)(2,1)S(1)}, bf16[3,3,48,128]{3,2,1,0:T(8,128)(2,1)S(1)}, u32[]{:S(2)}, u32[]{:S(2)}) collective-permute-start(bf16[3,3,48,128]{3,2,1,0:T(8,128)(2,1)S(1)} %pad_maximum_fusion.9), channel_id=1, source_target_pairs={{0,7},{1,0},{2,1},{3,2},{4,3},{5,4},{6,5},{7,6},{8,15},{9,8},{10,9... | collective-permute-start | bytes 331784 | tf_op jit(solution)/shard_map/ppermute | solution.py:95
  196.0 6.0 %collective-permute-start.45 = (bf16[3,3,48,128]{3,2,1,0:T(8,128)(2,1)S(1)}, bf16[3,3,48,128]{3,2,1,0:T(8,128)(2,1)S(1)}, u32[]{:S(2)}, u32[]{:S(2)}) collective-permute-start(bf16[3,3,48,128]{3,2,1,0:T(8,128)(2,1)S(1)} %pad_maximum_fusion.9), channel_id=1, source_target_pairs={{0,1},{1,2},{2,3},{3,4},{4,5},{5,6},{6,7},{7,0},{8,9},{9,10},{10,1... | collective-permute-start | bytes 331784 | tf_op jit(solution)/shard_map/ppermute | solution.py:95
  205.0 4.9 %collective-permute-start.47 = (bf16[3,48,128]{2,1,0:T(8,128)(2,1)S(1)}, bf16[3,48,128]{2,1,0:T(8,128)(2,1)S(1)}, u32[]{:S(2)}, u32[]{:S(2)}) collective-permute-start(bf16[3,48,128]{2,1,0:T(8,128)(2,1)S(1)} %reshape.298), channel_id=1, source_target_pairs={{0,8},{8,16},{16,24},{24,0},{1,9},{9,17},{17,25},{25,1},{2,10},{10... | collective-permute-start | bytes 110600 | tf_op jit(solution)/shard_map/ppermute | solution.py:95
  206.4 4.0 %collective-permute-start.48 = (bf16[3,48,128]{2,1,0:T(8,128)(2,1)S(1)}, bf16[3,48,128]{2,1,0:T(8,128)(2,1)S(1)}, u32[]{:S(2)}, u32[]{:S(2)}) collective-permute-start(bf16[3,48,128]{2,1,0:T(8,128)(2,1)S(1)} %reshape.298), channel_id=1, source_target_pairs={{0,24},{8,0},{16,8},{24,16},{1,25},{9,1},{17,9},{25,17},{2,26},{10... | collective-permute-start | bytes 110600 | tf_op jit(solution)/shard_map/ppermute | solution.py:95
  210.4 4.6 %collective-permute-start.50 = (bf16[3,3,48,128]{3,2,1,0:T(8,128)(2,1)S(1)}, bf16[3,3,48,128]{3,2,1,0:T(8,128)(2,1)S(1)}, u32[]{:S(2)}, u32[]{:S(2)}) collective-permute-start(bf16[3,3,48,128]{3,2,1,0:T(8,128)(2,1)S(1)} %pad_maximum_fusion.10), channel_id=1, source_target_pairs={{0,7},{1,0},{2,1},{3,2},{4,3},{5,4},{6,5},{7,6},{8,15},{9,8},{10,9... | collective-permute-start | bytes 331784 | tf_op jit(solution)/shard_map/ppermute | solution.py:95
  212.6 6.0 %collective-permute-start.49 = (bf16[3,3,48,128]{3,2,1,0:T(8,128)(2,1)S(1)}, bf16[3,3,48,128]{3,2,1,0:T(8,128)(2,1)S(1)}, u32[]{:S(2)}, u32[]{:S(2)}) collective-permute-start(bf16[3,3,48,128]{3,2,1,0:T(8,128)(2,1)S(1)} %pad_maximum_fusion.10), channel_id=1, source_target_pairs={{0,1},{1,2},{2,3},{3,4},{4,5},{5,6},{6,7},{7,0},{8,9},{9,10},{10,1... | collective-permute-start | bytes 331784 | tf_op jit(solution)/shard_map/ppermute | solution.py:95
  221.6 4.9 %collective-permute-start.51 = (bf16[3,48,128]{2,1,0:T(8,128)(2,1)S(1)}, bf16[3,48,128]{2,1,0:T(8,128)(2,1)S(1)}, u32[]{:S(2)}, u32[]{:S(2)}) collective-permute-start(bf16[3,48,128]{2,1,0:T(8,128)(2,1)S(1)} %reshape.301), channel_id=1, source_target_pairs={{0,8},{8,16},{16,24},{24,0},{1,9},{9,17},{17,25},{25,1},{2,10},{10... | collective-permute-start | bytes 110600 | tf_op jit(solution)/shard_map/ppermute | solution.py:95
  223.2 4.0 %collective-permute-start.52 = (bf16[3,48,128]{2,1,0:T(8,128)(2,1)S(1)}, bf16[3,48,128]{2,1,0:T(8,128)(2,1)S(1)}, u32[]{:S(2)}, u32[]{:S(2)}) collective-permute-start(bf16[3,48,128]{2,1,0:T(8,128)(2,1)S(1)} %reshape.301), channel_id=1, source_target_pairs={{0,24},{8,0},{16,8},{24,16},{1,25},{9,1},{17,9},{25,17},{2,26},{10... | collective-permute-start | bytes 110600 | tf_op jit(solution)/shard_map/ppermute | solution.py:95
  227.1 3.8 %collective-permute-start.54 = (bf16[3,3,48,128]{3,2,1,0:T(8,128)(2,1)S(1)}, bf16[3,3,48,128]{3,2,1,0:T(8,128)(2,1)S(1)}, u32[]{:S(2)}, u32[]{:S(2)}) collective-permute-start(bf16[3,3,48,128]{3,2,1,0:T(8,128)(2,1)S(1)} %pad_maximum_fusion.11), channel_id=1, source_target_pairs={{0,7},{1,0},{2,1},{3,2},{4,3},{5,4},{6,5},{7,6},{8,15},{9,8},{10,9... | collective-permute-start | bytes 331784 | tf_op jit(solution)/shard_map/ppermute | solution.py:95
  228.6 6.0 %collective-permute-start.53 = (bf16[3,3,48,128]{3,2,1,0:T(8,128)(2,1)S(1)}, bf16[3,3,48,128]{3,2,1,0:T(8,128)(2,1)S(1)}, u32[]{:S(2)}, u32[]{:S(2)}) collective-permute-start(bf16[3,3,48,128]{3,2,1,0:T(8,128)(2,1)S(1)} %pad_maximum_fusion.11), channel_id=1, source_target_pairs={{0,1},{1,2},{2,3},{3,4},{4,5},{5,6},{6,7},{7,0},{8,9},{9,10},{10,1... | collective-permute-start | bytes 331784 | tf_op jit(solution)/shard_map/ppermute | solution.py:95
  237.5 4.9 %collective-permute-start.55 = (bf16[3,48,128]{2,1,0:T(8,128)(2,1)S(1)}, bf16[3,48,128]{2,1,0:T(8,128)(2,1)S(1)}, u32[]{:S(2)}, u32[]{:S(2)}) collective-permute-start(bf16[3,48,128]{2,1,0:T(8,128)(2,1)S(1)} %reshape.304), channel_id=1, source_target_pairs={{0,8},{8,16},{16,24},{24,0},{1,9},{9,17},{17,25},{25,1},{2,10},{10... | collective-permute-start | bytes 110600 | tf_op jit(solution)/shard_map/ppermute | solution.py:95
  239.2 4.0 %collective-permute-start.56 = (bf16[3,48,128]{2,1,0:T(8,128)(2,1)S(1)}, bf16[3,48,128]{2,1,0:T(8,128)(2,1)S(1)}, u32[]{:S(2)}, u32[]{:S(2)}) collective-permute-start(bf16[3,48,128]{2,1,0:T(8,128)(2,1)S(1)} %reshape.304), channel_id=1, source_target_pairs={{0,24},{8,0},{16,8},{24,16},{1,25},{9,1},{17,9},{25,17},{2,26},{10... | collective-permute-start | bytes 110600 | tf_op jit(solution)/shard_map/ppermute | solution.py:95
  244.6 6.0 %collective-permute-start.57 = (bf16[3,3,48,128]{3,2,1,0:T(8,128)(2,1)S(1)}, bf16[3,3,48,128]{3,2,1,0:T(8,128)(2,1)S(1)}, u32[]{:S(2)}, u32[]{:S(2)}) collective-permute-start(bf16[3,3,48,128]{3,2,1,0:T(8,128)(2,1)S(1)} %pad_maximum_fusion.12), channel_id=1, source_target_pairs={{0,1},{1,2},{2,3},{3,4},{4,5},{5,6},{6,7},{7,0},{8,9},{9,10},{10,1... | collective-permute-start | bytes 331784 | tf_op jit(solution)/shard_map/ppermute | solution.py:95
  253.5 4.9 %collective-permute-start.59 = (bf16[3,48,128]{2,1,0:T(8,128)(2,1)S(1)}, bf16[3,48,128]{2,1,0:T(8,128)(2,1)S(1)}, u32[]{:S(2)}, u32[]{:S(2)}) collective-permute-start(bf16[3,48,128]{2,1,0:T(8,128)(2,1)S(1)} %reshape.307), channel_id=1, source_target_pairs={{0,8},{8,16},{16,24},{24,0},{1,9},{9,17},{17,25},{25,1},{2,10},{10... | collective-permute-start | bytes 110600 | tf_op jit(solution)/shard_map/ppermute | solution.py:95
  255.1 4.0 %collective-permute-start.60 = (bf16[3,48,128]{2,1,0:T(8,128)(2,1)S(1)}, bf16[3,48,128]{2,1,0:T(8,128)(2,1)S(1)}, u32[]{:S(2)}, u32[]{:S(2)}) collective-permute-start(bf16[3,48,128]{2,1,0:T(8,128)(2,1)S(1)} %reshape.307), channel_id=1, source_target_pairs={{0,24},{8,0},{16,8},{24,16},{1,25},{9,1},{17,9},{25,17},{2,26},{10... | collective-permute-start | bytes 110600 | tf_op jit(solution)/shard_map/ppermute | solution.py:95
  260.5 6.0 %collective-permute-start.61 = (bf16[3,3,48,128]{3,2,1,0:T(8,128)(2,1)S(1)}, bf16[3,3,48,128]{3,2,1,0:T(8,128)(2,1)S(1)}, u32[]{:S(2)}, u32[]{:S(2)}) collective-permute-start(bf16[3,3,48,128]{3,2,1,0:T(8,128)(2,1)S(1)} %pad_maximum_fusion.13), channel_id=1, source_target_pairs={{0,1},{1,2},{2,3},{3,4},{4,5},{5,6},{6,7},{7,0},{8,9},{9,10},{10,1... | collective-permute-start | bytes 331784 | tf_op jit(solution)/shard_map/ppermute | solution.py:95
  269.4 4.9 %collective-permute-start.63 = (bf16[3,48,128]{2,1,0:T(8,128)(2,1)S(1)}, bf16[3,48,128]{2,1,0:T(8,128)(2,1)S(1)}, u32[]{:S(2)}, u32[]{:S(2)}) collective-permute-start(bf16[3,48,128]{2,1,0:T(8,128)(2,1)S(1)} %reshape.310), channel_id=1, source_target_pairs={{0,8},{8,16},{16,24},{24,0},{1,9},{9,17},{17,25},{25,1},{2,10},{10... | collective-permute-start | bytes 110600 | tf_op jit(solution)/shard_map/ppermute | solution.py:95
  271.6 4.0 %collective-permute-start.64 = (bf16[3,48,128]{2,1,0:T(8,128)(2,1)S(1)}, bf16[3,48,128]{2,1,0:T(8,128)(2,1)S(1)}, u32[]{:S(2)}, u32[]{:S(2)}) collective-permute-start(bf16[3,48,128]{2,1,0:T(8,128)(2,1)S(1)} %reshape.310), channel_id=1, source_target_pairs={{0,24},{8,0},{16,8},{24,16},{1,25},{9,1},{17,9},{25,17},{2,26},{10... | collective-permute-start | bytes 110600 | tf_op jit(solution)/shard_map/ppermute | solution.py:95
  277.0 6.0 %collective-permute-start.65 = (bf16[3,3,48,128]{3,2,1,0:T(8,128)(2,1)S(1)}, bf16[3,3,48,128]{3,2,1,0:T(8,128)(2,1)S(1)}, u32[]{:S(2)}, u32[]{:S(2)}) collective-permute-start(bf16[3,3,48,128]{3,2,1,0:T(8,128)(2,1)S(1)} %pad_maximum_fusion.14), channel_id=1, source_target_pairs={{0,1},{1,2},{2,3},{3,4},{4,5},{5,6},{6,7},{7,0},{8,9},{9,10},{10,1... | collective-permute-start | bytes 331784 | tf_op jit(solution)/shard_map/ppermute | solution.py:95
  285.9 4.9 %collective-permute-start.67 = (bf16[3,48,128]{2,1,0:T(8,128)(2,1)S(1)}, bf16[3,48,128]{2,1,0:T(8,128)(2,1)S(1)}, u32[]{:S(2)}, u32[]{:S(2)}) collective-permute-start(bf16[3,48,128]{2,1,0:T(8,128)(2,1)S(1)} %reshape.313), channel_id=1, source_target_pairs={{0,8},{8,16},{16,24},{24,0},{1,9},{9,17},{17,25},{25,1},{2,10},{10... | collective-permute-start | bytes 110600 | tf_op jit(solution)/shard_map/ppermute | solution.py:95
  287.5 4.0 %collective-permute-start.68 = (bf16[3,48,128]{2,1,0:T(8,128)(2,1)S(1)}, bf16[3,48,128]{2,1,0:T(8,128)(2,1)S(1)}, u32[]{:S(2)}, u32[]{:S(2)}) collective-permute-start(bf16[3,48,128]{2,1,0:T(8,128)(2,1)S(1)} %reshape.313), channel_id=1, source_target_pairs={{0,24},{8,0},{16,8},{24,16},{1,25},{9,1},{17,9},{25,17},{2,26},{10... | collective-permute-start | bytes 110600 | tf_op jit(solution)/shard_map/ppermute | solution.py:95
  292.9 6.0 %collective-permute-start.69 = (bf16[3,3,48,128]{3,2,1,0:T(8,128)(2,1)S(1)}, bf16[3,3,48,128]{3,2,1,0:T(8,128)(2,1)S(1)}, u32[]{:S(2)}, u32[]{:S(2)}) collective-permute-start(bf16[3,3,48,128]{3,2,1,0:T(8,128)(2,1)S(1)} %pad_maximum_fusion.15), channel_id=1, source_target_pairs={{0,1},{1,2},{2,3},{3,4},{4,5},{5,6},{6,7},{7,0},{8,9},{9,10},{10,1... | collective-permute-start | bytes 331784 | tf_op jit(solution)/shard_map/ppermute | solution.py:95
  302.0 3.8 %collective-permute-start.71 = (f32[32,32]{0,1:T(8,128)S(1)}, f32[32,32]{0,1:T(8,128)S(1)}, u32[]{:S(2)}, u32[]{:S(2)}) collective-permute-start(f32[32,32]{0,1:T(8,128)S(1)} %convolution_bitcast_fusion.65), channel_id=1, source_target_pairs={{0,8},{8,0},{16,24},{24,16},{1,9},{9,1},{17,25},{25,17},{2,10},{10... | collective-permute-start | bytes 12296 | tf_op jit(solution)/shard_map/ppermute | solution.py:58
  304.9 4.6 %collective-permute-start.73 = (f32[32,32]{0,1:T(8,128)S(1)}, f32[32,32]{0,1:T(8,128)S(1)}, u32[]{:S(2)}, u32[]{:S(2)}) collective-permute-start(f32[32,32]{0,1:T(8,128)S(1)} %convolution_bitcast_fusion.65), channel_id=1, source_target_pairs={{0,24},{8,16},{16,8},{24,0},{1,25},{9,17},{17,9},{25,1},{2,26},{10... | collective-permute-start | bytes 12296 | tf_op jit(solution)/shard_map/ppermute | solution.py:58
  309.6 3.8 %collective-permute-start.75 = (f32[32,32]{0,1:T(8,128)S(1)}, f32[32,32]{0,1:T(8,128)S(1)}, u32[]{:S(2)}, u32[]{:S(2)}) collective-permute-start(f32[32,32]{0,1:T(8,128)S(1)} %add_add_fusion.1), channel_id=1, source_target_pairs={{0,2},{1,3},{2,0},{3,1},{4,6},{5,7},{6,4},{7,5},{8,10},{9,11},{10,... | collective-permute-start | bytes 12296 | tf_op jit(solution)/shard_map/ppermute | solution.py:58
  313.4 4.7 %collective-permute-start.77 = (f32[32,32]{0,1:T(8,128)S(1)}, f32[32,32]{0,1:T(8,128)S(1)}, u32[]{:S(2)}, u32[]{:S(2)}) collective-permute-start(f32[32,32]{0,1:T(8,128)S(1)} %add_add_fusion), channel_id=1, source_target_pairs={{0,4},{1,5},{2,6},{3,7},{4,0},{5,1},{6,2},{7,3},{8,12},{9,13},{10,... | collective-permute-start | bytes 12296 | tf_op jit(solution)/shard_map/ppermute | solution.py:58
  (16 other events, 59.8 us)

commit v9 on v6

--- a/solution.py
+++ b/solution.py
@@ -58,6 +58,9 @@
             return lax.ppermute(v, axis, [(i, i ^ stride) for i in range(count)])
 
         stride = 1
+        if (count.bit_length() - 1) % 2:
+            value = value + swap(value, stride)
+            stride *= 2
         while stride < count:
             if 4 * stride <= count:
                 near, far, both = swap(value, stride), swap(value, 2 * stride), swap(value, 3 * stride)

time: 286 us -> 286 us (level)
    ppermute x14, waiting for transfers between devices: 18.9 us -> 14.3 us  [swap(): return lax.ppermute(v, axis, [(i, i ^ stride) for i in range(count)])]
    ppermute x64, waiting for transfers between devices: 103 us -> 107 us  [shift(): lax.ppermute(value, axis, [(i, (i + step) % count) for i in range(count)])]
    ppermute x14, starting transfers between devices: 12.7 us -> 16 us  [swap(): return lax.ppermute(v, axis, [(i, i ^ stride) for i in range(count)])]
  transfers between devices with their start and end apart: 78 -> 78, of which waited for: 71 -> 73; matrix products, arithmetic and copies ran while one was open for 18% -> 18% of each run, Pallas kernels for 0% -> 0%
where the time goes in v9:
time: 286 us
  waiting for transfers between devices  121 us (42%)
  starting transfers between devices  79.2 us (28%)
  matrix products  52.5 us (18%)
  other arithmetic  21.5 us (8%)
  local copies, waits for them, and re-layouts  10.6 us (4%)
    ppermute x64, waiting for transfers between devices, shift(): lax.ppermute(value, axis, [(i, (i + step) % count) for i in range(count)])  107 us
    ppermute x64, starting transfers between devices, shift(): lax.ppermute(value, axis, [(i, (i + step) % count) for i in range(count)])  63.2 us
    dot_general x64, matrix products, part(): jnp.einsum('kvj,tkij->tvi', cells, blocks, preferred_element_type=jnp.flo...  50.4 us
    ppermute x14, starting transfers between devices, swap(): return lax.ppermute(v, axis, [(i, i ^ stride) for i in range(count)])  16 us
    ppermute x14, waiting for transfers between devices, swap(): return lax.ppermute(v, axis, [(i, i ^ stride) for i in range(count)])  14.3 us
    gather x1, local copies, waits for them, and re-layouts, dense_coupling(): jnp.take(matrices, index.reshape(-1), axis=0)  10.3 us
    another operation x6, other arithmetic, orthonormal(): factor = jnp.linalg.cholesky(gram_matrix)  7.19 us
    another operation x4, other arithmetic, orthonormal(): inverse = jax.scipy.linalg.solve_triangular(factor, identity, lower=True)  6.17 us
  transfers between devices with their start and end apart: 78, of which 73 were waited for; matrix products, arithmetic and copies ran while one was open for 18% of the time, Pallas kernels for 0%

profile of v9, /device:TPU:0, one launch (start us, length us, event | category | flops | bytes accessed | tf_op | source)
XLA Modules:
  0.0 285.6 jit_solution(18013492383657063180)
XLA Ops:
  0.9 3.0 %collective-permute-start = (bf16[3,32,192]{2,1,0:T(8,128)(2,1)S(1)}, bf16[3,32,192]{2,1,0:T(8,128)(2,1)S(1)}, u32[]{:S(2)}, u32[]{:S(2)}) collective-permute-start(bf16[3,32,192]{2,1,0:T(8,128)(2,1)S(1)} %get-tuple-element.18), channel_id=1, source_target_pairs={{0,8},{8,16},{16,24},{24,0},{1,9},{9,17},{17,25},{25,1},{2,10},{10... | collective-permute-start | bytes 110600 | tf_op jit(solution)/shard_map/ppermute | solution.py:98
  8.7 1.9 collective-permute-start.3
  10.6 10.3 %gather_fusion = bf16[81,192,192]{2,1,0:T(8,128)(2,1)} fusion(bf16[81,192,192]{2,1,0:T(8,128)(2,1)} %bitcast.915, s32[1024]{0:T(1024)S(1)} %pad_clamp_fusion), kind=kCustom, calls=%fused_computation | custom fusion | bytes 11944260 | tf_op jit(solution)/shard_map/jit(_take)/gather | solution.py:42
  20.9 4.3 %select_select_fusion = bf16[3,27,192,192]{3,2,1,0:T(8,128)(2,1)S(1)} fusion(bf16[3,27,192,192]{3,2,1,0:T(8,128)(2,1)} %bitcast.914, pred[3,27]{1,0:T(4,128)(4,1)S(1)} %compare_and_fusion, pred[3,27]{1,0:T(4,128)(4,1)S(1)} %and_reduce_fusion), kind=kLoop, calls=%fused_computation.1 | loop fusion | flops 5971968 | bytes 11944098 | tf_op jit(solution)/shard_map/jit(_where)/select_n | solution.py:46
  26.3 2.0 convolution_bitcast_fusion.30
  29.2 2.7 collective-permute-start.4
  32.6 2.2 collective-permute-done.4
  36.0 2.2 collective-permute-start.7
  38.8 2.1 collective-permute-done.7
  41.7 2.8 collective-permute-done.6
  52.4 2.9 %collective-permute-done.11 = bf16[3,3,32,192]{3,2,1,0:T(8,128)(2,1)S(1)} collective-permute-done((bf16[3,3,32,192]{3,2,1,0:T(8,128)(2,1)S(1)}, bf16[3,3,32,192]{3,2,1,0:T(8,128)(2,1)S(1)}, u32[]{:S(2)}, u32[]{:S(2)}) %collective-permute-start.11) | collective-permute-done | bytes 110624 | tf_op jit(solution)/shard_map/ppermute | solution.py:98
  66.0 2.3 collective-permute-done.15
  69.2 2.6 collective-permute-done.14
  76.1 1.7 collective-permute-done.16
  79.5 2.9 %collective-permute-done.19 = bf16[3,3,32,192]{3,2,1,0:T(8,128)(2,1)S(1)} collective-permute-done((bf16[3,3,32,192]{3,2,1,0:T(8,128)(2,1)S(1)}, bf16[3,3,32,192]{3,2,1,0:T(8,128)(2,1)S(1)}, u32[]{:S(2)}, u32[]{:S(2)}) %collective-permute-start.19) | collective-permute-done | bytes 110624 | tf_op jit(solution)/shard_map/ppermute | solution.py:98
  83.4 1.8 collective-permute-done.18
  86.1 2.1 collective-permute-start.20
  89.4 1.7 collective-permute-done.20
  93.8 2.6 collective-permute-done.23
  97.3 2.3 collective-permute-done.22
  107.3 2.8 collective-permute-done.27
  111.0 2.1 collective-permute-done.26
  120.8 2.8 collective-permute-done.31
  124.4 2.1 collective-permute-done.30
  127.7 1.7 collective-permute-start.32
  133.2 2.0 collective-permute-done.34
  137.4 3.4 %collective-permute-start.38 = (f32[32,32]{0,1:T(8,128)S(1)}, f32[32,32]{0,1:T(8,128)S(1)}, u32[]{:S(2)}, u32[]{:S(2)}) collective-permute-start(f32[32,32]{0,1:T(8,128)S(1)} %add.334), channel_id=1, source_target_pairs={{0,6},{1,7},{2,4},{3,5},{4,2},{5,3},{6,0},{7,1},{8,14},{9,15},{10,... | collective-permute-start | bytes 12296 | tf_op jit(solution)/shard_map/ppermute | solution.py:58
  141.1 1.8 collective-permute-done.38
  143.0 2.9 %cholesky.44 = f32[32,32]{1,0:T(8,128)S(1)} custom-call(f32[32,32]{1,0:T(8,128)S(1)} %fusion.162), custom_call_target="Cholesky" | custom-call | tf_op jit(solution)/shard_map/jit(cholesky)/cholesky | solution.py:80
  147.2 2.4 custom-call.6
  150.7 2.4 collective-permute-start.40
  155.8 2.1 fusion.98
  159.4 2.6 convolution_bitcast_fusion.14
  164.4 2.5 collective-permute-start.43
  167.8 1.7 collective-permute-done.43
  172.5 2.6 collective-permute-done.46
  176.0 2.3 collective-permute-done.45
  179.2 2.6 collective-permute-start.47
  182.6 1.7 collective-permute-done.47
  187.1 2.9 %collective-permute-done.50 = bf16[3,3,32,192]{3,2,1,0:T(8,128)(2,1)S(1)} collective-permute-done((bf16[3,3,32,192]{3,2,1,0:T(8,128)(2,1)S(1)}, bf16[3,3,32,192]{3,2,1,0:T(8,128)(2,1)S(1)}, u32[]{:S(2)}, u32[]{:S(2)}) %collective-permute-start.50) | collective-permute-done | bytes 110624 | tf_op jit(solution)/shard_map/ppermute | solution.py:98
  190.9 1.7 collective-permute-done.49
  194.7 1.9 collective-permute-start.52
  197.0 1.7 collective-permute-done.51
  200.3 2.6 collective-permute-done.54
  203.8 2.3 collective-permute-done.53
  207.0 1.9 collective-permute-start.55
  210.4 1.7 collective-permute-done.55
  214.2 2.9 %collective-permute-done.58 = bf16[3,3,32,192]{3,2,1,0:T(8,128)(2,1)S(1)} collective-permute-done((bf16[3,3,32,192]{3,2,1,0:T(8,128)(2,1)S(1)}, bf16[3,3,32,192]{3,2,1,0:T(8,128)(2,1)S(1)}, u32[]{:S(2)}, u32[]{:S(2)}) %collective-permute-start.58) | collective-permute-done | bytes 110624 | tf_op jit(solution)/shard_map/ppermute | solution.py:98
  224.0 1.7 collective-permute-done.59
  227.7 2.9 %collective-permute-done.62 = bf16[3,3,32,192]{3,2,1,0:T(8,128)(2,1)S(1)} collective-permute-done((bf16[3,3,32,192]{3,2,1,0:T(8,128)(2,1)S(1)}, bf16[3,3,32,192]{3,2,1,0:T(8,128)(2,1)S(1)}, u32[]{:S(2)}, u32[]{:S(2)}) %collective-permute-start.62) | collective-permute-done | bytes 110624 | tf_op jit(solution)/shard_map/ppermute | solution.py:98
  231.4 2.0 collective-permute-done.61
  234.4 2.2 collective-permute-start.63
  237.7 1.7 collective-permute-done.63
  242.1 2.7 collective-permute-done.66
  245.6 2.2 collective-permute-done.65
  249.9 1.8 collective-permute-start.68
  252.1 1.7 collective-permute-done.67
  255.6 2.6 collective-permute-done.70
  259.0 2.3 collective-permute-done.69
  267.6 2.2 collective-permute-done.73
  272.1 3.3 %collective-permute-start.77 = (f32[32,32]{0,1:T(8,128)S(1)}, f32[32,32]{0,1:T(8,128)S(1)}, u32[]{:S(2)}, u32[]{:S(2)}) collective-permute-start(f32[32,32]{0,1:T(8,128)S(1)} %add.372), channel_id=1, source_target_pairs={{0,6},{1,7},{2,4},{3,5},{4,2},{5,3},{6,0},{7,1},{8,14},{9,15},{10,... | collective-permute-start | bytes 12296 | tf_op jit(solution)/shard_map/ppermute | solution.py:58
  275.7 1.9 collective-permute-done.77
  277.8 2.9 %cholesky.55 = f32[32,32]{1,0:T(8,128)S(1)} custom-call(f32[32,32]{1,0:T(8,128)S(1)} %fusion.160), custom_call_target="Cholesky" | custom-call | tf_op jit(solution)/shard_map/jit(cholesky)/cholesky | solution.py:80
  282.0 2.4 custom-call.7
  (219 shorter events, 128.4 us)
Async XLA Ops:
  0.9 6.0 %collective-permute-start = (bf16[3,32,192]{2,1,0:T(8,128)(2,1)S(1)}, bf16[3,32,192]{2,1,0:T(8,128)(2,1)S(1)}, u32[]{:S(2)}, u32[]{:S(2)}) collective-permute-start(bf16[3,32,192]{2,1,0:T(8,128)(2,1)S(1)} %get-tuple-element.18), channel_id=1, source_target_pairs={{0,8},{8,16},{16,24},{24,0},{1,9},{9,17},{17,25},{25,1},{2,10},{10... | collective-permute-start | bytes 110600 | tf_op jit(solution)/shard_map/ppermute | solution.py:98
  3.9 4.1 %collective-permute-start.1 = (bf16[3,32,192]{2,1,0:T(8,128)(2,1)S(1)}, bf16[3,32,192]{2,1,0:T(8,128)(2,1)S(1)}, u32[]{:S(2)}, u32[]{:S(2)}) collective-permute-start(bf16[3,32,192]{2,1,0:T(8,128)(2,1)S(1)} %get-tuple-element.18), channel_id=1, source_target_pairs={{0,24},{8,0},{16,8},{24,16},{1,25},{9,1},{17,9},{25,17},{2,26},{10... | collective-permute-start | bytes 110600 | tf_op jit(solution)/shard_map/ppermute | solution.py:98
  8.7 17.6 %collective-permute-start.3 = (bf16[3,3,32,192]{3,2,1,0:T(8,128)(2,1)}, bf16[3,3,32,192]{3,2,1,0:T(8,128)(2,1)}, u32[]{:S(2)}, u32[]{:S(2)}) collective-permute-start(bf16[3,3,32,192]{3,2,1,0:T(8,128)(2,1)} %pad_maximum_fusion), channel_id=1, source_target_pairs={{0,7},{1,0},{2,1},{3,2},{4,3},{5,4},{6,5},{7,6},{8,15},{9,8},{10,9... | collective-permute-start | bytes 331784 | tf_op jit(solution)/shard_map/ppermute | solution.py:98
  10.6 17.7 %collective-permute-start.2 = (bf16[3,3,32,192]{3,2,1,0:T(8,128)(2,1)}, bf16[3,3,32,192]{3,2,1,0:T(8,128)(2,1)S(1)}, u32[]{:S(2)}, u32[]{:S(2)}) collective-permute-start(bf16[3,3,32,192]{3,2,1,0:T(8,128)(2,1)} %pad_maximum_fusion), channel_id=1, source_target_pairs={{0,1},{1,2},{2,3},{3,4},{4,5},{5,6},{6,7},{7,0},{8,9},{9,10},{10,1... | collective-permute-start | bytes 331784 | tf_op jit(solution)/shard_map/ppermute | solution.py:98
  29.2 5.5 %collective-permute-start.4 = (bf16[3,32,192]{2,1,0:T(8,128)(2,1)S(1)}, bf16[3,32,192]{2,1,0:T(8,128)(2,1)S(1)}, u32[]{:S(2)}, u32[]{:S(2)}) collective-permute-start(bf16[3,32,192]{2,1,0:T(8,128)(2,1)S(1)} %get-tuple-element.19), channel_id=1, source_target_pairs={{0,8},{8,16},{16,24},{24,0},{1,9},{9,17},{17,25},{25,1},{2,10},{10... | collective-permute-start | bytes 110600 | tf_op jit(solution)/shard_map/ppermute | solution.py:98
  31.9 4.1 %collective-permute-start.5 = (bf16[3,32,192]{2,1,0:T(8,128)(2,1)S(1)}, bf16[3,32,192]{2,1,0:T(8,128)(2,1)S(1)}, u32[]{:S(2)}, u32[]{:S(2)}) collective-permute-start(bf16[3,32,192]{2,1,0:T(8,128)(2,1)S(1)} %get-tuple-element.19), channel_id=1, source_target_pairs={{0,24},{8,0},{16,8},{24,16},{1,25},{9,1},{17,9},{25,17},{2,26},{10... | collective-permute-start | bytes 110600 | tf_op jit(solution)/shard_map/ppermute | solution.py:98
  36.0 4.9 %collective-permute-start.7 = (bf16[3,3,32,192]{3,2,1,0:T(8,128)(2,1)S(1)}, bf16[3,3,32,192]{3,2,1,0:T(8,128)(2,1)S(1)}, u32[]{:S(2)}, u32[]{:S(2)}) collective-permute-start(bf16[3,3,32,192]{3,2,1,0:T(8,128)(2,1)S(1)} %pad_maximum_fusion.1), channel_id=1, source_target_pairs={{0,7},{1,0},{2,1},{3,2},{4,3},{5,4},{6,5},{7,6},{8,15},{9,8},{10,9... | collective-permute-start | bytes 331784 | tf_op jit(solution)/shard_map/ppermute | solution.py:98
  38.2 6.4 %collective-permute-start.6 = (bf16[3,3,32,192]{3,2,1,0:T(8,128)(2,1)S(1)}, bf16[3,3,32,192]{3,2,1,0:T(8,128)(2,1)S(1)}, u32[]{:S(2)}, u32[]{:S(2)}) collective-permute-start(bf16[3,3,32,192]{3,2,1,0:T(8,128)(2,1)S(1)} %pad_maximum_fusion.1), channel_id=1, source_target_pairs={{0,1},{1,2},{2,3},{3,4},{4,5},{5,6},{6,7},{7,0},{8,9},{9,10},{10,1... | collective-permute-start | bytes 331784 | tf_op jit(solution)/shard_map/ppermute | solution.py:98
  45.5 5.0 %collective-permute-start.8 = (bf16[3,32,192]{2,1,0:T(8,128)(2,1)S(1)}, bf16[3,32,192]{2,1,0:T(8,128)(2,1)S(1)}, u32[]{:S(2)}, u32[]{:S(2)}) collective-permute-start(bf16[3,32,192]{2,1,0:T(8,128)(2,1)S(1)} %get-tuple-element.21), channel_id=1, source_target_pairs={{0,8},{8,16},{16,24},{24,0},{1,9},{9,17},{17,25},{25,1},{2,10},{10... | collective-permute-start | bytes 110600 | tf_op jit(solution)/shard_map/ppermute | solution.py:98
  47.1 4.1 %collective-permute-start.9 = (bf16[3,32,192]{2,1,0:T(8,128)(2,1)S(1)}, bf16[3,32,192]{2,1,0:T(8,128)(2,1)S(1)}, u32[]{:S(2)}, u32[]{:S(2)}) collective-permute-start(bf16[3,32,192]{2,1,0:T(8,128)(2,1)S(1)} %get-tuple-element.21), channel_id=1, source_target_pairs={{0,24},{8,0},{16,8},{24,16},{1,25},{9,1},{17,9},{25,17},{2,26},{10... | collective-permute-start | bytes 110600 | tf_op jit(solution)/shard_map/ppermute | solution.py:98
  51.3 4.1 %collective-permute-start.11 = (bf16[3,3,32,192]{3,2,1,0:T(8,128)(2,1)S(1)}, bf16[3,3,32,192]{3,2,1,0:T(8,128)(2,1)S(1)}, u32[]{:S(2)}, u32[]{:S(2)}) collective-permute-start(bf16[3,3,32,192]{3,2,1,0:T(8,128)(2,1)S(1)} %pad_maximum_fusion.2), channel_id=1, source_target_pairs={{0,7},{1,0},{2,1},{3,2},{4,3},{5,4},{6,5},{7,6},{8,15},{9,8},{10,9... | collective-permute-start | bytes 331784 | tf_op jit(solution)/shard_map/ppermute | solution.py:98
  51.3 6.4 %collective-permute-start.10 = (bf16[3,3,32,192]{3,2,1,0:T(8,128)(2,1)S(1)}, bf16[3,3,32,192]{3,2,1,0:T(8,128)(2,1)S(1)}, u32[]{:S(2)}, u32[]{:S(2)}) collective-permute-start(bf16[3,3,32,192]{3,2,1,0:T(8,128)(2,1)S(1)} %pad_maximum_fusion.2), channel_id=1, source_target_pairs={{0,1},{1,2},{2,3},{3,4},{4,5},{5,6},{6,7},{7,0},{8,9},{9,10},{10,1... | collective-permute-start | bytes 331784 | tf_op jit(solution)/shard_map/ppermute | solution.py:98
  58.7 5.0 %collective-permute-start.12 = (bf16[3,32,192]{2,1,0:T(8,128)(2,1)S(1)}, bf16[3,32,192]{2,1,0:T(8,128)(2,1)S(1)}, u32[]{:S(2)}, u32[]{:S(2)}) collective-permute-start(bf16[3,32,192]{2,1,0:T(8,128)(2,1)S(1)} %get-tuple-element.23), channel_id=1, source_target_pairs={{0,8},{8,16},{16,24},{24,0},{1,9},{9,17},{17,25},{25,1},{2,10},{10... | collective-permute-start | bytes 110600 | tf_op jit(solution)/shard_map/ppermute | solution.py:98
  60.1 4.1 %collective-permute-start.13 = (bf16[3,32,192]{2,1,0:T(8,128)(2,1)S(1)}, bf16[3,32,192]{2,1,0:T(8,128)(2,1)S(1)}, u32[]{:S(2)}, u32[]{:S(2)}) collective-permute-start(bf16[3,32,192]{2,1,0:T(8,128)(2,1)S(1)} %get-tuple-element.23), channel_id=1, source_target_pairs={{0,24},{8,0},{16,8},{24,16},{1,25},{9,1},{17,9},{25,17},{2,26},{10... | collective-permute-start | bytes 110600 | tf_op jit(solution)/shard_map/ppermute | solution.py:98
  64.2 4.1 %collective-permute-start.15 = (bf16[3,3,32,192]{3,2,1,0:T(8,128)(2,1)S(1)}, bf16[3,3,32,192]{3,2,1,0:T(8,128)(2,1)S(1)}, u32[]{:S(2)}, u32[]{:S(2)}) collective-permute-start(bf16[3,3,32,192]{3,2,1,0:T(8,128)(2,1)S(1)} %pad_maximum_fusion.3), channel_id=1, source_target_pairs={{0,7},{1,0},{2,1},{3,2},{4,3},{5,4},{6,5},{7,6},{8,15},{9,8},{10,9... | collective-permute-start | bytes 331784 | tf_op jit(solution)/shard_map/ppermute | solution.py:98
  65.4 6.4 %collective-permute-start.14 = (bf16[3,3,32,192]{3,2,1,0:T(8,128)(2,1)S(1)}, bf16[3,3,32,192]{3,2,1,0:T(8,128)(2,1)S(1)}, u32[]{:S(2)}, u32[]{:S(2)}) collective-permute-start(bf16[3,3,32,192]{3,2,1,0:T(8,128)(2,1)S(1)} %pad_maximum_fusion.3), channel_id=1, source_target_pairs={{0,1},{1,2},{2,3},{3,4},{4,5},{5,6},{6,7},{7,0},{8,9},{9,10},{10,1... | collective-permute-start | bytes 331784 | tf_op jit(solution)/shard_map/ppermute | solution.py:98
  72.7 5.0 %collective-permute-start.16 = (bf16[3,32,192]{2,1,0:T(8,128)(2,1)S(1)}, bf16[3,32,192]{2,1,0:T(8,128)(2,1)S(1)}, u32[]{:S(2)}, u32[]{:S(2)}) collective-permute-start(bf16[3,32,192]{2,1,0:T(8,128)(2,1)S(1)} %get-tuple-element.25), channel_id=1, source_target_pairs={{0,8},{8,16},{16,24},{24,0},{1,9},{9,17},{17,25},{25,1},{2,10},{10... | collective-permute-start | bytes 110600 | tf_op jit(solution)/shard_map/ppermute | solution.py:98
  74.2 4.1 %collective-permute-start.17 = (bf16[3,32,192]{2,1,0:T(8,128)(2,1)S(1)}, bf16[3,32,192]{2,1,0:T(8,128)(2,1)S(1)}, u32[]{:S(2)}, u32[]{:S(2)}) collective-permute-start(bf16[3,32,192]{2,1,0:T(8,128)(2,1)S(1)} %get-tuple-element.25), channel_id=1, source_target_pairs={{0,24},{8,0},{16,8},{24,16},{1,25},{9,1},{17,9},{25,17},{2,26},{10... | collective-permute-start | bytes 110600 | tf_op jit(solution)/shard_map/ppermute | solution.py:98
  78.4 4.1 %collective-permute-start.19 = (bf16[3,3,32,192]{3,2,1,0:T(8,128)(2,1)S(1)}, bf16[3,3,32,192]{3,2,1,0:T(8,128)(2,1)S(1)}, u32[]{:S(2)}, u32[]{:S(2)}) collective-permute-start(bf16[3,3,32,192]{3,2,1,0:T(8,128)(2,1)S(1)} %pad_maximum_fusion.4), channel_id=1, source_target_pairs={{0,7},{1,0},{2,1},{3,2},{4,3},{5,4},{6,5},{7,6},{8,15},{9,8},{10,9... | collective-permute-start | bytes 331784 | tf_op jit(solution)/shard_map/ppermute | solution.py:98
  78.8 6.4 %collective-permute-start.18 = (bf16[3,3,32,192]{3,2,1,0:T(8,128)(2,1)S(1)}, bf16[3,3,32,192]{3,2,1,0:T(8,128)(2,1)S(1)}, u32[]{:S(2)}, u32[]{:S(2)}) collective-permute-start(bf16[3,3,32,192]{3,2,1,0:T(8,128)(2,1)S(1)} %pad_maximum_fusion.4), channel_id=1, source_target_pairs={{0,1},{1,2},{2,3},{3,4},{4,5},{5,6},{6,7},{7,0},{8,9},{9,10},{10,1... | collective-permute-start | bytes 331784 | tf_op jit(solution)/shard_map/ppermute | solution.py:98
  86.1 5.0 %collective-permute-start.20 = (bf16[3,32,192]{2,1,0:T(8,128)(2,1)S(1)}, bf16[3,32,192]{2,1,0:T(8,128)(2,1)S(1)}, u32[]{:S(2)}, u32[]{:S(2)}) collective-permute-start(bf16[3,32,192]{2,1,0:T(8,128)(2,1)S(1)} %get-tuple-element.27), channel_id=1, source_target_pairs={{0,8},{8,16},{16,24},{24,0},{1,9},{9,17},{17,25},{25,1},{2,10},{10... | collective-permute-start | bytes 110600 | tf_op jit(solution)/shard_map/ppermute | solution.py:98
  88.2 4.1 %collective-permute-start.21 = (bf16[3,32,192]{2,1,0:T(8,128)(2,1)S(1)}, bf16[3,32,192]{2,1,0:T(8,128)(2,1)S(1)}, u32[]{:S(2)}, u32[]{:S(2)}) collective-permute-start(bf16[3,32,192]{2,1,0:T(8,128)(2,1)S(1)} %get-tuple-element.27), channel_id=1, source_target_pairs={{0,24},{8,0},{16,8},{24,16},{1,25},{9,1},{17,9},{25,17},{2,26},{10... | collective-permute-start | bytes 110600 | tf_op jit(solution)/shard_map/ppermute | solution.py:98
  92.3 4.1 %collective-permute-start.23 = (bf16[3,3,32,192]{3,2,1,0:T(8,128)(2,1)S(1)}, bf16[3,3,32,192]{3,2,1,0:T(8,128)(2,1)S(1)}, u32[]{:S(2)}, u32[]{:S(2)}) collective-permute-start(bf16[3,3,32,192]{3,2,1,0:T(8,128)(2,1)S(1)} %pad_maximum_fusion.5), channel_id=1, source_target_pairs={{0,7},{1,0},{2,1},{3,2},{4,3},{5,4},{6,5},{7,6},{8,15},{9,8},{10,9... | collective-permute-start | bytes 331784 | tf_op jit(solution)/shard_map/ppermute | solution.py:98
  93.2 6.4 %collective-permute-start.22 = (bf16[3,3,32,192]{3,2,1,0:T(8,128)(2,1)S(1)}, bf16[3,3,32,192]{3,2,1,0:T(8,128)(2,1)S(1)}, u32[]{:S(2)}, u32[]{:S(2)}) collective-permute-start(bf16[3,3,32,192]{3,2,1,0:T(8,128)(2,1)S(1)} %pad_maximum_fusion.5), channel_id=1, source_target_pairs={{0,1},{1,2},{2,3},{3,4},{4,5},{5,6},{6,7},{7,0},{8,9},{9,10},{10,1... | collective-permute-start | bytes 331784 | tf_op jit(solution)/shard_map/ppermute | solution.py:98
  100.5 5.0 %collective-permute-start.24 = (bf16[3,32,192]{2,1,0:T(8,128)(2,1)S(1)}, bf16[3,32,192]{2,1,0:T(8,128)(2,1)S(1)}, u32[]{:S(2)}, u32[]{:S(2)}) collective-permute-start(bf16[3,32,192]{2,1,0:T(8,128)(2,1)S(1)} %get-tuple-element.29), channel_id=1, source_target_pairs={{0,8},{8,16},{16,24},{24,0},{1,9},{9,17},{17,25},{25,1},{2,10},{10... | collective-permute-start | bytes 110600 | tf_op jit(solution)/shard_map/ppermute | solution.py:98
  106.0 4.1 %collective-permute-start.27 = (bf16[3,3,32,192]{3,2,1,0:T(8,128)(2,1)S(1)}, bf16[3,3,32,192]{3,2,1,0:T(8,128)(2,1)S(1)}, u32[]{:S(2)}, u32[]{:S(2)}) collective-permute-start(bf16[3,3,32,192]{3,2,1,0:T(8,128)(2,1)S(1)} %pad_maximum_fusion.6), channel_id=1, source_target_pairs={{0,7},{1,0},{2,1},{3,2},{4,3},{5,4},{6,5},{7,6},{8,15},{9,8},{10,9... | collective-permute-start | bytes 331784 | tf_op jit(solution)/shard_map/ppermute | solution.py:98
  106.7 6.4 %collective-permute-start.26 = (bf16[3,3,32,192]{3,2,1,0:T(8,128)(2,1)S(1)}, bf16[3,3,32,192]{3,2,1,0:T(8,128)(2,1)S(1)}, u32[]{:S(2)}, u32[]{:S(2)}) collective-permute-start(bf16[3,3,32,192]{3,2,1,0:T(8,128)(2,1)S(1)} %pad_maximum_fusion.6), channel_id=1, source_target_pairs={{0,1},{1,2},{2,3},{3,4},{4,5},{5,6},{6,7},{7,0},{8,9},{9,10},{10,1... | collective-permute-start | bytes 331784 | tf_op jit(solution)/shard_map/ppermute | solution.py:98
  114.0 5.0 %collective-permute-start.28 = (bf16[3,32,192]{2,1,0:T(8,128)(2,1)S(1)}, bf16[3,32,192]{2,1,0:T(8,128)(2,1)S(1)}, u32[]{:S(2)}, u32[]{:S(2)}) collective-permute-start(bf16[3,32,192]{2,1,0:T(8,128)(2,1)S(1)} %get-tuple-element.31), channel_id=1, source_target_pairs={{0,8},{8,16},{16,24},{24,0},{1,9},{9,17},{17,25},{25,1},{2,10},{10... | collective-permute-start | bytes 110600 | tf_op jit(solution)/shard_map/ppermute | solution.py:98
  119.4 4.1 %collective-permute-start.31 = (bf16[3,3,32,192]{3,2,1,0:T(8,128)(2,1)S(1)}, bf16[3,3,32,192]{3,2,1,0:T(8,128)(2,1)S(1)}, u32[]{:S(2)}, u32[]{:S(2)}) collective-permute-start(bf16[3,3,32,192]{3,2,1,0:T(8,128)(2,1)S(1)} %pad_maximum_fusion.7), channel_id=1, source_target_pairs={{0,7},{1,0},{2,1},{3,2},{4,3},{5,4},{6,5},{7,6},{8,15},{9,8},{10,9... | collective-permute-start | bytes 331784 | tf_op jit(solution)/shard_map/ppermute | solution.py:98
  120.1 6.4 %collective-permute-start.30 = (bf16[3,3,32,192]{3,2,1,0:T(8,128)(2,1)S(1)}, bf16[3,3,32,192]{3,2,1,0:T(8,128)(2,1)S(1)}, u32[]{:S(2)}, u32[]{:S(2)}) collective-permute-start(bf16[3,3,32,192]{3,2,1,0:T(8,128)(2,1)S(1)} %pad_maximum_fusion.7), channel_id=1, source_target_pairs={{0,1},{1,2},{2,3},{3,4},{4,5},{5,6},{6,7},{7,0},{8,9},{9,10},{10,1... | collective-permute-start | bytes 331784 | tf_op jit(solution)/shard_map/ppermute | solution.py:98
  130.5 4.6 %collective-permute-start.34 = (f32[32,32]{0,1:T(8,128)S(1)}, f32[32,32]{0,1:T(8,128)S(1)}, u32[]{:S(2)}, u32[]{:S(2)}) collective-permute-start(f32[32,32]{0,1:T(8,128)S(1)} %convolution_bitcast_fusion.67), channel_id=1, source_target_pairs={{0,24},{8,16},{16,8},{24,0},{1,25},{9,17},{17,9},{25,1},{2,26},{10... | collective-permute-start | bytes 12296 | tf_op jit(solution)/shard_map/ppermute | solution.py:58
  136.4 4.4 %collective-permute-start.36 = (f32[32,32]{0,1:T(8,128)S(1)}, f32[32,32]{0,1:T(8,128)S(1)}, u32[]{:S(2)}, u32[]{:S(2)}) collective-permute-start(f32[32,32]{0,1:T(8,128)S(1)} %add.334), channel_id=1, source_target_pairs={{0,2},{1,3},{2,0},{3,1},{4,6},{5,7},{6,4},{7,5},{8,10},{9,11},{10,... | collective-permute-start | bytes 12296 | tf_op jit(solution)/shard_map/ppermute | solution.py:58
  136.4 4.7 %collective-permute-start.37 = (f32[32,32]{0,1:T(8,128)S(1)}, f32[32,32]{0,1:T(8,128)S(1)}, u32[]{:S(2)}, u32[]{:S(2)}) collective-permute-start(f32[32,32]{0,1:T(8,128)S(1)} %add.334), channel_id=1, source_target_pairs={{0,4},{1,5},{2,6},{3,7},{4,0},{5,1},{6,2},{7,3},{8,12},{9,13},{10,... | collective-permute-start | bytes 12296 | tf_op jit(solution)/shard_map/ppermute | solution.py:58
  137.4 5.5 %collective-permute-start.38 = (f32[32,32]{0,1:T(8,128)S(1)}, f32[32,32]{0,1:T(8,128)S(1)}, u32[]{:S(2)}, u32[]{:S(2)}) collective-permute-start(f32[32,32]{0,1:T(8,128)S(1)} %add.334), channel_id=1, source_target_pairs={{0,6},{1,7},{2,4},{3,5},{4,2},{5,3},{6,0},{7,1},{8,14},{9,15},{10,... | collective-permute-start | bytes 12296 | tf_op jit(solution)/shard_map/ppermute | solution.py:58
  150.2 5.0 %collective-permute-start.39 = (bf16[3,32,192]{2,1,0:T(8,128)(2,1)S(1)}, bf16[3,32,192]{2,1,0:T(8,128)(2,1)S(1)}, u32[]{:S(2)}, u32[]{:S(2)}) collective-permute-start(bf16[3,32,192]{2,1,0:T(8,128)(2,1)S(1)} %get-tuple-element.16), channel_id=1, source_target_pairs={{0,8},{8,16},{16,24},{24,0},{1,9},{9,17},{17,25},{25,1},{2,10},{10... | collective-permute-start | bytes 110600 | tf_op jit(solution)/shard_map/ppermute | solution.py:98
  150.7 4.5 %collective-permute-start.40 = (bf16[3,32,192]{2,1,0:T(8,128)(2,1)S(1)}, bf16[3,32,192]{2,1,0:T(8,128)(2,1)S(1)}, u32[]{:S(2)}, u32[]{:S(2)}) collective-permute-start(bf16[3,32,192]{2,1,0:T(8,128)(2,1)S(1)} %get-tuple-element.16), channel_id=1, source_target_pairs={{0,24},{8,0},{16,8},{24,16},{1,25},{9,1},{17,9},{25,17},{2,26},{10... | collective-permute-start | bytes 110600 | tf_op jit(solution)/shard_map/ppermute | solution.py:98
  155.3 4.1 %collective-permute-start.42 = (bf16[3,3,32,192]{3,2,1,0:T(8,128)(2,1)S(1)}, bf16[3,3,32,192]{3,2,1,0:T(8,128)(2,1)S(1)}, u32[]{:S(2)}, u32[]{:S(2)}) collective-permute-start(bf16[3,3,32,192]{3,2,1,0:T(8,128)(2,1)S(1)} %pad_maximum_fusion.8), channel_id=1, source_target_pairs={{0,7},{1,0},{2,1},{3,2},{4,3},{5,4},{6,5},{7,6},{8,15},{9,8},{10,9... | collective-permute-start | bytes 331784 | tf_op jit(solution)/shard_map/ppermute | solution.py:98
  155.7 7.7 %collective-permute-start.41 = (bf16[3,3,32,192]{3,2,1,0:T(8,128)(2,1)S(1)}, bf16[3,3,32,192]{3,2,1,0:T(8,128)(2,1)S(1)}, u32[]{:S(2)}, u32[]{:S(2)}) collective-permute-start(bf16[3,3,32,192]{3,2,1,0:T(8,128)(2,1)S(1)} %pad_maximum_fusion.8), channel_id=1, source_target_pairs={{0,1},{1,2},{2,3},{3,4},{4,5},{5,6},{6,7},{7,0},{8,9},{9,10},{10,1... | collective-permute-start | bytes 331784 | tf_op jit(solution)/shard_map/ppermute | solution.py:98
  164.4 5.0 %collective-permute-start.43 = (bf16[3,32,192]{2,1,0:T(8,128)(2,1)S(1)}, bf16[3,32,192]{2,1,0:T(8,128)(2,1)S(1)}, u32[]{:S(2)}, u32[]{:S(2)}) collective-permute-start(bf16[3,32,192]{2,1,0:T(8,128)(2,1)S(1)} %get-tuple-element.14), channel_id=1, source_target_pairs={{0,8},{8,16},{16,24},{24,0},{1,9},{9,17},{17,25},{25,1},{2,10},{10... | collective-permute-start | bytes 110600 | tf_op jit(solution)/shard_map/ppermute | solution.py:98
  171.0 4.1 %collective-permute-start.46 = (bf16[3,3,32,192]{3,2,1,0:T(8,128)(2,1)S(1)}, bf16[3,3,32,192]{3,2,1,0:T(8,128)(2,1)S(1)}, u32[]{:S(2)}, u32[]{:S(2)}) collective-permute-start(bf16[3,3,32,192]{3,2,1,0:T(8,128)(2,1)S(1)} %pad_maximum_fusion.9), channel_id=1, source_target_pairs={{0,7},{1,0},{2,1},{3,2},{4,3},{5,4},{6,5},{7,6},{8,15},{9,8},{10,9... | collective-permute-start | bytes 331784 | tf_op jit(solution)/shard_map/ppermute | solution.py:98
  171.9 6.4 %collective-permute-start.45 = (bf16[3,3,32,192]{3,2,1,0:T(8,128)(2,1)S(1)}, bf16[3,3,32,192]{3,2,1,0:T(8,128)(2,1)S(1)}, u32[]{:S(2)}, u32[]{:S(2)}) collective-permute-start(bf16[3,3,32,192]{3,2,1,0:T(8,128)(2,1)S(1)} %pad_maximum_fusion.9), channel_id=1, source_target_pairs={{0,1},{1,2},{2,3},{3,4},{4,5},{5,6},{6,7},{7,0},{8,9},{9,10},{10,1... | collective-permute-start | bytes 331784 | tf_op jit(solution)/shard_map/ppermute | solution.py:98
  179.2 5.0 %collective-permute-start.47 = (bf16[3,32,192]{2,1,0:T(8,128)(2,1)S(1)}, bf16[3,32,192]{2,1,0:T(8,128)(2,1)S(1)}, u32[]{:S(2)}, u32[]{:S(2)}) collective-permute-start(bf16[3,32,192]{2,1,0:T(8,128)(2,1)S(1)} %get-tuple-element.12), channel_id=1, source_target_pairs={{0,8},{8,16},{16,24},{24,0},{1,9},{9,17},{17,25},{25,1},{2,10},{10... | collective-permute-start | bytes 110600 | tf_op jit(solution)/shard_map/ppermute | solution.py:98
  185.9 4.1 %collective-permute-start.50 = (bf16[3,3,32,192]{3,2,1,0:T(8,128)(2,1)S(1)}, bf16[3,3,32,192]{3,2,1,0:T(8,128)(2,1)S(1)}, u32[]{:S(2)}, u32[]{:S(2)}) collective-permute-start(bf16[3,3,32,192]{3,2,1,0:T(8,128)(2,1)S(1)} %pad_maximum_fusion.10), channel_id=1, source_target_pairs={{0,7},{1,0},{2,1},{3,2},{4,3},{5,4},{6,5},{7,6},{8,15},{9,8},{10,9... | collective-permute-start | bytes 331784 | tf_op jit(solution)/shard_map/ppermute | solution.py:98
  186.3 6.4 %collective-permute-start.49 = (bf16[3,3,32,192]{3,2,1,0:T(8,128)(2,1)S(1)}, bf16[3,3,32,192]{3,2,1,0:T(8,128)(2,1)S(1)}, u32[]{:S(2)}, u32[]{:S(2)}) collective-permute-start(bf16[3,3,32,192]{3,2,1,0:T(8,128)(2,1)S(1)} %pad_maximum_fusion.10), channel_id=1, source_target_pairs={{0,1},{1,2},{2,3},{3,4},{4,5},{5,6},{6,7},{7,0},{8,9},{9,10},{10,1... | collective-permute-start | bytes 331784 | tf_op jit(solution)/shard_map/ppermute | solution.py:98
  193.6 5.0 %collective-permute-start.51 = (bf16[3,32,192]{2,1,0:T(8,128)(2,1)S(1)}, bf16[3,32,192]{2,1,0:T(8,128)(2,1)S(1)}, u32[]{:S(2)}, u32[]{:S(2)}) collective-permute-start(bf16[3,32,192]{2,1,0:T(8,128)(2,1)S(1)} %get-tuple-element.10), channel_id=1, source_target_pairs={{0,8},{8,16},{16,24},{24,0},{1,9},{9,17},{17,25},{25,1},{2,10},{10... | collective-permute-start | bytes 110600 | tf_op jit(solution)/shard_map/ppermute | solution.py:98
  198.8 4.1 %collective-permute-start.54 = (bf16[3,3,32,192]{3,2,1,0:T(8,128)(2,1)S(1)}, bf16[3,3,32,192]{3,2,1,0:T(8,128)(2,1)S(1)}, u32[]{:S(2)}, u32[]{:S(2)}) collective-permute-start(bf16[3,3,32,192]{3,2,1,0:T(8,128)(2,1)S(1)} %pad_maximum_fusion.11), channel_id=1, source_target_pairs={{0,7},{1,0},{2,1},{3,2},{4,3},{5,4},{6,5},{7,6},{8,15},{9,8},{10,9... | collective-permute-start | bytes 331784 | tf_op jit(solution)/shard_map/ppermute | solution.py:98
  199.7 6.4 %collective-permute-start.53 = (bf16[3,3,32,192]{3,2,1,0:T(8,128)(2,1)S(1)}, bf16[3,3,32,192]{3,2,1,0:T(8,128)(2,1)S(1)}, u32[]{:S(2)}, u32[]{:S(2)}) collective-permute-start(bf16[3,3,32,192]{3,2,1,0:T(8,128)(2,1)S(1)} %pad_maximum_fusion.11), channel_id=1, source_target_pairs={{0,1},{1,2},{2,3},{3,4},{4,5},{5,6},{6,7},{7,0},{8,9},{9,10},{10,1... | collective-permute-start | bytes 331784 | tf_op jit(solution)/shard_map/ppermute | solution.py:98
  207.0 5.0 %collective-permute-start.55 = (bf16[3,32,192]{2,1,0:T(8,128)(2,1)S(1)}, bf16[3,32,192]{2,1,0:T(8,128)(2,1)S(1)}, u32[]{:S(2)}, u32[]{:S(2)}) collective-permute-start(bf16[3,32,192]{2,1,0:T(8,128)(2,1)S(1)} %get-tuple-element.33), channel_id=1, source_target_pairs={{0,8},{8,16},{16,24},{24,0},{1,9},{9,17},{17,25},{25,1},{2,10},{10... | collective-permute-start | bytes 110600 | tf_op jit(solution)/shard_map/ppermute | solution.py:98
  213.1 4.1 %collective-permute-start.58 = (bf16[3,3,32,192]{3,2,1,0:T(8,128)(2,1)S(1)}, bf16[3,3,32,192]{3,2,1,0:T(8,128)(2,1)S(1)}, u32[]{:S(2)}, u32[]{:S(2)}) collective-permute-start(bf16[3,3,32,192]{3,2,1,0:T(8,128)(2,1)S(1)} %pad_maximum_fusion.12), channel_id=1, source_target_pairs={{0,7},{1,0},{2,1},{3,2},{4,3},{5,4},{6,5},{7,6},{8,15},{9,8},{10,9... | collective-permute-start | bytes 331784 | tf_op jit(solution)/shard_map/ppermute | solution.py:98
  213.4 6.4 %collective-permute-start.57 = (bf16[3,3,32,192]{3,2,1,0:T(8,128)(2,1)S(1)}, bf16[3,3,32,192]{3,2,1,0:T(8,128)(2,1)S(1)}, u32[]{:S(2)}, u32[]{:S(2)}) collective-permute-start(bf16[3,3,32,192]{3,2,1,0:T(8,128)(2,1)S(1)} %pad_maximum_fusion.12), channel_id=1, source_target_pairs={{0,1},{1,2},{2,3},{3,4},{4,5},{5,6},{6,7},{7,0},{8,9},{9,10},{10,1... | collective-permute-start | bytes 331784 | tf_op jit(solution)/shard_map/ppermute | solution.py:98
  220.7 5.0 %collective-permute-start.59 = (bf16[3,32,192]{2,1,0:T(8,128)(2,1)S(1)}, bf16[3,32,192]{2,1,0:T(8,128)(2,1)S(1)}, u32[]{:S(2)}, u32[]{:S(2)}) collective-permute-start(bf16[3,32,192]{2,1,0:T(8,128)(2,1)S(1)} %get-tuple-element.35), channel_id=1, source_target_pairs={{0,8},{8,16},{16,24},{24,0},{1,9},{9,17},{17,25},{25,1},{2,10},{10... | collective-permute-start | bytes 110600 | tf_op jit(solution)/shard_map/ppermute | solution.py:98
  222.3 4.1 %collective-permute-start.60 = (bf16[3,32,192]{2,1,0:T(8,128)(2,1)S(1)}, bf16[3,32,192]{2,1,0:T(8,128)(2,1)S(1)}, u32[]{:S(2)}, u32[]{:S(2)}) collective-permute-start(bf16[3,32,192]{2,1,0:T(8,128)(2,1)S(1)} %get-tuple-element.35), channel_id=1, source_target_pairs={{0,24},{8,0},{16,8},{24,16},{1,25},{9,1},{17,9},{25,17},{2,26},{10... | collective-permute-start | bytes 110600 | tf_op jit(solution)/shard_map/ppermute | solution.py:98
  226.4 4.1 %collective-permute-start.62 = (bf16[3,3,32,192]{3,2,1,0:T(8,128)(2,1)S(1)}, bf16[3,3,32,192]{3,2,1,0:T(8,128)(2,1)S(1)}, u32[]{:S(2)}, u32[]{:S(2)}) collective-permute-start(bf16[3,3,32,192]{3,2,1,0:T(8,128)(2,1)S(1)} %pad_maximum_fusion.13), channel_id=1, source_target_pairs={{0,7},{1,0},{2,1},{3,2},{4,3},{5,4},{6,5},{7,6},{8,15},{9,8},{10,9... | collective-permute-start | bytes 331784 | tf_op jit(solution)/shard_map/ppermute | solution.py:98
  227.1 6.4 %collective-permute-start.61 = (bf16[3,3,32,192]{3,2,1,0:T(8,128)(2,1)S(1)}, bf16[3,3,32,192]{3,2,1,0:T(8,128)(2,1)S(1)}, u32[]{:S(2)}, u32[]{:S(2)}) collective-permute-start(bf16[3,3,32,192]{3,2,1,0:T(8,128)(2,1)S(1)} %pad_maximum_fusion.13), channel_id=1, source_target_pairs={{0,1},{1,2},{2,3},{3,4},{4,5},{5,6},{6,7},{7,0},{8,9},{9,10},{10,1... | collective-permute-start | bytes 331784 | tf_op jit(solution)/shard_map/ppermute | solution.py:98
  234.4 5.0 %collective-permute-start.63 = (bf16[3,32,192]{2,1,0:T(8,128)(2,1)S(1)}, bf16[3,32,192]{2,1,0:T(8,128)(2,1)S(1)}, u32[]{:S(2)}, u32[]{:S(2)}) collective-permute-start(bf16[3,32,192]{2,1,0:T(8,128)(2,1)S(1)} %get-tuple-element.37), channel_id=1, source_target_pairs={{0,8},{8,16},{16,24},{24,0},{1,9},{9,17},{17,25},{25,1},{2,10},{10... | collective-permute-start | bytes 110600 | tf_op jit(solution)/shard_map/ppermute | solution.py:98
  240.6 4.1 %collective-permute-start.66 = (bf16[3,3,32,192]{3,2,1,0:T(8,128)(2,1)S(1)}, bf16[3,3,32,192]{3,2,1,0:T(8,128)(2,1)S(1)}, u32[]{:S(2)}, u32[]{:S(2)}) collective-permute-start(bf16[3,3,32,192]{3,2,1,0:T(8,128)(2,1)S(1)} %pad_maximum_fusion.14), channel_id=1, source_target_pairs={{0,7},{1,0},{2,1},{3,2},{4,3},{5,4},{6,5},{7,6},{8,15},{9,8},{10,9... | collective-permute-start | bytes 331784 | tf_op jit(solution)/shard_map/ppermute | solution.py:98
  241.5 6.4 %collective-permute-start.65 = (bf16[3,3,32,192]{3,2,1,0:T(8,128)(2,1)S(1)}, bf16[3,3,32,192]{3,2,1,0:T(8,128)(2,1)S(1)}, u32[]{:S(2)}, u32[]{:S(2)}) collective-permute-start(bf16[3,3,32,192]{3,2,1,0:T(8,128)(2,1)S(1)} %pad_maximum_fusion.14), channel_id=1, source_target_pairs={{0,1},{1,2},{2,3},{3,4},{4,5},{5,6},{6,7},{7,0},{8,9},{9,10},{10,1... | collective-permute-start | bytes 331784 | tf_op jit(solution)/shard_map/ppermute | solution.py:98
  248.8 5.0 %collective-permute-start.67 = (bf16[3,32,192]{2,1,0:T(8,128)(2,1)S(1)}, bf16[3,32,192]{2,1,0:T(8,128)(2,1)S(1)}, u32[]{:S(2)}, u32[]{:S(2)}) collective-permute-start(bf16[3,32,192]{2,1,0:T(8,128)(2,1)S(1)} %get-tuple-element.39), channel_id=1, source_target_pairs={{0,8},{8,16},{16,24},{24,0},{1,9},{9,17},{17,25},{25,1},{2,10},{10... | collective-permute-start | bytes 110600 | tf_op jit(solution)/shard_map/ppermute | solution.py:98
  254.0 4.1 %collective-permute-start.70 = (bf16[3,3,32,192]{3,2,1,0:T(8,128)(2,1)S(1)}, bf16[3,3,32,192]{3,2,1,0:T(8,128)(2,1)S(1)}, u32[]{:S(2)}, u32[]{:S(2)}) collective-permute-start(bf16[3,3,32,192]{3,2,1,0:T(8,128)(2,1)S(1)} %pad_maximum_fusion.15), channel_id=1, source_target_pairs={{0,7},{1,0},{2,1},{3,2},{4,3},{5,4},{6,5},{7,6},{8,15},{9,8},{10,9... | collective-permute-start | bytes 331784 | tf_op jit(solution)/shard_map/ppermute | solution.py:98
  254.9 6.4 %collective-permute-start.69 = (bf16[3,3,32,192]{3,2,1,0:T(8,128)(2,1)S(1)}, bf16[3,3,32,192]{3,2,1,0:T(8,128)(2,1)S(1)}, u32[]{:S(2)}, u32[]{:S(2)}) collective-permute-start(bf16[3,3,32,192]{3,2,1,0:T(8,128)(2,1)S(1)} %pad_maximum_fusion.15), channel_id=1, source_target_pairs={{0,1},{1,2},{2,3},{3,4},{4,5},{5,6},{6,7},{7,0},{8,9},{9,10},{10,1... | collective-permute-start | bytes 331784 | tf_op jit(solution)/shard_map/ppermute | solution.py:98
  265.1 4.6 %collective-permute-start.73 = (f32[32,32]{0,1:T(8,128)S(1)}, f32[32,32]{0,1:T(8,128)S(1)}, u32[]{:S(2)}, u32[]{:S(2)}) collective-permute-start(f32[32,32]{0,1:T(8,128)S(1)} %convolution_bitcast_fusion.65), channel_id=1, source_target_pairs={{0,24},{8,16},{16,8},{24,0},{1,25},{9,17},{17,9},{25,1},{2,26},{10... | collective-permute-start | bytes 12296 | tf_op jit(solution)/shard_map/ppermute | solution.py:58
  271.0 4.4 %collective-permute-start.75 = (f32[32,32]{0,1:T(8,128)S(1)}, f32[32,32]{0,1:T(8,128)S(1)}, u32[]{:S(2)}, u32[]{:S(2)}) collective-permute-start(f32[32,32]{0,1:T(8,128)S(1)} %add.372), channel_id=1, source_target_pairs={{0,2},{1,3},{2,0},{3,1},{4,6},{5,7},{6,4},{7,5},{8,10},{9,11},{10,... | collective-permute-start | bytes 12296 | tf_op jit(solution)/shard_map/ppermute | solution.py:58
  271.0 4.7 %collective-permute-start.76 = (f32[32,32]{0,1:T(8,128)S(1)}, f32[32,32]{0,1:T(8,128)S(1)}, u32[]{:S(2)}, u32[]{:S(2)}) collective-permute-start(f32[32,32]{0,1:T(8,128)S(1)} %add.372), channel_id=1, source_target_pairs={{0,4},{1,5},{2,6},{3,7},{4,0},{5,1},{6,2},{7,3},{8,12},{9,13},{10,... | collective-permute-start | bytes 12296 | tf_op jit(solution)/shard_map/ppermute | solution.py:58
  272.1 5.5 %collective-permute-start.77 = (f32[32,32]{0,1:T(8,128)S(1)}, f32[32,32]{0,1:T(8,128)S(1)}, u32[]{:S(2)}, u32[]{:S(2)}) collective-permute-start(f32[32,32]{0,1:T(8,128)S(1)} %add.372), channel_id=1, source_target_pairs={{0,6},{1,7},{2,4},{3,5},{4,2},{5,3},{6,0},{7,1},{8,14},{9,15},{10,... | collective-permute-start | bytes 12296 | tf_op jit(solution)/shard_map/ppermute | solution.py:58
  (17 other events, 169.7 us)

commit v10 on v6

--- a/solution.py
+++ b/solution.py
@@ -75,9 +75,10 @@
     )
     gram_matrix = all_sum(partial_gram, ("gx", "gy"))
     factor = jnp.linalg.cholesky(gram_matrix)
-    identity = jnp.eye(filtered.shape[1], dtype=jnp.float32)
-    inverse = jax.scipy.linalg.solve_triangular(factor, identity, lower=True)
-    result = jnp.einsum("vw,zwd->zvd", inverse, filtered, precision=lax.Precision.HIGHEST)
+    depth, vectors, rows = filtered.shape
+    stacked = jnp.transpose(filtered, (1, 0, 2)).reshape(vectors, depth * rows)
+    solved = lax.linalg.triangular_solve(factor, stacked, left_side=True, lower=True)
+    result = jnp.transpose(solved.reshape(vectors, depth, rows), (1, 0, 2))
     return result * math.sqrt(rows_total)
 
 

time: 286 us -> 286 us (level)
  transfers between devices with their start and end apart: 78 -> 78, of which waited for: 71 -> 71; matrix products, arithmetic and copies ran while one was open for 18% -> 19% of each run, Pallas kernels for 0% -> 0%
where the time goes in v10:
time: 286 us
  waiting for transfers between devices  121 us (42%)
  starting transfers between devices  78.3 us (27%)
  matrix products  52 us (18%)
  other arithmetic  21.5 us (8%)
  local copies, waits for them, and re-layouts  12 us (4%)
    ppermute x64, waiting for transfers between devices, shift(): lax.ppermute(value, axis, [(i, (i + step) % count) for i in range(count)])  103 us
    ppermute x64, starting transfers between devices, shift(): lax.ppermute(value, axis, [(i, (i + step) % count) for i in range(count)])  65.6 us
    dot_general x64, matrix products, part(): jnp.einsum('kvj,tkij->tvi', cells, blocks, preferred_element_type=jnp.flo...  50.8 us
    ppermute x14, waiting for transfers between devices, swap(): return lax.ppermute(v, axis, [(i, i ^ stride) for i in range(count)])  18.6 us
    ppermute x14, starting transfers between devices, swap(): return lax.ppermute(v, axis, [(i, i ^ stride) for i in range(count)])  12.7 us
    gather x1, local copies, waits for them, and re-layouts, dense_coupling(): jnp.take(matrices, index.reshape(-1), axis=0)  10.3 us
    another operation x6, other arithmetic, orthonormal(): factor = jnp.linalg.cholesky(gram_matrix)  7.19 us
    another operation x4, other arithmetic, orthonormal(): lax.linalg.triangular_solve(factor, stacked, left_side=True, lower=True)  6.17 us
  transfers between devices with their start and end apart: 78, of which 71 were waited for; matrix products, arithmetic and copies ran while one was open for 19% of the time, Pallas kernels for 0%

profile of v10, /device:TPU:0, one launch (start us, length us, event | category | flops | bytes accessed | tf_op | source)
XLA Modules:
  0.0 285.6 jit_solution(7364138700046759204)
XLA Ops:
  0.9 3.0 %collective-permute-start = (bf16[3,32,192]{2,1,0:T(8,128)(2,1)S(1)}, bf16[3,32,192]{2,1,0:T(8,128)(2,1)S(1)}, u32[]{:S(2)}, u32[]{:S(2)}) collective-permute-start(bf16[3,32,192]{2,1,0:T(8,128)(2,1)S(1)} %get-tuple-element.20), channel_id=1, source_target_pairs={{0,8},{8,16},{16,24},{24,0},{1,9},{9,17},{17,25},{25,1},{2,10},{10... | collective-permute-start | bytes 110600 | tf_op jit(solution)/shard_map/ppermute | solution.py:96
  8.7 1.9 collective-permute-start.3
  10.6 10.3 %gather_fusion = bf16[81,192,192]{2,1,0:T(8,128)(2,1)} fusion(bf16[81,192,192]{2,1,0:T(8,128)(2,1)} %bitcast.933, s32[1024]{0:T(1024)S(1)} %pad_clamp_fusion), kind=kCustom, calls=%fused_computation | custom fusion | bytes 11944260 | tf_op jit(solution)/shard_map/jit(_take)/gather | solution.py:42
  20.9 4.3 %select_select_fusion = bf16[3,27,192,192]{3,2,1,0:T(8,128)(2,1)S(1)} fusion(bf16[3,27,192,192]{3,2,1,0:T(8,128)(2,1)} %bitcast.932, pred[3,27]{1,0:T(4,128)(4,1)S(1)} %compare_and_fusion, pred[3,27]{1,0:T(4,128)(4,1)S(1)} %and_reduce_fusion), kind=kLoop, calls=%fused_computation.1 | loop fusion | flops 5971968 | bytes 11944098 | tf_op jit(solution)/shard_map/jit(_where)/select_n | solution.py:46
  26.3 2.0 convolution_bitcast_fusion.30
  29.2 2.6 collective-permute-start.4
  32.6 2.2 collective-permute-done.4
  36.0 2.2 collective-permute-start.7
  38.8 2.1 collective-permute-done.7
  41.8 2.8 collective-permute-done.6
  52.5 2.9 %collective-permute-done.11 = bf16[3,3,32,192]{3,2,1,0:T(8,128)(2,1)S(1)} collective-permute-done((bf16[3,3,32,192]{3,2,1,0:T(8,128)(2,1)S(1)}, bf16[3,3,32,192]{3,2,1,0:T(8,128)(2,1)S(1)}, u32[]{:S(2)}, u32[]{:S(2)}) %collective-permute-start.11) | collective-permute-done | bytes 110624 | tf_op jit(solution)/shard_map/ppermute | solution.py:96
  66.1 2.3 collective-permute-done.15
  69.3 2.6 collective-permute-done.14
  76.1 1.7 collective-permute-done.16
  79.5 2.9 %collective-permute-done.19 = bf16[3,3,32,192]{3,2,1,0:T(8,128)(2,1)S(1)} collective-permute-done((bf16[3,3,32,192]{3,2,1,0:T(8,128)(2,1)S(1)}, bf16[3,3,32,192]{3,2,1,0:T(8,128)(2,1)S(1)}, u32[]{:S(2)}, u32[]{:S(2)}) %collective-permute-start.19) | collective-permute-done | bytes 110624 | tf_op jit(solution)/shard_map/ppermute | solution.py:96
  83.3 1.8 collective-permute-done.18
  86.1 2.1 collective-permute-start.20
  89.4 1.7 collective-permute-done.20
  93.8 2.6 collective-permute-done.23
  97.3 2.3 collective-permute-done.22
  107.3 2.8 collective-permute-done.27
  111.0 2.1 collective-permute-done.26
  120.8 2.8 collective-permute-done.31
  124.5 2.1 collective-permute-done.30
  127.7 1.7 collective-permute-start.32
  133.2 2.0 collective-permute-done.34
  135.3 1.8 collective-permute-start.37
  137.1 1.9 collective-permute-done.36
  140.1 3.6 %collective-permute-done.38 = f32[32,32]{0,1:T(8,128)S(1)} collective-permute-done((f32[32,32]{0,1:T(8,128)S(1)}, f32[32,32]{0,1:T(8,128)S(1)}, u32[]{:S(2)}, u32[]{:S(2)}) %collective-permute-start.38) | collective-permute-done | bytes 4128 | tf_op jit(solution)/shard_map/ppermute | solution.py:58
  143.8 2.9 %cholesky.44 = f32[32,32]{1,0:T(8,128)S(1)} custom-call(f32[32,32]{1,0:T(8,128)S(1)} %fusion.171), custom_call_target="Cholesky" | custom-call | tf_op jit(solution)/shard_map/jit(cholesky)/cholesky | solution.py:77
  148.1 2.4 custom-call.6
  151.7 2.2 collective-permute-start.40
  156.6 2.5 fusion.70
  159.5 2.6 convolution_bitcast_fusion.14
  163.5 2.4 collective-permute-start.43
  166.9 2.1 collective-permute-done.43
  170.1 1.9 collective-permute-start.46
  172.6 2.1 collective-permute-done.46
  175.6 2.8 collective-permute-done.45
  182.7 1.7 collective-permute-done.47
  186.3 2.6 collective-permute-done.50
  189.8 2.3 collective-permute-done.49
  196.3 1.7 collective-permute-done.51
  200.0 2.6 collective-permute-done.54
  203.5 2.3 collective-permute-done.53
  210.0 1.7 collective-permute-done.55
  213.8 2.4 collective-permute-done.58
  217.1 2.5 collective-permute-done.57
  221.7 1.8 collective-permute-start.60
  223.9 1.7 collective-permute-done.59
  227.4 2.5 collective-permute-done.62
  230.8 2.4 collective-permute-done.61
  237.5 1.7 collective-permute-done.63
  241.2 2.8 collective-permute-done.66
  244.9 2.0 collective-permute-done.65
  251.2 1.7 collective-permute-done.67
  255.0 2.4 collective-permute-done.70
  258.3 2.5 collective-permute-done.69
  267.2 1.9 collective-permute-done.73
  269.2 1.8 collective-permute-start.76
  271.0 1.9 collective-permute-done.75
  274.0 3.7 %collective-permute-done.77 = f32[32,32]{0,1:T(8,128)S(1)} collective-permute-done((f32[32,32]{0,1:T(8,128)S(1)}, f32[32,32]{0,1:T(8,128)S(1)}, u32[]{:S(2)}, u32[]{:S(2)}) %collective-permute-start.77) | collective-permute-done | bytes 4128 | tf_op jit(solution)/shard_map/ppermute | solution.py:58
  277.8 2.9 %cholesky.55 = f32[32,32]{1,0:T(8,128)S(1)} custom-call(f32[32,32]{1,0:T(8,128)S(1)} %fusion.168), custom_call_target="Cholesky" | custom-call | tf_op jit(solution)/shard_map/jit(cholesky)/cholesky | solution.py:77
  282.0 2.4 custom-call.7
  (223 shorter events, 128.3 us)
Async XLA Ops:
  0.9 6.0 %collective-permute-start = (bf16[3,32,192]{2,1,0:T(8,128)(2,1)S(1)}, bf16[3,32,192]{2,1,0:T(8,128)(2,1)S(1)}, u32[]{:S(2)}, u32[]{:S(2)}) collective-permute-start(bf16[3,32,192]{2,1,0:T(8,128)(2,1)S(1)} %get-tuple-element.20), channel_id=1, source_target_pairs={{0,8},{8,16},{16,24},{24,0},{1,9},{9,17},{17,25},{25,1},{2,10},{10... | collective-permute-start | bytes 110600 | tf_op jit(solution)/shard_map/ppermute | solution.py:96
  3.9 4.1 %collective-permute-start.1 = (bf16[3,32,192]{2,1,0:T(8,128)(2,1)S(1)}, bf16[3,32,192]{2,1,0:T(8,128)(2,1)S(1)}, u32[]{:S(2)}, u32[]{:S(2)}) collective-permute-start(bf16[3,32,192]{2,1,0:T(8,128)(2,1)S(1)} %get-tuple-element.20), channel_id=1, source_target_pairs={{0,24},{8,0},{16,8},{24,16},{1,25},{9,1},{17,9},{25,17},{2,26},{10... | collective-permute-start | bytes 110600 | tf_op jit(solution)/shard_map/ppermute | solution.py:96
  8.7 17.6 %collective-permute-start.3 = (bf16[3,3,32,192]{3,2,1,0:T(8,128)(2,1)}, bf16[3,3,32,192]{3,2,1,0:T(8,128)(2,1)}, u32[]{:S(2)}, u32[]{:S(2)}) collective-permute-start(bf16[3,3,32,192]{3,2,1,0:T(8,128)(2,1)} %pad_maximum_fusion), channel_id=1, source_target_pairs={{0,7},{1,0},{2,1},{3,2},{4,3},{5,4},{6,5},{7,6},{8,15},{9,8},{10,9... | collective-permute-start | bytes 331784 | tf_op jit(solution)/shard_map/ppermute | solution.py:96
  10.6 17.7 %collective-permute-start.2 = (bf16[3,3,32,192]{3,2,1,0:T(8,128)(2,1)}, bf16[3,3,32,192]{3,2,1,0:T(8,128)(2,1)S(1)}, u32[]{:S(2)}, u32[]{:S(2)}) collective-permute-start(bf16[3,3,32,192]{3,2,1,0:T(8,128)(2,1)} %pad_maximum_fusion), channel_id=1, source_target_pairs={{0,1},{1,2},{2,3},{3,4},{4,5},{5,6},{6,7},{7,0},{8,9},{9,10},{10,1... | collective-permute-start | bytes 331784 | tf_op jit(solution)/shard_map/ppermute | solution.py:96
  29.2 5.5 %collective-permute-start.4 = (bf16[3,32,192]{2,1,0:T(8,128)(2,1)S(1)}, bf16[3,32,192]{2,1,0:T(8,128)(2,1)S(1)}, u32[]{:S(2)}, u32[]{:S(2)}) collective-permute-start(bf16[3,32,192]{2,1,0:T(8,128)(2,1)S(1)} %get-tuple-element.26), channel_id=1, source_target_pairs={{0,8},{8,16},{16,24},{24,0},{1,9},{9,17},{17,25},{25,1},{2,10},{10... | collective-permute-start | bytes 110600 | tf_op jit(solution)/shard_map/ppermute | solution.py:96
  31.8 4.1 %collective-permute-start.5 = (bf16[3,32,192]{2,1,0:T(8,128)(2,1)S(1)}, bf16[3,32,192]{2,1,0:T(8,128)(2,1)S(1)}, u32[]{:S(2)}, u32[]{:S(2)}) collective-permute-start(bf16[3,32,192]{2,1,0:T(8,128)(2,1)S(1)} %get-tuple-element.26), channel_id=1, source_target_pairs={{0,24},{8,0},{16,8},{24,16},{1,25},{9,1},{17,9},{25,17},{2,26},{10... | collective-permute-start | bytes 110600 | tf_op jit(solution)/shard_map/ppermute | solution.py:96
  36.0 4.9 %collective-permute-start.7 = (bf16[3,3,32,192]{3,2,1,0:T(8,128)(2,1)S(1)}, bf16[3,3,32,192]{3,2,1,0:T(8,128)(2,1)S(1)}, u32[]{:S(2)}, u32[]{:S(2)}) collective-permute-start(bf16[3,3,32,192]{3,2,1,0:T(8,128)(2,1)S(1)} %pad_maximum_fusion.1), channel_id=1, source_target_pairs={{0,7},{1,0},{2,1},{3,2},{4,3},{5,4},{6,5},{7,6},{8,15},{9,8},{10,9... | collective-permute-start | bytes 331784 | tf_op jit(solution)/shard_map/ppermute | solution.py:96
  38.2 6.4 %collective-permute-start.6 = (bf16[3,3,32,192]{3,2,1,0:T(8,128)(2,1)S(1)}, bf16[3,3,32,192]{3,2,1,0:T(8,128)(2,1)S(1)}, u32[]{:S(2)}, u32[]{:S(2)}) collective-permute-start(bf16[3,3,32,192]{3,2,1,0:T(8,128)(2,1)S(1)} %pad_maximum_fusion.1), channel_id=1, source_target_pairs={{0,1},{1,2},{2,3},{3,4},{4,5},{5,6},{6,7},{7,0},{8,9},{9,10},{10,1... | collective-permute-start | bytes 331784 | tf_op jit(solution)/shard_map/ppermute | solution.py:96
  45.5 5.0 %collective-permute-start.8 = (bf16[3,32,192]{2,1,0:T(8,128)(2,1)S(1)}, bf16[3,32,192]{2,1,0:T(8,128)(2,1)S(1)}, u32[]{:S(2)}, u32[]{:S(2)}) collective-permute-start(bf16[3,32,192]{2,1,0:T(8,128)(2,1)S(1)} %get-tuple-element.28), channel_id=1, source_target_pairs={{0,8},{8,16},{16,24},{24,0},{1,9},{9,17},{17,25},{25,1},{2,10},{10... | collective-permute-start | bytes 110600 | tf_op jit(solution)/shard_map/ppermute | solution.py:96
  47.2 4.1 %collective-permute-start.9 = (bf16[3,32,192]{2,1,0:T(8,128)(2,1)S(1)}, bf16[3,32,192]{2,1,0:T(8,128)(2,1)S(1)}, u32[]{:S(2)}, u32[]{:S(2)}) collective-permute-start(bf16[3,32,192]{2,1,0:T(8,128)(2,1)S(1)} %get-tuple-element.28), channel_id=1, source_target_pairs={{0,24},{8,0},{16,8},{24,16},{1,25},{9,1},{17,9},{25,17},{2,26},{10... | collective-permute-start | bytes 110600 | tf_op jit(solution)/shard_map/ppermute | solution.py:96
  51.3 4.1 %collective-permute-start.11 = (bf16[3,3,32,192]{3,2,1,0:T(8,128)(2,1)S(1)}, bf16[3,3,32,192]{3,2,1,0:T(8,128)(2,1)S(1)}, u32[]{:S(2)}, u32[]{:S(2)}) collective-permute-start(bf16[3,3,32,192]{3,2,1,0:T(8,128)(2,1)S(1)} %pad_maximum_fusion.2), channel_id=1, source_target_pairs={{0,7},{1,0},{2,1},{3,2},{4,3},{5,4},{6,5},{7,6},{8,15},{9,8},{10,9... | collective-permute-start | bytes 331784 | tf_op jit(solution)/shard_map/ppermute | solution.py:96
  51.4 6.4 %collective-permute-start.10 = (bf16[3,3,32,192]{3,2,1,0:T(8,128)(2,1)S(1)}, bf16[3,3,32,192]{3,2,1,0:T(8,128)(2,1)S(1)}, u32[]{:S(2)}, u32[]{:S(2)}) collective-permute-start(bf16[3,3,32,192]{3,2,1,0:T(8,128)(2,1)S(1)} %pad_maximum_fusion.2), channel_id=1, source_target_pairs={{0,1},{1,2},{2,3},{3,4},{4,5},{5,6},{6,7},{7,0},{8,9},{9,10},{10,1... | collective-permute-start | bytes 331784 | tf_op jit(solution)/shard_map/ppermute | solution.py:96
  58.7 5.0 %collective-permute-start.12 = (bf16[3,32,192]{2,1,0:T(8,128)(2,1)S(1)}, bf16[3,32,192]{2,1,0:T(8,128)(2,1)S(1)}, u32[]{:S(2)}, u32[]{:S(2)}) collective-permute-start(bf16[3,32,192]{2,1,0:T(8,128)(2,1)S(1)} %get-tuple-element.30), channel_id=1, source_target_pairs={{0,8},{8,16},{16,24},{24,0},{1,9},{9,17},{17,25},{25,1},{2,10},{10... | collective-permute-start | bytes 110600 | tf_op jit(solution)/shard_map/ppermute | solution.py:96
  60.2 4.1 %collective-permute-start.13 = (bf16[3,32,192]{2,1,0:T(8,128)(2,1)S(1)}, bf16[3,32,192]{2,1,0:T(8,128)(2,1)S(1)}, u32[]{:S(2)}, u32[]{:S(2)}) collective-permute-start(bf16[3,32,192]{2,1,0:T(8,128)(2,1)S(1)} %get-tuple-element.30), channel_id=1, source_target_pairs={{0,24},{8,0},{16,8},{24,16},{1,25},{9,1},{17,9},{25,17},{2,26},{10... | collective-permute-start | bytes 110600 | tf_op jit(solution)/shard_map/ppermute | solution.py:96
  64.3 4.1 %collective-permute-start.15 = (bf16[3,3,32,192]{3,2,1,0:T(8,128)(2,1)S(1)}, bf16[3,3,32,192]{3,2,1,0:T(8,128)(2,1)S(1)}, u32[]{:S(2)}, u32[]{:S(2)}) collective-permute-start(bf16[3,3,32,192]{3,2,1,0:T(8,128)(2,1)S(1)} %pad_maximum_fusion.3), channel_id=1, source_target_pairs={{0,7},{1,0},{2,1},{3,2},{4,3},{5,4},{6,5},{7,6},{8,15},{9,8},{10,9... | collective-permute-start | bytes 331784 | tf_op jit(solution)/shard_map/ppermute | solution.py:96
  65.5 6.4 %collective-permute-start.14 = (bf16[3,3,32,192]{3,2,1,0:T(8,128)(2,1)S(1)}, bf16[3,3,32,192]{3,2,1,0:T(8,128)(2,1)S(1)}, u32[]{:S(2)}, u32[]{:S(2)}) collective-permute-start(bf16[3,3,32,192]{3,2,1,0:T(8,128)(2,1)S(1)} %pad_maximum_fusion.3), channel_id=1, source_target_pairs={{0,1},{1,2},{2,3},{3,4},{4,5},{5,6},{6,7},{7,0},{8,9},{9,10},{10,1... | collective-permute-start | bytes 331784 | tf_op jit(solution)/shard_map/ppermute | solution.py:96
  72.8 5.0 %collective-permute-start.16 = (bf16[3,32,192]{2,1,0:T(8,128)(2,1)S(1)}, bf16[3,32,192]{2,1,0:T(8,128)(2,1)S(1)}, u32[]{:S(2)}, u32[]{:S(2)}) collective-permute-start(bf16[3,32,192]{2,1,0:T(8,128)(2,1)S(1)} %get-tuple-element.32), channel_id=1, source_target_pairs={{0,8},{8,16},{16,24},{24,0},{1,9},{9,17},{17,25},{25,1},{2,10},{10... | collective-permute-start | bytes 110600 | tf_op jit(solution)/shard_map/ppermute | solution.py:96
  74.2 4.1 %collective-permute-start.17 = (bf16[3,32,192]{2,1,0:T(8,128)(2,1)S(1)}, bf16[3,32,192]{2,1,0:T(8,128)(2,1)S(1)}, u32[]{:S(2)}, u32[]{:S(2)}) collective-permute-start(bf16[3,32,192]{2,1,0:T(8,128)(2,1)S(1)} %get-tuple-element.32), channel_id=1, source_target_pairs={{0,24},{8,0},{16,8},{24,16},{1,25},{9,1},{17,9},{25,17},{2,26},{10... | collective-permute-start | bytes 110600 | tf_op jit(solution)/shard_map/ppermute | solution.py:96
  78.3 4.1 %collective-permute-start.19 = (bf16[3,3,32,192]{3,2,1,0:T(8,128)(2,1)S(1)}, bf16[3,3,32,192]{3,2,1,0:T(8,128)(2,1)S(1)}, u32[]{:S(2)}, u32[]{:S(2)}) collective-permute-start(bf16[3,3,32,192]{3,2,1,0:T(8,128)(2,1)S(1)} %pad_maximum_fusion.4), channel_id=1, source_target_pairs={{0,7},{1,0},{2,1},{3,2},{4,3},{5,4},{6,5},{7,6},{8,15},{9,8},{10,9... | collective-permute-start | bytes 331784 | tf_op jit(solution)/shard_map/ppermute | solution.py:96
  78.8 6.4 %collective-permute-start.18 = (bf16[3,3,32,192]{3,2,1,0:T(8,128)(2,1)S(1)}, bf16[3,3,32,192]{3,2,1,0:T(8,128)(2,1)S(1)}, u32[]{:S(2)}, u32[]{:S(2)}) collective-permute-start(bf16[3,3,32,192]{3,2,1,0:T(8,128)(2,1)S(1)} %pad_maximum_fusion.4), channel_id=1, source_target_pairs={{0,1},{1,2},{2,3},{3,4},{4,5},{5,6},{6,7},{7,0},{8,9},{9,10},{10,1... | collective-permute-start | bytes 331784 | tf_op jit(solution)/shard_map/ppermute | solution.py:96
  86.1 5.0 %collective-permute-start.20 = (bf16[3,32,192]{2,1,0:T(8,128)(2,1)S(1)}, bf16[3,32,192]{2,1,0:T(8,128)(2,1)S(1)}, u32[]{:S(2)}, u32[]{:S(2)}) collective-permute-start(bf16[3,32,192]{2,1,0:T(8,128)(2,1)S(1)} %get-tuple-element.34), channel_id=1, source_target_pairs={{0,8},{8,16},{16,24},{24,0},{1,9},{9,17},{17,25},{25,1},{2,10},{10... | collective-permute-start | bytes 110600 | tf_op jit(solution)/shard_map/ppermute | solution.py:96
  88.2 4.1 %collective-permute-start.21 = (bf16[3,32,192]{2,1,0:T(8,128)(2,1)S(1)}, bf16[3,32,192]{2,1,0:T(8,128)(2,1)S(1)}, u32[]{:S(2)}, u32[]{:S(2)}) collective-permute-start(bf16[3,32,192]{2,1,0:T(8,128)(2,1)S(1)} %get-tuple-element.34), channel_id=1, source_target_pairs={{0,24},{8,0},{16,8},{24,16},{1,25},{9,1},{17,9},{25,17},{2,26},{10... | collective-permute-start | bytes 110600 | tf_op jit(solution)/shard_map/ppermute | solution.py:96
  92.3 4.1 %collective-permute-start.23 = (bf16[3,3,32,192]{3,2,1,0:T(8,128)(2,1)S(1)}, bf16[3,3,32,192]{3,2,1,0:T(8,128)(2,1)S(1)}, u32[]{:S(2)}, u32[]{:S(2)}) collective-permute-start(bf16[3,3,32,192]{3,2,1,0:T(8,128)(2,1)S(1)} %pad_maximum_fusion.5), channel_id=1, source_target_pairs={{0,7},{1,0},{2,1},{3,2},{4,3},{5,4},{6,5},{7,6},{8,15},{9,8},{10,9... | collective-permute-start | bytes 331784 | tf_op jit(solution)/shard_map/ppermute | solution.py:96
  93.2 6.4 %collective-permute-start.22 = (bf16[3,3,32,192]{3,2,1,0:T(8,128)(2,1)S(1)}, bf16[3,3,32,192]{3,2,1,0:T(8,128)(2,1)S(1)}, u32[]{:S(2)}, u32[]{:S(2)}) collective-permute-start(bf16[3,3,32,192]{3,2,1,0:T(8,128)(2,1)S(1)} %pad_maximum_fusion.5), channel_id=1, source_target_pairs={{0,1},{1,2},{2,3},{3,4},{4,5},{5,6},{6,7},{7,0},{8,9},{9,10},{10,1... | collective-permute-start | bytes 331784 | tf_op jit(solution)/shard_map/ppermute | solution.py:96
  100.5 5.0 %collective-permute-start.24 = (bf16[3,32,192]{2,1,0:T(8,128)(2,1)S(1)}, bf16[3,32,192]{2,1,0:T(8,128)(2,1)S(1)}, u32[]{:S(2)}, u32[]{:S(2)}) collective-permute-start(bf16[3,32,192]{2,1,0:T(8,128)(2,1)S(1)} %get-tuple-element.36), channel_id=1, source_target_pairs={{0,8},{8,16},{16,24},{24,0},{1,9},{9,17},{17,25},{25,1},{2,10},{10... | collective-permute-start | bytes 110600 | tf_op jit(solution)/shard_map/ppermute | solution.py:96
  101.9 4.1 %collective-permute-start.25 = (bf16[3,32,192]{2,1,0:T(8,128)(2,1)S(1)}, bf16[3,32,192]{2,1,0:T(8,128)(2,1)S(1)}, u32[]{:S(2)}, u32[]{:S(2)}) collective-permute-start(bf16[3,32,192]{2,1,0:T(8,128)(2,1)S(1)} %get-tuple-element.36), channel_id=1, source_target_pairs={{0,24},{8,0},{16,8},{24,16},{1,25},{9,1},{17,9},{25,17},{2,26},{10... | collective-permute-start | bytes 110600 | tf_op jit(solution)/shard_map/ppermute | solution.py:96
  106.0 4.1 %collective-permute-start.27 = (bf16[3,3,32,192]{3,2,1,0:T(8,128)(2,1)S(1)}, bf16[3,3,32,192]{3,2,1,0:T(8,128)(2,1)S(1)}, u32[]{:S(2)}, u32[]{:S(2)}) collective-permute-start(bf16[3,3,32,192]{3,2,1,0:T(8,128)(2,1)S(1)} %pad_maximum_fusion.6), channel_id=1, source_target_pairs={{0,7},{1,0},{2,1},{3,2},{4,3},{5,4},{6,5},{7,6},{8,15},{9,8},{10,9... | collective-permute-start | bytes 331784 | tf_op jit(solution)/shard_map/ppermute | solution.py:96
  106.7 6.4 %collective-permute-start.26 = (bf16[3,3,32,192]{3,2,1,0:T(8,128)(2,1)S(1)}, bf16[3,3,32,192]{3,2,1,0:T(8,128)(2,1)S(1)}, u32[]{:S(2)}, u32[]{:S(2)}) collective-permute-start(bf16[3,3,32,192]{3,2,1,0:T(8,128)(2,1)S(1)} %pad_maximum_fusion.6), channel_id=1, source_target_pairs={{0,1},{1,2},{2,3},{3,4},{4,5},{5,6},{6,7},{7,0},{8,9},{9,10},{10,1... | collective-permute-start | bytes 331784 | tf_op jit(solution)/shard_map/ppermute | solution.py:96
  114.0 5.0 %collective-permute-start.28 = (bf16[3,32,192]{2,1,0:T(8,128)(2,1)S(1)}, bf16[3,32,192]{2,1,0:T(8,128)(2,1)S(1)}, u32[]{:S(2)}, u32[]{:S(2)}) collective-permute-start(bf16[3,32,192]{2,1,0:T(8,128)(2,1)S(1)} %get-tuple-element.38), channel_id=1, source_target_pairs={{0,8},{8,16},{16,24},{24,0},{1,9},{9,17},{17,25},{25,1},{2,10},{10... | collective-permute-start | bytes 110600 | tf_op jit(solution)/shard_map/ppermute | solution.py:96
  115.4 4.1 %collective-permute-start.29 = (bf16[3,32,192]{2,1,0:T(8,128)(2,1)S(1)}, bf16[3,32,192]{2,1,0:T(8,128)(2,1)S(1)}, u32[]{:S(2)}, u32[]{:S(2)}) collective-permute-start(bf16[3,32,192]{2,1,0:T(8,128)(2,1)S(1)} %get-tuple-element.38), channel_id=1, source_target_pairs={{0,24},{8,0},{16,8},{24,16},{1,25},{9,1},{17,9},{25,17},{2,26},{10... | collective-permute-start | bytes 110600 | tf_op jit(solution)/shard_map/ppermute | solution.py:96
  119.5 4.1 %collective-permute-start.31 = (bf16[3,3,32,192]{3,2,1,0:T(8,128)(2,1)S(1)}, bf16[3,3,32,192]{3,2,1,0:T(8,128)(2,1)S(1)}, u32[]{:S(2)}, u32[]{:S(2)}) collective-permute-start(bf16[3,3,32,192]{3,2,1,0:T(8,128)(2,1)S(1)} %pad_maximum_fusion.7), channel_id=1, source_target_pairs={{0,7},{1,0},{2,1},{3,2},{4,3},{5,4},{6,5},{7,6},{8,15},{9,8},{10,9... | collective-permute-start | bytes 331784 | tf_op jit(solution)/shard_map/ppermute | solution.py:96
  120.2 6.4 %collective-permute-start.30 = (bf16[3,3,32,192]{3,2,1,0:T(8,128)(2,1)S(1)}, bf16[3,3,32,192]{3,2,1,0:T(8,128)(2,1)S(1)}, u32[]{:S(2)}, u32[]{:S(2)}) collective-permute-start(bf16[3,3,32,192]{3,2,1,0:T(8,128)(2,1)S(1)} %pad_maximum_fusion.7), channel_id=1, source_target_pairs={{0,1},{1,2},{2,3},{3,4},{4,5},{5,6},{6,7},{7,0},{8,9},{9,10},{10,1... | collective-permute-start | bytes 331784 | tf_op jit(solution)/shard_map/ppermute | solution.py:96
  130.5 4.6 %collective-permute-start.34 = (f32[32,32]{0,1:T(8,128)S(1)}, f32[32,32]{0,1:T(8,128)S(1)}, u32[]{:S(2)}, u32[]{:S(2)}) collective-permute-start(f32[32,32]{0,1:T(8,128)S(1)} %convolution_bitcast_fusion.65), channel_id=1, source_target_pairs={{0,24},{8,16},{16,8},{24,0},{1,25},{9,17},{17,9},{25,1},{2,26},{10... | collective-permute-start | bytes 12296 | tf_op jit(solution)/shard_map/ppermute | solution.py:58
  139.0 4.7 %collective-permute-start.38 = (f32[32,32]{0,1:T(8,128)S(1)}, f32[32,32]{0,1:T(8,128)S(1)}, u32[]{:S(2)}, u32[]{:S(2)}) collective-permute-start(f32[32,32]{0,1:T(8,128)S(1)} %add_add_fusion.2), channel_id=1, source_target_pairs={{0,4},{1,5},{2,6},{3,7},{4,0},{5,1},{6,2},{7,3},{8,12},{9,13},{10,... | collective-permute-start | bytes 12296 | tf_op jit(solution)/shard_map/ppermute | solution.py:58
  151.0 5.0 %collective-permute-start.39 = (bf16[3,32,192]{2,1,0:T(8,128)(2,1)S(1)}, bf16[3,32,192]{2,1,0:T(8,128)(2,1)S(1)}, u32[]{:S(2)}, u32[]{:S(2)}) collective-permute-start(bf16[3,32,192]{2,1,0:T(8,128)(2,1)S(1)} %bitcast.982), channel_id=1, source_target_pairs={{0,8},{8,16},{16,24},{24,0},{1,9},{9,17},{17,25},{25,1},{2,10},{10... | collective-permute-start | bytes 110600 | tf_op jit(solution)/shard_map/ppermute | solution.py:96
  151.7 4.3 %collective-permute-start.40 = (bf16[3,32,192]{2,1,0:T(8,128)(2,1)S(1)}, bf16[3,32,192]{2,1,0:T(8,128)(2,1)S(1)}, u32[]{:S(2)}, u32[]{:S(2)}) collective-permute-start(bf16[3,32,192]{2,1,0:T(8,128)(2,1)S(1)} %bitcast.983), channel_id=1, source_target_pairs={{0,24},{8,0},{16,8},{24,16},{1,25},{9,1},{17,9},{25,17},{2,26},{10... | collective-permute-start | bytes 110600 | tf_op jit(solution)/shard_map/ppermute | solution.py:96
  156.1 6.4 %collective-permute-start.41 = (bf16[3,3,32,192]{3,2,1,0:T(8,128)(2,1)S(1)}, bf16[3,3,32,192]{3,2,1,0:T(8,128)(2,1)S(1)}, u32[]{:S(2)}, u32[]{:S(2)}) collective-permute-start(bf16[3,3,32,192]{3,2,1,0:T(8,128)(2,1)S(1)} %pad_maximum_fusion.8), channel_id=1, source_target_pairs={{0,1},{1,2},{2,3},{3,4},{4,5},{5,6},{6,7},{7,0},{8,9},{9,10},{10,1... | collective-permute-start | bytes 331784 | tf_op jit(solution)/shard_map/ppermute | solution.py:96
  163.5 5.5 %collective-permute-start.43 = (bf16[3,32,192]{2,1,0:T(8,128)(2,1)S(1)}, bf16[3,32,192]{2,1,0:T(8,128)(2,1)S(1)}, u32[]{:S(2)}, u32[]{:S(2)}) collective-permute-start(bf16[3,32,192]{2,1,0:T(8,128)(2,1)S(1)} %get-tuple-element.17), channel_id=1, source_target_pairs={{0,8},{8,16},{16,24},{24,0},{1,9},{9,17},{17,25},{25,1},{2,10},{10... | collective-permute-start | bytes 110600 | tf_op jit(solution)/shard_map/ppermute | solution.py:96
  165.9 4.1 %collective-permute-start.44 = (bf16[3,32,192]{2,1,0:T(8,128)(2,1)S(1)}, bf16[3,32,192]{2,1,0:T(8,128)(2,1)S(1)}, u32[]{:S(2)}, u32[]{:S(2)}) collective-permute-start(bf16[3,32,192]{2,1,0:T(8,128)(2,1)S(1)} %get-tuple-element.17), channel_id=1, source_target_pairs={{0,24},{8,0},{16,8},{24,16},{1,25},{9,1},{17,9},{25,17},{2,26},{10... | collective-permute-start | bytes 110600 | tf_op jit(solution)/shard_map/ppermute | solution.py:96
  170.1 4.6 %collective-permute-start.46 = (bf16[3,3,32,192]{3,2,1,0:T(8,128)(2,1)S(1)}, bf16[3,3,32,192]{3,2,1,0:T(8,128)(2,1)S(1)}, u32[]{:S(2)}, u32[]{:S(2)}) collective-permute-start(bf16[3,3,32,192]{3,2,1,0:T(8,128)(2,1)S(1)} %pad_maximum_fusion.9), channel_id=1, source_target_pairs={{0,7},{1,0},{2,1},{3,2},{4,3},{5,4},{6,5},{7,6},{8,15},{9,8},{10,9... | collective-permute-start | bytes 331784 | tf_op jit(solution)/shard_map/ppermute | solution.py:96
  172.0 6.4 %collective-permute-start.45 = (bf16[3,3,32,192]{3,2,1,0:T(8,128)(2,1)S(1)}, bf16[3,3,32,192]{3,2,1,0:T(8,128)(2,1)S(1)}, u32[]{:S(2)}, u32[]{:S(2)}) collective-permute-start(bf16[3,3,32,192]{3,2,1,0:T(8,128)(2,1)S(1)} %pad_maximum_fusion.9), channel_id=1, source_target_pairs={{0,1},{1,2},{2,3},{3,4},{4,5},{5,6},{6,7},{7,0},{8,9},{9,10},{10,1... | collective-permute-start | bytes 331784 | tf_op jit(solution)/shard_map/ppermute | solution.py:96
  179.3 5.0 %collective-permute-start.47 = (bf16[3,32,192]{2,1,0:T(8,128)(2,1)S(1)}, bf16[3,32,192]{2,1,0:T(8,128)(2,1)S(1)}, u32[]{:S(2)}, u32[]{:S(2)}) collective-permute-start(bf16[3,32,192]{2,1,0:T(8,128)(2,1)S(1)} %get-tuple-element.15), channel_id=1, source_target_pairs={{0,8},{8,16},{16,24},{24,0},{1,9},{9,17},{17,25},{25,1},{2,10},{10... | collective-permute-start | bytes 110600 | tf_op jit(solution)/shard_map/ppermute | solution.py:96
  180.7 4.1 %collective-permute-start.48 = (bf16[3,32,192]{2,1,0:T(8,128)(2,1)S(1)}, bf16[3,32,192]{2,1,0:T(8,128)(2,1)S(1)}, u32[]{:S(2)}, u32[]{:S(2)}) collective-permute-start(bf16[3,32,192]{2,1,0:T(8,128)(2,1)S(1)} %get-tuple-element.15), channel_id=1, source_target_pairs={{0,24},{8,0},{16,8},{24,16},{1,25},{9,1},{17,9},{25,17},{2,26},{10... | collective-permute-start | bytes 110600 | tf_op jit(solution)/shard_map/ppermute | solution.py:96
  184.8 4.1 %collective-permute-start.50 = (bf16[3,3,32,192]{3,2,1,0:T(8,128)(2,1)S(1)}, bf16[3,3,32,192]{3,2,1,0:T(8,128)(2,1)S(1)}, u32[]{:S(2)}, u32[]{:S(2)}) collective-permute-start(bf16[3,3,32,192]{3,2,1,0:T(8,128)(2,1)S(1)} %pad_maximum_fusion.10), channel_id=1, source_target_pairs={{0,7},{1,0},{2,1},{3,2},{4,3},{5,4},{6,5},{7,6},{8,15},{9,8},{10,9... | collective-permute-start | bytes 331784 | tf_op jit(solution)/shard_map/ppermute | solution.py:96
  185.7 6.4 %collective-permute-start.49 = (bf16[3,3,32,192]{3,2,1,0:T(8,128)(2,1)S(1)}, bf16[3,3,32,192]{3,2,1,0:T(8,128)(2,1)S(1)}, u32[]{:S(2)}, u32[]{:S(2)}) collective-permute-start(bf16[3,3,32,192]{3,2,1,0:T(8,128)(2,1)S(1)} %pad_maximum_fusion.10), channel_id=1, source_target_pairs={{0,1},{1,2},{2,3},{3,4},{4,5},{5,6},{6,7},{7,0},{8,9},{9,10},{10,1... | collective-permute-start | bytes 331784 | tf_op jit(solution)/shard_map/ppermute | solution.py:96
  193.0 5.0 %collective-permute-start.51 = (bf16[3,32,192]{2,1,0:T(8,128)(2,1)S(1)}, bf16[3,32,192]{2,1,0:T(8,128)(2,1)S(1)}, u32[]{:S(2)}, u32[]{:S(2)}) collective-permute-start(bf16[3,32,192]{2,1,0:T(8,128)(2,1)S(1)} %get-tuple-element.13), channel_id=1, source_target_pairs={{0,8},{8,16},{16,24},{24,0},{1,9},{9,17},{17,25},{25,1},{2,10},{10... | collective-permute-start | bytes 110600 | tf_op jit(solution)/shard_map/ppermute | solution.py:96
  194.4 4.1 %collective-permute-start.52 = (bf16[3,32,192]{2,1,0:T(8,128)(2,1)S(1)}, bf16[3,32,192]{2,1,0:T(8,128)(2,1)S(1)}, u32[]{:S(2)}, u32[]{:S(2)}) collective-permute-start(bf16[3,32,192]{2,1,0:T(8,128)(2,1)S(1)} %get-tuple-element.13), channel_id=1, source_target_pairs={{0,24},{8,0},{16,8},{24,16},{1,25},{9,1},{17,9},{25,17},{2,26},{10... | collective-permute-start | bytes 110600 | tf_op jit(solution)/shard_map/ppermute | solution.py:96
  198.5 4.1 %collective-permute-start.54 = (bf16[3,3,32,192]{3,2,1,0:T(8,128)(2,1)S(1)}, bf16[3,3,32,192]{3,2,1,0:T(8,128)(2,1)S(1)}, u32[]{:S(2)}, u32[]{:S(2)}) collective-permute-start(bf16[3,3,32,192]{3,2,1,0:T(8,128)(2,1)S(1)} %pad_maximum_fusion.11), channel_id=1, source_target_pairs={{0,7},{1,0},{2,1},{3,2},{4,3},{5,4},{6,5},{7,6},{8,15},{9,8},{10,9... | collective-permute-start | bytes 331784 | tf_op jit(solution)/shard_map/ppermute | solution.py:96
  199.4 6.4 %collective-permute-start.53 = (bf16[3,3,32,192]{3,2,1,0:T(8,128)(2,1)S(1)}, bf16[3,3,32,192]{3,2,1,0:T(8,128)(2,1)S(1)}, u32[]{:S(2)}, u32[]{:S(2)}) collective-permute-start(bf16[3,3,32,192]{3,2,1,0:T(8,128)(2,1)S(1)} %pad_maximum_fusion.11), channel_id=1, source_target_pairs={{0,1},{1,2},{2,3},{3,4},{4,5},{5,6},{6,7},{7,0},{8,9},{9,10},{10,1... | collective-permute-start | bytes 331784 | tf_op jit(solution)/shard_map/ppermute | solution.py:96
  206.7 5.0 %collective-permute-start.55 = (bf16[3,32,192]{2,1,0:T(8,128)(2,1)S(1)}, bf16[3,32,192]{2,1,0:T(8,128)(2,1)S(1)}, u32[]{:S(2)}, u32[]{:S(2)}) collective-permute-start(bf16[3,32,192]{2,1,0:T(8,128)(2,1)S(1)} %get-tuple-element.11), channel_id=1, source_target_pairs={{0,8},{8,16},{16,24},{24,0},{1,9},{9,17},{17,25},{25,1},{2,10},{10... | collective-permute-start | bytes 110600 | tf_op jit(solution)/shard_map/ppermute | solution.py:96
  208.0 4.1 %collective-permute-start.56 = (bf16[3,32,192]{2,1,0:T(8,128)(2,1)S(1)}, bf16[3,32,192]{2,1,0:T(8,128)(2,1)S(1)}, u32[]{:S(2)}, u32[]{:S(2)}) collective-permute-start(bf16[3,32,192]{2,1,0:T(8,128)(2,1)S(1)} %get-tuple-element.11), channel_id=1, source_target_pairs={{0,24},{8,0},{16,8},{24,16},{1,25},{9,1},{17,9},{25,17},{2,26},{10... | collective-permute-start | bytes 110600 | tf_op jit(solution)/shard_map/ppermute | solution.py:96
  212.1 4.1 %collective-permute-start.58 = (bf16[3,3,32,192]{3,2,1,0:T(8,128)(2,1)S(1)}, bf16[3,3,32,192]{3,2,1,0:T(8,128)(2,1)S(1)}, u32[]{:S(2)}, u32[]{:S(2)}) collective-permute-start(bf16[3,3,32,192]{3,2,1,0:T(8,128)(2,1)S(1)} %pad_maximum_fusion.12), channel_id=1, source_target_pairs={{0,7},{1,0},{2,1},{3,2},{4,3},{5,4},{6,5},{7,6},{8,15},{9,8},{10,9... | collective-permute-start | bytes 331784 | tf_op jit(solution)/shard_map/ppermute | solution.py:96
  213.2 6.4 %collective-permute-start.57 = (bf16[3,3,32,192]{3,2,1,0:T(8,128)(2,1)S(1)}, bf16[3,3,32,192]{3,2,1,0:T(8,128)(2,1)S(1)}, u32[]{:S(2)}, u32[]{:S(2)}) collective-permute-start(bf16[3,3,32,192]{3,2,1,0:T(8,128)(2,1)S(1)} %pad_maximum_fusion.12), channel_id=1, source_target_pairs={{0,1},{1,2},{2,3},{3,4},{4,5},{5,6},{6,7},{7,0},{8,9},{9,10},{10,1... | collective-permute-start | bytes 331784 | tf_op jit(solution)/shard_map/ppermute | solution.py:96
  220.5 5.0 %collective-permute-start.59 = (bf16[3,32,192]{2,1,0:T(8,128)(2,1)S(1)}, bf16[3,32,192]{2,1,0:T(8,128)(2,1)S(1)}, u32[]{:S(2)}, u32[]{:S(2)}) collective-permute-start(bf16[3,32,192]{2,1,0:T(8,128)(2,1)S(1)} %get-tuple-element.9), channel_id=1, source_target_pairs={{0,8},{8,16},{16,24},{24,0},{1,9},{9,17},{17,25},{25,1},{2,10},{10... | collective-permute-start | bytes 110600 | tf_op jit(solution)/shard_map/ppermute | solution.py:96
  225.8 4.1 %collective-permute-start.62 = (bf16[3,3,32,192]{3,2,1,0:T(8,128)(2,1)S(1)}, bf16[3,3,32,192]{3,2,1,0:T(8,128)(2,1)S(1)}, u32[]{:S(2)}, u32[]{:S(2)}) collective-permute-start(bf16[3,3,32,192]{3,2,1,0:T(8,128)(2,1)S(1)} %pad_maximum_fusion.13), channel_id=1, source_target_pairs={{0,7},{1,0},{2,1},{3,2},{4,3},{5,4},{6,5},{7,6},{8,15},{9,8},{10,9... | collective-permute-start | bytes 331784 | tf_op jit(solution)/shard_map/ppermute | solution.py:96
  226.8 6.4 %collective-permute-start.61 = (bf16[3,3,32,192]{3,2,1,0:T(8,128)(2,1)S(1)}, bf16[3,3,32,192]{3,2,1,0:T(8,128)(2,1)S(1)}, u32[]{:S(2)}, u32[]{:S(2)}) collective-permute-start(bf16[3,3,32,192]{3,2,1,0:T(8,128)(2,1)S(1)} %pad_maximum_fusion.13), channel_id=1, source_target_pairs={{0,1},{1,2},{2,3},{3,4},{4,5},{5,6},{6,7},{7,0},{8,9},{9,10},{10,1... | collective-permute-start | bytes 331784 | tf_op jit(solution)/shard_map/ppermute | solution.py:96
  234.1 5.0 %collective-permute-start.63 = (bf16[3,32,192]{2,1,0:T(8,128)(2,1)S(1)}, bf16[3,32,192]{2,1,0:T(8,128)(2,1)S(1)}, u32[]{:S(2)}, u32[]{:S(2)}) collective-permute-start(bf16[3,32,192]{2,1,0:T(8,128)(2,1)S(1)} %get-tuple-element.45), channel_id=1, source_target_pairs={{0,8},{8,16},{16,24},{24,0},{1,9},{9,17},{17,25},{25,1},{2,10},{10... | collective-permute-start | bytes 110600 | tf_op jit(solution)/shard_map/ppermute | solution.py:96
  239.9 4.1 %collective-permute-start.66 = (bf16[3,3,32,192]{3,2,1,0:T(8,128)(2,1)S(1)}, bf16[3,3,32,192]{3,2,1,0:T(8,128)(2,1)S(1)}, u32[]{:S(2)}, u32[]{:S(2)}) collective-permute-start(bf16[3,3,32,192]{3,2,1,0:T(8,128)(2,1)S(1)} %pad_maximum_fusion.14), channel_id=1, source_target_pairs={{0,7},{1,0},{2,1},{3,2},{4,3},{5,4},{6,5},{7,6},{8,15},{9,8},{10,9... | collective-permute-start | bytes 331784 | tf_op jit(solution)/shard_map/ppermute | solution.py:96
  240.6 6.4 %collective-permute-start.65 = (bf16[3,3,32,192]{3,2,1,0:T(8,128)(2,1)S(1)}, bf16[3,3,32,192]{3,2,1,0:T(8,128)(2,1)S(1)}, u32[]{:S(2)}, u32[]{:S(2)}) collective-permute-start(bf16[3,3,32,192]{3,2,1,0:T(8,128)(2,1)S(1)} %pad_maximum_fusion.14), channel_id=1, source_target_pairs={{0,1},{1,2},{2,3},{3,4},{4,5},{5,6},{6,7},{7,0},{8,9},{9,10},{10,1... | collective-permute-start | bytes 331784 | tf_op jit(solution)/shard_map/ppermute | solution.py:96
  247.9 5.0 %collective-permute-start.67 = (bf16[3,32,192]{2,1,0:T(8,128)(2,1)S(1)}, bf16[3,32,192]{2,1,0:T(8,128)(2,1)S(1)}, u32[]{:S(2)}, u32[]{:S(2)}) collective-permute-start(bf16[3,32,192]{2,1,0:T(8,128)(2,1)S(1)} %get-tuple-element.47), channel_id=1, source_target_pairs={{0,8},{8,16},{16,24},{24,0},{1,9},{9,17},{17,25},{25,1},{2,10},{10... | collective-permute-start | bytes 110600 | tf_op jit(solution)/shard_map/ppermute | solution.py:96
  253.3 4.1 %collective-permute-start.70 = (bf16[3,3,32,192]{3,2,1,0:T(8,128)(2,1)S(1)}, bf16[3,3,32,192]{3,2,1,0:T(8,128)(2,1)S(1)}, u32[]{:S(2)}, u32[]{:S(2)}) collective-permute-start(bf16[3,3,32,192]{3,2,1,0:T(8,128)(2,1)S(1)} %pad_maximum_fusion.15), channel_id=1, source_target_pairs={{0,7},{1,0},{2,1},{3,2},{4,3},{5,4},{6,5},{7,6},{8,15},{9,8},{10,9... | collective-permute-start | bytes 331784 | tf_op jit(solution)/shard_map/ppermute | solution.py:96
  254.4 6.4 %collective-permute-start.69 = (bf16[3,3,32,192]{3,2,1,0:T(8,128)(2,1)S(1)}, bf16[3,3,32,192]{3,2,1,0:T(8,128)(2,1)S(1)}, u32[]{:S(2)}, u32[]{:S(2)}) collective-permute-start(bf16[3,3,32,192]{3,2,1,0:T(8,128)(2,1)S(1)} %pad_maximum_fusion.15), channel_id=1, source_target_pairs={{0,1},{1,2},{2,3},{3,4},{4,5},{5,6},{6,7},{7,0},{8,9},{9,10},{10,1... | collective-permute-start | bytes 331784 | tf_op jit(solution)/shard_map/ppermute | solution.py:96
  264.4 4.6 %collective-permute-start.73 = (f32[32,32]{0,1:T(8,128)S(1)}, f32[32,32]{0,1:T(8,128)S(1)}, u32[]{:S(2)}, u32[]{:S(2)}) collective-permute-start(f32[32,32]{0,1:T(8,128)S(1)} %convolution_bitcast_fusion.64), channel_id=1, source_target_pairs={{0,24},{8,16},{16,8},{24,0},{1,25},{9,17},{17,9},{25,1},{2,26},{10... | collective-permute-start | bytes 12296 | tf_op jit(solution)/shard_map/ppermute | solution.py:58
  273.0 4.7 %collective-permute-start.77 = (f32[32,32]{0,1:T(8,128)S(1)}, f32[32,32]{0,1:T(8,128)S(1)}, u32[]{:S(2)}, u32[]{:S(2)}) collective-permute-start(f32[32,32]{0,1:T(8,128)S(1)} %add_add_fusion), channel_id=1, source_target_pairs={{0,4},{1,5},{2,6},{3,7},{4,0},{5,1},{6,2},{7,3},{8,12},{9,13},{10,... | collective-permute-start | bytes 12296 | tf_op jit(solution)/shard_map/ppermute | solution.py:58
  (17 other events, 162.2 us)

commit v11 on v10

--- a/solution.py
+++ b/solution.py
@@ -58,6 +58,9 @@
             return lax.ppermute(v, axis, [(i, i ^ stride) for i in range(count)])
 
         stride = 1
+        if (count.bit_length() - 1) % 2:
+            value = value + swap(value, stride)
+            stride *= 2
         while stride < count:
             if 4 * stride <= count:
                 near, far, both = swap(value, stride), swap(value, 2 * stride), swap(value, 3 * stride)

time: 286 us -> 286 us (level)
    ppermute x14, waiting for transfers between devices: 18.6 us -> 13.9 us  [swap(): return lax.ppermute(v, axis, [(i, i ^ stride) for i in range(count)])]
    ppermute x64, waiting for transfers between devices: 103 us -> 106 us  [shift(): lax.ppermute(value, axis, [(i, (i + step) % count) for i in range(count)])]
    ppermute x14, starting transfers between devices: 12.7 us -> 16 us  [swap(): return lax.ppermute(v, axis, [(i, i ^ stride) for i in range(count)])]
  transfers between devices with their start and end apart: 78 -> 78, of which waited for: 71 -> 73; matrix products, arithmetic and copies ran while one was open for 19% -> 19% of each run, Pallas kernels for 0% -> 0%
where the time goes in v11:
time: 286 us; the launch traced here: 285 us
  waiting for transfers between devices  120 us (42%)
  starting transfers between devices  79.4 us (28%)
  matrix products  52 us (18%)
  other arithmetic  21.5 us (8%)
  local copies, waits for them, and re-layouts  12 us (4%)
    ppermute x64, waiting for transfers between devices, shift(): lax.ppermute(value, axis, [(i, (i + step) % count) for i in range(count)])  106 us
    ppermute x64, starting transfers between devices, shift(): lax.ppermute(value, axis, [(i, (i + step) % count) for i in range(count)])  63.4 us
    dot_general x64, matrix products, part(): jnp.einsum('kvj,tkij->tvi', cells, blocks, preferred_element_type=jnp.flo...  50.9 us
    ppermute x14, starting transfers between devices, swap(): return lax.ppermute(v, axis, [(i, i ^ stride) for i in range(count)])  16 us
    ppermute x14, waiting for transfers between devices, swap(): return lax.ppermute(v, axis, [(i, i ^ stride) for i in range(count)])  13.9 us
    gather x1, local copies, waits for them, and re-layouts, dense_coupling(): jnp.take(matrices, index.reshape(-1), axis=0)  10.3 us
    another operation x6, other arithmetic, orthonormal(): factor = jnp.linalg.cholesky(gram_matrix)  7.19 us
    another operation x4, other arithmetic, orthonormal(): lax.linalg.triangular_solve(factor, stacked, left_side=True, lower=True)  6.17 us
  transfers between devices with their start and end apart: 78, of which 73 were waited for; matrix products, arithmetic and copies ran while one was open for 19% of the time, Pallas kernels for 0%

profile of v11, /device:TPU:0, one launch (start us, length us, event | category | flops | bytes accessed | tf_op | source)
XLA Modules:
  0.0 285.5 jit_solution(3690594514712217083)
XLA Ops:
  0.9 3.0 %collective-permute-start = (bf16[3,32,192]{2,1,0:T(8,128)(2,1)S(1)}, bf16[3,32,192]{2,1,0:T(8,128)(2,1)S(1)}, u32[]{:S(2)}, u32[]{:S(2)}) collective-permute-start(bf16[3,32,192]{2,1,0:T(8,128)(2,1)S(1)} %get-tuple-element.20), channel_id=1, source_target_pairs={{0,8},{8,16},{16,24},{24,0},{1,9},{9,17},{17,25},{25,1},{2,10},{10... | collective-permute-start | bytes 110600 | tf_op jit(solution)/shard_map/ppermute | solution.py:99
  8.7 1.9 collective-permute-start.3
  10.6 10.3 %gather_fusion = bf16[81,192,192]{2,1,0:T(8,128)(2,1)} fusion(bf16[81,192,192]{2,1,0:T(8,128)(2,1)} %bitcast.933, s32[1024]{0:T(1024)S(1)} %pad_clamp_fusion), kind=kCustom, calls=%fused_computation | custom fusion | bytes 11944260 | tf_op jit(solution)/shard_map/jit(_take)/gather | solution.py:42
  20.9 4.3 %select_select_fusion = bf16[3,27,192,192]{3,2,1,0:T(8,128)(2,1)S(1)} fusion(bf16[3,27,192,192]{3,2,1,0:T(8,128)(2,1)} %bitcast.932, pred[3,27]{1,0:T(4,128)(4,1)S(1)} %compare_and_fusion, pred[3,27]{1,0:T(4,128)(4,1)S(1)} %and_reduce_fusion), kind=kLoop, calls=%fused_computation.1 | loop fusion | flops 5971968 | bytes 11944098 | tf_op jit(solution)/shard_map/jit(_where)/select_n | solution.py:46
  26.3 2.0 convolution_bitcast_fusion.30
  29.2 2.7 collective-permute-start.4
  32.6 2.2 collective-permute-done.4
  36.0 2.2 collective-permute-start.7
  38.8 2.1 collective-permute-done.7
  41.8 2.8 collective-permute-done.6
  52.5 2.9 %collective-permute-done.11 = bf16[3,3,32,192]{3,2,1,0:T(8,128)(2,1)S(1)} collective-permute-done((bf16[3,3,32,192]{3,2,1,0:T(8,128)(2,1)S(1)}, bf16[3,3,32,192]{3,2,1,0:T(8,128)(2,1)S(1)}, u32[]{:S(2)}, u32[]{:S(2)}) %collective-permute-start.11) | collective-permute-done | bytes 110624 | tf_op jit(solution)/shard_map/ppermute | solution.py:99
  66.1 2.3 collective-permute-done.15
  69.3 2.6 collective-permute-done.14
  79.5 2.9 %collective-permute-done.19 = bf16[3,3,32,192]{3,2,1,0:T(8,128)(2,1)S(1)} collective-permute-done((bf16[3,3,32,192]{3,2,1,0:T(8,128)(2,1)S(1)}, bf16[3,3,32,192]{3,2,1,0:T(8,128)(2,1)S(1)}, u32[]{:S(2)}, u32[]{:S(2)}) %collective-permute-start.19) | collective-permute-done | bytes 110624 | tf_op jit(solution)/shard_map/ppermute | solution.py:99
  83.3 1.8 collective-permute-done.18
  86.1 2.1 collective-permute-start.20
  89.4 1.7 collective-permute-done.20
  93.8 2.6 collective-permute-done.23
  97.3 2.3 collective-permute-done.22
  103.9 1.7 collective-permute-done.24
  107.3 2.8 collective-permute-done.27
  111.0 2.1 collective-permute-done.26
  120.8 2.8 collective-permute-done.31
  124.5 2.1 collective-permute-done.30
  127.8 1.7 collective-permute-start.32
  133.2 2.0 collective-permute-done.34
  137.4 3.4 %collective-permute-start.38 = (f32[32,32]{0,1:T(8,128)S(1)}, f32[32,32]{0,1:T(8,128)S(1)}, u32[]{:S(2)}, u32[]{:S(2)}) collective-permute-start(f32[32,32]{0,1:T(8,128)S(1)} %add.399), channel_id=1, source_target_pairs={{0,6},{1,7},{2,4},{3,5},{4,2},{5,3},{6,0},{7,1},{8,14},{9,15},{10,... | collective-permute-start | bytes 12296 | tf_op jit(solution)/shard_map/ppermute | solution.py:58
  141.1 1.8 collective-permute-done.38
  143.0 2.9 %cholesky.44 = f32[32,32]{1,0:T(8,128)S(1)} custom-call(f32[32,32]{1,0:T(8,128)S(1)} %fusion.171), custom_call_target="Cholesky" | custom-call | tf_op jit(solution)/shard_map/jit(cholesky)/cholesky | solution.py:80
  147.3 2.4 custom-call.6
  150.7 2.4 collective-permute-start.40
  156.0 2.5 fusion.70
  159.3 2.6 convolution_bitcast_fusion.14
  164.4 2.4 collective-permute-start.43
  167.7 1.7 collective-permute-done.43
  172.4 2.6 collective-permute-done.46
  175.9 2.3 collective-permute-done.45
  179.2 2.6 collective-permute-start.47
  182.5 1.7 collective-permute-done.47
  187.0 2.9 %collective-permute-done.50 = bf16[3,3,32,192]{3,2,1,0:T(8,128)(2,1)S(1)} collective-permute-done((bf16[3,3,32,192]{3,2,1,0:T(8,128)(2,1)S(1)}, bf16[3,3,32,192]{3,2,1,0:T(8,128)(2,1)S(1)}, u32[]{:S(2)}, u32[]{:S(2)}) %collective-permute-start.50) | collective-permute-done | bytes 110624 | tf_op jit(solution)/shard_map/ppermute | solution.py:99
  190.9 1.7 collective-permute-done.49
  194.6 1.9 collective-permute-start.52
  196.9 1.7 collective-permute-done.51
  200.2 2.6 collective-permute-done.54
  203.7 2.3 collective-permute-done.53
  206.9 1.9 collective-permute-start.55
  210.3 1.7 collective-permute-done.55
  214.1 2.9 %collective-permute-done.58 = bf16[3,3,32,192]{3,2,1,0:T(8,128)(2,1)S(1)} collective-permute-done((bf16[3,3,32,192]{3,2,1,0:T(8,128)(2,1)S(1)}, bf16[3,3,32,192]{3,2,1,0:T(8,128)(2,1)S(1)}, u32[]{:S(2)}, u32[]{:S(2)}) %collective-permute-start.58) | collective-permute-done | bytes 110624 | tf_op jit(solution)/shard_map/ppermute | solution.py:99
  223.9 1.7 collective-permute-done.59
  227.6 2.9 %collective-permute-done.62 = bf16[3,3,32,192]{3,2,1,0:T(8,128)(2,1)S(1)} collective-permute-done((bf16[3,3,32,192]{3,2,1,0:T(8,128)(2,1)S(1)}, bf16[3,3,32,192]{3,2,1,0:T(8,128)(2,1)S(1)}, u32[]{:S(2)}, u32[]{:S(2)}) %collective-permute-start.62) | collective-permute-done | bytes 110624 | tf_op jit(solution)/shard_map/ppermute | solution.py:99
  231.3 2.0 collective-permute-done.61
  234.3 2.2 collective-permute-start.63
  237.6 1.7 collective-permute-done.63
  242.0 2.7 collective-permute-done.66
  245.6 2.2 collective-permute-done.65
  249.8 1.8 collective-permute-start.68
  252.0 1.7 collective-permute-done.67
  255.5 2.6 collective-permute-done.70
  259.0 2.3 collective-permute-done.69
  267.5 2.2 collective-permute-done.73
  272.1 3.3 %collective-permute-start.77 = (f32[32,32]{0,1:T(8,128)S(1)}, f32[32,32]{0,1:T(8,128)S(1)}, u32[]{:S(2)}, u32[]{:S(2)}) collective-permute-start(f32[32,32]{0,1:T(8,128)S(1)} %add.438), channel_id=1, source_target_pairs={{0,6},{1,7},{2,4},{3,5},{4,2},{5,3},{6,0},{7,1},{8,14},{9,15},{10,... | collective-permute-start | bytes 12296 | tf_op jit(solution)/shard_map/ppermute | solution.py:58
  275.7 1.9 collective-permute-done.77
  277.7 2.9 %cholesky.55 = f32[32,32]{1,0:T(8,128)S(1)} custom-call(f32[32,32]{1,0:T(8,128)S(1)} %fusion.168), custom_call_target="Cholesky" | custom-call | tf_op jit(solution)/shard_map/jit(cholesky)/cholesky | solution.py:80
  282.0 2.4 custom-call.7
  (223 shorter events, 127.8 us)
Async XLA Ops:
  0.9 6.0 %collective-permute-start = (bf16[3,32,192]{2,1,0:T(8,128)(2,1)S(1)}, bf16[3,32,192]{2,1,0:T(8,128)(2,1)S(1)}, u32[]{:S(2)}, u32[]{:S(2)}) collective-permute-start(bf16[3,32,192]{2,1,0:T(8,128)(2,1)S(1)} %get-tuple-element.20), channel_id=1, source_target_pairs={{0,8},{8,16},{16,24},{24,0},{1,9},{9,17},{17,25},{25,1},{2,10},{10... | collective-permute-start | bytes 110600 | tf_op jit(solution)/shard_map/ppermute | solution.py:99
  3.9 4.1 %collective-permute-start.1 = (bf16[3,32,192]{2,1,0:T(8,128)(2,1)S(1)}, bf16[3,32,192]{2,1,0:T(8,128)(2,1)S(1)}, u32[]{:S(2)}, u32[]{:S(2)}) collective-permute-start(bf16[3,32,192]{2,1,0:T(8,128)(2,1)S(1)} %get-tuple-element.20), channel_id=1, source_target_pairs={{0,24},{8,0},{16,8},{24,16},{1,25},{9,1},{17,9},{25,17},{2,26},{10... | collective-permute-start | bytes 110600 | tf_op jit(solution)/shard_map/ppermute | solution.py:99
  8.7 17.6 %collective-permute-start.3 = (bf16[3,3,32,192]{3,2,1,0:T(8,128)(2,1)}, bf16[3,3,32,192]{3,2,1,0:T(8,128)(2,1)}, u32[]{:S(2)}, u32[]{:S(2)}) collective-permute-start(bf16[3,3,32,192]{3,2,1,0:T(8,128)(2,1)} %pad_maximum_fusion), channel_id=1, source_target_pairs={{0,7},{1,0},{2,1},{3,2},{4,3},{5,4},{6,5},{7,6},{8,15},{9,8},{10,9... | collective-permute-start | bytes 331784 | tf_op jit(solution)/shard_map/ppermute | solution.py:99
  10.6 17.7 %collective-permute-start.2 = (bf16[3,3,32,192]{3,2,1,0:T(8,128)(2,1)}, bf16[3,3,32,192]{3,2,1,0:T(8,128)(2,1)S(1)}, u32[]{:S(2)}, u32[]{:S(2)}) collective-permute-start(bf16[3,3,32,192]{3,2,1,0:T(8,128)(2,1)} %pad_maximum_fusion), channel_id=1, source_target_pairs={{0,1},{1,2},{2,3},{3,4},{4,5},{5,6},{6,7},{7,0},{8,9},{9,10},{10,1... | collective-permute-start | bytes 331784 | tf_op jit(solution)/shard_map/ppermute | solution.py:99
  29.2 5.5 %collective-permute-start.4 = (bf16[3,32,192]{2,1,0:T(8,128)(2,1)S(1)}, bf16[3,32,192]{2,1,0:T(8,128)(2,1)S(1)}, u32[]{:S(2)}, u32[]{:S(2)}) collective-permute-start(bf16[3,32,192]{2,1,0:T(8,128)(2,1)S(1)} %get-tuple-element.26), channel_id=1, source_target_pairs={{0,8},{8,16},{16,24},{24,0},{1,9},{9,17},{17,25},{25,1},{2,10},{10... | collective-permute-start | bytes 110600 | tf_op jit(solution)/shard_map/ppermute | solution.py:99
  31.9 4.1 %collective-permute-start.5 = (bf16[3,32,192]{2,1,0:T(8,128)(2,1)S(1)}, bf16[3,32,192]{2,1,0:T(8,128)(2,1)S(1)}, u32[]{:S(2)}, u32[]{:S(2)}) collective-permute-start(bf16[3,32,192]{2,1,0:T(8,128)(2,1)S(1)} %get-tuple-element.26), channel_id=1, source_target_pairs={{0,24},{8,0},{16,8},{24,16},{1,25},{9,1},{17,9},{25,17},{2,26},{10... | collective-permute-start | bytes 110600 | tf_op jit(solution)/shard_map/ppermute | solution.py:99
  36.0 4.9 %collective-permute-start.7 = (bf16[3,3,32,192]{3,2,1,0:T(8,128)(2,1)S(1)}, bf16[3,3,32,192]{3,2,1,0:T(8,128)(2,1)S(1)}, u32[]{:S(2)}, u32[]{:S(2)}) collective-permute-start(bf16[3,3,32,192]{3,2,1,0:T(8,128)(2,1)S(1)} %pad_maximum_fusion.1), channel_id=1, source_target_pairs={{0,7},{1,0},{2,1},{3,2},{4,3},{5,4},{6,5},{7,6},{8,15},{9,8},{10,9... | collective-permute-start | bytes 331784 | tf_op jit(solution)/shard_map/ppermute | solution.py:99
  38.2 6.4 %collective-permute-start.6 = (bf16[3,3,32,192]{3,2,1,0:T(8,128)(2,1)S(1)}, bf16[3,3,32,192]{3,2,1,0:T(8,128)(2,1)S(1)}, u32[]{:S(2)}, u32[]{:S(2)}) collective-permute-start(bf16[3,3,32,192]{3,2,1,0:T(8,128)(2,1)S(1)} %pad_maximum_fusion.1), channel_id=1, source_target_pairs={{0,1},{1,2},{2,3},{3,4},{4,5},{5,6},{6,7},{7,0},{8,9},{9,10},{10,1... | collective-permute-start | bytes 331784 | tf_op jit(solution)/shard_map/ppermute | solution.py:99
  45.5 5.0 %collective-permute-start.8 = (bf16[3,32,192]{2,1,0:T(8,128)(2,1)S(1)}, bf16[3,32,192]{2,1,0:T(8,128)(2,1)S(1)}, u32[]{:S(2)}, u32[]{:S(2)}) collective-permute-start(bf16[3,32,192]{2,1,0:T(8,128)(2,1)S(1)} %get-tuple-element.28), channel_id=1, source_target_pairs={{0,8},{8,16},{16,24},{24,0},{1,9},{9,17},{17,25},{25,1},{2,10},{10... | collective-permute-start | bytes 110600 | tf_op jit(solution)/shard_map/ppermute | solution.py:99
  47.2 4.1 %collective-permute-start.9 = (bf16[3,32,192]{2,1,0:T(8,128)(2,1)S(1)}, bf16[3,32,192]{2,1,0:T(8,128)(2,1)S(1)}, u32[]{:S(2)}, u32[]{:S(2)}) collective-permute-start(bf16[3,32,192]{2,1,0:T(8,128)(2,1)S(1)} %get-tuple-element.28), channel_id=1, source_target_pairs={{0,24},{8,0},{16,8},{24,16},{1,25},{9,1},{17,9},{25,17},{2,26},{10... | collective-permute-start | bytes 110600 | tf_op jit(solution)/shard_map/ppermute | solution.py:99
  51.3 4.1 %collective-permute-start.11 = (bf16[3,3,32,192]{3,2,1,0:T(8,128)(2,1)S(1)}, bf16[3,3,32,192]{3,2,1,0:T(8,128)(2,1)S(1)}, u32[]{:S(2)}, u32[]{:S(2)}) collective-permute-start(bf16[3,3,32,192]{3,2,1,0:T(8,128)(2,1)S(1)} %pad_maximum_fusion.2), channel_id=1, source_target_pairs={{0,7},{1,0},{2,1},{3,2},{4,3},{5,4},{6,5},{7,6},{8,15},{9,8},{10,9... | collective-permute-start | bytes 331784 | tf_op jit(solution)/shard_map/ppermute | solution.py:99
  51.4 6.4 %collective-permute-start.10 = (bf16[3,3,32,192]{3,2,1,0:T(8,128)(2,1)S(1)}, bf16[3,3,32,192]{3,2,1,0:T(8,128)(2,1)S(1)}, u32[]{:S(2)}, u32[]{:S(2)}) collective-permute-start(bf16[3,3,32,192]{3,2,1,0:T(8,128)(2,1)S(1)} %pad_maximum_fusion.2), channel_id=1, source_target_pairs={{0,1},{1,2},{2,3},{3,4},{4,5},{5,6},{6,7},{7,0},{8,9},{9,10},{10,1... | collective-permute-start | bytes 331784 | tf_op jit(solution)/shard_map/ppermute | solution.py:99
  58.7 5.0 %collective-permute-start.12 = (bf16[3,32,192]{2,1,0:T(8,128)(2,1)S(1)}, bf16[3,32,192]{2,1,0:T(8,128)(2,1)S(1)}, u32[]{:S(2)}, u32[]{:S(2)}) collective-permute-start(bf16[3,32,192]{2,1,0:T(8,128)(2,1)S(1)} %get-tuple-element.30), channel_id=1, source_target_pairs={{0,8},{8,16},{16,24},{24,0},{1,9},{9,17},{17,25},{25,1},{2,10},{10... | collective-permute-start | bytes 110600 | tf_op jit(solution)/shard_map/ppermute | solution.py:99
  60.2 4.1 %collective-permute-start.13 = (bf16[3,32,192]{2,1,0:T(8,128)(2,1)S(1)}, bf16[3,32,192]{2,1,0:T(8,128)(2,1)S(1)}, u32[]{:S(2)}, u32[]{:S(2)}) collective-permute-start(bf16[3,32,192]{2,1,0:T(8,128)(2,1)S(1)} %get-tuple-element.30), channel_id=1, source_target_pairs={{0,24},{8,0},{16,8},{24,16},{1,25},{9,1},{17,9},{25,17},{2,26},{10... | collective-permute-start | bytes 110600 | tf_op jit(solution)/shard_map/ppermute | solution.py:99
  64.3 4.1 %collective-permute-start.15 = (bf16[3,3,32,192]{3,2,1,0:T(8,128)(2,1)S(1)}, bf16[3,3,32,192]{3,2,1,0:T(8,128)(2,1)S(1)}, u32[]{:S(2)}, u32[]{:S(2)}) collective-permute-start(bf16[3,3,32,192]{3,2,1,0:T(8,128)(2,1)S(1)} %pad_maximum_fusion.3), channel_id=1, source_target_pairs={{0,7},{1,0},{2,1},{3,2},{4,3},{5,4},{6,5},{7,6},{8,15},{9,8},{10,9... | collective-permute-start | bytes 331784 | tf_op jit(solution)/shard_map/ppermute | solution.py:99
  65.5 6.4 %collective-permute-start.14 = (bf16[3,3,32,192]{3,2,1,0:T(8,128)(2,1)S(1)}, bf16[3,3,32,192]{3,2,1,0:T(8,128)(2,1)S(1)}, u32[]{:S(2)}, u32[]{:S(2)}) collective-permute-start(bf16[3,3,32,192]{3,2,1,0:T(8,128)(2,1)S(1)} %pad_maximum_fusion.3), channel_id=1, source_target_pairs={{0,1},{1,2},{2,3},{3,4},{4,5},{5,6},{6,7},{7,0},{8,9},{9,10},{10,1... | collective-permute-start | bytes 331784 | tf_op jit(solution)/shard_map/ppermute | solution.py:99
  72.8 5.0 %collective-permute-start.16 = (bf16[3,32,192]{2,1,0:T(8,128)(2,1)S(1)}, bf16[3,32,192]{2,1,0:T(8,128)(2,1)S(1)}, u32[]{:S(2)}, u32[]{:S(2)}) collective-permute-start(bf16[3,32,192]{2,1,0:T(8,128)(2,1)S(1)} %get-tuple-element.32), channel_id=1, source_target_pairs={{0,8},{8,16},{16,24},{24,0},{1,9},{9,17},{17,25},{25,1},{2,10},{10... | collective-permute-start | bytes 110600 | tf_op jit(solution)/shard_map/ppermute | solution.py:99
  74.2 4.1 %collective-permute-start.17 = (bf16[3,32,192]{2,1,0:T(8,128)(2,1)S(1)}, bf16[3,32,192]{2,1,0:T(8,128)(2,1)S(1)}, u32[]{:S(2)}, u32[]{:S(2)}) collective-permute-start(bf16[3,32,192]{2,1,0:T(8,128)(2,1)S(1)} %get-tuple-element.32), channel_id=1, source_target_pairs={{0,24},{8,0},{16,8},{24,16},{1,25},{9,1},{17,9},{25,17},{2,26},{10... | collective-permute-start | bytes 110600 | tf_op jit(solution)/shard_map/ppermute | solution.py:99
  78.3 4.1 %collective-permute-start.19 = (bf16[3,3,32,192]{3,2,1,0:T(8,128)(2,1)S(1)}, bf16[3,3,32,192]{3,2,1,0:T(8,128)(2,1)S(1)}, u32[]{:S(2)}, u32[]{:S(2)}) collective-permute-start(bf16[3,3,32,192]{3,2,1,0:T(8,128)(2,1)S(1)} %pad_maximum_fusion.4), channel_id=1, source_target_pairs={{0,7},{1,0},{2,1},{3,2},{4,3},{5,4},{6,5},{7,6},{8,15},{9,8},{10,9... | collective-permute-start | bytes 331784 | tf_op jit(solution)/shard_map/ppermute | solution.py:99
  78.8 6.4 %collective-permute-start.18 = (bf16[3,3,32,192]{3,2,1,0:T(8,128)(2,1)S(1)}, bf16[3,3,32,192]{3,2,1,0:T(8,128)(2,1)S(1)}, u32[]{:S(2)}, u32[]{:S(2)}) collective-permute-start(bf16[3,3,32,192]{3,2,1,0:T(8,128)(2,1)S(1)} %pad_maximum_fusion.4), channel_id=1, source_target_pairs={{0,1},{1,2},{2,3},{3,4},{4,5},{5,6},{6,7},{7,0},{8,9},{9,10},{10,1... | collective-permute-start | bytes 331784 | tf_op jit(solution)/shard_map/ppermute | solution.py:99
  86.1 5.0 %collective-permute-start.20 = (bf16[3,32,192]{2,1,0:T(8,128)(2,1)S(1)}, bf16[3,32,192]{2,1,0:T(8,128)(2,1)S(1)}, u32[]{:S(2)}, u32[]{:S(2)}) collective-permute-start(bf16[3,32,192]{2,1,0:T(8,128)(2,1)S(1)} %get-tuple-element.34), channel_id=1, source_target_pairs={{0,8},{8,16},{16,24},{24,0},{1,9},{9,17},{17,25},{25,1},{2,10},{10... | collective-permute-start | bytes 110600 | tf_op jit(solution)/shard_map/ppermute | solution.py:99
  88.2 4.1 %collective-permute-start.21 = (bf16[3,32,192]{2,1,0:T(8,128)(2,1)S(1)}, bf16[3,32,192]{2,1,0:T(8,128)(2,1)S(1)}, u32[]{:S(2)}, u32[]{:S(2)}) collective-permute-start(bf16[3,32,192]{2,1,0:T(8,128)(2,1)S(1)} %get-tuple-element.34), channel_id=1, source_target_pairs={{0,24},{8,0},{16,8},{24,16},{1,25},{9,1},{17,9},{25,17},{2,26},{10... | collective-permute-start | bytes 110600 | tf_op jit(solution)/shard_map/ppermute | solution.py:99
  92.3 4.1 %collective-permute-start.23 = (bf16[3,3,32,192]{3,2,1,0:T(8,128)(2,1)S(1)}, bf16[3,3,32,192]{3,2,1,0:T(8,128)(2,1)S(1)}, u32[]{:S(2)}, u32[]{:S(2)}) collective-permute-start(bf16[3,3,32,192]{3,2,1,0:T(8,128)(2,1)S(1)} %pad_maximum_fusion.5), channel_id=1, source_target_pairs={{0,7},{1,0},{2,1},{3,2},{4,3},{5,4},{6,5},{7,6},{8,15},{9,8},{10,9... | collective-permute-start | bytes 331784 | tf_op jit(solution)/shard_map/ppermute | solution.py:99
  93.2 6.4 %collective-permute-start.22 = (bf16[3,3,32,192]{3,2,1,0:T(8,128)(2,1)S(1)}, bf16[3,3,32,192]{3,2,1,0:T(8,128)(2,1)S(1)}, u32[]{:S(2)}, u32[]{:S(2)}) collective-permute-start(bf16[3,3,32,192]{3,2,1,0:T(8,128)(2,1)S(1)} %pad_maximum_fusion.5), channel_id=1, source_target_pairs={{0,1},{1,2},{2,3},{3,4},{4,5},{5,6},{6,7},{7,0},{8,9},{9,10},{10,1... | collective-permute-start | bytes 331784 | tf_op jit(solution)/shard_map/ppermute | solution.py:99
  100.5 5.0 %collective-permute-start.24 = (bf16[3,32,192]{2,1,0:T(8,128)(2,1)S(1)}, bf16[3,32,192]{2,1,0:T(8,128)(2,1)S(1)}, u32[]{:S(2)}, u32[]{:S(2)}) collective-permute-start(bf16[3,32,192]{2,1,0:T(8,128)(2,1)S(1)} %get-tuple-element.36), channel_id=1, source_target_pairs={{0,8},{8,16},{16,24},{24,0},{1,9},{9,17},{17,25},{25,1},{2,10},{10... | collective-permute-start | bytes 110600 | tf_op jit(solution)/shard_map/ppermute | solution.py:99
  106.0 4.1 %collective-permute-start.27 = (bf16[3,3,32,192]{3,2,1,0:T(8,128)(2,1)S(1)}, bf16[3,3,32,192]{3,2,1,0:T(8,128)(2,1)S(1)}, u32[]{:S(2)}, u32[]{:S(2)}) collective-permute-start(bf16[3,3,32,192]{3,2,1,0:T(8,128)(2,1)S(1)} %pad_maximum_fusion.6), channel_id=1, source_target_pairs={{0,7},{1,0},{2,1},{3,2},{4,3},{5,4},{6,5},{7,6},{8,15},{9,8},{10,9... | collective-permute-start | bytes 331784 | tf_op jit(solution)/shard_map/ppermute | solution.py:99
  106.7 6.4 %collective-permute-start.26 = (bf16[3,3,32,192]{3,2,1,0:T(8,128)(2,1)S(1)}, bf16[3,3,32,192]{3,2,1,0:T(8,128)(2,1)S(1)}, u32[]{:S(2)}, u32[]{:S(2)}) collective-permute-start(bf16[3,3,32,192]{3,2,1,0:T(8,128)(2,1)S(1)} %pad_maximum_fusion.6), channel_id=1, source_target_pairs={{0,1},{1,2},{2,3},{3,4},{4,5},{5,6},{6,7},{7,0},{8,9},{9,10},{10,1... | collective-permute-start | bytes 331784 | tf_op jit(solution)/shard_map/ppermute | solution.py:99
  114.0 5.0 %collective-permute-start.28 = (bf16[3,32,192]{2,1,0:T(8,128)(2,1)S(1)}, bf16[3,32,192]{2,1,0:T(8,128)(2,1)S(1)}, u32[]{:S(2)}, u32[]{:S(2)}) collective-permute-start(bf16[3,32,192]{2,1,0:T(8,128)(2,1)S(1)} %get-tuple-element.38), channel_id=1, source_target_pairs={{0,8},{8,16},{16,24},{24,0},{1,9},{9,17},{17,25},{25,1},{2,10},{10... | collective-permute-start | bytes 110600 | tf_op jit(solution)/shard_map/ppermute | solution.py:99
  119.5 4.1 %collective-permute-start.31 = (bf16[3,3,32,192]{3,2,1,0:T(8,128)(2,1)S(1)}, bf16[3,3,32,192]{3,2,1,0:T(8,128)(2,1)S(1)}, u32[]{:S(2)}, u32[]{:S(2)}) collective-permute-start(bf16[3,3,32,192]{3,2,1,0:T(8,128)(2,1)S(1)} %pad_maximum_fusion.7), channel_id=1, source_target_pairs={{0,7},{1,0},{2,1},{3,2},{4,3},{5,4},{6,5},{7,6},{8,15},{9,8},{10,9... | collective-permute-start | bytes 331784 | tf_op jit(solution)/shard_map/ppermute | solution.py:99
  120.2 6.4 %collective-permute-start.30 = (bf16[3,3,32,192]{3,2,1,0:T(8,128)(2,1)S(1)}, bf16[3,3,32,192]{3,2,1,0:T(8,128)(2,1)S(1)}, u32[]{:S(2)}, u32[]{:S(2)}) collective-permute-start(bf16[3,3,32,192]{3,2,1,0:T(8,128)(2,1)S(1)} %pad_maximum_fusion.7), channel_id=1, source_target_pairs={{0,1},{1,2},{2,3},{3,4},{4,5},{5,6},{6,7},{7,0},{8,9},{9,10},{10,1... | collective-permute-start | bytes 331784 | tf_op jit(solution)/shard_map/ppermute | solution.py:99
  130.5 4.6 %collective-permute-start.34 = (f32[32,32]{0,1:T(8,128)S(1)}, f32[32,32]{0,1:T(8,128)S(1)}, u32[]{:S(2)}, u32[]{:S(2)}) collective-permute-start(f32[32,32]{0,1:T(8,128)S(1)} %convolution_bitcast_fusion.65), channel_id=1, source_target_pairs={{0,24},{8,16},{16,8},{24,0},{1,25},{9,17},{17,9},{25,1},{2,26},{10... | collective-permute-start | bytes 12296 | tf_op jit(solution)/shard_map/ppermute | solution.py:58
  136.4 4.6 %collective-permute-start.36 = (f32[32,32]{0,1:T(8,128)S(1)}, f32[32,32]{0,1:T(8,128)S(1)}, u32[]{:S(2)}, u32[]{:S(2)}) collective-permute-start(f32[32,32]{0,1:T(8,128)S(1)} %add.399), channel_id=1, source_target_pairs={{0,2},{1,3},{2,0},{3,1},{4,6},{5,7},{6,4},{7,5},{8,10},{9,11},{10,... | collective-permute-start | bytes 12296 | tf_op jit(solution)/shard_map/ppermute | solution.py:58
  136.4 4.7 %collective-permute-start.37 = (f32[32,32]{0,1:T(8,128)S(1)}, f32[32,32]{0,1:T(8,128)S(1)}, u32[]{:S(2)}, u32[]{:S(2)}) collective-permute-start(f32[32,32]{0,1:T(8,128)S(1)} %add.399), channel_id=1, source_target_pairs={{0,4},{1,5},{2,6},{3,7},{4,0},{5,1},{6,2},{7,3},{8,12},{9,13},{10,... | collective-permute-start | bytes 12296 | tf_op jit(solution)/shard_map/ppermute | solution.py:58
  137.4 5.5 %collective-permute-start.38 = (f32[32,32]{0,1:T(8,128)S(1)}, f32[32,32]{0,1:T(8,128)S(1)}, u32[]{:S(2)}, u32[]{:S(2)}) collective-permute-start(f32[32,32]{0,1:T(8,128)S(1)} %add.399), channel_id=1, source_target_pairs={{0,6},{1,7},{2,4},{3,5},{4,2},{5,3},{6,0},{7,1},{8,14},{9,15},{10,... | collective-permute-start | bytes 12296 | tf_op jit(solution)/shard_map/ppermute | solution.py:58
  150.1 5.0 %collective-permute-start.39 = (bf16[3,32,192]{2,1,0:T(8,128)(2,1)S(1)}, bf16[3,32,192]{2,1,0:T(8,128)(2,1)S(1)}, u32[]{:S(2)}, u32[]{:S(2)}) collective-permute-start(bf16[3,32,192]{2,1,0:T(8,128)(2,1)S(1)} %bitcast.982), channel_id=1, source_target_pairs={{0,8},{8,16},{16,24},{24,0},{1,9},{9,17},{17,25},{25,1},{2,10},{10... | collective-permute-start | bytes 110600 | tf_op jit(solution)/shard_map/ppermute | solution.py:99
  150.7 4.5 %collective-permute-start.40 = (bf16[3,32,192]{2,1,0:T(8,128)(2,1)S(1)}, bf16[3,32,192]{2,1,0:T(8,128)(2,1)S(1)}, u32[]{:S(2)}, u32[]{:S(2)}) collective-permute-start(bf16[3,32,192]{2,1,0:T(8,128)(2,1)S(1)} %bitcast.983), channel_id=1, source_target_pairs={{0,24},{8,0},{16,8},{24,16},{1,25},{9,1},{17,9},{25,17},{2,26},{10... | collective-permute-start | bytes 110600 | tf_op jit(solution)/shard_map/ppermute | solution.py:99
  155.2 4.1 %collective-permute-start.42 = (bf16[3,3,32,192]{3,2,1,0:T(8,128)(2,1)S(1)}, bf16[3,3,32,192]{3,2,1,0:T(8,128)(2,1)S(1)}, u32[]{:S(2)}, u32[]{:S(2)}) collective-permute-start(bf16[3,3,32,192]{3,2,1,0:T(8,128)(2,1)S(1)} %pad_maximum_fusion.8), channel_id=1, source_target_pairs={{0,7},{1,0},{2,1},{3,2},{4,3},{5,4},{6,5},{7,6},{8,15},{9,8},{10,9... | collective-permute-start | bytes 331784 | tf_op jit(solution)/shard_map/ppermute | solution.py:99
  155.9 7.5 %collective-permute-start.41 = (bf16[3,3,32,192]{3,2,1,0:T(8,128)(2,1)S(1)}, bf16[3,3,32,192]{3,2,1,0:T(8,128)(2,1)S(1)}, u32[]{:S(2)}, u32[]{:S(2)}) collective-permute-start(bf16[3,3,32,192]{3,2,1,0:T(8,128)(2,1)S(1)} %pad_maximum_fusion.8), channel_id=1, source_target_pairs={{0,1},{1,2},{2,3},{3,4},{4,5},{5,6},{6,7},{7,0},{8,9},{9,10},{10,1... | collective-permute-start | bytes 331784 | tf_op jit(solution)/shard_map/ppermute | solution.py:99
  164.4 5.0 %collective-permute-start.43 = (bf16[3,32,192]{2,1,0:T(8,128)(2,1)S(1)}, bf16[3,32,192]{2,1,0:T(8,128)(2,1)S(1)}, u32[]{:S(2)}, u32[]{:S(2)}) collective-permute-start(bf16[3,32,192]{2,1,0:T(8,128)(2,1)S(1)} %get-tuple-element.17), channel_id=1, source_target_pairs={{0,8},{8,16},{16,24},{24,0},{1,9},{9,17},{17,25},{25,1},{2,10},{10... | collective-permute-start | bytes 110600 | tf_op jit(solution)/shard_map/ppermute | solution.py:99
  170.9 4.1 %collective-permute-start.46 = (bf16[3,3,32,192]{3,2,1,0:T(8,128)(2,1)S(1)}, bf16[3,3,32,192]{3,2,1,0:T(8,128)(2,1)S(1)}, u32[]{:S(2)}, u32[]{:S(2)}) collective-permute-start(bf16[3,3,32,192]{3,2,1,0:T(8,128)(2,1)S(1)} %pad_maximum_fusion.9), channel_id=1, source_target_pairs={{0,7},{1,0},{2,1},{3,2},{4,3},{5,4},{6,5},{7,6},{8,15},{9,8},{10,9... | collective-permute-start | bytes 331784 | tf_op jit(solution)/shard_map/ppermute | solution.py:99
  171.8 6.4 %collective-permute-start.45 = (bf16[3,3,32,192]{3,2,1,0:T(8,128)(2,1)S(1)}, bf16[3,3,32,192]{3,2,1,0:T(8,128)(2,1)S(1)}, u32[]{:S(2)}, u32[]{:S(2)}) collective-permute-start(bf16[3,3,32,192]{3,2,1,0:T(8,128)(2,1)S(1)} %pad_maximum_fusion.9), channel_id=1, source_target_pairs={{0,1},{1,2},{2,3},{3,4},{4,5},{5,6},{6,7},{7,0},{8,9},{9,10},{10,1... | collective-permute-start | bytes 331784 | tf_op jit(solution)/shard_map/ppermute | solution.py:99
  179.2 5.0 %collective-permute-start.47 = (bf16[3,32,192]{2,1,0:T(8,128)(2,1)S(1)}, bf16[3,32,192]{2,1,0:T(8,128)(2,1)S(1)}, u32[]{:S(2)}, u32[]{:S(2)}) collective-permute-start(bf16[3,32,192]{2,1,0:T(8,128)(2,1)S(1)} %get-tuple-element.15), channel_id=1, source_target_pairs={{0,8},{8,16},{16,24},{24,0},{1,9},{9,17},{17,25},{25,1},{2,10},{10... | collective-permute-start | bytes 110600 | tf_op jit(solution)/shard_map/ppermute | solution.py:99
  185.9 4.1 %collective-permute-start.50 = (bf16[3,3,32,192]{3,2,1,0:T(8,128)(2,1)S(1)}, bf16[3,3,32,192]{3,2,1,0:T(8,128)(2,1)S(1)}, u32[]{:S(2)}, u32[]{:S(2)}) collective-permute-start(bf16[3,3,32,192]{3,2,1,0:T(8,128)(2,1)S(1)} %pad_maximum_fusion.10), channel_id=1, source_target_pairs={{0,7},{1,0},{2,1},{3,2},{4,3},{5,4},{6,5},{7,6},{8,15},{9,8},{10,9... | collective-permute-start | bytes 331784 | tf_op jit(solution)/shard_map/ppermute | solution.py:99
  186.2 6.4 %collective-permute-start.49 = (bf16[3,3,32,192]{3,2,1,0:T(8,128)(2,1)S(1)}, bf16[3,3,32,192]{3,2,1,0:T(8,128)(2,1)S(1)}, u32[]{:S(2)}, u32[]{:S(2)}) collective-permute-start(bf16[3,3,32,192]{3,2,1,0:T(8,128)(2,1)S(1)} %pad_maximum_fusion.10), channel_id=1, source_target_pairs={{0,1},{1,2},{2,3},{3,4},{4,5},{5,6},{6,7},{7,0},{8,9},{9,10},{10,1... | collective-permute-start | bytes 331784 | tf_op jit(solution)/shard_map/ppermute | solution.py:99
  193.5 5.0 %collective-permute-start.51 = (bf16[3,32,192]{2,1,0:T(8,128)(2,1)S(1)}, bf16[3,32,192]{2,1,0:T(8,128)(2,1)S(1)}, u32[]{:S(2)}, u32[]{:S(2)}) collective-permute-start(bf16[3,32,192]{2,1,0:T(8,128)(2,1)S(1)} %get-tuple-element.13), channel_id=1, source_target_pairs={{0,8},{8,16},{16,24},{24,0},{1,9},{9,17},{17,25},{25,1},{2,10},{10... | collective-permute-start | bytes 110600 | tf_op jit(solution)/shard_map/ppermute | solution.py:99
  198.7 4.1 %collective-permute-start.54 = (bf16[3,3,32,192]{3,2,1,0:T(8,128)(2,1)S(1)}, bf16[3,3,32,192]{3,2,1,0:T(8,128)(2,1)S(1)}, u32[]{:S(2)}, u32[]{:S(2)}) collective-permute-start(bf16[3,3,32,192]{3,2,1,0:T(8,128)(2,1)S(1)} %pad_maximum_fusion.11), channel_id=1, source_target_pairs={{0,7},{1,0},{2,1},{3,2},{4,3},{5,4},{6,5},{7,6},{8,15},{9,8},{10,9... | collective-permute-start | bytes 331784 | tf_op jit(solution)/shard_map/ppermute | solution.py:99
  199.6 6.4 %collective-permute-start.53 = (bf16[3,3,32,192]{3,2,1,0:T(8,128)(2,1)S(1)}, bf16[3,3,32,192]{3,2,1,0:T(8,128)(2,1)S(1)}, u32[]{:S(2)}, u32[]{:S(2)}) collective-permute-start(bf16[3,3,32,192]{3,2,1,0:T(8,128)(2,1)S(1)} %pad_maximum_fusion.11), channel_id=1, source_target_pairs={{0,1},{1,2},{2,3},{3,4},{4,5},{5,6},{6,7},{7,0},{8,9},{9,10},{10,1... | collective-permute-start | bytes 331784 | tf_op jit(solution)/shard_map/ppermute | solution.py:99
  206.9 5.0 %collective-permute-start.55 = (bf16[3,32,192]{2,1,0:T(8,128)(2,1)S(1)}, bf16[3,32,192]{2,1,0:T(8,128)(2,1)S(1)}, u32[]{:S(2)}, u32[]{:S(2)}) collective-permute-start(bf16[3,32,192]{2,1,0:T(8,128)(2,1)S(1)} %get-tuple-element.11), channel_id=1, source_target_pairs={{0,8},{8,16},{16,24},{24,0},{1,9},{9,17},{17,25},{25,1},{2,10},{10... | collective-permute-start | bytes 110600 | tf_op jit(solution)/shard_map/ppermute | solution.py:99
  212.9 4.1 %collective-permute-start.58 = (bf16[3,3,32,192]{3,2,1,0:T(8,128)(2,1)S(1)}, bf16[3,3,32,192]{3,2,1,0:T(8,128)(2,1)S(1)}, u32[]{:S(2)}, u32[]{:S(2)}) collective-permute-start(bf16[3,3,32,192]{3,2,1,0:T(8,128)(2,1)S(1)} %pad_maximum_fusion.12), channel_id=1, source_target_pairs={{0,7},{1,0},{2,1},{3,2},{4,3},{5,4},{6,5},{7,6},{8,15},{9,8},{10,9... | collective-permute-start | bytes 331784 | tf_op jit(solution)/shard_map/ppermute | solution.py:99
  213.2 6.4 %collective-permute-start.57 = (bf16[3,3,32,192]{3,2,1,0:T(8,128)(2,1)S(1)}, bf16[3,3,32,192]{3,2,1,0:T(8,128)(2,1)S(1)}, u32[]{:S(2)}, u32[]{:S(2)}) collective-permute-start(bf16[3,3,32,192]{3,2,1,0:T(8,128)(2,1)S(1)} %pad_maximum_fusion.12), channel_id=1, source_target_pairs={{0,1},{1,2},{2,3},{3,4},{4,5},{5,6},{6,7},{7,0},{8,9},{9,10},{10,1... | collective-permute-start | bytes 331784 | tf_op jit(solution)/shard_map/ppermute | solution.py:99
  220.5 5.0 %collective-permute-start.59 = (bf16[3,32,192]{2,1,0:T(8,128)(2,1)S(1)}, bf16[3,32,192]{2,1,0:T(8,128)(2,1)S(1)}, u32[]{:S(2)}, u32[]{:S(2)}) collective-permute-start(bf16[3,32,192]{2,1,0:T(8,128)(2,1)S(1)} %get-tuple-element.9), channel_id=1, source_target_pairs={{0,8},{8,16},{16,24},{24,0},{1,9},{9,17},{17,25},{25,1},{2,10},{10... | collective-permute-start | bytes 110600 | tf_op jit(solution)/shard_map/ppermute | solution.py:99
  222.2 4.1 %collective-permute-start.60 = (bf16[3,32,192]{2,1,0:T(8,128)(2,1)S(1)}, bf16[3,32,192]{2,1,0:T(8,128)(2,1)S(1)}, u32[]{:S(2)}, u32[]{:S(2)}) collective-permute-start(bf16[3,32,192]{2,1,0:T(8,128)(2,1)S(1)} %get-tuple-element.9), channel_id=1, source_target_pairs={{0,24},{8,0},{16,8},{24,16},{1,25},{9,1},{17,9},{25,17},{2,26},{10... | collective-permute-start | bytes 110600 | tf_op jit(solution)/shard_map/ppermute | solution.py:99
  226.3 4.1 %collective-permute-start.62 = (bf16[3,3,32,192]{3,2,1,0:T(8,128)(2,1)S(1)}, bf16[3,3,32,192]{3,2,1,0:T(8,128)(2,1)S(1)}, u32[]{:S(2)}, u32[]{:S(2)}) collective-permute-start(bf16[3,3,32,192]{3,2,1,0:T(8,128)(2,1)S(1)} %pad_maximum_fusion.13), channel_id=1, source_target_pairs={{0,7},{1,0},{2,1},{3,2},{4,3},{5,4},{6,5},{7,6},{8,15},{9,8},{10,9... | collective-permute-start | bytes 331784 | tf_op jit(solution)/shard_map/ppermute | solution.py:99
  226.9 6.4 %collective-permute-start.61 = (bf16[3,3,32,192]{3,2,1,0:T(8,128)(2,1)S(1)}, bf16[3,3,32,192]{3,2,1,0:T(8,128)(2,1)S(1)}, u32[]{:S(2)}, u32[]{:S(2)}) collective-permute-start(bf16[3,3,32,192]{3,2,1,0:T(8,128)(2,1)S(1)} %pad_maximum_fusion.13), channel_id=1, source_target_pairs={{0,1},{1,2},{2,3},{3,4},{4,5},{5,6},{6,7},{7,0},{8,9},{9,10},{10,1... | collective-permute-start | bytes 331784 | tf_op jit(solution)/shard_map/ppermute | solution.py:99
  234.3 5.0 %collective-permute-start.63 = (bf16[3,32,192]{2,1,0:T(8,128)(2,1)S(1)}, bf16[3,32,192]{2,1,0:T(8,128)(2,1)S(1)}, u32[]{:S(2)}, u32[]{:S(2)}) collective-permute-start(bf16[3,32,192]{2,1,0:T(8,128)(2,1)S(1)} %get-tuple-element.45), channel_id=1, source_target_pairs={{0,8},{8,16},{16,24},{24,0},{1,9},{9,17},{17,25},{25,1},{2,10},{10... | collective-permute-start | bytes 110600 | tf_op jit(solution)/shard_map/ppermute | solution.py:99
  240.6 4.1 %collective-permute-start.66 = (bf16[3,3,32,192]{3,2,1,0:T(8,128)(2,1)S(1)}, bf16[3,3,32,192]{3,2,1,0:T(8,128)(2,1)S(1)}, u32[]{:S(2)}, u32[]{:S(2)}) collective-permute-start(bf16[3,3,32,192]{3,2,1,0:T(8,128)(2,1)S(1)} %pad_maximum_fusion.14), channel_id=1, source_target_pairs={{0,7},{1,0},{2,1},{3,2},{4,3},{5,4},{6,5},{7,6},{8,15},{9,8},{10,9... | collective-permute-start | bytes 331784 | tf_op jit(solution)/shard_map/ppermute | solution.py:99
  241.4 6.4 %collective-permute-start.65 = (bf16[3,3,32,192]{3,2,1,0:T(8,128)(2,1)S(1)}, bf16[3,3,32,192]{3,2,1,0:T(8,128)(2,1)S(1)}, u32[]{:S(2)}, u32[]{:S(2)}) collective-permute-start(bf16[3,3,32,192]{3,2,1,0:T(8,128)(2,1)S(1)} %pad_maximum_fusion.14), channel_id=1, source_target_pairs={{0,1},{1,2},{2,3},{3,4},{4,5},{5,6},{6,7},{7,0},{8,9},{9,10},{10,1... | collective-permute-start | bytes 331784 | tf_op jit(solution)/shard_map/ppermute | solution.py:99
  248.7 5.0 %collective-permute-start.67 = (bf16[3,32,192]{2,1,0:T(8,128)(2,1)S(1)}, bf16[3,32,192]{2,1,0:T(8,128)(2,1)S(1)}, u32[]{:S(2)}, u32[]{:S(2)}) collective-permute-start(bf16[3,32,192]{2,1,0:T(8,128)(2,1)S(1)} %get-tuple-element.47), channel_id=1, source_target_pairs={{0,8},{8,16},{16,24},{24,0},{1,9},{9,17},{17,25},{25,1},{2,10},{10... | collective-permute-start | bytes 110600 | tf_op jit(solution)/shard_map/ppermute | solution.py:99
  254.0 4.1 %collective-permute-start.70 = (bf16[3,3,32,192]{3,2,1,0:T(8,128)(2,1)S(1)}, bf16[3,3,32,192]{3,2,1,0:T(8,128)(2,1)S(1)}, u32[]{:S(2)}, u32[]{:S(2)}) collective-permute-start(bf16[3,3,32,192]{3,2,1,0:T(8,128)(2,1)S(1)} %pad_maximum_fusion.15), channel_id=1, source_target_pairs={{0,7},{1,0},{2,1},{3,2},{4,3},{5,4},{6,5},{7,6},{8,15},{9,8},{10,9... | collective-permute-start | bytes 331784 | tf_op jit(solution)/shard_map/ppermute | solution.py:99
  254.9 6.4 %collective-permute-start.69 = (bf16[3,3,32,192]{3,2,1,0:T(8,128)(2,1)S(1)}, bf16[3,3,32,192]{3,2,1,0:T(8,128)(2,1)S(1)}, u32[]{:S(2)}, u32[]{:S(2)}) collective-permute-start(bf16[3,3,32,192]{3,2,1,0:T(8,128)(2,1)S(1)} %pad_maximum_fusion.15), channel_id=1, source_target_pairs={{0,1},{1,2},{2,3},{3,4},{4,5},{5,6},{6,7},{7,0},{8,9},{9,10},{10,1... | collective-permute-start | bytes 331784 | tf_op jit(solution)/shard_map/ppermute | solution.py:99
  265.1 4.6 %collective-permute-start.73 = (f32[32,32]{0,1:T(8,128)S(1)}, f32[32,32]{0,1:T(8,128)S(1)}, u32[]{:S(2)}, u32[]{:S(2)}) collective-permute-start(f32[32,32]{0,1:T(8,128)S(1)} %convolution_bitcast_fusion.64), channel_id=1, source_target_pairs={{0,24},{8,16},{16,8},{24,0},{1,25},{9,17},{17,9},{25,1},{2,26},{10... | collective-permute-start | bytes 12296 | tf_op jit(solution)/shard_map/ppermute | solution.py:58
  271.0 4.6 %collective-permute-start.75 = (f32[32,32]{0,1:T(8,128)S(1)}, f32[32,32]{0,1:T(8,128)S(1)}, u32[]{:S(2)}, u32[]{:S(2)}) collective-permute-start(f32[32,32]{0,1:T(8,128)S(1)} %add.438), channel_id=1, source_target_pairs={{0,2},{1,3},{2,0},{3,1},{4,6},{5,7},{6,4},{7,5},{8,10},{9,11},{10,... | collective-permute-start | bytes 12296 | tf_op jit(solution)/shard_map/ppermute | solution.py:58
  271.0 4.7 %collective-permute-start.76 = (f32[32,32]{0,1:T(8,128)S(1)}, f32[32,32]{0,1:T(8,128)S(1)}, u32[]{:S(2)}, u32[]{:S(2)}) collective-permute-start(f32[32,32]{0,1:T(8,128)S(1)} %add.438), channel_id=1, source_target_pairs={{0,4},{1,5},{2,6},{3,7},{4,0},{5,1},{6,2},{7,3},{8,12},{9,13},{10,... | collective-permute-start | bytes 12296 | tf_op jit(solution)/shard_map/ppermute | solution.py:58
  272.1 5.5 %collective-permute-start.77 = (f32[32,32]{0,1:T(8,128)S(1)}, f32[32,32]{0,1:T(8,128)S(1)}, u32[]{:S(2)}, u32[]{:S(2)}) collective-permute-start(f32[32,32]{0,1:T(8,128)S(1)} %add.438), channel_id=1, source_target_pairs={{0,6},{1,7},{2,4},{3,5},{4,2},{5,3},{6,0},{7,1},{8,14},{9,15},{10,... | collective-permute-start | bytes 12296 | tf_op jit(solution)/shard_map/ppermute | solution.py:58
  (17 other events, 164.5 us)
